TPU v7x, 256 devices: a whole 4x4x8 slice. The times are simulated.
256 devices in a mesh: row: 8 (over z), col: 32 (over y, x, core).
Axes of the slice: x: 4, y: 4, z: 8, core: 2. Of those that a mesh axis runs over, the one named last changes fastest.
Arguments:
- hidden_in: bfloat16 [3072, 2, 7168], P('row', None, 'col'), may hold values from -16 to 16
- final_gain: float32 [2, 7168], P(None, 'col'), may hold values from 0.25 to 1.75
- unembed: bfloat16 [7168, 32768], P('row', 'col'), may hold values from -2 to 2
- lengths: int32 [16], replicated, may hold values from 1 to 768, 3072 in all
- targets: int32 [3072], P('row'), may hold values from 0 to 32767
- owner: int32 [16], replicated, may hold values from 0 to 31
Outputs:
- owner_table: float32 [32, 3, 16], P('col')
Inputs may be any that keep to these rules, and one draw needn't show every extreme that they name: The lengths sum to 3072; the longest is exactly 768.
All inputs are finite; a program needn't handle non-finite values.
Results may differ from a plain program's by a relative error of at most 0.00056.
Values may be sent and summed in bfloat16 or wider, within the bound.
No kernel may reach another device: no remote copies, remote signals or barrier semaphores. Data moves between devices by JAX's collectives and lax.ppermute only.
A program may use at most 128 MiB of HBM per device.

v0:
```python
import jax
import jax.numpy as jnp
from jax import lax
from jax.sharding import PartitionSpec as P

D = 7168


EPS = 1e-05


def per_device(hidden_in, final_gain, unembed, lengths, targets, owner):
    tok_rows = hidden_in.shape[0]
    vocab_cols = unembed.shape[1]
    col_index = lax.axis_index("col")
    row_index = lax.axis_index("row")
    stream = hidden_in.astype(jnp.float32)
    square_sum = lax.psum(jnp.sum(stream * stream, axis=2), "col")
    normed = (stream * lax.rsqrt(square_sum[:, :, None] / D + EPS) * final_gain[None, :, :]).astype(
        jnp.bfloat16
    )
    features = lax.all_gather(normed, "col", axis=2, tiled=True)
    logits = jnp.einsum(
        "tmd,dv->tmv",
        features,
        lax.all_gather(unembed, "row", axis=0, tiled=True),
        preferred_element_type=jnp.float32,
    )
    row_max = jnp.max(logits, axis=2)
    exp_total = jnp.sum(jnp.exp(logits - row_max[:, :, None]), axis=2)
    vocab_ids = col_index * vocab_cols + jnp.arange(vocab_cols, dtype=jnp.int32)
    picked = jnp.sum(
        jnp.where(targets[:, None, None] == vocab_ids[None, None, :], logits, 0.0), axis=2
    )
    max_logit = lax.pmax(row_max, "col")
    exp_total, picked = lax.psum((exp_total * jnp.exp(row_max - max_logit), picked), "col")
    logp = picked - (max_logit + jnp.log(exp_total))
    log_ratio = logp[:, 0] - logp[:, 1]
    token_index = row_index * tok_rows + jnp.arange(tok_rows, dtype=jnp.int32)
    seq_ends = jnp.cumsum(lengths)
    segment = jnp.sum((seq_ends[None, :] <= token_index[:, None]).astype(jnp.int32), axis=1)
    member = segment[:, None] == jnp.arange(lengths.shape[0], dtype=jnp.int32)[None, :]
    ratio_sums = jnp.sum(jnp.where(member, log_ratio[:, None], 0.0), axis=0)
    squares = jnp.sum(jnp.where(member, (log_ratio * log_ratio)[:, None], 0.0), axis=0)
    ratio_max = jnp.max(jnp.where(member, log_ratio[:, None], -1e30), axis=0)
    ratio_sums, squares = lax.psum((ratio_sums, squares), "row")
    ratio_max = lax.pmax(ratio_max, "row")
    seq_stats = jnp.stack([ratio_sums, squares, ratio_max])
    owned = owner == col_index
    return jnp.where(owned[None, :], seq_stats, 0.0)[None]


def solution(mesh):
    in_specs = (P("row", None, "col"), P(None, "col"), P("row", "col"), P(), P("row"), P())
    out_specs = P("col", None, None)
    return jax.shard_map(
        per_device, mesh=mesh, in_specs=in_specs, out_specs=out_specs, check_vma=False
    )
```

profile of v0, /device:TPU:2, one launch (start us, length us, event | category | flops | bytes accessed | tf_op | source)
XLA Modules:
  0.0 475.7 jit_solution(16518178330957214767)
XLA Ops:
  6.5 0.0 copy-start.1
  6.5 0.0 copy-start.2
  6.5 0.0 copy-start
  6.5 0.0 all-gather.3.cloned.1.call-start
  6.5 1.1 fusion.2
  7.6 62.3 %psum.35 = f32[384,2]{0,1:T(2,128)S(1)} all-reduce(f32[384,2]{0,1:T(2,128)S(1)} %fusion.2), channel_id=1, replica_groups=mesh['row'=8,'col'=32] {'col'}, use_global_device_ids=true, to_apply=%region_3.0 | all-reduce | flops 768 | bytes 6144 | tf_op jit(solution)/shard_map/psum | solution.py:18
  69.9 1.9 fusion.4
  71.8 0.0 all-gather.3.cloned.1.call-update
  71.8 0.0 all-gather.5.cloned.1.call-start
  71.9 0.7 all-gather.5.cloned.1.call-update
  72.6 0.0 copy-done.1
  72.6 0.1 copy.11
  72.7 0.1 reduce
  72.9 0.1 convert_reduce_fusion
  72.9 0.0 copy-done.2
  73.0 0.5 broadcast_compare_fusion.1
  73.5 0.0 copy-done
  73.5 0.3 broadcast_compare_fusion
  73.8 65.1 %all-gather.3.cloned.1.call-done = bf16[384,2,7168]{0,2,1:T(8,128)(2,1)} async-done(((bf16[384,2,224]{0,2,1:T(8,128)(2,1)}), bf16[384,2,7168]{0,2,1:T(8,128)(2,1)}) %all-gather.3.cloned.1.call-update) | async-done | bytes 11010064 | tf_op jit(solution)/shard_map/all_gather | solution.py:22
  138.8 154.5 %all-gather.5.cloned.1.call-done = bf16[7168,1024]{1,0:T(8,128)(2,1)} async-done(((bf16[896,1024]{1,0:T(8,128)(2,1)}), bf16[7168,1024]{1,0:T(8,128)(2,1)}) %all-gather.5.cloned.1.call-update) | async-done | bytes 14680080 | tf_op jit(solution)/shard_map/all_gather | solution.py:26
  293.3 17.2 %fusion.6 = (f32[384,2]{0,1:T(2,128)S(1)}, f32[384,2,1024]{2,0,1:T(8,128)S(1)}) fusion(bf16[384,2,7168]{0,2,1:T(8,128)(2,1)} %all-gather.3.cloned.1.call-done, bf16[7168,1024]{1,0:T(8,128)(2,1)} %all-gather.5.cloned.1.call-done), kind=kOutput, calls=%fused_computation.25 | convolution fusion | flops 11275074560 | bytes 28838912 | tf_op jit(solution)/shard_map/tmd,dv->tmv/dot_general | solution.py:23
  310.6 61.8 %pmax.14 = f32[384,2]{0,1:T(2,128)S(1)} all-reduce(f32[384,2]{0,1:T(2,128)S(1)} %get-tuple-element.16), channel_id=1, replica_groups=mesh['row'=8,'col'=32] {'col'}, use_global_device_ids=true, to_apply=%region_7.8 | all-reduce | flops 768 | bytes 6144 | tf_op jit(solution)/shard_map/pmax | solution.py:35
  372.3 1.1 exponential_reduce_fusion
  373.5 63.6 %all-reduce = (f32[384,2]{0,1:T(2,128)S(1)}, f32[384,2]{0,1:T(2,128)S(1)}) all-reduce(f32[384,2]{0,1:T(2,128)S(1)} %get-tuple-element.6, f32[384,2]{0,1:T(2,128)S(1)} %exponential_multiply_fusion), channel_id=1, replica_groups=mesh['row'=8,'col'=32] {'col'}, use_global_device_ids=true, to_apply=%region_5.6 | all-reduce | flops 1536 | bytes 12288 | tf_op jit(solution)/shard_map/psum | solution.py:36
  437.1 0.2 select_reduce_fusion.3
  437.3 15.5 %pmax.15 = f32[1,1,16]{2,1,0:T(1,128)S(1)} all-reduce(f32[1,1,16]{2,1,0:T(1,128)S(1)} %bitcast.13), channel_id=1, replica_groups=mesh['row'=8,'col'=32] {'row'}, use_global_device_ids=true, to_apply=%region_15.16 | all-reduce | flops 16 | bytes 128 | tf_op jit(solution)/shard_map/pmax | solution.py:47
  452.8 14.8 %all-reduce.1 = (f32[1,1,16]{2,1,0:T(1,128)S(1)}, f32[1,1,16]{2,1,0:T(1,128)S(1)}) all-reduce(f32[1,1,16]{2,1,0:T(1,128)S(1)} %bitcast.12, f32[1,1,16]{2,1,0:T(1,128)S(1)} %bitcast.11), channel_id=1, replica_groups=mesh['row'=8,'col'=32] {'row'}, use_global_device_ids=true, to_apply=%region_13.14 | all-reduce | flops 32 | bytes 256 | tf_op jit(solution)/shard_map/psum | solution.py:46
  467.6 0.7 maximum_select_fusion
  468.3 0.6 copy.12
  (7 shorter events, 0.1 us)
Async XLA Ops:
  6.5 66.1 %copy-start.1 = (s32[16]{0:T(128)S(1)}, s32[16]{0:T(128)}, u32[]{:S(2)}) copy-start(s32[16]{0:T(128)} %param.9) | copy-start | bytes 196
  6.5 66.4 %copy-start.2 = (s32[16]{0:T(128)S(1)}, s32[16]{0:T(128)}, u32[]{:S(2)}) copy-start(s32[16]{0:T(128)} %param.11) | copy-start | bytes 196
  6.5 66.9 %copy-start = (s32[384]{0:T(512)S(1)}, s32[384]{0:T(512)}, u32[]{:S(2)}) copy-start(s32[384]{0:T(512)} %param.10) | copy-start | bytes 4612
  6.5 132.3 %all-gather.3.cloned.1.call-start = ((), (), s32[]{:S(2)}) async-start(), calls=%async_computation | async-start | bytes 11354112 | tf_op jit(solution)/shard_map/all_gather | solution.py:22
  71.8 221.5 %all-gather.5.cloned.1.call-start = ((), (), s32[]{:S(2)}) async-start(), calls=%async_computation.1 | async-start | bytes 16515072 | tf_op jit(solution)/shard_map/all_gather | solution.py:26
Sparse Core Ops, SparseCore 0:
  72.0 66.8 all-gather.2
  140.6 152.6 all-gather.4
where the time goes:
time: 480 us; the launch traced here: 476 us
  waiting for transfers between devices  220 us (46%)
  blocking collectives  218 us (45%)
  matrix products  17.2 us (4%)
  between operations  13.5 us (3%)
  other arithmetic  6.02 us (1%)
    all_gather x1, waiting for transfers between devices, per_device(): lax.all_gather(unembed, 'row', axis=0, tiled=True)  155 us
    all_gather x1, waiting for transfers between devices, per_device(): features = lax.all_gather(normed, 'col', axis=2, tiled=True)  65.1 us
    psum x1, blocking collectives, per_device(): lax.psum((exp_total * jnp.exp(row_max - max_logit), picked), 'col')  63.6 us
    psum x1, blocking collectives, per_device(): square_sum = lax.psum(jnp.sum(stream * stream, axis=2), 'col')  62.3 us
    pmax x1, blocking collectives, per_device(): max_logit = lax.pmax(row_max, 'col')  61.8 us
    dot_general x1, matrix products, per_device(): jnp.einsum('tmd,dv->tmv', features, lax.all_gather(unembed, 'row', axis=0...  17.2 us
    pmax x1, blocking collectives, per_device(): ratio_max = lax.pmax(ratio_max, 'row')  15.5 us
    psum x1, blocking collectives, per_device(): ratio_sums, squares = lax.psum((ratio_sums, squares), 'row')  14.8 us
  transfers between devices with their start and end apart: 2, of which 2 were waited for; matrix products, arithmetic and copies ran while one was open for 0% of the time, Pallas kernels for 0%

commit v1 on v0

v1 whole, which is shorter than its diff:
```python
import jax
import jax.numpy as jnp
from jax import lax
from jax.sharding import PartitionSpec as P

D = 7168


EPS = 1e-05


def per_device(hidden_in, final_gain, unembed, lengths, targets, owner):
    tok_rows = hidden_in.shape[0]
    vocab_cols = unembed.shape[1]
    col_index = lax.axis_index("col")
    row_index = lax.axis_index("row")
    full_unembed = lax.all_gather(unembed, "row", axis=0, tiled=True)
    full_hidden = lax.all_gather(hidden_in, "col", axis=2, tiled=True)
    full_gain = lax.all_gather(final_gain, "col", axis=1, tiled=True)
    stream = full_hidden.astype(jnp.float32)
    mean_square = jnp.sum(stream * stream, axis=2) / D
    features = (stream * lax.rsqrt(mean_square[:, :, None] + EPS) * full_gain[None, :, :]).astype(
        jnp.bfloat16
    )
    logits = jnp.einsum(
        "tmd,dv->tmv", features, full_unembed, preferred_element_type=jnp.float32
    )
    row_max = jnp.max(logits, axis=2)
    exp_total = jnp.sum(jnp.exp(logits - row_max[:, :, None]), axis=2)
    vocab_ids = col_index * vocab_cols + jnp.arange(vocab_cols, dtype=jnp.int32)
    picked = jnp.sum(
        jnp.where(targets[:, None, None] == vocab_ids[None, None, :], logits, 0.0), axis=2
    )
    parts = lax.all_gather(jnp.stack([row_max, exp_total, picked]), "col")
    max_logit = jnp.max(parts[:, 0], axis=0)
    exp_total = jnp.sum(parts[:, 1] * jnp.exp(parts[:, 0] - max_logit[None]), axis=0)
    picked = jnp.sum(parts[:, 2], axis=0)
    logp = picked - (max_logit + jnp.log(exp_total))
    log_ratio = logp[:, 0] - logp[:, 1]
    token_index = row_index * tok_rows + jnp.arange(tok_rows, dtype=jnp.int32)
    seq_ends = jnp.cumsum(lengths)
    segment = jnp.sum((seq_ends[None, :] <= token_index[:, None]).astype(jnp.int32), axis=1)
    member = segment[:, None] == jnp.arange(lengths.shape[0], dtype=jnp.int32)[None, :]
    ratio_sums = jnp.sum(jnp.where(member, log_ratio[:, None], 0.0), axis=0)
    squares = jnp.sum(jnp.where(member, (log_ratio * log_ratio)[:, None], 0.0), axis=0)
    ratio_max = jnp.max(jnp.where(member, log_ratio[:, None], -1e30), axis=0)
    stats = lax.all_gather(jnp.stack([ratio_sums, squares, ratio_max]), "row")
    seq_stats = jnp.stack(
        [jnp.sum(stats[:, 0], axis=0), jnp.sum(stats[:, 1], axis=0), jnp.max(stats[:, 2], axis=0)]
    )
    owned = owner == col_index
    return jnp.where(owned[None, :], seq_stats, 0.0)[None]


def solution(mesh):
    in_specs = (P("row", None, "col"), P(None, "col"), P("row", "col"), P(), P("row"), P())
    out_specs = P("col", None, None)
    return jax.shard_map(
        per_device, mesh=mesh, in_specs=in_specs, out_specs=out_specs, check_vma=False
    )
```

time: 480 us -> 306 us (0.64)
  blocking collectives: 218 us -> 70.3 us
  waiting for transfers between devices: 220 us -> 191 us
    psum x3 -> x0, blocking collectives: 141 us -> none  [the longest x1 63.6 us: per_device(): lax.psum((exp_total * jnp.exp(row_max - max_logit), picked), 'col')]
    pmax x2 -> x0, blocking collectives: 77.3 us -> none  [the longest x1 61.8 us: per_device(): max_logit = lax.pmax(row_max, 'col')]
    all_gather x0 -> x3, blocking collectives: none -> 70.3 us  [the longest x1 24.6 us: per_device(): parts = lax.all_gather(jnp.stack([row_max, exp_total, picked]), 'col')]
    all_gather x2, waiting for transfers between devices: 220 us -> 190 us  [the longest x1 148 us: per_device(): full_unembed = lax.all_gather(unembed, 'row', axis=0, tiled=True)]
    reduce_sum x1 -> x4, other arithmetic: 1.1 us -> 6.51 us  [the longest x1 6.34 us: per_device(): mean_square = jnp.sum(stream * stream, axis=2) / D]
  transfers between devices with their start and end apart: 2 -> 2, of which waited for: 2 -> 2; matrix products, arithmetic and copies ran while one was open for 0% -> 3% of each run, Pallas kernels for 0% -> 0%
where the time goes in v1:
time: 306 us; the launch traced here: 305 us
  waiting for transfers between devices  191 us (62%)
  blocking collectives  70.3 us (23%)
  matrix products  18.9 us (6%)
  between operations  13.5 us (4%)
  other arithmetic  9.79 us (3%)
    all_gather x1, waiting for transfers between devices, per_device(): full_unembed = lax.all_gather(unembed, 'row', axis=0, tiled=True)  148 us
    all_gather x1, waiting for transfers between devices, per_device(): full_hidden = lax.all_gather(hidden_in, 'col', axis=2, tiled=True)  41.9 us
    all_gather x1, blocking collectives, per_device(): parts = lax.all_gather(jnp.stack([row_max, exp_total, picked]), 'col')  24.6 us
    all_gather x1, blocking collectives, per_device(): full_gain = lax.all_gather(final_gain, 'col', axis=1, tiled=True)  24.3 us
    all_gather x1, blocking collectives, per_device(): stats = lax.all_gather(jnp.stack([ratio_sums, squares, ratio_max]), 'row')  21.4 us
    dot_general x1, matrix products, per_device(): jnp.einsum('tmd,dv->tmv', features, full_unembed, preferred_element_type=...  18.9 us
    reduce_sum x1, other arithmetic, per_device(): mean_square = jnp.sum(stream * stream, axis=2) / D  6.34 us
  transfers between devices with their start and end apart: 2, of which 2 were waited for; matrix products, arithmetic and copies ran while one was open for 3% of the time, Pallas kernels for 0%

profile of v1, /device:TPU:2, one launch (start us, length us, event | category | flops | bytes accessed | tf_op | source)
XLA Modules:
  0.0 305.3 jit_solution(1823025273057362841)
XLA Ops:
  6.5 0.0 all-gather.7.cloned.1.call-start
  6.5 0.7 all-gather.7.cloned.1.call-update
  7.3 0.0 all-gather.9.cloned.1.call-start
  7.3 0.7 all-gather.9.cloned.1.call-update
  8.0 24.3 %all-gather.2 = f32[32,224,2]{1,2,0:T(2,128)S(1)} all-gather(f32[1,224,2]{1,2,0:T(2,128)} %bitcast.49), channel_id=1, replica_groups=mesh['row'=8,'col'=32] {'col'}, dimensions={0}, use_global_device_ids=true | all-gather | bytes 59136 | tf_op jit(solution)/shard_map/all_gather | solution.py:19
  32.3 0.1 reshape.144
  32.4 0.7 copy.21
  33.2 0.1 reduce.5
  33.3 0.1 convert_reduce_fusion
  33.4 0.7 broadcast_compare_fusion.1
  34.1 1.0 broadcast_compare_fusion
  35.0 41.9 %all-gather.7.cloned.1.call-done = bf16[384,2,7168]{0,2,1:T(8,128)(2,1)} async-done(((bf16[384,2,224]{0,2,1:T(8,128)(2,1)}), bf16[384,2,7168]{0,2,1:T(8,128)(2,1)}) %all-gather.7.cloned.1.call-update) | async-done | bytes 11010064 | tf_op jit(solution)/shard_map/all_gather | solution.py:18
  76.9 6.3 %fusion = f32[384,2]{0,1:T(2,128)S(1)} fusion(bf16[384,2,7168]{0,2,1:T(8,128)(2,1)} %all-gather.7.cloned.1.call-done), kind=kLoop, calls=%fused_computation.2 | loop fusion | flops 16514304 | bytes 11013120 | tf_op jit(solution)/shard_map/reduce_sum | solution.py:21
  83.3 148.2 %all-gather.9.cloned.1.call-done = bf16[7168,1024]{1,0:T(8,128)(2,1)} async-done(((bf16[896,1024]{1,0:T(8,128)(2,1)}), bf16[7168,1024]{1,0:T(8,128)(2,1)}) %all-gather.9.cloned.1.call-update) | async-done | bytes 14680080 | tf_op jit(solution)/shard_map/all_gather | solution.py:17
  231.4 18.9 %fusion.12 = (f32[384,2]{0,1:T(2,128)S(1)}, f32[384,2,1024]{2,0,1:T(8,128)S(1)}) fusion(bf16[7168,1024]{1,0:T(8,128)(2,1)} %all-gather.9.cloned.1.call-done, bf16[384,2,7168]{0,2,1:T(8,128)(2,1)} %all-gather.7.cloned.1.call-done, f32[2,7168]{1,0:T(2,128)S(1)} %bitcast.42, f32[384,2]{0,1:T(2,128)S(1)} %add_rsqrt_fusion), kind=kOutput, calls=%fused_computation.38 | convolution fusion | flops 11297094656 | bytes 28899328 | tf_op jit(solution)/shard_map/tmd,dv->tmv/dot_general | solution.py:25
  250.3 1.1 exponential_reduce_fusion
  251.4 24.6 %all-gather = f32[96,384,2]{1,2,0:T(2,128)S(1)} all-gather(f32[3,384,2]{1,2,0:T(2,128)S(1)} %pad_maximum_fusion), channel_id=2, replica_groups=mesh['row'=8,'col'=32] {'col'}, dimensions={0}, use_global_device_ids=true | all-gather | bytes 304128 | tf_op jit(solution)/shard_map/all_gather | solution.py:34
  276.0 0.1 bitcast_reduce_fusion
  276.1 0.1 fusion.9
  276.2 0.2 select_reduce_fusion.3
  276.4 21.4 %all-gather.3 = f32[8,3,16]{2,1,0:T(4,128)S(1)} all-gather(f32[1,3,16]{2,1,0:T(4,128)S(1)} %maximum_bitcast_fusion), channel_id=3, replica_groups=mesh['row'=8,'col'=32] {'row'}, dimensions={0}, use_global_device_ids=true | all-gather | bytes 1728 | tf_op jit(solution)/shard_map/all_gather | solution.py:47
  297.9 0.6 copy.25
  (12 shorter events, 0.2 us)
Async XLA Ops:
  6.5 70.4 %all-gather.7.cloned.1.call-start = ((), (), s32[]{:S(2)}) async-start(), calls=%async_computation | async-start | bytes 11354112 | tf_op jit(solution)/shard_map/all_gather | solution.py:18
  7.3 224.2 %all-gather.9.cloned.1.call-start = ((), (), s32[]{:S(2)}) async-start(), calls=%async_computation.1 | async-start | bytes 16515072 | tf_op jit(solution)/shard_map/all_gather | solution.py:17
Sparse Core Ops, SparseCore 0:
  9.9 66.9 all-gather.6
  78.7 152.6 all-gather.8

commit v2 on v1

--- a/solution.py
+++ b/solution.py
@@ -11,10 +11,11 @@
 
 def per_device(hidden_in, final_gain, unembed, lengths, targets, owner):
     tok_rows = hidden_in.shape[0]
-    vocab_cols = unembed.shape[1]
+    shard_rows, vocab_cols = unembed.shape
+    half = vocab_cols // 2
+    n_row = lax.axis_size("row")
     col_index = lax.axis_index("col")
     row_index = lax.axis_index("row")
-    full_unembed = lax.all_gather(unembed, "row", axis=0, tiled=True)
     full_hidden = lax.all_gather(hidden_in, "col", axis=2, tiled=True)
     full_gain = lax.all_gather(final_gain, "col", axis=1, tiled=True)
     stream = full_hidden.astype(jnp.float32)
@@ -22,9 +23,22 @@
     features = (stream * lax.rsqrt(mean_square[:, :, None] + EPS) * full_gain[None, :, :]).astype(
         jnp.bfloat16
     )
-    logits = jnp.einsum(
-        "tmd,dv->tmv", features, full_unembed, preferred_element_type=jnp.float32
-    )
+
+    def block_logits(block, shard):
+        rows = lax.dynamic_slice_in_dim(features, shard * shard_rows, shard_rows, axis=2)
+        return jnp.einsum("tmd,dv->tmv", rows, block, preferred_element_type=jnp.float32)
+
+    forward = [(i, (i + 1) % n_row) for i in range(n_row)]
+    backward = [(i, (i - 1) % n_row) for i in range(n_row)]
+    left, right = unembed[:, :half], unembed[:, half:]
+    logits_left = block_logits(left, row_index)
+    logits_right = block_logits(right, row_index)
+    for step in range(1, n_row):
+        left = lax.ppermute(left, "row", forward)
+        right = lax.ppermute(right, "row", backward)
+        logits_left = logits_left + block_logits(left, (row_index - step) % n_row)
+        logits_right = logits_right + block_logits(right, (row_index + step) % n_row)
+    logits = jnp.concatenate([logits_left, logits_right], axis=2)
     row_max = jnp.max(logits, axis=2)
     exp_total = jnp.sum(jnp.exp(logits - row_max[:, :, None]), axis=2)
     vocab_ids = col_index * vocab_cols + jnp.arange(vocab_cols, dtype=jnp.int32)

time: 306 us -> 273 us (0.89)
  waiting for transfers between devices: 191 us -> 93.4 us
  local copies, waits for them, and re-layouts: 1.43 us -> 34 us
  starting transfers between devices: 0.04 us -> 25.6 us
  matrix products: 18.9 us -> 23.6 us
    all_gather x1 -> x0, waiting for transfers between devices: 148 us -> none  [per_device(): full_unembed = lax.all_gather(unembed, 'row', axis=0, tiled=True)]
    ppermute x0 -> x14, waiting for transfers between devices: none -> 93.3 us  [the longest x7 93.3 us: per_device(): left = lax.ppermute(left, 'row', forward)]
    all_gather x1, waiting for transfers between devices: 41.9 us -> 0.01 us  [per_device(): full_hidden = lax.all_gather(hidden_in, 'col', axis=2, tiled=True)]
    all_gather x0 -> x1, local copies, waits for them, and re-layouts: none -> 27.5 us  [per_device(): full_hidden = lax.all_gather(hidden_in, 'col', axis=2, tiled=True)]
    ppermute x0 -> x14, starting transfers between devices: none -> 25.6 us  [the longest x7 23.5 us: per_device(): right = lax.ppermute(right, 'row', backward)]
    dot_general x1 -> x16, matrix products: 18.9 us -> 23.6 us  [block_logits(): jnp.einsum('tmd,dv->tmv', rows, block, preferred_element_type=jnp.float32)]
    unnamed x1 -> x46, local copies, waits for them, and re-layouts: 0.13 us -> 4.29 us
    convert_element_type x0 -> x1, other arithmetic: none -> 3.15 us  [per_device(): (stream * lax.rsqrt(mean_square[:, :, None] + EPS) * full_gain[None, :, :...]
  transfers between devices with their start and end apart: 2 -> 15, of which waited for: 2 -> 5; matrix products, arithmetic and copies ran while one was open for 3% -> 22% of each run, Pallas kernels for 0% -> 0%
where the time goes in v2:
time: 273 us; the launch traced here: 271 us
  waiting for transfers between devices  93.4 us (34%)
  blocking collectives  69.2 us (25%)
  local copies, waits for them, and re-layouts  34 us (12%)
  starting transfers between devices  25.6 us (9%)
  matrix products  23.6 us (9%)
  between operations  13.8 us (5%)
  other arithmetic  11.7 us (4%)
    ppermute x7, waiting for transfers between devices, per_device(): left = lax.ppermute(left, 'row', forward)  93.3 us
    all_gather x1, local copies, waits for them, and re-layouts, per_device(): full_hidden = lax.all_gather(hidden_in, 'col', axis=2, tiled=True)  27.5 us
    all_gather x1, blocking collectives, per_device(): full_gain = lax.all_gather(final_gain, 'col', axis=1, tiled=True)  24.6 us
    dot_general x16, matrix products, block_logits(): jnp.einsum('tmd,dv->tmv', rows, block, preferred_element_type=jnp.float32)  23.6 us
    ppermute x7, starting transfers between devices, per_device(): right = lax.ppermute(right, 'row', backward)  23.5 us
    all_gather x1, blocking collectives, per_device(): parts = lax.all_gather(jnp.stack([row_max, exp_total, picked]), 'col')  22.8 us
    all_gather x1, blocking collectives, per_device(): stats = lax.all_gather(jnp.stack([ratio_sums, squares, ratio_max]), 'row')  21.8 us
    reduce_sum x1, other arithmetic, per_device(): mean_square = jnp.sum(stream * stream, axis=2) / D  6.49 us
  transfers between devices with their start and end apart: 15, of which 5 were waited for; matrix products, arithmetic and copies ran while one was open for 22% of the time, Pallas kernels for 0%

profile of v2, /device:TPU:2, one launch (start us, length us, event | category | flops | bytes accessed | tf_op | source)
XLA Modules:
  0.0 271.3 jit_solution(8542437442919710231)
XLA Ops:
  6.5 2.0 copy.23
  8.6 1.6 fusion.71
  10.2 2.0 collective-permute-start
  12.2 4.0 %collective-permute-start.7 = (bf16[896,512]{1,0:T(8,128)(2,1)S(1)}, bf16[896,512]{1,0:T(8,128)(2,1)S(1)}, u32[]{:S(2)}, u32[]{:S(2)}) collective-permute-start(bf16[896,512]{1,0:T(8,128)(2,1)S(1)} %get-tuple-element.16), channel_id=1, source_target_pairs={{0,224},{32,0},{64,32},{96,64},{128,96},{160,128},{192,160},{224,1... | collective-permute-start | bytes 2752520 | tf_op jit(solution)/shard_map/ppermute | solution.py:38
  16.2 20.3 %collective-permute-done = bf16[896,512]{1,0:T(8,128)(2,1)S(1)} collective-permute-done((bf16[896,512]{1,0:T(8,128)(2,1)S(1)}, bf16[896,512]{1,0:T(8,128)(2,1)S(1)}, u32[]{:S(2)}, u32[]{:S(2)}) %collective-permute-start) | collective-permute-done | bytes 917536 | tf_op jit(solution)/shard_map/ppermute | solution.py:37
  36.5 3.2 %collective-permute-start.8 = (bf16[896,512]{1,0:T(8,128)(2,1)S(1)}, bf16[896,512]{1,0:T(8,128)(2,1)S(1)}, u32[]{:S(2)}, u32[]{:S(2)}) collective-permute-start(bf16[896,512]{1,0:T(8,128)(2,1)S(1)} %collective-permute-done.7), channel_id=1, source_target_pairs={{0,224},{32,0},{64,32},{96,64},{128,96},{160,128},{192,160},{224,1... | collective-permute-start | bytes 2752520 | tf_op jit(solution)/shard_map/ppermute | solution.py:38
  39.7 19.5 %collective-permute-done.1 = bf16[896,512]{1,0:T(8,128)(2,1)S(1)} collective-permute-done((bf16[896,512]{1,0:T(8,128)(2,1)S(1)}, bf16[896,512]{1,0:T(8,128)(2,1)S(1)}, u32[]{:S(2)}, u32[]{:S(2)}) %collective-permute-start.1) | collective-permute-done | bytes 917536 | tf_op jit(solution)/shard_map/ppermute | solution.py:37
  59.2 3.2 %collective-permute-start.9 = (bf16[896,512]{1,0:T(8,128)(2,1)S(1)}, bf16[896,512]{1,0:T(8,128)(2,1)S(1)}, u32[]{:S(2)}, u32[]{:S(2)}) collective-permute-start(bf16[896,512]{1,0:T(8,128)(2,1)S(1)} %collective-permute-done.8), channel_id=1, source_target_pairs={{0,224},{32,0},{64,32},{96,64},{128,96},{160,128},{192,160},{224,1... | collective-permute-start | bytes 2752520 | tf_op jit(solution)/shard_map/ppermute | solution.py:38
  62.4 18.7 %collective-permute-done.2 = bf16[896,512]{1,0:T(8,128)(2,1)S(1)} collective-permute-done((bf16[896,512]{1,0:T(8,128)(2,1)S(1)}, bf16[896,512]{1,0:T(8,128)(2,1)S(1)}, u32[]{:S(2)}, u32[]{:S(2)}) %collective-permute-start.2) | collective-permute-done | bytes 917536 | tf_op jit(solution)/shard_map/ppermute | solution.py:37
  81.2 3.3 %collective-permute-start.10 = (bf16[896,512]{1,0:T(8,128)(2,1)S(1)}, bf16[896,512]{1,0:T(8,128)(2,1)S(1)}, u32[]{:S(2)}, u32[]{:S(2)}) collective-permute-start(bf16[896,512]{1,0:T(8,128)(2,1)S(1)} %collective-permute-done.9), channel_id=1, source_target_pairs={{0,224},{32,0},{64,32},{96,64},{128,96},{160,128},{192,160},{224,1... | collective-permute-start | bytes 2752520 | tf_op jit(solution)/shard_map/ppermute | solution.py:38
  84.5 17.8 %collective-permute-done.3 = bf16[896,512]{1,0:T(8,128)(2,1)S(1)} collective-permute-done((bf16[896,512]{1,0:T(8,128)(2,1)S(1)}, bf16[896,512]{1,0:T(8,128)(2,1)S(1)}, u32[]{:S(2)}, u32[]{:S(2)}) %collective-permute-start.3) | collective-permute-done | bytes 917536 | tf_op jit(solution)/shard_map/ppermute | solution.py:37
  102.3 3.3 %collective-permute-start.11 = (bf16[896,512]{1,0:T(8,128)(2,1)S(1)}, bf16[896,512]{1,0:T(8,128)(2,1)}, u32[]{:S(2)}, u32[]{:S(2)}) collective-permute-start(bf16[896,512]{1,0:T(8,128)(2,1)S(1)} %collective-permute-done.10), channel_id=1, source_target_pairs={{0,224},{32,0},{64,32},{96,64},{128,96},{160,128},{192,160},{224,1... | collective-permute-start | bytes 2752520 | tf_op jit(solution)/shard_map/ppermute | solution.py:38
  105.6 17.0 %collective-permute-done.4 = bf16[896,512]{1,0:T(8,128)(2,1)} collective-permute-done((bf16[896,512]{1,0:T(8,128)(2,1)S(1)}, bf16[896,512]{1,0:T(8,128)(2,1)}, u32[]{:S(2)}, u32[]{:S(2)}) %collective-permute-start.4) | collective-permute-done | bytes 917536 | tf_op jit(solution)/shard_map/ppermute | solution.py:37
  122.7 3.2 %collective-permute-start.12 = (bf16[896,512]{1,0:T(8,128)(2,1)}, bf16[896,512]{1,0:T(8,128)(2,1)}, u32[]{:S(2)}, u32[]{:S(2)}) collective-permute-start(bf16[896,512]{1,0:T(8,128)(2,1)} %collective-permute-done.11), channel_id=1, source_target_pairs={{0,224},{32,0},{64,32},{96,64},{128,96},{160,128},{192,160},{224,1... | collective-permute-start | bytes 2752520 | tf_op jit(solution)/shard_map/ppermute | solution.py:38
  125.9 24.6 %all-gather.2 = f32[32,224,2]{1,2,0:T(2,128)S(1)} all-gather(f32[1,224,2]{1,2,0:T(2,128)S(1)} %bitcast.96), channel_id=1, replica_groups=mesh['row'=8,'col'=32] {'col'}, dimensions={0}, use_global_device_ids=true | all-gather | bytes 59136 | tf_op jit(solution)/shard_map/all_gather | solution.py:20
  151.2 0.3 broadcast_compare_fusion
  151.6 3.2 %collective-permute-start.13 = (bf16[896,512]{1,0:T(8,128)(2,1)}, bf16[896,512]{1,0:T(8,128)(2,1)}, u32[]{:S(2)}, u32[]{:S(2)}) collective-permute-start(bf16[896,512]{1,0:T(8,128)(2,1)} %collective-permute-done.12), channel_id=1, source_target_pairs={{0,224},{32,0},{64,32},{96,64},{128,96},{160,128},{192,160},{224,1... | collective-permute-start | bytes 2752520 | tf_op jit(solution)/shard_map/ppermute | solution.py:38
  154.8 27.5 %copy.24 = bf16[384,2,7168]{2,0,1:T(8,128)(2,1)} copy(bf16[384,2,7168]{0,1,2:T(2,128)(2,1)} %all-gather.6.cloned.1.call-done) | data formatting | bytes 22020096 | tf_op jit(solution)/shard_map/all_gather | solution.py:19
  182.3 6.5 %fusion = f32[384,2]{0,1:T(2,128)S(1)} fusion(bf16[384,2,7168]{2,0,1:T(8,128)(2,1)} %copy.24), kind=kLoop, calls=%fused_computation.2 | loop fusion | flops 16514304 | bytes 11013120 | tf_op jit(solution)/shard_map/reduce_sum | solution.py:22
  188.8 0.8 copy-done
  189.5 3.1 %fusion.2 = bf16[384,2,7168]{2,0,1:T(8,128)(2,1)S(1)} fusion(bf16[384,2,7168]{2,0,1:T(8,128)(2,1)S(1)} %copy-done, f32[2,7168]{1,0:T(2,128)S(1)} %bitcast.89, f32[384,2]{0,1:T(2,128)S(1)} %add_rsqrt_fusion), kind=kLoop, calls=%fused_computation.4 | loop fusion | flops 22020096 | bytes 22080512 | tf_op jit(solution)/shard_map/convert_element_type | solution.py:23
  192.7 1.0 fusion.31
  193.7 1.0 fusion.29
  194.7 2.2 fusion.17
  196.9 2.2 fusion.19
  199.1 1.0 fusion.21
  200.1 0.2 copy-done.16
  200.3 1.0 fusion.23
  201.3 0.2 copy-done.12
  201.5 1.0 fusion.25
  202.5 0.2 copy-done.8
  202.7 1.0 fusion.27
  203.6 0.2 copy-done.14
  203.8 1.0 fusion.10
  204.8 0.2 copy-done.10
  205.0 1.0 fusion.12
  206.0 0.2 copy-done.18
  206.2 1.0 fusion.8
  207.2 0.2 copy-done.6
  207.4 1.0 fusion.14
  208.4 2.2 fusion.6
  210.5 2.2 fusion.4
  212.7 2.5 fusion.72
  215.3 2.5 fusion.73
  217.8 1.1 exponential_reduce_fusion
  218.9 22.8 %all-gather = f32[96,384,2]{1,2,0:T(2,128)S(1)} all-gather(f32[3,384,2]{1,2,0:T(2,128)S(1)} %pad_maximum_fusion.1), channel_id=2, replica_groups=mesh['row'=8,'col'=32] {'col'}, dimensions={0}, use_global_device_ids=true | all-gather | bytes 304128 | tf_op jit(solution)/shard_map/all_gather | solution.py:48
  242.1 21.8 %all-gather.3 = f32[8,3,16]{2,1,0:T(4,128)S(1)} all-gather(f32[1,3,16]{2,1,0:T(4,128)S(1)} %maximum_bitcast_fusion), channel_id=3, replica_groups=mesh['row'=8,'col'=32] {'row'}, dimensions={0}, use_global_device_ids=true | all-gather | bytes 1728 | tf_op jit(solution)/shard_map/all_gather | solution.py:61
  263.9 0.6 copy.27
  (75 shorter events, 1.2 us)
Async XLA Ops:
  6.5 148.2 %all-gather.6.cloned.1.call-start = ((), (), s32[]{:S(2)}) async-start(), calls=%async_computation | async-start | bytes 11354112 | tf_op jit(solution)/shard_map/all_gather | solution.py:19
  8.5 117.4 %copy-start.3 = (f32[2,224]{1,0:T(2,128)S(1)}, f32[2,224]{1,0:T(2,128)}, u32[]{:S(2)}) copy-start(f32[2,224]{1,0:T(2,128)} %param.7) | copy-start | bytes 5380
  8.6 142.1 %copy-start.4 = (s32[16]{0:T(128)S(1)}, s32[16]{0:T(128)}, u32[]{:S(2)}) copy-start(s32[16]{0:T(128)} %param.9) | copy-start | bytes 196
  8.6 142.6 %copy-start.21 = (s32[16]{0:T(128)S(1)}, s32[16]{0:T(128)}, u32[]{:S(2)}) copy-start(s32[16]{0:T(128)} %param.11) | copy-start | bytes 196
  8.6 142.6 %copy-start.2 = (s32[384]{0:T(512)S(1)}, s32[384]{0:T(512)}, u32[]{:S(2)}) copy-start(s32[384]{0:T(512)} %param.10) | copy-start | bytes 4612
  10.2 26.3 %collective-permute-start = (bf16[896,512]{1,0:T(8,128)(2,1)S(1)}, bf16[896,512]{1,0:T(8,128)(2,1)S(1)}, u32[]{:S(2)}, u32[]{:S(2)}) collective-permute-start(bf16[896,512]{1,0:T(8,128)(2,1)S(1)} %get-tuple-element.15), channel_id=1, source_target_pairs={{0,32},{32,64},{64,96},{96,128},{128,160},{160,192},{192,224},{224... | collective-permute-start | bytes 2752520 | tf_op jit(solution)/shard_map/ppermute | solution.py:37
  12.2 24.3 %collective-permute-start.7 = (bf16[896,512]{1,0:T(8,128)(2,1)S(1)}, bf16[896,512]{1,0:T(8,128)(2,1)S(1)}, u32[]{:S(2)}, u32[]{:S(2)}) collective-permute-start(bf16[896,512]{1,0:T(8,128)(2,1)S(1)} %get-tuple-element.16), channel_id=1, source_target_pairs={{0,224},{32,0},{64,32},{96,64},{128,96},{160,128},{192,160},{224,1... | collective-permute-start | bytes 2752520 | tf_op jit(solution)/shard_map/ppermute | solution.py:38
  36.5 118.3 %copy-start.7 = (bf16[896,512]{1,0:T(8,128)(2,1)}, bf16[896,512]{1,0:T(8,128)(2,1)S(1)}, u32[]{:S(2)}) copy-start(bf16[896,512]{1,0:T(8,128)(2,1)S(1)} %collective-permute-done) | copy-start | bytes 2752516
  36.5 22.7 %collective-permute-start.1 = (bf16[896,512]{1,0:T(8,128)(2,1)S(1)}, bf16[896,512]{1,0:T(8,128)(2,1)S(1)}, u32[]{:S(2)}, u32[]{:S(2)}) collective-permute-start(bf16[896,512]{1,0:T(8,128)(2,1)S(1)} %collective-permute-done), channel_id=1, source_target_pairs={{0,32},{32,64},{64,96},{96,128},{128,160},{160,192},{192,224},{224... | collective-permute-start | bytes 2752520 | tf_op jit(solution)/shard_map/ppermute | solution.py:37
  36.5 118.3 %copy-start.5 = (bf16[896,512]{1,0:T(8,128)(2,1)}, bf16[896,512]{1,0:T(8,128)(2,1)S(1)}, u32[]{:S(2)}) copy-start(bf16[896,512]{1,0:T(8,128)(2,1)S(1)} %collective-permute-done.7) | copy-start | bytes 2752516
  36.5 22.7 %collective-permute-start.8 = (bf16[896,512]{1,0:T(8,128)(2,1)S(1)}, bf16[896,512]{1,0:T(8,128)(2,1)S(1)}, u32[]{:S(2)}, u32[]{:S(2)}) collective-permute-start(bf16[896,512]{1,0:T(8,128)(2,1)S(1)} %collective-permute-done.7), channel_id=1, source_target_pairs={{0,224},{32,0},{64,32},{96,64},{128,96},{160,128},{192,160},{224,1... | collective-permute-start | bytes 2752520 | tf_op jit(solution)/shard_map/ppermute | solution.py:38
  59.2 22.0 %copy-start.11 = (bf16[896,512]{1,0:T(8,128)(2,1)}, bf16[896,512]{1,0:T(8,128)(2,1)S(1)}, u32[]{:S(2)}) copy-start(bf16[896,512]{1,0:T(8,128)(2,1)S(1)} %collective-permute-done.1) | copy-start | bytes 2752516
  59.2 22.0 %collective-permute-start.2 = (bf16[896,512]{1,0:T(8,128)(2,1)S(1)}, bf16[896,512]{1,0:T(8,128)(2,1)S(1)}, u32[]{:S(2)}, u32[]{:S(2)}) collective-permute-start(bf16[896,512]{1,0:T(8,128)(2,1)S(1)} %collective-permute-done.1), channel_id=1, source_target_pairs={{0,32},{32,64},{64,96},{96,128},{128,160},{160,192},{192,224},{224... | collective-permute-start | bytes 2752520 | tf_op jit(solution)/shard_map/ppermute | solution.py:37
  59.2 95.6 %copy-start.9 = (bf16[896,512]{1,0:T(8,128)(2,1)}, bf16[896,512]{1,0:T(8,128)(2,1)S(1)}, u32[]{:S(2)}) copy-start(bf16[896,512]{1,0:T(8,128)(2,1)S(1)} %collective-permute-done.8) | copy-start | bytes 2752516
  59.2 22.0 %collective-permute-start.9 = (bf16[896,512]{1,0:T(8,128)(2,1)S(1)}, bf16[896,512]{1,0:T(8,128)(2,1)S(1)}, u32[]{:S(2)}, u32[]{:S(2)}) collective-permute-start(bf16[896,512]{1,0:T(8,128)(2,1)S(1)} %collective-permute-done.8), channel_id=1, source_target_pairs={{0,224},{32,0},{64,32},{96,64},{128,96},{160,128},{192,160},{224,1... | collective-permute-start | bytes 2752520 | tf_op jit(solution)/shard_map/ppermute | solution.py:38
  81.2 21.1 %copy-start.15 = (bf16[896,512]{1,0:T(8,128)(2,1)}, bf16[896,512]{1,0:T(8,128)(2,1)S(1)}, u32[]{:S(2)}) copy-start(bf16[896,512]{1,0:T(8,128)(2,1)S(1)} %collective-permute-done.2) | copy-start | bytes 2752516
  81.2 21.1 %collective-permute-start.3 = (bf16[896,512]{1,0:T(8,128)(2,1)S(1)}, bf16[896,512]{1,0:T(8,128)(2,1)S(1)}, u32[]{:S(2)}, u32[]{:S(2)}) collective-permute-start(bf16[896,512]{1,0:T(8,128)(2,1)S(1)} %collective-permute-done.2), channel_id=1, source_target_pairs={{0,32},{32,64},{64,96},{96,128},{128,160},{160,192},{192,224},{224... | collective-permute-start | bytes 2752520 | tf_op jit(solution)/shard_map/ppermute | solution.py:37
  81.2 3.3 %copy-start.13 = (bf16[896,512]{1,0:T(8,128)(2,1)}, bf16[896,512]{1,0:T(8,128)(2,1)S(1)}, u32[]{:S(2)}) copy-start(bf16[896,512]{1,0:T(8,128)(2,1)S(1)} %collective-permute-done.9) | copy-start | bytes 2752516
  81.2 21.1 %collective-permute-start.10 = (bf16[896,512]{1,0:T(8,128)(2,1)S(1)}, bf16[896,512]{1,0:T(8,128)(2,1)S(1)}, u32[]{:S(2)}, u32[]{:S(2)}) collective-permute-start(bf16[896,512]{1,0:T(8,128)(2,1)S(1)} %collective-permute-done.9), channel_id=1, source_target_pairs={{0,224},{32,0},{64,32},{96,64},{128,96},{160,128},{192,160},{224,1... | collective-permute-start | bytes 2752520 | tf_op jit(solution)/shard_map/ppermute | solution.py:38
  102.3 20.4 %copy-start.19 = (bf16[896,512]{1,0:T(8,128)(2,1)}, bf16[896,512]{1,0:T(8,128)(2,1)S(1)}, u32[]{:S(2)}) copy-start(bf16[896,512]{1,0:T(8,128)(2,1)S(1)} %collective-permute-done.3) | copy-start | bytes 2752516
  102.3 20.4 %collective-permute-start.4 = (bf16[896,512]{1,0:T(8,128)(2,1)S(1)}, bf16[896,512]{1,0:T(8,128)(2,1)}, u32[]{:S(2)}, u32[]{:S(2)}) collective-permute-start(bf16[896,512]{1,0:T(8,128)(2,1)S(1)} %collective-permute-done.3), channel_id=1, source_target_pairs={{0,32},{32,64},{64,96},{96,128},{128,160},{160,192},{192,224},{224... | collective-permute-start | bytes 2752520 | tf_op jit(solution)/shard_map/ppermute | solution.py:37
  102.3 3.3 %copy-start.17 = (bf16[896,512]{1,0:T(8,128)(2,1)}, bf16[896,512]{1,0:T(8,128)(2,1)S(1)}, u32[]{:S(2)}) copy-start(bf16[896,512]{1,0:T(8,128)(2,1)S(1)} %collective-permute-done.10) | copy-start | bytes 2752516
  102.3 20.3 %collective-permute-start.11 = (bf16[896,512]{1,0:T(8,128)(2,1)S(1)}, bf16[896,512]{1,0:T(8,128)(2,1)}, u32[]{:S(2)}, u32[]{:S(2)}) collective-permute-start(bf16[896,512]{1,0:T(8,128)(2,1)S(1)} %collective-permute-done.10), channel_id=1, source_target_pairs={{0,224},{32,0},{64,32},{96,64},{128,96},{160,128},{192,160},{224,1... | collective-permute-start | bytes 2752520 | tf_op jit(solution)/shard_map/ppermute | solution.py:38
  122.7 28.8 %collective-permute-start.5 = (bf16[896,512]{1,0:T(8,128)(2,1)}, bf16[896,512]{1,0:T(8,128)(2,1)}, u32[]{:S(2)}, u32[]{:S(2)}) collective-permute-start(bf16[896,512]{1,0:T(8,128)(2,1)} %collective-permute-done.4), channel_id=1, source_target_pairs={{0,32},{32,64},{64,96},{96,128},{128,160},{160,192},{192,224},{224... | collective-permute-start | bytes 2752520 | tf_op jit(solution)/shard_map/ppermute | solution.py:37
  122.7 28.9 %collective-permute-start.12 = (bf16[896,512]{1,0:T(8,128)(2,1)}, bf16[896,512]{1,0:T(8,128)(2,1)}, u32[]{:S(2)}, u32[]{:S(2)}) collective-permute-start(bf16[896,512]{1,0:T(8,128)(2,1)} %collective-permute-done.11), channel_id=1, source_target_pairs={{0,224},{32,0},{64,32},{96,64},{128,96},{160,128},{192,160},{224,1... | collective-permute-start | bytes 2752520 | tf_op jit(solution)/shard_map/ppermute | solution.py:38
  151.5 61.2 %collective-permute-start.6 = (bf16[896,512]{1,0:T(8,128)(2,1)}, bf16[896,512]{1,0:T(8,128)(2,1)}, u32[]{:S(2)}, u32[]{:S(2)}) collective-permute-start(bf16[896,512]{1,0:T(8,128)(2,1)} %collective-permute-done.5), channel_id=1, source_target_pairs={{0,32},{32,64},{64,96},{96,128},{128,160},{160,192},{192,224},{224... | collective-permute-start | bytes 2752520 | tf_op jit(solution)/shard_map/ppermute | solution.py:37
  151.6 63.7 %collective-permute-start.13 = (bf16[896,512]{1,0:T(8,128)(2,1)}, bf16[896,512]{1,0:T(8,128)(2,1)}, u32[]{:S(2)}, u32[]{:S(2)}) collective-permute-start(bf16[896,512]{1,0:T(8,128)(2,1)} %collective-permute-done.12), channel_id=1, source_target_pairs={{0,224},{32,0},{64,32},{96,64},{128,96},{160,128},{192,160},{224,1... | collective-permute-start | bytes 2752520 | tf_op jit(solution)/shard_map/ppermute | solution.py:38
  182.3 7.3 %copy-start = (bf16[384,2,7168]{2,0,1:T(8,128)(2,1)S(1)}, bf16[384,2,7168]{2,0,1:T(8,128)(2,1)}, u32[]{:S(2)}) copy-start(bf16[384,2,7168]{2,0,1:T(8,128)(2,1)} %copy.24) | copy-start | bytes 33030148
  189.5 3.2 %copy-start.1 = (bf16[896,1024]{1,0:T(8,128)(2,1)S(1)}, bf16[896,1024]{1,0:T(8,128)(2,1)}, u32[]{:S(2)}) copy-start(bf16[896,1024]{1,0:T(8,128)(2,1)} %param.8) | copy-start | bytes 5505028
  196.8 2.3 copy-start.20
  199.1 1.2 copy-start.16
  200.3 1.2 copy-start.12
  201.5 1.2 copy-start.8
  202.7 1.2 copy-start.14
  203.8 1.2 copy-start.10
  205.0 1.2 copy-start.18
  206.2 1.2 copy-start.6
Sparse Core Ops, SparseCore 0:
  9.9 66.7 all-gather.5

commit v3 on v2

--- a/solution.py
+++ b/solution.py
@@ -23,10 +23,10 @@
     features = (stream * lax.rsqrt(mean_square[:, :, None] + EPS) * full_gain[None, :, :]).astype(
         jnp.bfloat16
     )
+    features = features.reshape(tok_rows, 2, n_row, shard_rows).transpose(2, 0, 1, 3)
 
     def block_logits(block, shard):
-        rows = lax.dynamic_slice_in_dim(features, shard * shard_rows, shard_rows, axis=2)
-        return jnp.einsum("tmd,dv->tmv", rows, block, preferred_element_type=jnp.float32)
+        return jnp.einsum("tmd,dv->tmv", features[shard], block, preferred_element_type=jnp.float32)
 
     forward = [(i, (i + 1) % n_row) for i in range(n_row)]
     backward = [(i, (i - 1) % n_row) for i in range(n_row)]
@@ -45,23 +45,22 @@
     picked = jnp.sum(
         jnp.where(targets[:, None, None] == vocab_ids[None, None, :], logits, 0.0), axis=2
     )
-    parts = lax.all_gather(jnp.stack([row_max, exp_total, picked]), "col")
-    max_logit = jnp.max(parts[:, 0], axis=0)
-    exp_total = jnp.sum(parts[:, 1] * jnp.exp(parts[:, 0] - max_logit[None]), axis=0)
-    picked = jnp.sum(parts[:, 2], axis=0)
+    n_col = lax.axis_size("col")
+    parts = lax.all_gather(jnp.stack([row_max, exp_total, picked]), ("row", "col"))
+    parts = parts.reshape(n_row, n_col, 3, tok_rows, 2)
+    max_logit = jnp.max(parts[:, :, 0], axis=1)
+    exp_total = jnp.sum(parts[:, :, 1] * jnp.exp(parts[:, :, 0] - max_logit[:, None]), axis=1)
+    picked = jnp.sum(parts[:, :, 2], axis=1)
     logp = picked - (max_logit + jnp.log(exp_total))
-    log_ratio = logp[:, 0] - logp[:, 1]
-    token_index = row_index * tok_rows + jnp.arange(tok_rows, dtype=jnp.int32)
+    log_ratio = (logp[:, :, 0] - logp[:, :, 1]).reshape(n_row * tok_rows)
+    token_index = jnp.arange(n_row * tok_rows, dtype=jnp.int32)
     seq_ends = jnp.cumsum(lengths)
     segment = jnp.sum((seq_ends[None, :] <= token_index[:, None]).astype(jnp.int32), axis=1)
     member = segment[:, None] == jnp.arange(lengths.shape[0], dtype=jnp.int32)[None, :]
     ratio_sums = jnp.sum(jnp.where(member, log_ratio[:, None], 0.0), axis=0)
     squares = jnp.sum(jnp.where(member, (log_ratio * log_ratio)[:, None], 0.0), axis=0)
     ratio_max = jnp.max(jnp.where(member, log_ratio[:, None], -1e30), axis=0)
-    stats = lax.all_gather(jnp.stack([ratio_sums, squares, ratio_max]), "row")
-    seq_stats = jnp.stack(
-        [jnp.sum(stats[:, 0], axis=0), jnp.sum(stats[:, 1], axis=0), jnp.max(stats[:, 2], axis=0)]
-    )
+    seq_stats = jnp.stack([ratio_sums, squares, ratio_max])
     owned = owner == col_index
     return jnp.where(owned[None, :], seq_stats, 0.0)[None]
 

time: 273 us -> 305 us (1.12)
  waiting for transfers between devices: 93.4 us -> 194 us
  blocking collectives: 69.2 us -> 23.9 us
  local copies, waits for them, and re-layouts: 34 us -> 5.37 us
  other arithmetic: 11.7 us -> 16.8 us
    all_gather x0 -> x1, waiting for transfers between devices: none -> 102 us  [per_device(): lax.all_gather(jnp.stack([row_max, exp_total, picked]), ('row', 'col'))]
    all_gather x2 -> x0, blocking collectives: 44.6 us -> none  [the longest x1 22.8 us: per_device(): parts = lax.all_gather(jnp.stack([row_max, exp_total, picked]), 'col')]
    all_gather x1 -> x0, local copies, waits for them, and re-layouts: 27.5 us -> none  [per_device(): full_hidden = lax.all_gather(hidden_in, 'col', axis=2, tiled=True)]
    reduce_sum x3 -> x2, other arithmetic: 0.17 us -> 3.32 us  [the longest x1 2.02 us: per_device(): jnp.sum(parts[:, :, 1] * jnp.exp(parts[:, :, 0] - max_logit[:, None]), ax...]
  transfers between devices with their start and end apart: 15 -> 16, of which waited for: 5 -> 7; matrix products, arithmetic and copies ran while one was open for 22% -> 11% of each run, Pallas kernels for 0% -> 0%
where the time goes in v3:
time: 305 us; the launch traced here: 304 us
  waiting for transfers between devices  194 us (64%)
  starting transfers between devices  26.3 us (9%)
  blocking collectives  23.9 us (8%)
  matrix products  22.9 us (8%)
  other arithmetic  16.8 us (6%)
  between operations  13.8 us (5%)
  local copies, waits for them, and re-layouts  5.37 us (2%)
    all_gather x1, waiting for transfers between devices, per_device(): lax.all_gather(jnp.stack([row_max, exp_total, picked]), ('row', 'col'))  102 us
    ppermute x7, waiting for transfers between devices, per_device(): left = lax.ppermute(left, 'row', forward)  91.9 us
    ppermute x7, starting transfers between devices, per_device(): right = lax.ppermute(right, 'row', backward)  24.2 us
    all_gather x1, blocking collectives, per_device(): full_gain = lax.all_gather(final_gain, 'col', axis=1, tiled=True)  23.9 us
    dot_general x16, matrix products, block_logits(): jnp.einsum('tmd,dv->tmv', features[shard], block, preferred_element_type=...  22.9 us
    reduce_sum x1, other arithmetic, per_device(): mean_square = jnp.sum(stream * stream, axis=2) / D  6.49 us
  transfers between devices with their start and end apart: 16, of which 7 were waited for; matrix products, arithmetic and copies ran while one was open for 11% of the time, Pallas kernels for 0%

profile of v3, /device:TPU:2, one launch (start us, length us, event | category | flops | bytes accessed | tf_op | source)
XLA Modules:
  0.0 303.5 jit_solution(7634196972265478063)
XLA Ops:
  6.5 0.7 all-gather.5.cloned.1.call-update
  7.3 1.6 fusion.86
  8.9 2.0 collective-permute-start
  10.9 4.0 %collective-permute-start.7 = (bf16[896,512]{1,0:T(8,128)(2,1)S(1)}, bf16[896,512]{1,0:T(8,128)(2,1)S(1)}, u32[]{:S(2)}, u32[]{:S(2)}) collective-permute-start(bf16[896,512]{1,0:T(8,128)(2,1)S(1)} %get-tuple-element.11), channel_id=1, source_target_pairs={{0,224},{32,0},{64,32},{96,64},{128,96},{160,128},{192,160},{224,1... | collective-permute-start | bytes 2752520 | tf_op jit(solution)/shard_map/ppermute | solution.py:38
  14.9 20.3 %collective-permute-done = bf16[896,512]{1,0:T(8,128)(2,1)S(1)} collective-permute-done((bf16[896,512]{1,0:T(8,128)(2,1)S(1)}, bf16[896,512]{1,0:T(8,128)(2,1)S(1)}, u32[]{:S(2)}, u32[]{:S(2)}) %collective-permute-start) | collective-permute-done | bytes 917536 | tf_op jit(solution)/shard_map/ppermute | solution.py:37
  35.2 3.2 %collective-permute-start.8 = (bf16[896,512]{1,0:T(8,128)(2,1)S(1)}, bf16[896,512]{1,0:T(8,128)(2,1)S(1)}, u32[]{:S(2)}, u32[]{:S(2)}) collective-permute-start(bf16[896,512]{1,0:T(8,128)(2,1)S(1)} %collective-permute-done.7), channel_id=1, source_target_pairs={{0,224},{32,0},{64,32},{96,64},{128,96},{160,128},{192,160},{224,1... | collective-permute-start | bytes 2752520 | tf_op jit(solution)/shard_map/ppermute | solution.py:38
  38.4 19.6 %collective-permute-done.1 = bf16[896,512]{1,0:T(8,128)(2,1)S(1)} collective-permute-done((bf16[896,512]{1,0:T(8,128)(2,1)S(1)}, bf16[896,512]{1,0:T(8,128)(2,1)S(1)}, u32[]{:S(2)}, u32[]{:S(2)}) %collective-permute-start.1) | collective-permute-done | bytes 917536 | tf_op jit(solution)/shard_map/ppermute | solution.py:37
  58.0 1.2 copy-done.9
  59.2 3.0 collective-permute-start.9
  62.2 17.9 %collective-permute-done.2 = bf16[896,512]{1,0:T(8,128)(2,1)S(1)} collective-permute-done((bf16[896,512]{1,0:T(8,128)(2,1)S(1)}, bf16[896,512]{1,0:T(8,128)(2,1)S(1)}, u32[]{:S(2)}, u32[]{:S(2)}) %collective-permute-start.2) | collective-permute-done | bytes 917536 | tf_op jit(solution)/shard_map/ppermute | solution.py:37
  80.1 0.2 collective-permute-done.9
  80.3 3.7 %collective-permute-start.10 = (bf16[896,512]{1,0:T(8,128)(2,1)S(1)}, bf16[896,512]{1,0:T(8,128)(2,1)S(1)}, u32[]{:S(2)}, u32[]{:S(2)}) collective-permute-start(bf16[896,512]{1,0:T(8,128)(2,1)S(1)} %collective-permute-done.9), channel_id=1, source_target_pairs={{0,224},{32,0},{64,32},{96,64},{128,96},{160,128},{192,160},{224,1... | collective-permute-start | bytes 2752520 | tf_op jit(solution)/shard_map/ppermute | solution.py:38
  84.0 17.3 %collective-permute-done.3 = bf16[896,512]{1,0:T(8,128)(2,1)S(1)} collective-permute-done((bf16[896,512]{1,0:T(8,128)(2,1)S(1)}, bf16[896,512]{1,0:T(8,128)(2,1)S(1)}, u32[]{:S(2)}, u32[]{:S(2)}) %collective-permute-start.3) | collective-permute-done | bytes 917536 | tf_op jit(solution)/shard_map/ppermute | solution.py:37
  101.4 3.6 %collective-permute-start.11 = (bf16[896,512]{1,0:T(8,128)(2,1)S(1)}, bf16[896,512]{1,0:T(8,128)(2,1)}, u32[]{:S(2)}, u32[]{:S(2)}) collective-permute-start(bf16[896,512]{1,0:T(8,128)(2,1)S(1)} %collective-permute-done.10), channel_id=1, source_target_pairs={{0,224},{32,0},{64,32},{96,64},{128,96},{160,128},{192,160},{224,1... | collective-permute-start | bytes 2752520 | tf_op jit(solution)/shard_map/ppermute | solution.py:38
  105.0 16.8 %collective-permute-done.4 = bf16[896,512]{1,0:T(8,128)(2,1)} collective-permute-done((bf16[896,512]{1,0:T(8,128)(2,1)S(1)}, bf16[896,512]{1,0:T(8,128)(2,1)}, u32[]{:S(2)}, u32[]{:S(2)}) %collective-permute-start.4) | collective-permute-done | bytes 917536 | tf_op jit(solution)/shard_map/ppermute | solution.py:37
  121.8 3.5 %collective-permute-start.12 = (bf16[896,512]{1,0:T(8,128)(2,1)}, bf16[896,512]{1,0:T(8,128)(2,1)}, u32[]{:S(2)}, u32[]{:S(2)}) collective-permute-start(bf16[896,512]{1,0:T(8,128)(2,1)} %collective-permute-done.11), channel_id=1, source_target_pairs={{0,224},{32,0},{64,32},{96,64},{128,96},{160,128},{192,160},{224,1... | collective-permute-start | bytes 2752520 | tf_op jit(solution)/shard_map/ppermute | solution.py:38
  125.3 23.9 %all-gather.1 = f32[32,224,2]{1,2,0:T(2,128)S(1)} all-gather(f32[1,224,2]{1,2,0:T(2,128)S(1)} %bitcast.187), channel_id=1, replica_groups=mesh['row'=8,'col'=32] {'col'}, dimensions={0}, use_global_device_ids=true | all-gather | bytes 59136 | tf_op jit(solution)/shard_map/all_gather | solution.py:20
  149.4 0.3 broadcast_compare_fusion
  149.8 3.2 %collective-permute-start.13 = (bf16[896,512]{1,0:T(8,128)(2,1)}, bf16[896,512]{1,0:T(8,128)(2,1)S(1)}, u32[]{:S(2)}, u32[]{:S(2)}) collective-permute-start(bf16[896,512]{1,0:T(8,128)(2,1)} %collective-permute-done.12), channel_id=1, source_target_pairs={{0,224},{32,0},{64,32},{96,64},{128,96},{160,128},{192,160},{224,1... | collective-permute-start | bytes 2752520 | tf_op jit(solution)/shard_map/ppermute | solution.py:38
  153.1 6.5 %fusion = f32[384,2]{0,1:T(2,128)S(1)} fusion(bf16[384,2,7168]{0,2,1:T(8,128)(2,1)} %all-gather.5.cloned.1.call-done), kind=kLoop, calls=%fused_computation.2 | loop fusion | flops 16514304 | bytes 11013120 | tf_op jit(solution)/shard_map/reduce_sum | solution.py:22
  159.6 0.8 copy-done
  160.3 3.1 %fusion.2 = bf16[384,2,7168]{0,2,1:T(8,128)(2,1)S(1)} fusion(bf16[384,2,7168]{0,2,1:T(8,128)(2,1)S(1)} %copy-done, f32[2,7168]{1,0:T(2,128)S(1)} %bitcast.173, f32[384,2]{0,1:T(2,128)S(1)} %add_rsqrt_fusion), kind=kLoop, calls=%fused_computation.4 | loop fusion | flops 22020096 | bytes 22080512 | tf_op jit(solution)/shard_map/convert_element_type | solution.py:23
  163.4 1.0 fusion.31
  164.4 1.0 fusion.29
  165.5 2.2 fusion.17
  167.7 2.3 fusion.19
  169.9 1.0 fusion.21
  171.1 1.0 fusion.23
  172.1 0.2 copy-done.12
  172.3 1.0 fusion.25
  173.3 0.2 copy-done.8
  173.5 1.0 fusion.27
  174.5 2.2 fusion.4
  176.7 2.3 fusion.6
  179.0 1.0 fusion.8
  180.2 1.0 fusion.10
  181.3 1.0 fusion.12
  182.5 1.0 fusion.14
  183.5 2.5 fusion.87
  186.1 1.3 fusion.88
  187.4 1.1 exponential_reduce_fusion
  188.5 0.6 pad_maximum_fusion.1
  189.5 101.6 %all-gather.7.cloned.1.call-done = f32[768,384,2]{1,2,0:T(2,128)} async-done(((f32[3,384,2]{1,2,0:T(2,128)}), f32[768,384,2]{1,2,0:T(2,128)}) %all-gather.7.cloned.1.call-update) | async-done | bytes 2359312 | tf_op jit(solution)/shard_map/all_gather | solution.py:49
  291.2 1.4 bitcast_reduce_fusion
  292.5 1.3 slice_reduce_fusion
  293.8 2.0 fusion.66
  295.9 0.2 select_reduce_fusion.3
  296.1 0.6 copy.81
  (72 shorter events, 1.4 us)
Async XLA Ops:
  6.5 146.5 %all-gather.5.cloned.1.call-start = ((), (), s32[]{:S(2)}) async-start(), calls=%async_computation | async-start | bytes 11354112 | tf_op jit(solution)/shard_map/all_gather | solution.py:19
  7.3 118.0 %copy-start.3 = (f32[2,224]{1,0:T(2,128)S(1)}, f32[2,224]{1,0:T(2,128)}, u32[]{:S(2)}) copy-start(f32[2,224]{1,0:T(2,128)} %param.7) | copy-start | bytes 5380
  7.3 142.2 %copy-start.2 = (s32[384]{0:T(512)S(1)}, s32[384]{0:T(512)}, u32[]{:S(2)}) copy-start(s32[384]{0:T(512)} %param.10) | copy-start | bytes 4612
  7.3 283.9 %all-gather.7.cloned.1.call-start = ((), (), s32[]{:S(2)}) async-start(), calls=%async_computation.1 | async-start | bytes 2368512 | tf_op jit(solution)/shard_map/all_gather | solution.py:49
  8.9 26.3 %collective-permute-start = (bf16[896,512]{1,0:T(8,128)(2,1)S(1)}, bf16[896,512]{1,0:T(8,128)(2,1)S(1)}, u32[]{:S(2)}, u32[]{:S(2)}) collective-permute-start(bf16[896,512]{1,0:T(8,128)(2,1)S(1)} %get-tuple-element.10), channel_id=1, source_target_pairs={{0,32},{32,64},{64,96},{96,128},{128,160},{160,192},{192,224},{224... | collective-permute-start | bytes 2752520 | tf_op jit(solution)/shard_map/ppermute | solution.py:37
  10.9 24.3 %collective-permute-start.7 = (bf16[896,512]{1,0:T(8,128)(2,1)S(1)}, bf16[896,512]{1,0:T(8,128)(2,1)S(1)}, u32[]{:S(2)}, u32[]{:S(2)}) collective-permute-start(bf16[896,512]{1,0:T(8,128)(2,1)S(1)} %get-tuple-element.11), channel_id=1, source_target_pairs={{0,224},{32,0},{64,32},{96,64},{128,96},{160,128},{192,160},{224,1... | collective-permute-start | bytes 2752520 | tf_op jit(solution)/shard_map/ppermute | solution.py:38
  35.2 114.2 %copy-start.7 = (bf16[896,512]{1,0:T(8,128)(2,1)}, bf16[896,512]{1,0:T(8,128)(2,1)S(1)}, u32[]{:S(2)}) copy-start(bf16[896,512]{1,0:T(8,128)(2,1)S(1)} %collective-permute-done) | copy-start | bytes 2752516
  35.2 22.8 %collective-permute-start.1 = (bf16[896,512]{1,0:T(8,128)(2,1)S(1)}, bf16[896,512]{1,0:T(8,128)(2,1)S(1)}, u32[]{:S(2)}, u32[]{:S(2)}) collective-permute-start(bf16[896,512]{1,0:T(8,128)(2,1)S(1)} %collective-permute-done), channel_id=1, source_target_pairs={{0,32},{32,64},{64,96},{96,128},{128,160},{160,192},{192,224},{224... | collective-permute-start | bytes 2752520 | tf_op jit(solution)/shard_map/ppermute | solution.py:37
  35.2 90.1 %copy-start.5 = (bf16[896,512]{1,0:T(8,128)(2,1)}, bf16[896,512]{1,0:T(8,128)(2,1)S(1)}, u32[]{:S(2)}) copy-start(bf16[896,512]{1,0:T(8,128)(2,1)S(1)} %collective-permute-done.7) | copy-start | bytes 2752516
  35.2 22.8 %collective-permute-start.8 = (bf16[896,512]{1,0:T(8,128)(2,1)S(1)}, bf16[896,512]{1,0:T(8,128)(2,1)S(1)}, u32[]{:S(2)}, u32[]{:S(2)}) collective-permute-start(bf16[896,512]{1,0:T(8,128)(2,1)S(1)} %collective-permute-done.7), channel_id=1, source_target_pairs={{0,224},{32,0},{64,32},{96,64},{128,96},{160,128},{192,160},{224,1... | collective-permute-start | bytes 2752520 | tf_op jit(solution)/shard_map/ppermute | solution.py:38
  58.0 22.3 %copy-start.11 = (bf16[896,512]{1,0:T(8,128)(2,1)}, bf16[896,512]{1,0:T(8,128)(2,1)S(1)}, u32[]{:S(2)}) copy-start(bf16[896,512]{1,0:T(8,128)(2,1)S(1)} %collective-permute-done.1) | copy-start | bytes 2752516
  58.0 22.1 %collective-permute-start.2 = (bf16[896,512]{1,0:T(8,128)(2,1)S(1)}, bf16[896,512]{1,0:T(8,128)(2,1)S(1)}, u32[]{:S(2)}, u32[]{:S(2)}) collective-permute-start(bf16[896,512]{1,0:T(8,128)(2,1)S(1)} %collective-permute-done.1), channel_id=1, source_target_pairs={{0,32},{32,64},{64,96},{96,128},{128,160},{160,192},{192,224},{224... | collective-permute-start | bytes 2752520 | tf_op jit(solution)/shard_map/ppermute | solution.py:37
  58.0 1.2 copy-start.9
  59.2 21.1 %collective-permute-start.9 = (bf16[896,512]{1,0:T(8,128)(2,1)S(1)}, bf16[896,512]{1,0:T(8,128)(2,1)S(1)}, u32[]{:S(2)}, u32[]{:S(2)}) collective-permute-start(bf16[896,512]{1,0:T(8,128)(2,1)S(1)} %collective-permute-done.8), channel_id=1, source_target_pairs={{0,224},{32,0},{64,32},{96,64},{128,96},{160,128},{192,160},{224,1... | collective-permute-start | bytes 2752520 | tf_op jit(solution)/shard_map/ppermute | solution.py:38
  80.1 21.2 %copy-start.15 = (bf16[896,512]{1,0:T(8,128)(2,1)}, bf16[896,512]{1,0:T(8,128)(2,1)S(1)}, u32[]{:S(2)}) copy-start(bf16[896,512]{1,0:T(8,128)(2,1)S(1)} %collective-permute-done.2) | copy-start | bytes 2752516
  80.1 21.2 %collective-permute-start.3 = (bf16[896,512]{1,0:T(8,128)(2,1)S(1)}, bf16[896,512]{1,0:T(8,128)(2,1)S(1)}, u32[]{:S(2)}, u32[]{:S(2)}) collective-permute-start(bf16[896,512]{1,0:T(8,128)(2,1)S(1)} %collective-permute-done.2), channel_id=1, source_target_pairs={{0,32},{32,64},{64,96},{96,128},{128,160},{160,192},{192,224},{224... | collective-permute-start | bytes 2752520 | tf_op jit(solution)/shard_map/ppermute | solution.py:37
  80.3 3.7 %copy-start.13 = (bf16[896,512]{1,0:T(8,128)(2,1)}, bf16[896,512]{1,0:T(8,128)(2,1)S(1)}, u32[]{:S(2)}) copy-start(bf16[896,512]{1,0:T(8,128)(2,1)S(1)} %collective-permute-done.9) | copy-start | bytes 2752516
  80.3 21.0 %collective-permute-start.10 = (bf16[896,512]{1,0:T(8,128)(2,1)S(1)}, bf16[896,512]{1,0:T(8,128)(2,1)S(1)}, u32[]{:S(2)}, u32[]{:S(2)}) collective-permute-start(bf16[896,512]{1,0:T(8,128)(2,1)S(1)} %collective-permute-done.9), channel_id=1, source_target_pairs={{0,224},{32,0},{64,32},{96,64},{128,96},{160,128},{192,160},{224,1... | collective-permute-start | bytes 2752520 | tf_op jit(solution)/shard_map/ppermute | solution.py:38
  101.3 20.5 %copy-start.19 = (bf16[896,512]{1,0:T(8,128)(2,1)}, bf16[896,512]{1,0:T(8,128)(2,1)S(1)}, u32[]{:S(2)}) copy-start(bf16[896,512]{1,0:T(8,128)(2,1)S(1)} %collective-permute-done.3) | copy-start | bytes 2752516
  101.3 20.5 %collective-permute-start.4 = (bf16[896,512]{1,0:T(8,128)(2,1)S(1)}, bf16[896,512]{1,0:T(8,128)(2,1)}, u32[]{:S(2)}, u32[]{:S(2)}) collective-permute-start(bf16[896,512]{1,0:T(8,128)(2,1)S(1)} %collective-permute-done.3), channel_id=1, source_target_pairs={{0,32},{32,64},{64,96},{96,128},{128,160},{160,192},{192,224},{224... | collective-permute-start | bytes 2752520 | tf_op jit(solution)/shard_map/ppermute | solution.py:37
  101.3 3.6 %copy-start.17 = (bf16[896,512]{1,0:T(8,128)(2,1)}, bf16[896,512]{1,0:T(8,128)(2,1)S(1)}, u32[]{:S(2)}) copy-start(bf16[896,512]{1,0:T(8,128)(2,1)S(1)} %collective-permute-done.10) | copy-start | bytes 2752516
  101.4 20.4 %collective-permute-start.11 = (bf16[896,512]{1,0:T(8,128)(2,1)S(1)}, bf16[896,512]{1,0:T(8,128)(2,1)}, u32[]{:S(2)}, u32[]{:S(2)}) collective-permute-start(bf16[896,512]{1,0:T(8,128)(2,1)S(1)} %collective-permute-done.10), channel_id=1, source_target_pairs={{0,224},{32,0},{64,32},{96,64},{128,96},{160,128},{192,160},{224,1... | collective-permute-start | bytes 2752520 | tf_op jit(solution)/shard_map/ppermute | solution.py:38
  121.8 27.9 %collective-permute-start.5 = (bf16[896,512]{1,0:T(8,128)(2,1)}, bf16[896,512]{1,0:T(8,128)(2,1)}, u32[]{:S(2)}, u32[]{:S(2)}) collective-permute-start(bf16[896,512]{1,0:T(8,128)(2,1)} %collective-permute-done.4), channel_id=1, source_target_pairs={{0,32},{32,64},{64,96},{96,128},{128,160},{160,192},{192,224},{224... | collective-permute-start | bytes 2752520 | tf_op jit(solution)/shard_map/ppermute | solution.py:37
  121.8 28.0 %collective-permute-start.12 = (bf16[896,512]{1,0:T(8,128)(2,1)}, bf16[896,512]{1,0:T(8,128)(2,1)}, u32[]{:S(2)}, u32[]{:S(2)}) collective-permute-start(bf16[896,512]{1,0:T(8,128)(2,1)} %collective-permute-done.11), channel_id=1, source_target_pairs={{0,224},{32,0},{64,32},{96,64},{128,96},{160,128},{192,160},{224,1... | collective-permute-start | bytes 2752520 | tf_op jit(solution)/shard_map/ppermute | solution.py:38
  149.7 33.8 %collective-permute-start.6 = (bf16[896,512]{1,0:T(8,128)(2,1)}, bf16[896,512]{1,0:T(8,128)(2,1)}, u32[]{:S(2)}, u32[]{:S(2)}) collective-permute-start(bf16[896,512]{1,0:T(8,128)(2,1)} %collective-permute-done.5), channel_id=1, source_target_pairs={{0,32},{32,64},{64,96},{96,128},{128,160},{160,192},{192,224},{224... | collective-permute-start | bytes 2752520 | tf_op jit(solution)/shard_map/ppermute | solution.py:37
  149.8 36.2 %collective-permute-start.13 = (bf16[896,512]{1,0:T(8,128)(2,1)}, bf16[896,512]{1,0:T(8,128)(2,1)S(1)}, u32[]{:S(2)}, u32[]{:S(2)}) collective-permute-start(bf16[896,512]{1,0:T(8,128)(2,1)} %collective-permute-done.12), channel_id=1, source_target_pairs={{0,224},{32,0},{64,32},{96,64},{128,96},{160,128},{192,160},{224,1... | collective-permute-start | bytes 2752520 | tf_op jit(solution)/shard_map/ppermute | solution.py:38
  153.1 7.3 %copy-start = (bf16[384,2,7168]{0,2,1:T(8,128)(2,1)S(1)}, bf16[384,2,7168]{0,2,1:T(8,128)(2,1)}, u32[]{:S(2)}) copy-start(bf16[384,2,7168]{0,2,1:T(8,128)(2,1)} %all-gather.5.cloned.1.call-done) | copy-start | bytes 33030148
  160.3 3.1 %copy-start.1 = (bf16[896,1024]{1,0:T(8,128)(2,1)S(1)}, bf16[896,1024]{1,0:T(8,128)(2,1)}, u32[]{:S(2)}) copy-start(bf16[896,1024]{1,0:T(8,128)(2,1)} %param.8) | copy-start | bytes 5505028
  167.6 2.3 copy-start.20
  169.9 1.2 copy-start.16
  171.1 1.2 copy-start.12
  172.3 1.2 copy-start.8
  176.7 2.3 copy-start.18
  179.0 1.2 copy-start.14
  180.2 1.2 copy-start.10
  181.3 1.2 copy-start.6
  187.4 1.7 copy-start.4
  187.4 2.1 copy-start.21
Sparse Core Ops, SparseCore 0:
  9.9 66.7 all-gather.4
  189.3 101.8 all-gather.6

commit v4 on v2

--- a/solution.py
+++ b/solution.py
@@ -23,10 +23,10 @@
     features = (stream * lax.rsqrt(mean_square[:, :, None] + EPS) * full_gain[None, :, :]).astype(
         jnp.bfloat16
     )
+    features = features.reshape(tok_rows, 2, n_row, shard_rows).transpose(2, 0, 1, 3)
 
     def block_logits(block, shard):
-        rows = lax.dynamic_slice_in_dim(features, shard * shard_rows, shard_rows, axis=2)
-        return jnp.einsum("tmd,dv->tmv", rows, block, preferred_element_type=jnp.float32)
+        return jnp.einsum("tmd,dv->tmv", features[shard], block, preferred_element_type=jnp.float32)
 
     forward = [(i, (i + 1) % n_row) for i in range(n_row)]
     backward = [(i, (i - 1) % n_row) for i in range(n_row)]

time: 273 us -> 242 us (0.89)
  local copies, waits for them, and re-layouts: 34 us -> 4.18 us
    all_gather x1 -> x0, local copies, waits for them, and re-layouts: 27.5 us -> none  [per_device(): full_hidden = lax.all_gather(hidden_in, 'col', axis=2, tiled=True)]
  transfers between devices with their start and end apart: 15 -> 15, of which waited for: 5 -> 5; matrix products, arithmetic and copies ran while one was open for 22% -> 14% of each run, Pallas kernels for 0% -> 0%
where the time goes in v4:
time: 242 us
  waiting for transfers between devices  94.5 us (39%)
  blocking collectives  69.1 us (29%)
  starting transfers between devices  25.6 us (11%)
  matrix products  22.9 us (9%)
  between operations  13.8 us (6%)
  other arithmetic  11.7 us (5%)
  local copies, waits for them, and re-layouts  4.18 us (2%)
    ppermute x7, waiting for transfers between devices, per_device(): left = lax.ppermute(left, 'row', forward)  93.7 us
    all_gather x1, blocking collectives, per_device(): full_gain = lax.all_gather(final_gain, 'col', axis=1, tiled=True)  23.8 us
    ppermute x7, starting transfers between devices, per_device(): right = lax.ppermute(right, 'row', backward)  23.5 us
    all_gather x1, blocking collectives, per_device(): parts = lax.all_gather(jnp.stack([row_max, exp_total, picked]), 'col')  23.2 us
    dot_general x16, matrix products, block_logits(): jnp.einsum('tmd,dv->tmv', features[shard], block, preferred_element_type=...  22.9 us
    all_gather x1, blocking collectives, per_device(): stats = lax.all_gather(jnp.stack([ratio_sums, squares, ratio_max]), 'row')  22.1 us
    reduce_sum x1, other arithmetic, per_device(): mean_square = jnp.sum(stream * stream, axis=2) / D  6.49 us
  transfers between devices with their start and end apart: 15, of which 5 were waited for; matrix products, arithmetic and copies ran while one was open for 14% of the time, Pallas kernels for 0%

profile of v4, /device:TPU:2, one launch (start us, length us, event | category | flops | bytes accessed | tf_op | source)
XLA Modules:
  0.0 241.7 jit_solution(9763126338925372901)
XLA Ops:
  6.5 0.7 all-gather.6.cloned.1.call-update
  7.3 1.6 fusion.87
  8.9 2.0 collective-permute-start
  10.9 4.0 %collective-permute-start.7 = (bf16[896,512]{1,0:T(8,128)(2,1)S(1)}, bf16[896,512]{1,0:T(8,128)(2,1)S(1)}, u32[]{:S(2)}, u32[]{:S(2)}) collective-permute-start(bf16[896,512]{1,0:T(8,128)(2,1)S(1)} %get-tuple-element.16), channel_id=1, source_target_pairs={{0,224},{32,0},{64,32},{96,64},{128,96},{160,128},{192,160},{224,1... | collective-permute-start | bytes 2752520 | tf_op jit(solution)/shard_map/ppermute | solution.py:38
  14.9 20.3 %collective-permute-done = bf16[896,512]{1,0:T(8,128)(2,1)S(1)} collective-permute-done((bf16[896,512]{1,0:T(8,128)(2,1)S(1)}, bf16[896,512]{1,0:T(8,128)(2,1)S(1)}, u32[]{:S(2)}, u32[]{:S(2)}) %collective-permute-start) | collective-permute-done | bytes 917536 | tf_op jit(solution)/shard_map/ppermute | solution.py:37
  35.2 3.2 %collective-permute-start.8 = (bf16[896,512]{1,0:T(8,128)(2,1)S(1)}, bf16[896,512]{1,0:T(8,128)(2,1)S(1)}, u32[]{:S(2)}, u32[]{:S(2)}) collective-permute-start(bf16[896,512]{1,0:T(8,128)(2,1)S(1)} %collective-permute-done.7), channel_id=1, source_target_pairs={{0,224},{32,0},{64,32},{96,64},{128,96},{160,128},{192,160},{224,1... | collective-permute-start | bytes 2752520 | tf_op jit(solution)/shard_map/ppermute | solution.py:38
  38.4 19.6 %collective-permute-done.1 = bf16[896,512]{1,0:T(8,128)(2,1)S(1)} collective-permute-done((bf16[896,512]{1,0:T(8,128)(2,1)S(1)}, bf16[896,512]{1,0:T(8,128)(2,1)S(1)}, u32[]{:S(2)}, u32[]{:S(2)}) %collective-permute-start.1) | collective-permute-done | bytes 917536 | tf_op jit(solution)/shard_map/ppermute | solution.py:37
  58.0 3.2 %collective-permute-start.9 = (bf16[896,512]{1,0:T(8,128)(2,1)S(1)}, bf16[896,512]{1,0:T(8,128)(2,1)S(1)}, u32[]{:S(2)}, u32[]{:S(2)}) collective-permute-start(bf16[896,512]{1,0:T(8,128)(2,1)S(1)} %collective-permute-done.8), channel_id=1, source_target_pairs={{0,224},{32,0},{64,32},{96,64},{128,96},{160,128},{192,160},{224,1... | collective-permute-start | bytes 2752520 | tf_op jit(solution)/shard_map/ppermute | solution.py:38
  61.3 18.8 %collective-permute-done.2 = bf16[896,512]{1,0:T(8,128)(2,1)S(1)} collective-permute-done((bf16[896,512]{1,0:T(8,128)(2,1)S(1)}, bf16[896,512]{1,0:T(8,128)(2,1)S(1)}, u32[]{:S(2)}, u32[]{:S(2)}) %collective-permute-start.2) | collective-permute-done | bytes 917536 | tf_op jit(solution)/shard_map/ppermute | solution.py:37
  80.1 3.3 %collective-permute-start.10 = (bf16[896,512]{1,0:T(8,128)(2,1)S(1)}, bf16[896,512]{1,0:T(8,128)(2,1)S(1)}, u32[]{:S(2)}, u32[]{:S(2)}) collective-permute-start(bf16[896,512]{1,0:T(8,128)(2,1)S(1)} %collective-permute-done.9), channel_id=1, source_target_pairs={{0,224},{32,0},{64,32},{96,64},{128,96},{160,128},{192,160},{224,1... | collective-permute-start | bytes 2752520 | tf_op jit(solution)/shard_map/ppermute | solution.py:38
  83.4 17.9 %collective-permute-done.3 = bf16[896,512]{1,0:T(8,128)(2,1)S(1)} collective-permute-done((bf16[896,512]{1,0:T(8,128)(2,1)S(1)}, bf16[896,512]{1,0:T(8,128)(2,1)S(1)}, u32[]{:S(2)}, u32[]{:S(2)}) %collective-permute-start.3) | collective-permute-done | bytes 917536 | tf_op jit(solution)/shard_map/ppermute | solution.py:37
  101.3 3.3 %collective-permute-start.11 = (bf16[896,512]{1,0:T(8,128)(2,1)S(1)}, bf16[896,512]{1,0:T(8,128)(2,1)}, u32[]{:S(2)}, u32[]{:S(2)}) collective-permute-start(bf16[896,512]{1,0:T(8,128)(2,1)S(1)} %collective-permute-done.10), channel_id=1, source_target_pairs={{0,224},{32,0},{64,32},{96,64},{128,96},{160,128},{192,160},{224,1... | collective-permute-start | bytes 2752520 | tf_op jit(solution)/shard_map/ppermute | solution.py:38
  104.6 17.2 %collective-permute-done.4 = bf16[896,512]{1,0:T(8,128)(2,1)} collective-permute-done((bf16[896,512]{1,0:T(8,128)(2,1)S(1)}, bf16[896,512]{1,0:T(8,128)(2,1)}, u32[]{:S(2)}, u32[]{:S(2)}) %collective-permute-start.4) | collective-permute-done | bytes 917536 | tf_op jit(solution)/shard_map/ppermute | solution.py:37
  121.8 3.2 %collective-permute-start.12 = (bf16[896,512]{1,0:T(8,128)(2,1)}, bf16[896,512]{1,0:T(8,128)(2,1)}, u32[]{:S(2)}, u32[]{:S(2)}) collective-permute-start(bf16[896,512]{1,0:T(8,128)(2,1)} %collective-permute-done.11), channel_id=1, source_target_pairs={{0,224},{32,0},{64,32},{96,64},{128,96},{160,128},{192,160},{224,1... | collective-permute-start | bytes 2752520 | tf_op jit(solution)/shard_map/ppermute | solution.py:38
  125.0 23.8 %all-gather.2 = f32[32,224,2]{1,2,0:T(2,128)S(1)} all-gather(f32[1,224,2]{1,2,0:T(2,128)S(1)} %bitcast.180), channel_id=1, replica_groups=mesh['row'=8,'col'=32] {'col'}, dimensions={0}, use_global_device_ids=true | all-gather | bytes 59136 | tf_op jit(solution)/shard_map/all_gather | solution.py:20
  148.9 0.1 reshape.194
  149.5 0.3 broadcast_compare_fusion
  149.9 3.2 %collective-permute-start.13 = (bf16[896,512]{1,0:T(8,128)(2,1)}, bf16[896,512]{1,0:T(8,128)(2,1)S(1)}, u32[]{:S(2)}, u32[]{:S(2)}) collective-permute-start(bf16[896,512]{1,0:T(8,128)(2,1)} %collective-permute-done.12), channel_id=1, source_target_pairs={{0,224},{32,0},{64,32},{96,64},{128,96},{160,128},{192,160},{224,1... | collective-permute-start | bytes 2752520 | tf_op jit(solution)/shard_map/ppermute | solution.py:38
  153.1 6.5 %fusion = f32[384,2]{0,1:T(2,128)S(1)} fusion(bf16[384,2,7168]{0,2,1:T(8,128)(2,1)} %all-gather.6.cloned.1.call-done), kind=kLoop, calls=%fused_computation.2 | loop fusion | flops 16514304 | bytes 11013120 | tf_op jit(solution)/shard_map/reduce_sum | solution.py:22
  159.6 0.8 copy-done
  160.3 3.1 %fusion.2 = bf16[384,2,7168]{0,2,1:T(8,128)(2,1)S(1)} fusion(bf16[384,2,7168]{0,2,1:T(8,128)(2,1)S(1)} %copy-done, f32[2,7168]{1,0:T(2,128)S(1)} %bitcast.173, f32[384,2]{0,1:T(2,128)S(1)} %add_rsqrt_fusion), kind=kLoop, calls=%fused_computation.4 | loop fusion | flops 22020096 | bytes 22080512 | tf_op jit(solution)/shard_map/convert_element_type | solution.py:23
  163.4 1.0 fusion.31
  164.5 1.0 fusion.29
  165.5 2.2 fusion.17
  167.7 2.3 fusion.19
  170.0 1.0 fusion.21
  171.0 0.2 copy-done.16
  171.1 1.0 fusion.23
  172.2 0.2 copy-done.12
  172.3 1.0 fusion.25
  173.3 0.2 copy-done.8
  173.5 1.0 fusion.27
  174.5 2.2 fusion.4
  176.7 2.3 fusion.6
  179.0 1.0 fusion.8
  180.0 0.2 copy-done.14
  180.2 1.0 fusion.10
  181.2 0.2 copy-done.10
  181.4 1.0 fusion.12
  182.4 0.2 copy-done.6
  182.5 1.0 fusion.14
  183.6 2.5 %fusion.88 = (f32[384,2]{0,1:T(2,128)S(1)}, f32[384,2,512]{2,0,1:T(8,128)S(1)}) fusion(bf16[896,512]{1,0:T(8,128)(2,1)} %collective-permute-done.6, bf16[384,2,8,896]{0,3,2,1:T(8,128)(2,1)S(1)} %bitcast.168, s32[]{:T(128)S(6)} %select_n.144, f32[384,2,512]{2,0,1:T(8,128)S(1)} %fusion.17, f32[384,2,512]{2,0,1:T(8,128)S(1)} %fusion.19, ...), kind=kOutput, calls=%fused_computation.118 | convolution fusion | flops 707788032 | bytes 14879748 | tf_op jit(solution)/shard_map/tmd,dv->tmv/dot_general | solution.py:29
  186.1 1.3 fusion.89
  187.4 1.1 exponential_reduce_fusion
  188.5 23.2 %all-gather = f32[96,384,2]{1,2,0:T(2,128)S(1)} all-gather(f32[3,384,2]{1,2,0:T(2,128)S(1)} %pad_maximum_fusion.1), channel_id=2, replica_groups=mesh['row'=8,'col'=32] {'col'}, dimensions={0}, use_global_device_ids=true | all-gather | bytes 304128 | tf_op jit(solution)/shard_map/all_gather | solution.py:48
  212.0 0.2 select_reduce_fusion.3
  212.1 22.1 %all-gather.3 = f32[8,3,16]{2,1,0:T(4,128)S(1)} all-gather(f32[1,3,16]{2,1,0:T(4,128)S(1)} %maximum_bitcast_fusion), channel_id=3, replica_groups=mesh['row'=8,'col'=32] {'row'}, dimensions={0}, use_global_device_ids=true | all-gather | bytes 1728 | tf_op jit(solution)/shard_map/all_gather | solution.py:61
  234.3 0.6 copy.81
  (73 shorter events, 0.9 us)
Async XLA Ops:
  6.5 146.5 %all-gather.6.cloned.1.call-start = ((), (), s32[]{:S(2)}) async-start(), calls=%async_computation | async-start | bytes 11354112 | tf_op jit(solution)/shard_map/all_gather | solution.py:19
  7.3 117.8 %copy-start.3 = (f32[2,224]{1,0:T(2,128)S(1)}, f32[2,224]{1,0:T(2,128)}, u32[]{:S(2)}) copy-start(f32[2,224]{1,0:T(2,128)} %param.7) | copy-start | bytes 5380
  7.3 141.7 %copy-start.4 = (s32[16]{0:T(128)S(1)}, s32[16]{0:T(128)}, u32[]{:S(2)}) copy-start(s32[16]{0:T(128)} %param.9) | copy-start | bytes 196
  7.3 142.2 %copy-start.21 = (s32[16]{0:T(128)S(1)}, s32[16]{0:T(128)}, u32[]{:S(2)}) copy-start(s32[16]{0:T(128)} %param.11) | copy-start | bytes 196
  7.3 142.2 %copy-start.2 = (s32[384]{0:T(512)S(1)}, s32[384]{0:T(512)}, u32[]{:S(2)}) copy-start(s32[384]{0:T(512)} %param.10) | copy-start | bytes 4612
  8.9 26.3 %collective-permute-start = (bf16[896,512]{1,0:T(8,128)(2,1)S(1)}, bf16[896,512]{1,0:T(8,128)(2,1)S(1)}, u32[]{:S(2)}, u32[]{:S(2)}) collective-permute-start(bf16[896,512]{1,0:T(8,128)(2,1)S(1)} %get-tuple-element.15), channel_id=1, source_target_pairs={{0,32},{32,64},{64,96},{96,128},{128,160},{160,192},{192,224},{224... | collective-permute-start | bytes 2752520 | tf_op jit(solution)/shard_map/ppermute | solution.py:37
  10.9 24.3 %collective-permute-start.7 = (bf16[896,512]{1,0:T(8,128)(2,1)S(1)}, bf16[896,512]{1,0:T(8,128)(2,1)S(1)}, u32[]{:S(2)}, u32[]{:S(2)}) collective-permute-start(bf16[896,512]{1,0:T(8,128)(2,1)S(1)} %get-tuple-element.16), channel_id=1, source_target_pairs={{0,224},{32,0},{64,32},{96,64},{128,96},{160,128},{192,160},{224,1... | collective-permute-start | bytes 2752520 | tf_op jit(solution)/shard_map/ppermute | solution.py:38
  35.2 113.9 %copy-start.7 = (bf16[896,512]{1,0:T(8,128)(2,1)}, bf16[896,512]{1,0:T(8,128)(2,1)S(1)}, u32[]{:S(2)}) copy-start(bf16[896,512]{1,0:T(8,128)(2,1)S(1)} %collective-permute-done) | copy-start | bytes 2752516
  35.2 22.8 %collective-permute-start.1 = (bf16[896,512]{1,0:T(8,128)(2,1)S(1)}, bf16[896,512]{1,0:T(8,128)(2,1)S(1)}, u32[]{:S(2)}, u32[]{:S(2)}) collective-permute-start(bf16[896,512]{1,0:T(8,128)(2,1)S(1)} %collective-permute-done), channel_id=1, source_target_pairs={{0,32},{32,64},{64,96},{96,128},{128,160},{160,192},{192,224},{224... | collective-permute-start | bytes 2752520 | tf_op jit(solution)/shard_map/ppermute | solution.py:37
  35.2 117.9 %copy-start.5 = (bf16[896,512]{1,0:T(8,128)(2,1)}, bf16[896,512]{1,0:T(8,128)(2,1)S(1)}, u32[]{:S(2)}) copy-start(bf16[896,512]{1,0:T(8,128)(2,1)S(1)} %collective-permute-done.7) | copy-start | bytes 2752516
  35.2 22.8 %collective-permute-start.8 = (bf16[896,512]{1,0:T(8,128)(2,1)S(1)}, bf16[896,512]{1,0:T(8,128)(2,1)S(1)}, u32[]{:S(2)}, u32[]{:S(2)}) collective-permute-start(bf16[896,512]{1,0:T(8,128)(2,1)S(1)} %collective-permute-done.7), channel_id=1, source_target_pairs={{0,224},{32,0},{64,32},{96,64},{128,96},{160,128},{192,160},{224,1... | collective-permute-start | bytes 2752520 | tf_op jit(solution)/shard_map/ppermute | solution.py:38
  58.0 22.1 %copy-start.11 = (bf16[896,512]{1,0:T(8,128)(2,1)}, bf16[896,512]{1,0:T(8,128)(2,1)S(1)}, u32[]{:S(2)}) copy-start(bf16[896,512]{1,0:T(8,128)(2,1)S(1)} %collective-permute-done.1) | copy-start | bytes 2752516
  58.0 22.1 %collective-permute-start.2 = (bf16[896,512]{1,0:T(8,128)(2,1)S(1)}, bf16[896,512]{1,0:T(8,128)(2,1)S(1)}, u32[]{:S(2)}, u32[]{:S(2)}) collective-permute-start(bf16[896,512]{1,0:T(8,128)(2,1)S(1)} %collective-permute-done.1), channel_id=1, source_target_pairs={{0,32},{32,64},{64,96},{96,128},{128,160},{160,192},{192,224},{224... | collective-permute-start | bytes 2752520 | tf_op jit(solution)/shard_map/ppermute | solution.py:37
  58.0 90.8 %copy-start.9 = (bf16[896,512]{1,0:T(8,128)(2,1)}, bf16[896,512]{1,0:T(8,128)(2,1)S(1)}, u32[]{:S(2)}) copy-start(bf16[896,512]{1,0:T(8,128)(2,1)S(1)} %collective-permute-done.8) | copy-start | bytes 2752516
  58.0 22.1 %collective-permute-start.9 = (bf16[896,512]{1,0:T(8,128)(2,1)S(1)}, bf16[896,512]{1,0:T(8,128)(2,1)S(1)}, u32[]{:S(2)}, u32[]{:S(2)}) collective-permute-start(bf16[896,512]{1,0:T(8,128)(2,1)S(1)} %collective-permute-done.8), channel_id=1, source_target_pairs={{0,224},{32,0},{64,32},{96,64},{128,96},{160,128},{192,160},{224,1... | collective-permute-start | bytes 2752520 | tf_op jit(solution)/shard_map/ppermute | solution.py:38
  80.1 21.2 %copy-start.15 = (bf16[896,512]{1,0:T(8,128)(2,1)}, bf16[896,512]{1,0:T(8,128)(2,1)S(1)}, u32[]{:S(2)}) copy-start(bf16[896,512]{1,0:T(8,128)(2,1)S(1)} %collective-permute-done.2) | copy-start | bytes 2752516
  80.1 21.2 %collective-permute-start.3 = (bf16[896,512]{1,0:T(8,128)(2,1)S(1)}, bf16[896,512]{1,0:T(8,128)(2,1)S(1)}, u32[]{:S(2)}, u32[]{:S(2)}) collective-permute-start(bf16[896,512]{1,0:T(8,128)(2,1)S(1)} %collective-permute-done.2), channel_id=1, source_target_pairs={{0,32},{32,64},{64,96},{96,128},{128,160},{160,192},{192,224},{224... | collective-permute-start | bytes 2752520 | tf_op jit(solution)/shard_map/ppermute | solution.py:37
  80.1 3.3 %copy-start.13 = (bf16[896,512]{1,0:T(8,128)(2,1)}, bf16[896,512]{1,0:T(8,128)(2,1)S(1)}, u32[]{:S(2)}) copy-start(bf16[896,512]{1,0:T(8,128)(2,1)S(1)} %collective-permute-done.9) | copy-start | bytes 2752516
  80.1 21.2 %collective-permute-start.10 = (bf16[896,512]{1,0:T(8,128)(2,1)S(1)}, bf16[896,512]{1,0:T(8,128)(2,1)S(1)}, u32[]{:S(2)}, u32[]{:S(2)}) collective-permute-start(bf16[896,512]{1,0:T(8,128)(2,1)S(1)} %collective-permute-done.9), channel_id=1, source_target_pairs={{0,224},{32,0},{64,32},{96,64},{128,96},{160,128},{192,160},{224,1... | collective-permute-start | bytes 2752520 | tf_op jit(solution)/shard_map/ppermute | solution.py:38
  101.3 20.5 %copy-start.19 = (bf16[896,512]{1,0:T(8,128)(2,1)}, bf16[896,512]{1,0:T(8,128)(2,1)S(1)}, u32[]{:S(2)}) copy-start(bf16[896,512]{1,0:T(8,128)(2,1)S(1)} %collective-permute-done.3) | copy-start | bytes 2752516
  101.3 20.5 %collective-permute-start.4 = (bf16[896,512]{1,0:T(8,128)(2,1)S(1)}, bf16[896,512]{1,0:T(8,128)(2,1)}, u32[]{:S(2)}, u32[]{:S(2)}) collective-permute-start(bf16[896,512]{1,0:T(8,128)(2,1)S(1)} %collective-permute-done.3), channel_id=1, source_target_pairs={{0,32},{32,64},{64,96},{96,128},{128,160},{160,192},{192,224},{224... | collective-permute-start | bytes 2752520 | tf_op jit(solution)/shard_map/ppermute | solution.py:37
  101.3 3.3 %copy-start.17 = (bf16[896,512]{1,0:T(8,128)(2,1)}, bf16[896,512]{1,0:T(8,128)(2,1)S(1)}, u32[]{:S(2)}) copy-start(bf16[896,512]{1,0:T(8,128)(2,1)S(1)} %collective-permute-done.10) | copy-start | bytes 2752516
  101.3 20.4 %collective-permute-start.11 = (bf16[896,512]{1,0:T(8,128)(2,1)S(1)}, bf16[896,512]{1,0:T(8,128)(2,1)}, u32[]{:S(2)}, u32[]{:S(2)}) collective-permute-start(bf16[896,512]{1,0:T(8,128)(2,1)S(1)} %collective-permute-done.10), channel_id=1, source_target_pairs={{0,224},{32,0},{64,32},{96,64},{128,96},{160,128},{192,160},{224,1... | collective-permute-start | bytes 2752520 | tf_op jit(solution)/shard_map/ppermute | solution.py:38
  121.8 28.0 %collective-permute-start.5 = (bf16[896,512]{1,0:T(8,128)(2,1)}, bf16[896,512]{1,0:T(8,128)(2,1)}, u32[]{:S(2)}, u32[]{:S(2)}) collective-permute-start(bf16[896,512]{1,0:T(8,128)(2,1)} %collective-permute-done.4), channel_id=1, source_target_pairs={{0,32},{32,64},{64,96},{96,128},{128,160},{160,192},{192,224},{224... | collective-permute-start | bytes 2752520 | tf_op jit(solution)/shard_map/ppermute | solution.py:37
  121.8 28.0 %collective-permute-start.12 = (bf16[896,512]{1,0:T(8,128)(2,1)}, bf16[896,512]{1,0:T(8,128)(2,1)}, u32[]{:S(2)}, u32[]{:S(2)}) collective-permute-start(bf16[896,512]{1,0:T(8,128)(2,1)} %collective-permute-done.11), channel_id=1, source_target_pairs={{0,224},{32,0},{64,32},{96,64},{128,96},{160,128},{192,160},{224,1... | collective-permute-start | bytes 2752520 | tf_op jit(solution)/shard_map/ppermute | solution.py:38
  149.8 33.8 %collective-permute-start.6 = (bf16[896,512]{1,0:T(8,128)(2,1)}, bf16[896,512]{1,0:T(8,128)(2,1)}, u32[]{:S(2)}, u32[]{:S(2)}) collective-permute-start(bf16[896,512]{1,0:T(8,128)(2,1)} %collective-permute-done.5), channel_id=1, source_target_pairs={{0,32},{32,64},{64,96},{96,128},{128,160},{160,192},{192,224},{224... | collective-permute-start | bytes 2752520 | tf_op jit(solution)/shard_map/ppermute | solution.py:37
  149.9 36.2 %collective-permute-start.13 = (bf16[896,512]{1,0:T(8,128)(2,1)}, bf16[896,512]{1,0:T(8,128)(2,1)S(1)}, u32[]{:S(2)}, u32[]{:S(2)}) collective-permute-start(bf16[896,512]{1,0:T(8,128)(2,1)} %collective-permute-done.12), channel_id=1, source_target_pairs={{0,224},{32,0},{64,32},{96,64},{128,96},{160,128},{192,160},{224,1... | collective-permute-start | bytes 2752520 | tf_op jit(solution)/shard_map/ppermute | solution.py:38
  153.1 7.3 %copy-start = (bf16[384,2,7168]{0,2,1:T(8,128)(2,1)S(1)}, bf16[384,2,7168]{0,2,1:T(8,128)(2,1)}, u32[]{:S(2)}) copy-start(bf16[384,2,7168]{0,2,1:T(8,128)(2,1)} %all-gather.6.cloned.1.call-done) | copy-start | bytes 33030148
  160.3 3.1 %copy-start.1 = (bf16[896,1024]{1,0:T(8,128)(2,1)S(1)}, bf16[896,1024]{1,0:T(8,128)(2,1)}, u32[]{:S(2)}) copy-start(bf16[896,1024]{1,0:T(8,128)(2,1)} %param.8) | copy-start | bytes 5505028
  167.7 2.3 copy-start.20
  170.0 1.2 copy-start.16
  171.1 1.2 copy-start.12
  172.3 1.2 copy-start.8
  176.7 2.3 copy-start.18
  179.0 1.2 copy-start.14
  180.2 1.2 copy-start.10
  181.4 1.2 copy-start.6
Sparse Core Ops, SparseCore 0:
  9.9 66.7 all-gather.5

commit v5 on v4

--- a/solution.py
+++ b/solution.py
@@ -16,9 +16,10 @@
     n_row = lax.axis_size("row")
     col_index = lax.axis_index("col")
     row_index = lax.axis_index("row")
-    full_hidden = lax.all_gather(hidden_in, "col", axis=2, tiled=True)
-    full_gain = lax.all_gather(final_gain, "col", axis=1, tiled=True)
-    stream = full_hidden.astype(jnp.float32)
+    packed = jnp.concatenate([hidden_in.astype(jnp.float32), final_gain[None]], axis=0)
+    full_packed = lax.all_gather(packed, "col", axis=2, tiled=True)
+    stream = full_packed[:tok_rows]
+    full_gain = full_packed[tok_rows]
     mean_square = jnp.sum(stream * stream, axis=2) / D
     features = (stream * lax.rsqrt(mean_square[:, :, None] + EPS) * full_gain[None, :, :]).astype(
         jnp.bfloat16

time: 242 us -> 250 us (1.033)
  blocking collectives: 69.1 us -> 46.8 us
  waiting for transfers between devices: 94.5 us -> 108 us
  other arithmetic: 11.7 us -> 23 us
  local copies, waits for them, and re-layouts: 4.18 us -> 9.01 us
    all_gather x1 -> x0, blocking collectives: 23.8 us -> none  [per_device(): full_gain = lax.all_gather(final_gain, 'col', axis=1, tiled=True)]
    ppermute x7, waiting for transfers between devices: 93.7 us -> 108 us  [per_device(): left = lax.ppermute(left, 'row', forward)]
    convert_element_type x1, other arithmetic: 3.08 us -> 10.5 us  [per_device(): (stream * lax.rsqrt(mean_square[:, :, None] + EPS) * full_gain[None, :, :...]
    slice x0 -> x1, local copies, waits for them, and re-layouts: none -> 5.08 us  [per_device(): full_gain = full_packed[tok_rows]]
  transfers between devices with their start and end apart: 15 -> 15, of which waited for: 5 -> 7; matrix products, arithmetic and copies ran while one was open for 14% -> 18% of each run, Pallas kernels for 0% -> 0%
where the time goes in v5:
time: 250 us; the launch traced here: 249 us
  waiting for transfers between devices  108 us (43%)
  blocking collectives  46.8 us (19%)
  starting transfers between devices  26.5 us (11%)
  other arithmetic  23 us (9%)
  matrix products  21.7 us (9%)
  between operations  13.8 us (6%)
  local copies, waits for them, and re-layouts  9.01 us (4%)
    ppermute x7, waiting for transfers between devices, per_device(): left = lax.ppermute(left, 'row', forward)  108 us
    all_gather x1, blocking collectives, per_device(): parts = lax.all_gather(jnp.stack([row_max, exp_total, picked]), 'col')  25.2 us
    ppermute x7, starting transfers between devices, per_device(): right = lax.ppermute(right, 'row', backward)  24.5 us
    dot_general x16, matrix products, block_logits(): jnp.einsum('tmd,dv->tmv', features[shard], block, preferred_element_type=...  21.7 us
    all_gather x1, blocking collectives, per_device(): stats = lax.all_gather(jnp.stack([ratio_sums, squares, ratio_max]), 'row')  21.6 us
    convert_element_type x1, other arithmetic, per_device(): (stream * lax.rsqrt(mean_square[:, :, None] + EPS) * full_gain[None, :, :...  10.5 us
    reduce_sum x1, other arithmetic, per_device(): mean_square = jnp.sum(stream * stream, axis=2) / D  8.41 us
    slice x1, local copies, waits for them, and re-layouts, per_device(): full_gain = full_packed[tok_rows]  5.08 us
  transfers between devices with their start and end apart: 15, of which 7 were waited for; matrix products, arithmetic and copies ran while one was open for 18% of the time, Pallas kernels for 0%

profile of v5, /device:TPU:2, one launch (start us, length us, event | category | flops | bytes accessed | tf_op | source)
XLA Modules:
  0.0 249.2 jit_solution(11491957920642252306)
XLA Ops:
  6.5 1.0 convert_element_type.10
  7.6 0.9 copy.65
  8.5 1.0 pad_maximum_fusion.1
  9.8 2.0 collective-permute-start
  11.8 4.0 %collective-permute-start.7 = (bf16[896,512]{1,0:T(8,128)(2,1)S(1)}, bf16[896,512]{1,0:T(8,128)(2,1)S(1)}, u32[]{:S(2)}, u32[]{:S(2)}) collective-permute-start(bf16[896,512]{1,0:T(8,128)(2,1)S(1)} %get-tuple-element.16), channel_id=1, source_target_pairs={{0,224},{32,0},{64,32},{96,64},{128,96},{160,128},{192,160},{224,1... | collective-permute-start | bytes 2752520 | tf_op jit(solution)/shard_map/ppermute | solution.py:39
  15.8 20.3 %collective-permute-done = bf16[896,512]{1,0:T(8,128)(2,1)S(1)} collective-permute-done((bf16[896,512]{1,0:T(8,128)(2,1)S(1)}, bf16[896,512]{1,0:T(8,128)(2,1)S(1)}, u32[]{:S(2)}, u32[]{:S(2)}) %collective-permute-start) | collective-permute-done | bytes 917536 | tf_op jit(solution)/shard_map/ppermute | solution.py:38
  36.1 1.0 copy-done.3
  37.1 3.2 %collective-permute-start.8 = (bf16[896,512]{1,0:T(8,128)(2,1)S(1)}, bf16[896,512]{1,0:T(8,128)(2,1)S(1)}, u32[]{:S(2)}, u32[]{:S(2)}) collective-permute-start(bf16[896,512]{1,0:T(8,128)(2,1)S(1)} %collective-permute-done.7), channel_id=1, source_target_pairs={{0,224},{32,0},{64,32},{96,64},{128,96},{160,128},{192,160},{224,1... | collective-permute-start | bytes 2752520 | tf_op jit(solution)/shard_map/ppermute | solution.py:39
  40.3 18.6 %collective-permute-done.1 = bf16[896,512]{1,0:T(8,128)(2,1)S(1)} collective-permute-done((bf16[896,512]{1,0:T(8,128)(2,1)S(1)}, bf16[896,512]{1,0:T(8,128)(2,1)S(1)}, u32[]{:S(2)}, u32[]{:S(2)}) %collective-permute-start.1) | collective-permute-done | bytes 917536 | tf_op jit(solution)/shard_map/ppermute | solution.py:38
  58.9 0.3 collective-permute-done.8
  59.1 3.7 %collective-permute-start.9 = (bf16[896,512]{1,0:T(8,128)(2,1)S(1)}, bf16[896,512]{1,0:T(8,128)(2,1)S(1)}, u32[]{:S(2)}, u32[]{:S(2)}) collective-permute-start(bf16[896,512]{1,0:T(8,128)(2,1)S(1)} %collective-permute-done.8), channel_id=1, source_target_pairs={{0,224},{32,0},{64,32},{96,64},{128,96},{160,128},{192,160},{224,1... | collective-permute-start | bytes 2752520 | tf_op jit(solution)/shard_map/ppermute | solution.py:39
  62.8 18.0 %collective-permute-done.2 = bf16[896,512]{1,0:T(8,128)(2,1)S(1)} collective-permute-done((bf16[896,512]{1,0:T(8,128)(2,1)S(1)}, bf16[896,512]{1,0:T(8,128)(2,1)S(1)}, u32[]{:S(2)}, u32[]{:S(2)}) %collective-permute-start.2) | collective-permute-done | bytes 917536 | tf_op jit(solution)/shard_map/ppermute | solution.py:38
  80.9 3.6 %collective-permute-start.10 = (bf16[896,512]{1,0:T(8,128)(2,1)S(1)}, bf16[896,512]{1,0:T(8,128)(2,1)S(1)}, u32[]{:S(2)}, u32[]{:S(2)}) collective-permute-start(bf16[896,512]{1,0:T(8,128)(2,1)S(1)} %collective-permute-done.9), channel_id=1, source_target_pairs={{0,224},{32,0},{64,32},{96,64},{128,96},{160,128},{192,160},{224,1... | collective-permute-start | bytes 2752520 | tf_op jit(solution)/shard_map/ppermute | solution.py:39
  84.5 17.5 %collective-permute-done.3 = bf16[896,512]{1,0:T(8,128)(2,1)S(1)} collective-permute-done((bf16[896,512]{1,0:T(8,128)(2,1)S(1)}, bf16[896,512]{1,0:T(8,128)(2,1)S(1)}, u32[]{:S(2)}, u32[]{:S(2)}) %collective-permute-start.3) | collective-permute-done | bytes 917536 | tf_op jit(solution)/shard_map/ppermute | solution.py:38
  102.1 3.4 %collective-permute-start.11 = (bf16[896,512]{1,0:T(8,128)(2,1)S(1)}, bf16[896,512]{1,0:T(8,128)(2,1)S(1)}, u32[]{:S(2)}, u32[]{:S(2)}) collective-permute-start(bf16[896,512]{1,0:T(8,128)(2,1)S(1)} %collective-permute-done.10), channel_id=1, source_target_pairs={{0,224},{32,0},{64,32},{96,64},{128,96},{160,128},{192,160},{224,1... | collective-permute-start | bytes 2752520 | tf_op jit(solution)/shard_map/ppermute | solution.py:39
  105.5 17.2 %collective-permute-done.4 = bf16[896,512]{1,0:T(8,128)(2,1)} collective-permute-done((bf16[896,512]{1,0:T(8,128)(2,1)S(1)}, bf16[896,512]{1,0:T(8,128)(2,1)}, u32[]{:S(2)}, u32[]{:S(2)}) %collective-permute-start.4) | collective-permute-done | bytes 917536 | tf_op jit(solution)/shard_map/ppermute | solution.py:38
  122.7 3.3 %collective-permute-start.12 = (bf16[896,512]{1,0:T(8,128)(2,1)S(1)}, bf16[896,512]{1,0:T(8,128)(2,1)}, u32[]{:S(2)}, u32[]{:S(2)}) collective-permute-start(bf16[896,512]{1,0:T(8,128)(2,1)S(1)} %collective-permute-done.11), channel_id=1, source_target_pairs={{0,224},{32,0},{64,32},{96,64},{128,96},{160,128},{192,160},{224,1... | collective-permute-start | bytes 2752520 | tf_op jit(solution)/shard_map/ppermute | solution.py:39
  126.4 0.3 broadcast_compare_fusion
  126.7 16.4 %collective-permute-done.5 = bf16[896,512]{1,0:T(8,128)(2,1)} collective-permute-done((bf16[896,512]{1,0:T(8,128)(2,1)}, bf16[896,512]{1,0:T(8,128)(2,1)}, u32[]{:S(2)}, u32[]{:S(2)}) %collective-permute-start.5) | collective-permute-done | bytes 917536 | tf_op jit(solution)/shard_map/ppermute | solution.py:38
  143.2 3.2 %collective-permute-start.13 = (bf16[896,512]{1,0:T(8,128)(2,1)}, bf16[896,512]{1,0:T(8,128)(2,1)S(1)}, u32[]{:S(2)}, u32[]{:S(2)}) collective-permute-start(bf16[896,512]{1,0:T(8,128)(2,1)} %collective-permute-done.12), channel_id=1, source_target_pairs={{0,224},{32,0},{64,32},{96,64},{128,96},{160,128},{192,160},{224,1... | collective-permute-start | bytes 2752520 | tf_op jit(solution)/shard_map/ppermute | solution.py:39
  146.4 8.4 %multiply_reduce_fusion = f32[384,2]{0,1:T(2,128)S(1)} fusion(f32[385,2,7168]{0,2,1:T(8,128)} %all-gather.5.cloned.1.call-done), kind=kLoop, calls=%fused_computation.1 | loop fusion | flops 11009280 | bytes 22023168 | tf_op jit(solution)/shard_map/reduce_sum | solution.py:23
  154.8 5.1 %slice_reduce_fusion = f32[2,7168]{1,0:T(2,128)S(1)} fusion(f32[385,2,7168]{0,2,1:T(8,128)} %all-gather.5.cloned.1.call-done), kind=kLoop, calls=%fused_computation.2 | loop fusion | bytes 114688 | tf_op jit(solution)/shard_map/slice | solution.py:22
  159.9 10.5 %multiply_convert_fusion = bf16[384,2,7168]{0,2,1:T(8,128)(2,1)S(1)} fusion(f32[385,2,7168]{0,2,1:T(8,128)} %all-gather.5.cloned.1.call-done, f32[2,7168]{1,0:T(2,128)S(1)} %slice_reduce_fusion, f32[384,2]{0,1:T(2,128)S(1)} %add_rsqrt_fusion), kind=kLoop, calls=%fused_computation | loop fusion | flops 16515072 | bytes 33090560 | tf_op jit(solution)/shard_map/convert_element_type | solution.py:24
  170.4 1.0 fusion.28
  171.5 1.0 fusion.26
  172.5 2.2 fusion.14
  174.7 2.3 fusion.16
  177.0 1.0 fusion.18
  178.1 1.0 fusion.20
  179.1 0.2 copy-done.10
  179.3 1.0 fusion.22
  180.3 0.2 copy-done.6
  180.5 1.0 fusion.24
  181.5 0.2 copy-done.20
  181.7 1.0 fusion.3
  182.7 0.2 copy-done.16
  182.9 1.0 fusion.5
  183.9 0.2 copy-done.12
  184.0 1.0 fusion.7
  185.1 2.3 fusion.1
  187.3 1.0 fusion.9
  188.5 1.0 fusion.11
  189.5 2.5 %fusion.85 = (f32[384,2]{0,1:T(2,128)S(1)}, f32[384,2,512]{2,0,1:T(8,128)S(1)}) fusion(bf16[896,512]{1,0:T(8,128)(2,1)} %collective-permute-done.6, bf16[384,2,8,896]{0,3,2,1:T(8,128)(2,1)S(1)} %bitcast.163, s32[]{:T(128)S(6)} %select_n.144, f32[384,2,512]{2,0,1:T(8,128)S(1)} %fusion.14, f32[384,2,512]{2,0,1:T(8,128)S(1)} %fusion.16, ...), kind=kOutput, calls=%fused_computation.117 | convolution fusion | flops 707788032 | bytes 14879748 | tf_op jit(solution)/shard_map/tmd,dv->tmv/dot_general | solution.py:30
  192.1 1.3 fusion.86
  193.4 1.1 exponential_reduce_fusion
  194.5 25.2 %all-gather = f32[96,384,2]{1,2,0:T(2,128)S(1)} all-gather(f32[3,384,2]{1,2,0:T(2,128)S(1)} %pad_maximum_fusion.2), channel_id=2, replica_groups=mesh['row'=8,'col'=32] {'col'}, dimensions={0}, use_global_device_ids=true | all-gather | bytes 304128 | tf_op jit(solution)/shard_map/all_gather | solution.py:49
  220.1 21.6 %all-gather.2 = f32[8,3,16]{2,1,0:T(4,128)S(1)} all-gather(f32[1,3,16]{2,1,0:T(4,128)S(1)} %maximum_bitcast_fusion), channel_id=3, replica_groups=mesh['row'=8,'col'=32] {'row'}, dimensions={0}, use_global_device_ids=true | all-gather | bytes 1728 | tf_op jit(solution)/shard_map/all_gather | solution.py:62
  241.8 0.6 copy.82
  (74 shorter events, 1.4 us)
Async XLA Ops:
  6.5 139.9 %all-gather.5.cloned.1.call-start = ((), (), s32[]{:S(2)}) async-start(), calls=%async_computation | async-start | bytes 30277632 | tf_op jit(solution)/shard_map/all_gather | solution.py:20
  7.6 2.0 copy-start
  9.6 116.4 %copy-start.2 = (s32[16]{0:T(128)S(1)}, s32[16]{0:T(128)}, u32[]{:S(2)}) copy-start(s32[16]{0:T(128)} %param.9) | copy-start | bytes 196
  9.6 116.8 %copy-start.21 = (s32[16]{0:T(128)S(1)}, s32[16]{0:T(128)}, u32[]{:S(2)}) copy-start(s32[16]{0:T(128)} %param.11) | copy-start | bytes 196
  9.6 116.8 %copy-start.1 = (s32[384]{0:T(512)S(1)}, s32[384]{0:T(512)}, u32[]{:S(2)}) copy-start(s32[384]{0:T(512)} %param.10) | copy-start | bytes 4612
  9.8 26.3 %collective-permute-start = (bf16[896,512]{1,0:T(8,128)(2,1)S(1)}, bf16[896,512]{1,0:T(8,128)(2,1)S(1)}, u32[]{:S(2)}, u32[]{:S(2)}) collective-permute-start(bf16[896,512]{1,0:T(8,128)(2,1)S(1)} %get-tuple-element.15), channel_id=1, source_target_pairs={{0,32},{32,64},{64,96},{96,128},{128,160},{160,192},{192,224},{224... | collective-permute-start | bytes 2752520 | tf_op jit(solution)/shard_map/ppermute | solution.py:38
  11.8 24.3 %collective-permute-start.7 = (bf16[896,512]{1,0:T(8,128)(2,1)S(1)}, bf16[896,512]{1,0:T(8,128)(2,1)S(1)}, u32[]{:S(2)}, u32[]{:S(2)}) collective-permute-start(bf16[896,512]{1,0:T(8,128)(2,1)S(1)} %get-tuple-element.16), channel_id=1, source_target_pairs={{0,224},{32,0},{64,32},{96,64},{128,96},{160,128},{192,160},{224,1... | collective-permute-start | bytes 2752520 | tf_op jit(solution)/shard_map/ppermute | solution.py:39
  36.0 23.1 %copy-start.5 = (bf16[896,512]{1,0:T(8,128)(2,1)}, bf16[896,512]{1,0:T(8,128)(2,1)S(1)}, u32[]{:S(2)}) copy-start(bf16[896,512]{1,0:T(8,128)(2,1)S(1)} %collective-permute-done) | copy-start | bytes 2752516
  36.0 22.8 %collective-permute-start.1 = (bf16[896,512]{1,0:T(8,128)(2,1)S(1)}, bf16[896,512]{1,0:T(8,128)(2,1)S(1)}, u32[]{:S(2)}, u32[]{:S(2)}) collective-permute-start(bf16[896,512]{1,0:T(8,128)(2,1)S(1)} %collective-permute-done), channel_id=1, source_target_pairs={{0,32},{32,64},{64,96},{96,128},{128,160},{160,192},{192,224},{224... | collective-permute-start | bytes 2752520 | tf_op jit(solution)/shard_map/ppermute | solution.py:38
  36.1 1.0 copy-start.3
  37.1 22.0 %collective-permute-start.8 = (bf16[896,512]{1,0:T(8,128)(2,1)S(1)}, bf16[896,512]{1,0:T(8,128)(2,1)S(1)}, u32[]{:S(2)}, u32[]{:S(2)}) collective-permute-start(bf16[896,512]{1,0:T(8,128)(2,1)S(1)} %collective-permute-done.7), channel_id=1, source_target_pairs={{0,224},{32,0},{64,32},{96,64},{128,96},{160,128},{192,160},{224,1... | collective-permute-start | bytes 2752520 | tf_op jit(solution)/shard_map/ppermute | solution.py:39
  58.9 22.0 %copy-start.9 = (bf16[896,512]{1,0:T(8,128)(2,1)}, bf16[896,512]{1,0:T(8,128)(2,1)S(1)}, u32[]{:S(2)}) copy-start(bf16[896,512]{1,0:T(8,128)(2,1)S(1)} %collective-permute-done.1) | copy-start | bytes 2752516
  58.9 22.0 %collective-permute-start.2 = (bf16[896,512]{1,0:T(8,128)(2,1)S(1)}, bf16[896,512]{1,0:T(8,128)(2,1)S(1)}, u32[]{:S(2)}, u32[]{:S(2)}) collective-permute-start(bf16[896,512]{1,0:T(8,128)(2,1)S(1)} %collective-permute-done.1), channel_id=1, source_target_pairs={{0,32},{32,64},{64,96},{96,128},{128,160},{160,192},{192,224},{224... | collective-permute-start | bytes 2752520 | tf_op jit(solution)/shard_map/ppermute | solution.py:38
  59.1 3.7 %copy-start.7 = (bf16[896,512]{1,0:T(8,128)(2,1)}, bf16[896,512]{1,0:T(8,128)(2,1)S(1)}, u32[]{:S(2)}) copy-start(bf16[896,512]{1,0:T(8,128)(2,1)S(1)} %collective-permute-done.8) | copy-start | bytes 2752516
  59.1 21.7 %collective-permute-start.9 = (bf16[896,512]{1,0:T(8,128)(2,1)S(1)}, bf16[896,512]{1,0:T(8,128)(2,1)S(1)}, u32[]{:S(2)}, u32[]{:S(2)}) collective-permute-start(bf16[896,512]{1,0:T(8,128)(2,1)S(1)} %collective-permute-done.8), channel_id=1, source_target_pairs={{0,224},{32,0},{64,32},{96,64},{128,96},{160,128},{192,160},{224,1... | collective-permute-start | bytes 2752520 | tf_op jit(solution)/shard_map/ppermute | solution.py:39
  80.9 21.2 %copy-start.13 = (bf16[896,512]{1,0:T(8,128)(2,1)}, bf16[896,512]{1,0:T(8,128)(2,1)S(1)}, u32[]{:S(2)}) copy-start(bf16[896,512]{1,0:T(8,128)(2,1)S(1)} %collective-permute-done.2) | copy-start | bytes 2752516
  80.9 21.2 %collective-permute-start.3 = (bf16[896,512]{1,0:T(8,128)(2,1)S(1)}, bf16[896,512]{1,0:T(8,128)(2,1)S(1)}, u32[]{:S(2)}, u32[]{:S(2)}) collective-permute-start(bf16[896,512]{1,0:T(8,128)(2,1)S(1)} %collective-permute-done.2), channel_id=1, source_target_pairs={{0,32},{32,64},{64,96},{96,128},{128,160},{160,192},{192,224},{224... | collective-permute-start | bytes 2752520 | tf_op jit(solution)/shard_map/ppermute | solution.py:38
  80.9 3.7 %copy-start.11 = (bf16[896,512]{1,0:T(8,128)(2,1)}, bf16[896,512]{1,0:T(8,128)(2,1)S(1)}, u32[]{:S(2)}) copy-start(bf16[896,512]{1,0:T(8,128)(2,1)S(1)} %collective-permute-done.9) | copy-start | bytes 2752516
  80.9 21.2 %collective-permute-start.10 = (bf16[896,512]{1,0:T(8,128)(2,1)S(1)}, bf16[896,512]{1,0:T(8,128)(2,1)S(1)}, u32[]{:S(2)}, u32[]{:S(2)}) collective-permute-start(bf16[896,512]{1,0:T(8,128)(2,1)S(1)} %collective-permute-done.9), channel_id=1, source_target_pairs={{0,224},{32,0},{64,32},{96,64},{128,96},{160,128},{192,160},{224,1... | collective-permute-start | bytes 2752520 | tf_op jit(solution)/shard_map/ppermute | solution.py:39
  102.1 20.6 %copy-start.17 = (bf16[896,512]{1,0:T(8,128)(2,1)}, bf16[896,512]{1,0:T(8,128)(2,1)S(1)}, u32[]{:S(2)}) copy-start(bf16[896,512]{1,0:T(8,128)(2,1)S(1)} %collective-permute-done.3) | copy-start | bytes 2752516
  102.1 20.6 %collective-permute-start.4 = (bf16[896,512]{1,0:T(8,128)(2,1)S(1)}, bf16[896,512]{1,0:T(8,128)(2,1)}, u32[]{:S(2)}, u32[]{:S(2)}) collective-permute-start(bf16[896,512]{1,0:T(8,128)(2,1)S(1)} %collective-permute-done.3), channel_id=1, source_target_pairs={{0,32},{32,64},{64,96},{96,128},{128,160},{160,192},{192,224},{224... | collective-permute-start | bytes 2752520 | tf_op jit(solution)/shard_map/ppermute | solution.py:38
  102.1 3.4 %copy-start.15 = (bf16[896,512]{1,0:T(8,128)(2,1)}, bf16[896,512]{1,0:T(8,128)(2,1)S(1)}, u32[]{:S(2)}) copy-start(bf16[896,512]{1,0:T(8,128)(2,1)S(1)} %collective-permute-done.10) | copy-start | bytes 2752516
  102.1 20.6 %collective-permute-start.11 = (bf16[896,512]{1,0:T(8,128)(2,1)S(1)}, bf16[896,512]{1,0:T(8,128)(2,1)S(1)}, u32[]{:S(2)}, u32[]{:S(2)}) collective-permute-start(bf16[896,512]{1,0:T(8,128)(2,1)S(1)} %collective-permute-done.10), channel_id=1, source_target_pairs={{0,224},{32,0},{64,32},{96,64},{128,96},{160,128},{192,160},{224,1... | collective-permute-start | bytes 2752520 | tf_op jit(solution)/shard_map/ppermute | solution.py:39
  122.7 20.5 %collective-permute-start.5 = (bf16[896,512]{1,0:T(8,128)(2,1)}, bf16[896,512]{1,0:T(8,128)(2,1)}, u32[]{:S(2)}, u32[]{:S(2)}) collective-permute-start(bf16[896,512]{1,0:T(8,128)(2,1)} %collective-permute-done.4), channel_id=1, source_target_pairs={{0,32},{32,64},{64,96},{96,128},{128,160},{160,192},{192,224},{224... | collective-permute-start | bytes 2752520 | tf_op jit(solution)/shard_map/ppermute | solution.py:38
  122.7 20.5 %copy-start.19 = (bf16[896,512]{1,0:T(8,128)(2,1)}, bf16[896,512]{1,0:T(8,128)(2,1)S(1)}, u32[]{:S(2)}) copy-start(bf16[896,512]{1,0:T(8,128)(2,1)S(1)} %collective-permute-done.11) | copy-start | bytes 2752516
  122.7 20.5 %collective-permute-start.12 = (bf16[896,512]{1,0:T(8,128)(2,1)S(1)}, bf16[896,512]{1,0:T(8,128)(2,1)}, u32[]{:S(2)}, u32[]{:S(2)}) collective-permute-start(bf16[896,512]{1,0:T(8,128)(2,1)S(1)} %collective-permute-done.11), channel_id=1, source_target_pairs={{0,224},{32,0},{64,32},{96,64},{128,96},{160,128},{192,160},{224,1... | collective-permute-start | bytes 2752520 | tf_op jit(solution)/shard_map/ppermute | solution.py:39
  143.2 46.4 %collective-permute-start.6 = (bf16[896,512]{1,0:T(8,128)(2,1)}, bf16[896,512]{1,0:T(8,128)(2,1)}, u32[]{:S(2)}, u32[]{:S(2)}) collective-permute-start(bf16[896,512]{1,0:T(8,128)(2,1)} %collective-permute-done.5), channel_id=1, source_target_pairs={{0,32},{32,64},{64,96},{96,128},{128,160},{160,192},{192,224},{224... | collective-permute-start | bytes 2752520 | tf_op jit(solution)/shard_map/ppermute | solution.py:38
  143.2 48.9 %collective-permute-start.13 = (bf16[896,512]{1,0:T(8,128)(2,1)}, bf16[896,512]{1,0:T(8,128)(2,1)S(1)}, u32[]{:S(2)}, u32[]{:S(2)}) collective-permute-start(bf16[896,512]{1,0:T(8,128)(2,1)} %collective-permute-done.12), channel_id=1, source_target_pairs={{0,224},{32,0},{64,32},{96,64},{128,96},{160,128},{192,160},{224,1... | collective-permute-start | bytes 2752520 | tf_op jit(solution)/shard_map/ppermute | solution.py:39
  174.7 2.3 copy-start.18
  177.0 1.2 copy-start.14
  178.1 1.2 copy-start.10
  179.3 1.2 copy-start.6
  180.5 1.2 copy-start.20
  181.7 1.2 copy-start.16
  182.9 1.2 copy-start.12
  185.0 2.3 copy-start.8
  187.3 1.2 copy-start.4
Sparse Core Ops, SparseCore 0:
  9.9 110.7 all-gather.4

commit v6 on v2

--- a/solution.py
+++ b/solution.py
@@ -18,26 +18,49 @@
     row_index = lax.axis_index("row")
     full_hidden = lax.all_gather(hidden_in, "col", axis=2, tiled=True)
     full_gain = lax.all_gather(final_gain, "col", axis=1, tiled=True)
-    stream = full_hidden.astype(jnp.float32)
-    mean_square = jnp.sum(stream * stream, axis=2) / D
-    features = (stream * lax.rsqrt(mean_square[:, :, None] + EPS) * full_gain[None, :, :]).astype(
-        jnp.bfloat16
-    )
-
-    def block_logits(block, shard):
-        rows = lax.dynamic_slice_in_dim(features, shard * shard_rows, shard_rows, axis=2)
-        return jnp.einsum("tmd,dv->tmv", rows, block, preferred_element_type=jnp.float32)
-
     forward = [(i, (i + 1) % n_row) for i in range(n_row)]
     backward = [(i, (i - 1) % n_row) for i in range(n_row)]
     left, right = unembed[:, :half], unembed[:, half:]
-    logits_left = block_logits(left, row_index)
-    logits_right = block_logits(right, row_index)
+    pending = [(left, right, row_index, row_index)]
+    features = None
+    logits_left = None
+    logits_right = None
+
+    def block_logits(block, shard):
+        return jnp.einsum("tmd,dv->tmv", features[shard], block, preferred_element_type=jnp.float32)
+
+    def add_pending(logits_left, logits_right):
+        for block_left, block_right, shard_left, shard_right in pending:
+            part_left = block_logits(block_left, shard_left)
+            part_right = block_logits(block_right, shard_right)
+            if logits_left is None:
+                logits_left, logits_right = part_left, part_right
+            else:
+                logits_left = logits_left + part_left
+                logits_right = logits_right + part_right
+        return logits_left, logits_right
+
     for step in range(1, n_row):
+        if step == 3:
+            left, right, full_gain = lax.optimization_barrier((left, right, full_gain))
+        if step == 5:
+            stream = full_hidden.astype(jnp.float32)
+            mean_square = jnp.sum(stream * stream, axis=2) / D
+            features = (
+                stream * lax.rsqrt(mean_square[:, :, None] + EPS) * full_gain[None, :, :]
+            ).astype(jnp.bfloat16)
+            features = features.reshape(tok_rows, 2, n_row, shard_rows).transpose(2, 0, 1, 3)
+            left, right, features = lax.optimization_barrier((left, right, features))
+        if step >= 6:
+            logits_left, logits_right = add_pending(logits_left, logits_right)
+            pending = []
+            left, right, logits_left, logits_right = lax.optimization_barrier(
+                (left, right, logits_left, logits_right)
+            )
         left = lax.ppermute(left, "row", forward)
         right = lax.ppermute(right, "row", backward)
-        logits_left = logits_left + block_logits(left, (row_index - step) % n_row)
-        logits_right = logits_right + block_logits(right, (row_index + step) % n_row)
+        pending.append((left, right, (row_index - step) % n_row, (row_index + step) % n_row))
+    logits_left, logits_right = add_pending(logits_left, logits_right)
     logits = jnp.concatenate([logits_left, logits_right], axis=2)
     row_max = jnp.max(logits, axis=2)
     exp_total = jnp.sum(jnp.exp(logits - row_max[:, :, None]), axis=2)

time: 273 us -> 263 us (0.963)
  local copies, waits for them, and re-layouts: 34 us -> 17.6 us
  matrix products: 23.6 us -> 33.9 us
  waiting for transfers between devices: 93.4 us -> 86.4 us
  other arithmetic: 11.7 us -> 15.9 us
    ppermute x7, waiting for transfers between devices: 93.3 us -> 58.1 us  [per_device(): left = lax.ppermute(left, 'row', forward)]
    ppermute x7, waiting for transfers between devices: 0.02 us -> 27.6 us  [per_device(): right = lax.ppermute(right, 'row', backward)]
    all_gather x1 -> x0, local copies, waits for them, and re-layouts: 27.5 us -> none  [per_device(): full_hidden = lax.all_gather(hidden_in, 'col', axis=2, tiled=True)]
    reshape x0 -> x1, local copies, waits for them, and re-layouts: none -> 14.2 us  [per_device(): features.reshape(tok_rows, 2, n_row, shard_rows).transpose(2, 0, 1, 3)]
    dot_general x16, matrix products: 23.6 us -> 33.9 us  [block_logits(): jnp.einsum('tmd,dv->tmv', features[shard], block, preferred_element_type=...]
    ppermute x7, starting transfers between devices: 23.5 us -> 18.6 us  [per_device(): right = lax.ppermute(right, 'row', backward)]
    unnamed x46 -> x33, local copies, waits for them, and re-layouts: 4.29 us -> 1.19 us
    ppermute x7, starting transfers between devices: 2.09 us -> 5.03 us  [per_device(): left = lax.ppermute(left, 'row', forward)]
  transfers between devices with their start and end apart: 15 -> 15, of which waited for: 5 -> 6; matrix products, arithmetic and copies ran while one was open for 22% -> 17% of each run, Pallas kernels for 0% -> 0%
where the time goes in v6:
time: 263 us; the launch traced here: 262 us
  waiting for transfers between devices  86.4 us (33%)
  blocking collectives  70.6 us (27%)
  matrix products  33.9 us (13%)
  starting transfers between devices  23.7 us (9%)
  local copies, waits for them, and re-layouts  17.6 us (7%)
  other arithmetic  15.9 us (6%)
  between operations  13.7 us (5%)
    ppermute x7, waiting for transfers between devices, per_device(): left = lax.ppermute(left, 'row', forward)  58.1 us
    dot_general x16, matrix products, block_logits(): jnp.einsum('tmd,dv->tmv', features[shard], block, preferred_element_type=...  33.9 us
    ppermute x7, waiting for transfers between devices, per_device(): right = lax.ppermute(right, 'row', backward)  27.6 us
    all_gather x1, blocking collectives, per_device(): full_gain = lax.all_gather(final_gain, 'col', axis=1, tiled=True)  24.7 us
    all_gather x1, blocking collectives, per_device(): parts = lax.all_gather(jnp.stack([row_max, exp_total, picked]), 'col')  23.2 us
    all_gather x1, blocking collectives, per_device(): stats = lax.all_gather(jnp.stack([ratio_sums, squares, ratio_max]), 'row')  22.7 us
    ppermute x7, starting transfers between devices, per_device(): right = lax.ppermute(right, 'row', backward)  18.6 us
    reshape x1, local copies, waits for them, and re-layouts, per_device(): features.reshape(tok_rows, 2, n_row, shard_rows).transpose(2, 0, 1, 3)  14.2 us
  transfers between devices with their start and end apart: 15, of which 6 were waited for; matrix products, arithmetic and copies ran while one was open for 17% of the time, Pallas kernels for 0%

profile of v6, /device:TPU:2, one launch (start us, length us, event | category | flops | bytes accessed | tf_op | source)
XLA Modules:
  0.0 261.8 jit_solution(13124418031170732497)
XLA Ops:
  6.5 0.7 all-gather.6.cloned.1.call-update
  7.3 1.6 fusion.89
  8.8 2.0 collective-permute-start
  10.8 4.0 %collective-permute-start.2 = (bf16[896,512]{1,0:T(8,128)(2,1)S(1)}, bf16[896,512]{1,0:T(8,128)(2,1)S(1)}, u32[]{:S(2)}, u32[]{:S(2)}) collective-permute-start(bf16[896,512]{1,0:T(8,128)(2,1)S(1)} %get-tuple-element.47), channel_id=1, source_target_pairs={{0,224},{32,0},{64,32},{96,64},{128,96},{160,128},{192,160},{224,1... | collective-permute-start | bytes 2752520 | tf_op jit(solution)/shard_map/ppermute | solution.py:61
  14.9 20.3 %collective-permute-done = bf16[896,512]{1,0:T(8,128)(2,1)S(1)} collective-permute-done((bf16[896,512]{1,0:T(8,128)(2,1)S(1)}, bf16[896,512]{1,0:T(8,128)(2,1)S(1)}, u32[]{:S(2)}, u32[]{:S(2)}) %collective-permute-start) | collective-permute-done | bytes 917536 | tf_op jit(solution)/shard_map/ppermute | solution.py:60
  35.2 3.2 %collective-permute-start.3 = (bf16[896,512]{1,0:T(8,128)(2,1)S(1)}, bf16[896,512]{1,0:T(8,128)(2,1)}, u32[]{:S(2)}, u32[]{:S(2)}) collective-permute-start(bf16[896,512]{1,0:T(8,128)(2,1)S(1)} %collective-permute-done.2), channel_id=1, source_target_pairs={{0,224},{32,0},{64,32},{96,64},{128,96},{160,128},{192,160},{224,1... | collective-permute-start | bytes 2752520 | tf_op jit(solution)/shard_map/ppermute | solution.py:61
  38.4 24.7 %all-gather.2 = f32[32,224,2]{1,2,0:T(2,128)S(1)} all-gather(f32[1,224,2]{1,2,0:T(2,128)S(1)} %bitcast.158), channel_id=1, replica_groups=mesh['row'=8,'col'=32] {'col'}, dimensions={0}, use_global_device_ids=true | all-gather | bytes 59136 | tf_op jit(solution)/shard_map/all_gather | solution.py:20
  63.4 3.2 %collective-permute-start.6 = (bf16[896,512]{1,0:T(8,128)(2,1)}, bf16[896,512]{1,0:T(8,128)(2,1)}, u32[]{:S(2)}, u32[]{:S(2)}) collective-permute-start(bf16[896,512]{1,0:T(8,128)(2,1)} %collective-permute-done.3), channel_id=1, source_target_pairs={{0,224},{32,0},{64,32},{96,64},{128,96},{160,128},{192,160},{224,1... | collective-permute-start | bytes 2752520 | tf_op jit(solution)/shard_map/ppermute | solution.py:61
  66.6 20.7 %collective-permute-done.4 = bf16[896,512]{1,0:T(8,128)(2,1)} collective-permute-done((bf16[896,512]{1,0:T(8,128)(2,1)S(1)}, bf16[896,512]{1,0:T(8,128)(2,1)}, u32[]{:S(2)}, u32[]{:S(2)}) %collective-permute-start.4) | collective-permute-done | bytes 917536 | tf_op jit(solution)/shard_map/ppermute | solution.py:60
  87.3 3.2 %collective-permute-start.7 = (bf16[896,512]{1,0:T(8,128)(2,1)}, bf16[896,512]{1,0:T(8,128)(2,1)}, u32[]{:S(2)}, u32[]{:S(2)}) collective-permute-start(bf16[896,512]{1,0:T(8,128)(2,1)} %collective-permute-done.6), channel_id=1, source_target_pairs={{0,224},{32,0},{64,32},{96,64},{128,96},{160,128},{192,160},{224,1... | collective-permute-start | bytes 2752520 | tf_op jit(solution)/shard_map/ppermute | solution.py:61
  90.5 6.5 %fusion = f32[384,2]{0,1:T(2,128)S(1)} fusion(bf16[384,2,7168]{0,2,1:T(8,128)(2,1)} %all-gather.6.cloned.1.call-done), kind=kLoop, calls=%fused_computation.2 | loop fusion | flops 16514304 | bytes 11013120 | tf_op jit(solution)/shard_map/reduce_sum | solution.py:48
  97.0 0.8 copy-done
  97.8 6.0 %fusion.2 = bf16[384,2,7168]{0,2,1:T(8,128)(2,1)} fusion(bf16[384,2,7168]{0,2,1:T(8,128)(2,1)S(1)} %copy-done, f32[2,7168]{1,0:T(2,128)S(1)} %bitcast.151, f32[384,2]{0,1:T(2,128)S(1)} %add_rsqrt_fusion), kind=kLoop, calls=%fused_computation.4 | loop fusion | flops 22020096 | bytes 22080512 | tf_op jit(solution)/shard_map/convert_element_type | solution.py:51
  103.8 14.2 %copy.23 = bf16[384,2,8,896]{3,0,1,2:T(8,128)(2,1)} copy(bf16[384,2,8,896]{0,3,2,1:T(8,128)(2,1)} %bitcast.131) | data formatting | bytes 22020096 | tf_op jit(solution)/shard_map/reshape | solution.py:52
  118.1 2.7 %fusion.29 = f32[384,2,512]{2,0,1:T(8,128)S(1)} fusion(bf16[8,384,2,896]{3,1,2,0:T(8,128)(2,1)} %bitcast.132, s32[]{:T(128)S(6)} %select_n.130, bf16[896,1024]{1,0:T(8,128)(2,1)S(1)} %copy-done.3), kind=kOutput, calls=%fused_computation.36 | convolution fusion | flops 704643072 | bytes 3866628 | tf_op jit(solution)/shard_map/tmd,dv->tmv/dot_general | solution.py:30
  120.7 3.1 %fusion.31 = f32[384,2,512]{2,0,1:T(8,128)S(1)} fusion(bf16[8,384,2,896]{3,1,2,0:T(8,128)(2,1)} %bitcast.133, s32[]{:T(128)S(6)} %select_n.130, bf16[896,1024]{1,0:T(8,128)(2,1)S(1)} %copy-done.3), kind=kOutput, calls=%fused_computation.38 | convolution fusion | flops 704643072 | bytes 3866628 | tf_op jit(solution)/shard_map/tmd,dv->tmv/dot_general | solution.py:30
  123.8 0.3 collective-permute-start.9
  124.1 2.0 collective-permute-start.8
  126.1 2.6 fusion.14
  128.7 2.2 fusion.16
  131.0 1.0 fusion.18
  132.1 1.0 fusion.25
  133.1 2.2 fusion.23
  135.4 1.0 fusion.27
  136.3 9.1 %collective-permute-done.9 = bf16[896,512]{1,0:T(8,128)(2,1)S(1)} collective-permute-done((bf16[896,512]{1,0:T(8,128)(2,1)}, bf16[896,512]{1,0:T(8,128)(2,1)S(1)}, u32[]{:S(2)}, u32[]{:S(2)}) %collective-permute-start.9) | collective-permute-done | bytes 917536 | tf_op jit(solution)/shard_map/ppermute | solution.py:61
  145.5 1.0 fusion.11
  146.4 0.2 collective-permute-done.8
  146.7 2.2 fusion.20
  148.9 2.4 add_add_fusion
  151.3 2.3 add_add_fusion.1
  153.6 1.3 collective-permute-start.11
  154.9 0.7 collective-permute-start.10
  155.6 18.4 %collective-permute-done.11 = bf16[896,512]{1,0:T(8,128)(2,1)} collective-permute-done((bf16[896,512]{1,0:T(8,128)(2,1)S(1)}, bf16[896,512]{1,0:T(8,128)(2,1)}, u32[]{:S(2)}, u32[]{:S(2)}) %collective-permute-start.11) | collective-permute-done | bytes 917536 | tf_op jit(solution)/shard_map/ppermute | solution.py:61
  174.0 2.6 fusion.7
  176.6 0.3 add.239
  176.9 2.7 %fusion.9 = f32[384,2,512]{2,0,1:T(8,128)S(1)} fusion(bf16[8,384,2,896]{3,1,2,0:T(8,128)(2,1)} %bitcast.136, s32[]{:T(128)S(6)} %select_n.152, bf16[896,512]{1,0:T(8,128)(2,1)} %collective-permute-done.10), kind=kOutput, calls=%fused_computation.16 | convolution fusion | flops 704643072 | bytes 3866628 | tf_op jit(solution)/shard_map/tmd,dv->tmv/dot_general | solution.py:30
  179.7 0.3 add.235
  180.6 3.3 %collective-permute-start.13 = (bf16[896,512]{1,0:T(8,128)(2,1)}, bf16[896,512]{1,0:T(8,128)(2,1)}, u32[]{:S(2)}, u32[]{:S(2)}) collective-permute-start(bf16[896,512]{1,0:T(8,128)(2,1)} %collective-permute-done.11), channel_id=1, source_target_pairs={{0,224},{32,0},{64,32},{96,64},{128,96},{160,128},{192,160},{224,1... | collective-permute-start | bytes 2752520 | tf_op jit(solution)/shard_map/ppermute | solution.py:61
  184.0 0.3 broadcast_compare_fusion
  184.3 16.9 %collective-permute-done.12 = bf16[896,512]{1,0:T(8,128)(2,1)} collective-permute-done((bf16[896,512]{1,0:T(8,128)(2,1)}, bf16[896,512]{1,0:T(8,128)(2,1)}, u32[]{:S(2)}, u32[]{:S(2)}) %collective-permute-start.12) | collective-permute-done | bytes 917536 | tf_op jit(solution)/shard_map/ppermute | solution.py:60
  201.2 2.6 fusion.5
  203.8 0.3 fusion.88
  204.1 2.6 fusion.3
  206.7 0.3 fusion.87
  207.0 1.1 exponential_reduce_fusion
  208.0 23.2 %all-gather = f32[96,384,2]{1,2,0:T(2,128)S(1)} all-gather(f32[3,384,2]{1,2,0:T(2,128)S(1)} %pad_maximum_fusion.1), channel_id=2, replica_groups=mesh['row'=8,'col'=32] {'col'}, dimensions={0}, use_global_device_ids=true | all-gather | bytes 304128 | tf_op jit(solution)/shard_map/all_gather | solution.py:71
  231.6 22.7 %all-gather.3 = f32[8,3,16]{2,1,0:T(4,128)S(1)} all-gather(f32[1,3,16]{2,1,0:T(4,128)S(1)} %maximum_bitcast_fusion), channel_id=3, replica_groups=mesh['row'=8,'col'=32] {'row'}, dimensions={0}, use_global_device_ids=true | all-gather | bytes 1728 | tf_op jit(solution)/shard_map/all_gather | solution.py:84
  254.4 0.6 copy.25
  (66 shorter events, 1.6 us)
Async XLA Ops:
  6.5 84.0 %all-gather.6.cloned.1.call-start = ((), (), s32[]{:S(2)}) async-start(), calls=%async_computation | async-start | bytes 11354112 | tf_op jit(solution)/shard_map/all_gather | solution.py:19
  7.3 31.1 %copy-start.7 = (f32[2,224]{1,0:T(2,128)S(1)}, f32[2,224]{1,0:T(2,128)}, u32[]{:S(2)}) copy-start(f32[2,224]{1,0:T(2,128)} %param.7) | copy-start | bytes 5380
  8.8 26.3 %collective-permute-start = (bf16[896,512]{1,0:T(8,128)(2,1)S(1)}, bf16[896,512]{1,0:T(8,128)(2,1)S(1)}, u32[]{:S(2)}, u32[]{:S(2)}) collective-permute-start(bf16[896,512]{1,0:T(8,128)(2,1)S(1)} %get-tuple-element.48), channel_id=1, source_target_pairs={{0,32},{32,64},{64,96},{96,128},{128,160},{160,192},{192,224},{224... | collective-permute-start | bytes 2752520 | tf_op jit(solution)/shard_map/ppermute | solution.py:60
  10.8 24.3 %collective-permute-start.2 = (bf16[896,512]{1,0:T(8,128)(2,1)S(1)}, bf16[896,512]{1,0:T(8,128)(2,1)S(1)}, u32[]{:S(2)}, u32[]{:S(2)}) collective-permute-start(bf16[896,512]{1,0:T(8,128)(2,1)S(1)} %get-tuple-element.47), channel_id=1, source_target_pairs={{0,224},{32,0},{64,32},{96,64},{128,96},{160,128},{192,160},{224,1... | collective-permute-start | bytes 2752520 | tf_op jit(solution)/shard_map/ppermute | solution.py:61
  35.1 55.4 %copy-start.9 = (bf16[896,512]{1,0:T(8,128)(2,1)}, bf16[896,512]{1,0:T(8,128)(2,1)S(1)}, u32[]{:S(2)}) copy-start(bf16[896,512]{1,0:T(8,128)(2,1)S(1)} %collective-permute-done) | copy-start | bytes 2752516
  35.1 28.1 %collective-permute-start.1 = (bf16[896,512]{1,0:T(8,128)(2,1)S(1)}, bf16[896,512]{1,0:T(8,128)(2,1)S(1)}, u32[]{:S(2)}, u32[]{:S(2)}) collective-permute-start(bf16[896,512]{1,0:T(8,128)(2,1)S(1)} %collective-permute-done), channel_id=1, source_target_pairs={{0,32},{32,64},{64,96},{96,128},{128,160},{160,192},{192,224},{224... | collective-permute-start | bytes 2752520 | tf_op jit(solution)/shard_map/ppermute | solution.py:60
  35.1 31.4 %copy-start.11 = (bf16[896,512]{1,0:T(8,128)(2,1)}, bf16[896,512]{1,0:T(8,128)(2,1)S(1)}, u32[]{:S(2)}) copy-start(bf16[896,512]{1,0:T(8,128)(2,1)S(1)} %collective-permute-done.2) | copy-start | bytes 2752516
  35.2 28.1 %collective-permute-start.3 = (bf16[896,512]{1,0:T(8,128)(2,1)S(1)}, bf16[896,512]{1,0:T(8,128)(2,1)}, u32[]{:S(2)}, u32[]{:S(2)}) collective-permute-start(bf16[896,512]{1,0:T(8,128)(2,1)S(1)} %collective-permute-done.2), channel_id=1, source_target_pairs={{0,224},{32,0},{64,32},{96,64},{128,96},{160,128},{192,160},{224,1... | collective-permute-start | bytes 2752520 | tf_op jit(solution)/shard_map/ppermute | solution.py:61
  63.3 3.3 %copy-start.13 = (bf16[896,512]{1,0:T(8,128)(2,1)}, bf16[896,512]{1,0:T(8,128)(2,1)S(1)}, u32[]{:S(2)}) copy-start(bf16[896,512]{1,0:T(8,128)(2,1)S(1)} %collective-permute-done.1) | copy-start | bytes 2752516
  63.3 24.0 %collective-permute-start.4 = (bf16[896,512]{1,0:T(8,128)(2,1)S(1)}, bf16[896,512]{1,0:T(8,128)(2,1)}, u32[]{:S(2)}, u32[]{:S(2)}) collective-permute-start(bf16[896,512]{1,0:T(8,128)(2,1)S(1)} %collective-permute-done.1), channel_id=1, source_target_pairs={{0,32},{32,64},{64,96},{96,128},{128,160},{160,192},{192,224},{224... | collective-permute-start | bytes 2752520 | tf_op jit(solution)/shard_map/ppermute | solution.py:60
  63.4 23.9 %collective-permute-start.6 = (bf16[896,512]{1,0:T(8,128)(2,1)}, bf16[896,512]{1,0:T(8,128)(2,1)}, u32[]{:S(2)}, u32[]{:S(2)}) collective-permute-start(bf16[896,512]{1,0:T(8,128)(2,1)} %collective-permute-done.3), channel_id=1, source_target_pairs={{0,224},{32,0},{64,32},{96,64},{128,96},{160,128},{192,160},{224,1... | collective-permute-start | bytes 2752520 | tf_op jit(solution)/shard_map/ppermute | solution.py:61
  87.3 30.8 %collective-permute-start.5 = (bf16[896,512]{1,0:T(8,128)(2,1)}, bf16[896,512]{1,0:T(8,128)(2,1)S(1)}, u32[]{:S(2)}, u32[]{:S(2)}) collective-permute-start(bf16[896,512]{1,0:T(8,128)(2,1)} %collective-permute-done.4), channel_id=1, source_target_pairs={{0,32},{32,64},{64,96},{96,128},{128,160},{160,192},{192,224},{224... | collective-permute-start | bytes 2752520 | tf_op jit(solution)/shard_map/ppermute | solution.py:60
  87.3 30.8 %collective-permute-start.7 = (bf16[896,512]{1,0:T(8,128)(2,1)}, bf16[896,512]{1,0:T(8,128)(2,1)}, u32[]{:S(2)}, u32[]{:S(2)}) collective-permute-start(bf16[896,512]{1,0:T(8,128)(2,1)} %collective-permute-done.6), channel_id=1, source_target_pairs={{0,224},{32,0},{64,32},{96,64},{128,96},{160,128},{192,160},{224,1... | collective-permute-start | bytes 2752520 | tf_op jit(solution)/shard_map/ppermute | solution.py:61
  90.5 7.3 %copy-start = (bf16[384,2,7168]{0,2,1:T(8,128)(2,1)S(1)}, bf16[384,2,7168]{0,2,1:T(8,128)(2,1)}, u32[]{:S(2)}) copy-start(bf16[384,2,7168]{0,2,1:T(8,128)(2,1)} %all-gather.6.cloned.1.call-done) | copy-start | bytes 33030148
  103.8 14.2 %copy-start.3 = (bf16[896,1024]{1,0:T(8,128)(2,1)S(1)}, bf16[896,1024]{1,0:T(8,128)(2,1)}, u32[]{:S(2)}) copy-start(bf16[896,1024]{1,0:T(8,128)(2,1)} %param.8) | copy-start | bytes 5505028
  118.0 6.1 %copy-start.4 = (bf16[896,512]{1,0:T(8,128)(2,1)}, bf16[896,512]{1,0:T(8,128)(2,1)S(1)}, u32[]{:S(2)}) copy-start(bf16[896,512]{1,0:T(8,128)(2,1)S(1)} %collective-permute-done.5) | copy-start | bytes 2752516
  118.0 10.6 %copy-start.1 = (bf16[384,2,8,896]{3,0,1,2:T(8,128)(2,1)S(1)}, bf16[384,2,8,896]{3,0,1,2:T(8,128)(2,1)}, u32[]{:S(2)}) copy-start(bf16[384,2,8,896]{3,0,1,2:T(8,128)(2,1)} %copy.23) | copy-start | bytes 33030148
  123.8 21.7 %collective-permute-start.9 = (bf16[896,512]{1,0:T(8,128)(2,1)}, bf16[896,512]{1,0:T(8,128)(2,1)S(1)}, u32[]{:S(2)}, u32[]{:S(2)}) collective-permute-start(bf16[896,512]{1,0:T(8,128)(2,1)} %collective-permute-done.7), channel_id=1, source_target_pairs={{0,224},{32,0},{64,32},{96,64},{128,96},{160,128},{192,160},{224,1... | collective-permute-start | bytes 2752520 | tf_op jit(solution)/shard_map/ppermute | solution.py:61
  124.1 22.6 %collective-permute-start.8 = (bf16[896,512]{1,0:T(8,128)(2,1)S(1)}, bf16[896,512]{1,0:T(8,128)(2,1)}, u32[]{:S(2)}, u32[]{:S(2)}) collective-permute-start(bf16[896,512]{1,0:T(8,128)(2,1)S(1)} %collective-permute-done.5), channel_id=1, source_target_pairs={{0,32},{32,64},{64,96},{96,128},{128,160},{160,192},{192,224},{224... | collective-permute-start | bytes 2752520 | tf_op jit(solution)/shard_map/ppermute | solution.py:60
  128.7 2.3 copy-start.12
  130.9 1.2 copy-start.14
  133.1 2.3 copy-start.10
  148.8 2.4 copy-start.5
  153.6 20.4 %collective-permute-start.11 = (bf16[896,512]{1,0:T(8,128)(2,1)S(1)}, bf16[896,512]{1,0:T(8,128)(2,1)}, u32[]{:S(2)}, u32[]{:S(2)}) collective-permute-start(bf16[896,512]{1,0:T(8,128)(2,1)S(1)} %collective-permute-done.9), channel_id=1, source_target_pairs={{0,224},{32,0},{64,32},{96,64},{128,96},{160,128},{192,160},{224,1... | collective-permute-start | bytes 2752520 | tf_op jit(solution)/shard_map/ppermute | solution.py:61
  154.9 22.1 %collective-permute-start.10 = (bf16[896,512]{1,0:T(8,128)(2,1)}, bf16[896,512]{1,0:T(8,128)(2,1)}, u32[]{:S(2)}, u32[]{:S(2)}) collective-permute-start(bf16[896,512]{1,0:T(8,128)(2,1)} %collective-permute-done.8), channel_id=1, source_target_pairs={{0,32},{32,64},{64,96},{96,128},{128,160},{160,192},{192,224},{224... | collective-permute-start | bytes 2752520 | tf_op jit(solution)/shard_map/ppermute | solution.py:60
  176.9 2.7 %copy-start.2 = (f32[384,2,512]{2,0,1:T(8,128)S(1)}, f32[384,2,512]{2,0,1:T(8,128)}, u32[]{:S(2)}) copy-start(f32[384,2,512]{2,0,1:T(8,128)} %add_add_fusion.1) | copy-start | bytes 4718596
  179.6 0.7 copy-start.8
  179.6 1.0 copy-start.15
  179.6 4.3 %copy-start.6 = (s32[384]{0:T(512)S(1)}, s32[384]{0:T(512)}, u32[]{:S(2)}) copy-start(s32[384]{0:T(512)} %param.10) | copy-start | bytes 4612
  180.0 21.2 %collective-permute-start.12 = (bf16[896,512]{1,0:T(8,128)(2,1)}, bf16[896,512]{1,0:T(8,128)(2,1)}, u32[]{:S(2)}, u32[]{:S(2)}) collective-permute-start(bf16[896,512]{1,0:T(8,128)(2,1)} %collective-permute-done.10), channel_id=1, source_target_pairs={{0,32},{32,64},{64,96},{96,128},{128,160},{160,192},{192,224},{224... | collective-permute-start | bytes 2752520 | tf_op jit(solution)/shard_map/ppermute | solution.py:60
  180.6 23.4 %collective-permute-start.13 = (bf16[896,512]{1,0:T(8,128)(2,1)}, bf16[896,512]{1,0:T(8,128)(2,1)}, u32[]{:S(2)}, u32[]{:S(2)}) collective-permute-start(bf16[896,512]{1,0:T(8,128)(2,1)} %collective-permute-done.11), channel_id=1, source_target_pairs={{0,224},{32,0},{64,32},{96,64},{128,96},{160,128},{192,160},{224,1... | collective-permute-start | bytes 2752520 | tf_op jit(solution)/shard_map/ppermute | solution.py:61
Sparse Core Ops, SparseCore 0:
  9.9 66.8 all-gather.5

commit v7 on v6

--- a/solution.py
+++ b/solution.py
@@ -49,9 +49,9 @@
             features = (
                 stream * lax.rsqrt(mean_square[:, :, None] + EPS) * full_gain[None, :, :]
             ).astype(jnp.bfloat16)
+            left, right, features = lax.optimization_barrier((left, right, features))
             features = features.reshape(tok_rows, 2, n_row, shard_rows).transpose(2, 0, 1, 3)
-            left, right, features = lax.optimization_barrier((left, right, features))
-        if step >= 6:
+        if step == 7:
             logits_left, logits_right = add_pending(logits_left, logits_right)
             pending = []
             left, right, logits_left, logits_right = lax.optimization_barrier(

time: 263 us -> 244 us (0.928)
  local copies, waits for them, and re-layouts: 17.6 us -> 3.16 us
  matrix products: 33.9 us -> 27 us
  waiting for transfers between devices: 86.4 us -> 91.1 us
  other arithmetic: 15.9 us -> 12.2 us
    reshape x1 -> x0, local copies, waits for them, and re-layouts: 14.2 us -> none  [per_device(): features.reshape(tok_rows, 2, n_row, shard_rows).transpose(2, 0, 1, 3)]
    ppermute x7, waiting for transfers between devices: 58.1 us -> 70.9 us  [per_device(): left = lax.ppermute(left, 'row', forward)]
    ppermute x7, waiting for transfers between devices: 27.6 us -> 19.5 us  [per_device(): right = lax.ppermute(right, 'row', backward)]
    dot_general x16, matrix products: 33.9 us -> 27 us  [block_logits(): jnp.einsum('tmd,dv->tmv', features[shard], block, preferred_element_type=...]
    ppermute x7, starting transfers between devices: 18.6 us -> 24 us  [per_device(): right = lax.ppermute(right, 'row', backward)]
    convert_element_type x1, other arithmetic: 6.03 us -> 3.08 us  [per_device(): features = (stream * lax.rsqrt(mean_square[:, :, None] + EPS) * full_gain...]
    ppermute x7, starting transfers between devices: 5.03 us -> 2.26 us  [per_device(): left = lax.ppermute(left, 'row', forward)]
  transfers between devices with their start and end apart: 15 -> 15, of which waited for: 6 -> 7; matrix products, arithmetic and copies ran while one was open for 17% -> 13% of each run, Pallas kernels for 0% -> 0%
where the time goes in v7:
time: 244 us
  waiting for transfers between devices  91.1 us (37%)
  blocking collectives  70.6 us (29%)
  matrix products  27 us (11%)
  starting transfers between devices  26.3 us (11%)
  between operations  13.7 us (6%)
  other arithmetic  12.2 us (5%)
  local copies, waits for them, and re-layouts  3.16 us (1%)
    ppermute x7, waiting for transfers between devices, per_device(): left = lax.ppermute(left, 'row', forward)  70.9 us
    dot_general x16, matrix products, block_logits(): jnp.einsum('tmd,dv->tmv', features[shard], block, preferred_element_type=...  27 us
    all_gather x1, blocking collectives, per_device(): full_gain = lax.all_gather(final_gain, 'col', axis=1, tiled=True)  24.7 us
    ppermute x7, starting transfers between devices, per_device(): right = lax.ppermute(right, 'row', backward)  24 us
    all_gather x1, blocking collectives, per_device(): parts = lax.all_gather(jnp.stack([row_max, exp_total, picked]), 'col')  23.2 us
    all_gather x1, blocking collectives, per_device(): stats = lax.all_gather(jnp.stack([ratio_sums, squares, ratio_max]), 'row')  22.7 us
    ppermute x7, waiting for transfers between devices, per_device(): right = lax.ppermute(right, 'row', backward)  19.5 us
    reduce_sum x1, other arithmetic, per_device(): mean_square = jnp.sum(stream * stream, axis=2) / D  6.49 us
  transfers between devices with their start and end apart: 15, of which 7 were waited for; matrix products, arithmetic and copies ran while one was open for 13% of the time, Pallas kernels for 0%

profile of v7, /device:TPU:2, one launch (start us, length us, event | category | flops | bytes accessed | tf_op | source)
XLA Modules:
  0.0 244.0 jit_solution(9653553168169861164)
XLA Ops:
  6.5 0.7 all-gather.6.cloned.1.call-update
  7.3 1.6 fusion.89
  8.8 2.0 collective-permute-start
  10.8 4.0 %collective-permute-start.2 = (bf16[896,512]{1,0:T(8,128)(2,1)S(1)}, bf16[896,512]{1,0:T(8,128)(2,1)S(1)}, u32[]{:S(2)}, u32[]{:S(2)}) collective-permute-start(bf16[896,512]{1,0:T(8,128)(2,1)S(1)} %get-tuple-element.39), channel_id=1, source_target_pairs={{0,224},{32,0},{64,32},{96,64},{128,96},{160,128},{192,160},{224,1... | collective-permute-start | bytes 2752520 | tf_op jit(solution)/shard_map/ppermute | solution.py:61
  14.9 20.3 %collective-permute-done = bf16[896,512]{1,0:T(8,128)(2,1)S(1)} collective-permute-done((bf16[896,512]{1,0:T(8,128)(2,1)S(1)}, bf16[896,512]{1,0:T(8,128)(2,1)S(1)}, u32[]{:S(2)}, u32[]{:S(2)}) %collective-permute-start) | collective-permute-done | bytes 917536 | tf_op jit(solution)/shard_map/ppermute | solution.py:60
  35.1 3.2 %collective-permute-start.3 = (bf16[896,512]{1,0:T(8,128)(2,1)S(1)}, bf16[896,512]{1,0:T(8,128)(2,1)}, u32[]{:S(2)}, u32[]{:S(2)}) collective-permute-start(bf16[896,512]{1,0:T(8,128)(2,1)S(1)} %collective-permute-done.2), channel_id=1, source_target_pairs={{0,224},{32,0},{64,32},{96,64},{128,96},{160,128},{192,160},{224,1... | collective-permute-start | bytes 2752520 | tf_op jit(solution)/shard_map/ppermute | solution.py:61
  38.4 24.7 %all-gather.2 = f32[32,224,2]{1,2,0:T(2,128)S(1)} all-gather(f32[1,224,2]{1,2,0:T(2,128)S(1)} %bitcast.172), channel_id=1, replica_groups=mesh['row'=8,'col'=32] {'col'}, dimensions={0}, use_global_device_ids=true | all-gather | bytes 59136 | tf_op jit(solution)/shard_map/all_gather | solution.py:20
  63.1 0.1 reshape.194
  63.4 3.2 %collective-permute-start.6 = (bf16[896,512]{1,0:T(8,128)(2,1)}, bf16[896,512]{1,0:T(8,128)(2,1)}, u32[]{:S(2)}, u32[]{:S(2)}) collective-permute-start(bf16[896,512]{1,0:T(8,128)(2,1)} %collective-permute-done.3), channel_id=1, source_target_pairs={{0,224},{32,0},{64,32},{96,64},{128,96},{160,128},{192,160},{224,1... | collective-permute-start | bytes 2752520 | tf_op jit(solution)/shard_map/ppermute | solution.py:61
  66.6 20.7 %collective-permute-done.4 = bf16[896,512]{1,0:T(8,128)(2,1)} collective-permute-done((bf16[896,512]{1,0:T(8,128)(2,1)S(1)}, bf16[896,512]{1,0:T(8,128)(2,1)}, u32[]{:S(2)}, u32[]{:S(2)}) %collective-permute-start.4) | collective-permute-done | bytes 917536 | tf_op jit(solution)/shard_map/ppermute | solution.py:60
  87.3 3.2 %collective-permute-start.7 = (bf16[896,512]{1,0:T(8,128)(2,1)}, bf16[896,512]{1,0:T(8,128)(2,1)}, u32[]{:S(2)}, u32[]{:S(2)}) collective-permute-start(bf16[896,512]{1,0:T(8,128)(2,1)} %collective-permute-done.6), channel_id=1, source_target_pairs={{0,224},{32,0},{64,32},{96,64},{128,96},{160,128},{192,160},{224,1... | collective-permute-start | bytes 2752520 | tf_op jit(solution)/shard_map/ppermute | solution.py:61
  90.5 6.5 %fusion = f32[384,2]{0,1:T(2,128)S(1)} fusion(bf16[384,2,7168]{0,2,1:T(8,128)(2,1)} %all-gather.6.cloned.1.call-done), kind=kLoop, calls=%fused_computation.2 | loop fusion | flops 16514304 | bytes 11013120 | tf_op jit(solution)/shard_map/reduce_sum | solution.py:48
  97.0 0.8 copy-done
  97.8 3.1 %fusion.2 = bf16[384,2,7168]{0,2,1:T(8,128)(2,1)S(1)} fusion(bf16[384,2,7168]{0,2,1:T(8,128)(2,1)S(1)} %copy-done, f32[2,7168]{1,0:T(2,128)S(1)} %bitcast.165, f32[384,2]{0,1:T(2,128)S(1)} %add_rsqrt_fusion), kind=kLoop, calls=%fused_computation.4 | loop fusion | flops 22020096 | bytes 22080512 | tf_op jit(solution)/shard_map/convert_element_type | solution.py:51
  100.9 9.7 %collective-permute-done.5 = bf16[896,512]{1,0:T(8,128)(2,1)} collective-permute-done((bf16[896,512]{1,0:T(8,128)(2,1)}, bf16[896,512]{1,0:T(8,128)(2,1)}, u32[]{:S(2)}, u32[]{:S(2)}) %collective-permute-start.5) | collective-permute-done | bytes 917536 | tf_op jit(solution)/shard_map/ppermute | solution.py:60
  110.5 1.0 fusion.29
  111.6 1.0 fusion.31
  112.6 3.2 %collective-permute-start.10 = (bf16[896,512]{1,0:T(8,128)(2,1)}, bf16[896,512]{1,0:T(8,128)(2,1)S(1)}, u32[]{:S(2)}, u32[]{:S(2)}) collective-permute-start(bf16[896,512]{1,0:T(8,128)(2,1)} %collective-permute-done.7), channel_id=1, source_target_pairs={{0,224},{32,0},{64,32},{96,64},{128,96},{160,128},{192,160},{224,1... | collective-permute-start | bytes 2752520 | tf_op jit(solution)/shard_map/ppermute | solution.py:61
  115.8 2.2 fusion.10
  118.0 2.2 fusion.12
  120.2 2.3 fusion.14
  122.5 1.0 fusion.16
  123.5 2.2 fusion.23
  125.7 2.2 fusion.21
  127.9 6.3 %collective-permute-done.10 = bf16[896,512]{1,0:T(8,128)(2,1)S(1)} collective-permute-done((bf16[896,512]{1,0:T(8,128)(2,1)}, bf16[896,512]{1,0:T(8,128)(2,1)S(1)}, u32[]{:S(2)}, u32[]{:S(2)}) %collective-permute-start.10) | collective-permute-done | bytes 917536 | tf_op jit(solution)/shard_map/ppermute | solution.py:61
  134.2 3.6 %collective-permute-start.11 = (bf16[896,512]{1,0:T(8,128)(2,1)S(1)}, bf16[896,512]{1,0:T(8,128)(2,1)S(1)}, u32[]{:S(2)}, u32[]{:S(2)}) collective-permute-start(bf16[896,512]{1,0:T(8,128)(2,1)S(1)} %collective-permute-done.10), channel_id=1, source_target_pairs={{0,224},{32,0},{64,32},{96,64},{128,96},{160,128},{192,160},{224,1... | collective-permute-start | bytes 2752520 | tf_op jit(solution)/shard_map/ppermute | solution.py:61
  137.8 1.0 fusion.25
  138.8 1.0 fusion.27
  140.0 1.0 fusion.8
  141.0 1.0 fusion.19
  142.0 13.1 %collective-permute-done.11 = bf16[896,512]{1,0:T(8,128)(2,1)S(1)} collective-permute-done((bf16[896,512]{1,0:T(8,128)(2,1)S(1)}, bf16[896,512]{1,0:T(8,128)(2,1)S(1)}, u32[]{:S(2)}, u32[]{:S(2)}) %collective-permute-start.11) | collective-permute-done | bytes 917536 | tf_op jit(solution)/shard_map/ppermute | solution.py:61
  155.1 1.2 add_add_fusion
  156.4 4.4 %collective-permute-done.9 = bf16[896,512]{1,0:T(8,128)(2,1)} collective-permute-done((bf16[896,512]{1,0:T(8,128)(2,1)S(1)}, bf16[896,512]{1,0:T(8,128)(2,1)}, u32[]{:S(2)}, u32[]{:S(2)}) %collective-permute-start.9) | collective-permute-done | bytes 917536 | tf_op jit(solution)/shard_map/ppermute | solution.py:60
  160.7 2.4 add_add_fusion.1
  163.4 0.1 reduce.7
  163.6 3.5 %collective-permute-start.13 = (bf16[896,512]{1,0:T(8,128)(2,1)}, bf16[896,512]{1,0:T(8,128)(2,1)}, u32[]{:S(2)}, u32[]{:S(2)}) collective-permute-start(bf16[896,512]{1,0:T(8,128)(2,1)} %copy-done.3), channel_id=1, source_target_pairs={{0,224},{32,0},{64,32},{96,64},{128,96},{160,128},{192,160},{224,1... | collective-permute-start | bytes 2752520 | tf_op jit(solution)/shard_map/ppermute | solution.py:61
  167.1 0.3 broadcast_compare_fusion
  167.4 16.0 %collective-permute-done.12 = bf16[896,512]{1,0:T(8,128)(2,1)} collective-permute-done((bf16[896,512]{1,0:T(8,128)(2,1)}, bf16[896,512]{1,0:T(8,128)(2,1)}, u32[]{:S(2)}, u32[]{:S(2)}) %collective-permute-start.12) | collective-permute-done | bytes 917536 | tf_op jit(solution)/shard_map/ppermute | solution.py:60
  183.4 2.6 %fusion.5 = f32[384,2,512]{2,0,1:T(8,128)S(1)} fusion(bf16[384,2,8,896]{0,3,2,1:T(8,128)(2,1)} %bitcast.160, s32[]{:T(128)S(6)} %select_n.156, bf16[896,512]{1,0:T(8,128)(2,1)} %collective-permute-done.12), kind=kOutput, calls=%fused_computation.12 | convolution fusion | flops 704643072 | bytes 3866628 | tf_op jit(solution)/shard_map/tmd,dv->tmv/dot_general | solution.py:30
  186.0 0.3 fusion.88
  186.3 2.6 %fusion.3 = f32[384,2,512]{2,0,1:T(8,128)S(1)} fusion(bf16[384,2,8,896]{0,3,2,1:T(8,128)(2,1)} %bitcast.161, s32[]{:T(128)S(6)} %select_n.158, bf16[896,512]{1,0:T(8,128)(2,1)} %collective-permute-done.13), kind=kOutput, calls=%fused_computation.10 | convolution fusion | flops 704643072 | bytes 3866628 | tf_op jit(solution)/shard_map/tmd,dv->tmv/dot_general | solution.py:30
  188.9 0.3 fusion.87
  189.2 1.1 exponential_reduce_fusion
  190.2 23.2 %all-gather = f32[96,384,2]{1,2,0:T(2,128)S(1)} all-gather(f32[3,384,2]{1,2,0:T(2,128)S(1)} %pad_maximum_fusion.1), channel_id=2, replica_groups=mesh['row'=8,'col'=32] {'col'}, dimensions={0}, use_global_device_ids=true | all-gather | bytes 304128 | tf_op jit(solution)/shard_map/all_gather | solution.py:71
  213.6 0.1 fusion.66
  213.7 0.2 select_reduce_fusion.3
  213.9 22.7 %all-gather.3 = f32[8,3,16]{2,1,0:T(4,128)S(1)} all-gather(f32[1,3,16]{2,1,0:T(4,128)S(1)} %maximum_bitcast_fusion), channel_id=3, replica_groups=mesh['row'=8,'col'=32] {'row'}, dimensions={0}, use_global_device_ids=true | all-gather | bytes 1728 | tf_op jit(solution)/shard_map/all_gather | solution.py:84
  236.6 0.6 copy.81
  (51 shorter events, 0.8 us)
Async XLA Ops:
  6.5 84.0 %all-gather.6.cloned.1.call-start = ((), (), s32[]{:S(2)}) async-start(), calls=%async_computation | async-start | bytes 11354112 | tf_op jit(solution)/shard_map/all_gather | solution.py:19
  7.3 31.1 %copy-start.5 = (f32[2,224]{1,0:T(2,128)S(1)}, f32[2,224]{1,0:T(2,128)}, u32[]{:S(2)}) copy-start(f32[2,224]{1,0:T(2,128)} %param.7) | copy-start | bytes 5380
  8.8 26.3 %collective-permute-start = (bf16[896,512]{1,0:T(8,128)(2,1)S(1)}, bf16[896,512]{1,0:T(8,128)(2,1)S(1)}, u32[]{:S(2)}, u32[]{:S(2)}) collective-permute-start(bf16[896,512]{1,0:T(8,128)(2,1)S(1)} %get-tuple-element.40), channel_id=1, source_target_pairs={{0,32},{32,64},{64,96},{96,128},{128,160},{160,192},{192,224},{224... | collective-permute-start | bytes 2752520 | tf_op jit(solution)/shard_map/ppermute | solution.py:60
  10.8 24.3 %collective-permute-start.2 = (bf16[896,512]{1,0:T(8,128)(2,1)S(1)}, bf16[896,512]{1,0:T(8,128)(2,1)S(1)}, u32[]{:S(2)}, u32[]{:S(2)}) collective-permute-start(bf16[896,512]{1,0:T(8,128)(2,1)S(1)} %get-tuple-element.39), channel_id=1, source_target_pairs={{0,224},{32,0},{64,32},{96,64},{128,96},{160,128},{192,160},{224,1... | collective-permute-start | bytes 2752520 | tf_op jit(solution)/shard_map/ppermute | solution.py:61
  35.1 28.1 %collective-permute-start.1 = (bf16[896,512]{1,0:T(8,128)(2,1)S(1)}, bf16[896,512]{1,0:T(8,128)(2,1)S(1)}, u32[]{:S(2)}, u32[]{:S(2)}) collective-permute-start(bf16[896,512]{1,0:T(8,128)(2,1)S(1)} %collective-permute-done), channel_id=1, source_target_pairs={{0,32},{32,64},{64,96},{96,128},{128,160},{160,192},{192,224},{224... | collective-permute-start | bytes 2752520 | tf_op jit(solution)/shard_map/ppermute | solution.py:60
  35.1 55.4 %copy-start.7 = (bf16[896,512]{1,0:T(8,128)(2,1)}, bf16[896,512]{1,0:T(8,128)(2,1)S(1)}, u32[]{:S(2)}) copy-start(bf16[896,512]{1,0:T(8,128)(2,1)S(1)} %collective-permute-done.2) | copy-start | bytes 2752516
  35.1 28.1 %collective-permute-start.3 = (bf16[896,512]{1,0:T(8,128)(2,1)S(1)}, bf16[896,512]{1,0:T(8,128)(2,1)}, u32[]{:S(2)}, u32[]{:S(2)}) collective-permute-start(bf16[896,512]{1,0:T(8,128)(2,1)S(1)} %collective-permute-done.2), channel_id=1, source_target_pairs={{0,224},{32,0},{64,32},{96,64},{128,96},{160,128},{192,160},{224,1... | collective-permute-start | bytes 2752520 | tf_op jit(solution)/shard_map/ppermute | solution.py:61
  63.3 24.0 %collective-permute-start.4 = (bf16[896,512]{1,0:T(8,128)(2,1)S(1)}, bf16[896,512]{1,0:T(8,128)(2,1)}, u32[]{:S(2)}, u32[]{:S(2)}) collective-permute-start(bf16[896,512]{1,0:T(8,128)(2,1)S(1)} %collective-permute-done.1), channel_id=1, source_target_pairs={{0,32},{32,64},{64,96},{96,128},{128,160},{160,192},{192,224},{224... | collective-permute-start | bytes 2752520 | tf_op jit(solution)/shard_map/ppermute | solution.py:60
  63.4 23.9 %collective-permute-start.6 = (bf16[896,512]{1,0:T(8,128)(2,1)}, bf16[896,512]{1,0:T(8,128)(2,1)}, u32[]{:S(2)}, u32[]{:S(2)}) collective-permute-start(bf16[896,512]{1,0:T(8,128)(2,1)} %collective-permute-done.3), channel_id=1, source_target_pairs={{0,224},{32,0},{64,32},{96,64},{128,96},{160,128},{192,160},{224,1... | collective-permute-start | bytes 2752520 | tf_op jit(solution)/shard_map/ppermute | solution.py:61
  87.3 23.3 %collective-permute-start.5 = (bf16[896,512]{1,0:T(8,128)(2,1)}, bf16[896,512]{1,0:T(8,128)(2,1)}, u32[]{:S(2)}, u32[]{:S(2)}) collective-permute-start(bf16[896,512]{1,0:T(8,128)(2,1)} %collective-permute-done.4), channel_id=1, source_target_pairs={{0,32},{32,64},{64,96},{96,128},{128,160},{160,192},{192,224},{224... | collective-permute-start | bytes 2752520 | tf_op jit(solution)/shard_map/ppermute | solution.py:60
  87.3 23.3 %collective-permute-start.7 = (bf16[896,512]{1,0:T(8,128)(2,1)}, bf16[896,512]{1,0:T(8,128)(2,1)}, u32[]{:S(2)}, u32[]{:S(2)}) collective-permute-start(bf16[896,512]{1,0:T(8,128)(2,1)} %collective-permute-done.6), channel_id=1, source_target_pairs={{0,224},{32,0},{64,32},{96,64},{128,96},{160,128},{192,160},{224,1... | collective-permute-start | bytes 2752520 | tf_op jit(solution)/shard_map/ppermute | solution.py:61
  90.5 7.3 %copy-start = (bf16[384,2,7168]{0,2,1:T(8,128)(2,1)S(1)}, bf16[384,2,7168]{0,2,1:T(8,128)(2,1)}, u32[]{:S(2)}) copy-start(bf16[384,2,7168]{0,2,1:T(8,128)(2,1)} %all-gather.6.cloned.1.call-done) | copy-start | bytes 33030148
  97.8 12.8 %copy-start.2 = (bf16[896,1024]{1,0:T(8,128)(2,1)S(1)}, bf16[896,1024]{1,0:T(8,128)(2,1)}, u32[]{:S(2)}) copy-start(bf16[896,1024]{1,0:T(8,128)(2,1)} %param.8) | copy-start | bytes 5505028
  100.9 59.9 %copy-start.1 = (bf16[384,2,7168]{0,2,1:T(8,128)(2,1)}, bf16[384,2,7168]{0,2,1:T(8,128)(2,1)S(1)}, u32[]{:S(2)}) copy-start(bf16[384,2,7168]{0,2,1:T(8,128)(2,1)S(1)} %fusion.2) | copy-start | bytes 33030148
  112.6 21.7 %collective-permute-start.10 = (bf16[896,512]{1,0:T(8,128)(2,1)}, bf16[896,512]{1,0:T(8,128)(2,1)S(1)}, u32[]{:S(2)}, u32[]{:S(2)}) collective-permute-start(bf16[896,512]{1,0:T(8,128)(2,1)} %collective-permute-done.7), channel_id=1, source_target_pairs={{0,224},{32,0},{64,32},{96,64},{128,96},{160,128},{192,160},{224,1... | collective-permute-start | bytes 2752520 | tf_op jit(solution)/shard_map/ppermute | solution.py:61
  115.8 24.1 %collective-permute-start.8 = (bf16[896,512]{1,0:T(8,128)(2,1)}, bf16[896,512]{1,0:T(8,128)(2,1)S(1)}, u32[]{:S(2)}, u32[]{:S(2)}) collective-permute-start(bf16[896,512]{1,0:T(8,128)(2,1)} %collective-permute-done.5), channel_id=1, source_target_pairs={{0,32},{32,64},{64,96},{96,128},{128,160},{160,192},{192,224},{224... | collective-permute-start | bytes 2752520 | tf_op jit(solution)/shard_map/ppermute | solution.py:60
  120.2 2.3 copy-start.8
  134.2 20.9 %collective-permute-start.11 = (bf16[896,512]{1,0:T(8,128)(2,1)S(1)}, bf16[896,512]{1,0:T(8,128)(2,1)S(1)}, u32[]{:S(2)}, u32[]{:S(2)}) collective-permute-start(bf16[896,512]{1,0:T(8,128)(2,1)S(1)} %collective-permute-done.10), channel_id=1, source_target_pairs={{0,224},{32,0},{64,32},{96,64},{128,96},{160,128},{192,160},{224,1... | collective-permute-start | bytes 2752520 | tf_op jit(solution)/shard_map/ppermute | solution.py:61
  139.9 20.9 %collective-permute-start.9 = (bf16[896,512]{1,0:T(8,128)(2,1)S(1)}, bf16[896,512]{1,0:T(8,128)(2,1)}, u32[]{:S(2)}, u32[]{:S(2)}) collective-permute-start(bf16[896,512]{1,0:T(8,128)(2,1)S(1)} %collective-permute-done.8), channel_id=1, source_target_pairs={{0,32},{32,64},{64,96},{96,128},{128,160},{160,192},{192,224},{224... | collective-permute-start | bytes 2752520 | tf_op jit(solution)/shard_map/ppermute | solution.py:60
  155.1 1.2 copy-start.3
  156.3 6.9 %copy-start.6 = (s32[16]{0:T(128)S(1)}, s32[16]{0:T(128)}, u32[]{:S(2)}) copy-start(s32[16]{0:T(128)} %param.9) | copy-start | bytes 196
  156.4 7.2 %copy-start.9 = (s32[16]{0:T(128)S(1)}, s32[16]{0:T(128)}, u32[]{:S(2)}) copy-start(s32[16]{0:T(128)} %param.11) | copy-start | bytes 196
  156.4 10.8 %copy-start.4 = (s32[384]{0:T(512)S(1)}, s32[384]{0:T(512)}, u32[]{:S(2)}) copy-start(s32[384]{0:T(512)} %param.10) | copy-start | bytes 4612
  163.1 20.2 %collective-permute-start.12 = (bf16[896,512]{1,0:T(8,128)(2,1)}, bf16[896,512]{1,0:T(8,128)(2,1)}, u32[]{:S(2)}, u32[]{:S(2)}) collective-permute-start(bf16[896,512]{1,0:T(8,128)(2,1)} %collective-permute-done.9), channel_id=1, source_target_pairs={{0,32},{32,64},{64,96},{96,128},{128,160},{160,192},{192,224},{224... | collective-permute-start | bytes 2752520 | tf_op jit(solution)/shard_map/ppermute | solution.py:60
  163.6 22.7 %collective-permute-start.13 = (bf16[896,512]{1,0:T(8,128)(2,1)}, bf16[896,512]{1,0:T(8,128)(2,1)}, u32[]{:S(2)}, u32[]{:S(2)}) collective-permute-start(bf16[896,512]{1,0:T(8,128)(2,1)} %copy-done.3), channel_id=1, source_target_pairs={{0,224},{32,0},{64,32},{96,64},{128,96},{160,128},{192,160},{224,1... | collective-permute-start | bytes 2752520 | tf_op jit(solution)/shard_map/ppermute | solution.py:61
Sparse Core Ops, SparseCore 0:
  9.9 66.8 all-gather.5

commit v8 on v7

--- a/solution.py
+++ b/solution.py
@@ -51,12 +51,6 @@
             ).astype(jnp.bfloat16)
             left, right, features = lax.optimization_barrier((left, right, features))
             features = features.reshape(tok_rows, 2, n_row, shard_rows).transpose(2, 0, 1, 3)
-        if step == 7:
-            logits_left, logits_right = add_pending(logits_left, logits_right)
-            pending = []
-            left, right, logits_left, logits_right = lax.optimization_barrier(
-                (left, right, logits_left, logits_right)
-            )
         left = lax.ppermute(left, "row", forward)
         right = lax.ppermute(right, "row", backward)
         pending.append((left, right, (row_index - step) % n_row, (row_index + step) % n_row))
@@ -81,7 +75,9 @@
     ratio_sums = jnp.sum(jnp.where(member, log_ratio[:, None], 0.0), axis=0)
     squares = jnp.sum(jnp.where(member, (log_ratio * log_ratio)[:, None], 0.0), axis=0)
     ratio_max = jnp.max(jnp.where(member, log_ratio[:, None], -1e30), axis=0)
-    stats = lax.all_gather(jnp.stack([ratio_sums, squares, ratio_max]), "row")
+    own_slot = (jnp.arange(n_row, dtype=jnp.int32) == row_index)[:, None, None]
+    own_stats = jnp.stack([ratio_sums, squares, ratio_max])[None]
+    stats = lax.psum(jnp.where(own_slot, own_stats, 0.0), "row")
     seq_stats = jnp.stack(
         [jnp.sum(stats[:, 0], axis=0), jnp.sum(stats[:, 1], axis=0), jnp.max(stats[:, 2], axis=0)]
     )

time: 244 us -> 246 us (level)
  blocking collectives: 70.6 us -> 78.5 us
  waiting for transfers between devices: 91.1 us -> 86.6 us
    psum x0 -> x1, blocking collectives: none -> 30.5 us  [per_device(): stats = lax.psum(jnp.where(own_slot, own_stats, 0.0), 'row')]
    all_gather x1 -> x0, blocking collectives: 22.7 us -> none  [per_device(): stats = lax.all_gather(jnp.stack([ratio_sums, squares, ratio_max]), 'row')]
    ppermute x7, waiting for transfers between devices: 19.5 us -> 4.42 us  [per_device(): right = lax.ppermute(right, 'row', backward)]
    ppermute x7, waiting for transfers between devices: 70.9 us -> 81.5 us  [per_device(): left = lax.ppermute(left, 'row', forward)]
  transfers between devices with their start and end apart: 15 -> 15, of which waited for: 7 -> 8; matrix products, arithmetic and copies ran while one was open for 13% -> 14% of each run, Pallas kernels for 0% -> 0%
where the time goes in v8:
time: 246 us; the launch traced here: 245 us
  waiting for transfers between devices  86.6 us (35%)
  blocking collectives  78.5 us (32%)
  starting transfers between devices  26.4 us (11%)
  matrix products  25.1 us (10%)
  between operations  13.7 us (6%)
  other arithmetic  11.7 us (5%)
  local copies, waits for them, and re-layouts  3.17 us (1%)
    ppermute x7, waiting for transfers between devices, per_device(): left = lax.ppermute(left, 'row', forward)  81.5 us
    psum x1, blocking collectives, per_device(): stats = lax.psum(jnp.where(own_slot, own_stats, 0.0), 'row')  30.5 us
    dot_general x16, matrix products, block_logits(): jnp.einsum('tmd,dv->tmv', features[shard], block, preferred_element_type=...  25.1 us
    all_gather x1, blocking collectives, per_device(): full_gain = lax.all_gather(final_gain, 'col', axis=1, tiled=True)  24.7 us
    ppermute x7, starting transfers between devices, per_device(): right = lax.ppermute(right, 'row', backward)  24.1 us
    all_gather x1, blocking collectives, per_device(): parts = lax.all_gather(jnp.stack([row_max, exp_total, picked]), 'col')  23.3 us
    reduce_sum x1, other arithmetic, per_device(): mean_square = jnp.sum(stream * stream, axis=2) / D  6.49 us
  transfers between devices with their start and end apart: 15, of which 8 were waited for; matrix products, arithmetic and copies ran while one was open for 14% of the time, Pallas kernels for 0%

profile of v8, /device:TPU:2, one launch (start us, length us, event | category | flops | bytes accessed | tf_op | source)
XLA Modules:
  0.0 245.3 jit_solution(16505177264951003882)
XLA Ops:
  6.5 0.7 all-gather.4.cloned.1.call-update
  7.3 1.6 fusion.87
  8.9 2.0 collective-permute-start
  10.9 4.0 %collective-permute-start.2 = (bf16[896,512]{1,0:T(8,128)(2,1)S(1)}, bf16[896,512]{1,0:T(8,128)(2,1)S(1)}, u32[]{:S(2)}, u32[]{:S(2)}) collective-permute-start(bf16[896,512]{1,0:T(8,128)(2,1)S(1)} %get-tuple-element.27), channel_id=1, source_target_pairs={{0,224},{32,0},{64,32},{96,64},{128,96},{160,128},{192,160},{224,1... | collective-permute-start | bytes 2752520 | tf_op jit(solution)/shard_map/ppermute | solution.py:55
  14.9 20.4 %collective-permute-done = bf16[896,512]{1,0:T(8,128)(2,1)} collective-permute-done((bf16[896,512]{1,0:T(8,128)(2,1)S(1)}, bf16[896,512]{1,0:T(8,128)(2,1)}, u32[]{:S(2)}, u32[]{:S(2)}) %collective-permute-start) | collective-permute-done | bytes 917536 | tf_op jit(solution)/shard_map/ppermute | solution.py:54
  35.3 3.2 %collective-permute-start.3 = (bf16[896,512]{1,0:T(8,128)(2,1)S(1)}, bf16[896,512]{1,0:T(8,128)(2,1)S(1)}, u32[]{:S(2)}, u32[]{:S(2)}) collective-permute-start(bf16[896,512]{1,0:T(8,128)(2,1)S(1)} %collective-permute-done.2), channel_id=1, source_target_pairs={{0,224},{32,0},{64,32},{96,64},{128,96},{160,128},{192,160},{224,1... | collective-permute-start | bytes 2752520 | tf_op jit(solution)/shard_map/ppermute | solution.py:55
  38.5 24.7 %all-gather.1 = f32[32,224,2]{1,2,0:T(2,128)S(1)} all-gather(f32[1,224,2]{1,2,0:T(2,128)S(1)} %bitcast.178), channel_id=1, replica_groups=mesh['row'=8,'col'=32] {'col'}, dimensions={0}, use_global_device_ids=true | all-gather | bytes 59136 | tf_op jit(solution)/shard_map/all_gather | solution.py:20
  63.3 0.1 reshape.198
  63.5 3.2 %collective-permute-start.6 = (bf16[896,512]{1,0:T(8,128)(2,1)S(1)}, bf16[896,512]{1,0:T(8,128)(2,1)}, u32[]{:S(2)}, u32[]{:S(2)}) collective-permute-start(bf16[896,512]{1,0:T(8,128)(2,1)S(1)} %collective-permute-done.3), channel_id=1, source_target_pairs={{0,224},{32,0},{64,32},{96,64},{128,96},{160,128},{192,160},{224,1... | collective-permute-start | bytes 2752520 | tf_op jit(solution)/shard_map/ppermute | solution.py:55
  66.9 0.1 reduce.7
  67.2 0.3 broadcast_compare_fusion
  67.5 20.1 %collective-permute-done.4 = bf16[896,512]{1,0:T(8,128)(2,1)} collective-permute-done((bf16[896,512]{1,0:T(8,128)(2,1)}, bf16[896,512]{1,0:T(8,128)(2,1)}, u32[]{:S(2)}, u32[]{:S(2)}) %collective-permute-start.4) | collective-permute-done | bytes 917536 | tf_op jit(solution)/shard_map/ppermute | solution.py:54
  87.6 3.2 %collective-permute-start.7 = (bf16[896,512]{1,0:T(8,128)(2,1)}, bf16[896,512]{1,0:T(8,128)(2,1)}, u32[]{:S(2)}, u32[]{:S(2)}) collective-permute-start(bf16[896,512]{1,0:T(8,128)(2,1)} %collective-permute-done.6), channel_id=1, source_target_pairs={{0,224},{32,0},{64,32},{96,64},{128,96},{160,128},{192,160},{224,1... | collective-permute-start | bytes 2752520 | tf_op jit(solution)/shard_map/ppermute | solution.py:55
  90.9 6.5 %fusion = f32[384,2]{0,1:T(2,128)S(1)} fusion(bf16[384,2,7168]{0,2,1:T(8,128)(2,1)} %all-gather.4.cloned.1.call-done), kind=kLoop, calls=%fused_computation.2 | loop fusion | flops 16514304 | bytes 11013120 | tf_op jit(solution)/shard_map/reduce_sum | solution.py:48
  97.4 0.8 copy-done
  98.1 3.1 %fusion.2 = bf16[384,2,7168]{0,2,1:T(8,128)(2,1)S(1)} fusion(bf16[384,2,7168]{0,2,1:T(8,128)(2,1)S(1)} %copy-done, f32[2,7168]{1,0:T(2,128)S(1)} %bitcast.171, f32[384,2]{0,1:T(2,128)S(1)} %add_rsqrt_fusion), kind=kLoop, calls=%fused_computation.4 | loop fusion | flops 22020096 | bytes 22080512 | tf_op jit(solution)/shard_map/convert_element_type | solution.py:51
  101.2 9.7 %collective-permute-done.5 = bf16[896,512]{1,0:T(8,128)(2,1)} collective-permute-done((bf16[896,512]{1,0:T(8,128)(2,1)}, bf16[896,512]{1,0:T(8,128)(2,1)}, u32[]{:S(2)}, u32[]{:S(2)}) %collective-permute-start.5) | collective-permute-done | bytes 917536 | tf_op jit(solution)/shard_map/ppermute | solution.py:54
  110.9 1.0 fusion.31
  111.9 1.0 fusion.29
  113.0 0.3 collective-permute-start.8
  113.2 3.2 %collective-permute-start.11 = (bf16[896,512]{1,0:T(8,128)(2,1)}, bf16[896,512]{1,0:T(8,128)(2,1)S(1)}, u32[]{:S(2)}, u32[]{:S(2)}) collective-permute-start(bf16[896,512]{1,0:T(8,128)(2,1)} %collective-permute-done.7), channel_id=1, source_target_pairs={{0,224},{32,0},{64,32},{96,64},{128,96},{160,128},{192,160},{224,1... | collective-permute-start | bytes 2752520 | tf_op jit(solution)/shard_map/ppermute | solution.py:55
  116.4 2.2 fusion.21
  118.6 2.2 fusion.23
  120.8 2.2 fusion.25
  123.0 2.2 fusion.27
  125.2 10.3 %collective-permute-done.8 = bf16[896,512]{1,0:T(8,128)(2,1)S(1)} collective-permute-done((bf16[896,512]{1,0:T(8,128)(2,1)}, bf16[896,512]{1,0:T(8,128)(2,1)S(1)}, u32[]{:S(2)}, u32[]{:S(2)}) %collective-permute-start.8) | collective-permute-done | bytes 917536 | tf_op jit(solution)/shard_map/ppermute | solution.py:54
  135.5 2.2 fusion.10
  137.7 2.3 fusion.8
  140.0 3.3 %collective-permute-start.12 = (bf16[896,512]{1,0:T(8,128)(2,1)S(1)}, bf16[896,512]{1,0:T(8,128)(2,1)}, u32[]{:S(2)}, u32[]{:S(2)}) collective-permute-start(bf16[896,512]{1,0:T(8,128)(2,1)S(1)} %collective-permute-done.11), channel_id=1, source_target_pairs={{0,224},{32,0},{64,32},{96,64},{128,96},{160,128},{192,160},{224,1... | collective-permute-start | bytes 2752520 | tf_op jit(solution)/shard_map/ppermute | solution.py:55
  143.3 1.0 fusion.12
  144.3 1.0 fusion.14
  145.4 11.4 %collective-permute-done.9 = bf16[896,512]{1,0:T(8,128)(2,1)S(1)} collective-permute-done((bf16[896,512]{1,0:T(8,128)(2,1)S(1)}, bf16[896,512]{1,0:T(8,128)(2,1)S(1)}, u32[]{:S(2)}, u32[]{:S(2)}) %collective-permute-start.9) | collective-permute-done | bytes 917536 | tf_op jit(solution)/shard_map/ppermute | solution.py:54
  156.8 1.0 fusion.19
  157.8 1.0 fusion.6
  158.8 1.8 collective-permute-done.12
  160.6 3.8 %collective-permute-start.13 = (bf16[896,512]{1,0:T(8,128)(2,1)}, bf16[896,512]{1,0:T(8,128)(2,1)S(1)}, u32[]{:S(2)}, u32[]{:S(2)}) collective-permute-start(bf16[896,512]{1,0:T(8,128)(2,1)} %collective-permute-done.12), channel_id=1, source_target_pairs={{0,224},{32,0},{64,32},{96,64},{128,96},{160,128},{192,160},{224,1... | collective-permute-start | bytes 2752520 | tf_op jit(solution)/shard_map/ppermute | solution.py:55
  164.4 1.0 fusion.17
  165.4 2.2 fusion.4
  167.6 9.6 %collective-permute-done.10 = bf16[896,512]{1,0:T(8,128)(2,1)S(1)} collective-permute-done((bf16[896,512]{1,0:T(8,128)(2,1)S(1)}, bf16[896,512]{1,0:T(8,128)(2,1)S(1)}, u32[]{:S(2)}, u32[]{:S(2)}) %collective-permute-start.10) | collective-permute-done | bytes 917536 | tf_op jit(solution)/shard_map/ppermute | solution.py:54
  177.2 1.3 fusion.88
  178.5 2.6 %collective-permute-done.13 = bf16[896,512]{1,0:T(8,128)(2,1)S(1)} collective-permute-done((bf16[896,512]{1,0:T(8,128)(2,1)}, bf16[896,512]{1,0:T(8,128)(2,1)S(1)}, u32[]{:S(2)}, u32[]{:S(2)}) %collective-permute-start.13) | collective-permute-done | bytes 917536 | tf_op jit(solution)/shard_map/ppermute | solution.py:55
  181.1 1.3 fusion.89
  182.5 1.1 exponential_reduce_fusion
  183.6 23.3 %all-gather = f32[96,384,2]{1,2,0:T(2,128)S(1)} all-gather(f32[3,384,2]{1,2,0:T(2,128)S(1)} %pad_maximum_fusion.1), channel_id=2, replica_groups=mesh['row'=8,'col'=32] {'col'}, dimensions={0}, use_global_device_ids=true | all-gather | bytes 304128 | tf_op jit(solution)/shard_map/all_gather | solution.py:65
  207.0 0.1 fusion.66
  207.1 0.2 select_reduce_fusion.3
  207.3 30.5 %psum.7 = f32[8,3,16]{2,0,1:T(8,128)S(1)} all-reduce(f32[8,3,16]{2,0,1:T(8,128)S(1)} %broadcast_select_fusion), channel_id=1, replica_groups=mesh['row'=8,'col'=32] {'row'}, use_global_device_ids=true, to_apply=%region_13.14 | all-reduce | flops 384 | bytes 3072 | tf_op jit(solution)/shard_map/psum | solution.py:80
  237.8 0.6 copy.81
  (47 shorter events, 0.7 us)
Async XLA Ops:
  6.5 84.4 %all-gather.4.cloned.1.call-start = ((), (), s32[]{:S(2)}) async-start(), calls=%async_computation | async-start | bytes 11354112 | tf_op jit(solution)/shard_map/all_gather | solution.py:19
  7.3 31.3 %copy-start.3 = (f32[2,224]{1,0:T(2,128)S(1)}, f32[2,224]{1,0:T(2,128)}, u32[]{:S(2)}) copy-start(f32[2,224]{1,0:T(2,128)} %param.7) | copy-start | bytes 5380
  7.3 59.5 %copy-start.4 = (s32[16]{0:T(128)S(1)}, s32[16]{0:T(128)}, u32[]{:S(2)}) copy-start(s32[16]{0:T(128)} %param.9) | copy-start | bytes 196
  7.3 59.9 %copy-start.7 = (s32[16]{0:T(128)S(1)}, s32[16]{0:T(128)}, u32[]{:S(2)}) copy-start(s32[16]{0:T(128)} %param.11) | copy-start | bytes 196
  7.3 59.9 %copy-start.2 = (s32[384]{0:T(512)S(1)}, s32[384]{0:T(512)}, u32[]{:S(2)}) copy-start(s32[384]{0:T(512)} %param.10) | copy-start | bytes 4612
  8.9 26.4 %collective-permute-start = (bf16[896,512]{1,0:T(8,128)(2,1)S(1)}, bf16[896,512]{1,0:T(8,128)(2,1)}, u32[]{:S(2)}, u32[]{:S(2)}) collective-permute-start(bf16[896,512]{1,0:T(8,128)(2,1)S(1)} %get-tuple-element.28), channel_id=1, source_target_pairs={{0,32},{32,64},{64,96},{96,128},{128,160},{160,192},{192,224},{224... | collective-permute-start | bytes 2752520 | tf_op jit(solution)/shard_map/ppermute | solution.py:54
  10.9 24.4 %collective-permute-start.2 = (bf16[896,512]{1,0:T(8,128)(2,1)S(1)}, bf16[896,512]{1,0:T(8,128)(2,1)S(1)}, u32[]{:S(2)}, u32[]{:S(2)}) collective-permute-start(bf16[896,512]{1,0:T(8,128)(2,1)S(1)} %get-tuple-element.27), channel_id=1, source_target_pairs={{0,224},{32,0},{64,32},{96,64},{128,96},{160,128},{192,160},{224,1... | collective-permute-start | bytes 2752520 | tf_op jit(solution)/shard_map/ppermute | solution.py:55
  35.3 28.1 %collective-permute-start.1 = (bf16[896,512]{1,0:T(8,128)(2,1)}, bf16[896,512]{1,0:T(8,128)(2,1)}, u32[]{:S(2)}, u32[]{:S(2)}) collective-permute-start(bf16[896,512]{1,0:T(8,128)(2,1)} %collective-permute-done), channel_id=1, source_target_pairs={{0,32},{32,64},{64,96},{96,128},{128,160},{160,192},{192,224},{224... | collective-permute-start | bytes 2752520 | tf_op jit(solution)/shard_map/ppermute | solution.py:54
  35.3 28.1 %collective-permute-start.3 = (bf16[896,512]{1,0:T(8,128)(2,1)S(1)}, bf16[896,512]{1,0:T(8,128)(2,1)S(1)}, u32[]{:S(2)}, u32[]{:S(2)}) collective-permute-start(bf16[896,512]{1,0:T(8,128)(2,1)S(1)} %collective-permute-done.2), channel_id=1, source_target_pairs={{0,224},{32,0},{64,32},{96,64},{128,96},{160,128},{192,160},{224,1... | collective-permute-start | bytes 2752520 | tf_op jit(solution)/shard_map/ppermute | solution.py:55
  63.4 27.5 %copy-start.5 = (bf16[896,512]{1,0:T(8,128)(2,1)}, bf16[896,512]{1,0:T(8,128)(2,1)S(1)}, u32[]{:S(2)}) copy-start(bf16[896,512]{1,0:T(8,128)(2,1)S(1)} %collective-permute-done.3) | copy-start | bytes 2752516
  63.4 24.2 %collective-permute-start.4 = (bf16[896,512]{1,0:T(8,128)(2,1)}, bf16[896,512]{1,0:T(8,128)(2,1)}, u32[]{:S(2)}, u32[]{:S(2)}) collective-permute-start(bf16[896,512]{1,0:T(8,128)(2,1)} %collective-permute-done.1), channel_id=1, source_target_pairs={{0,32},{32,64},{64,96},{96,128},{128,160},{160,192},{192,224},{224... | collective-permute-start | bytes 2752520 | tf_op jit(solution)/shard_map/ppermute | solution.py:54
  63.5 24.1 %collective-permute-start.6 = (bf16[896,512]{1,0:T(8,128)(2,1)S(1)}, bf16[896,512]{1,0:T(8,128)(2,1)}, u32[]{:S(2)}, u32[]{:S(2)}) collective-permute-start(bf16[896,512]{1,0:T(8,128)(2,1)S(1)} %collective-permute-done.3), channel_id=1, source_target_pairs={{0,224},{32,0},{64,32},{96,64},{128,96},{160,128},{192,160},{224,1... | collective-permute-start | bytes 2752520 | tf_op jit(solution)/shard_map/ppermute | solution.py:55
  87.6 23.3 %collective-permute-start.5 = (bf16[896,512]{1,0:T(8,128)(2,1)}, bf16[896,512]{1,0:T(8,128)(2,1)}, u32[]{:S(2)}, u32[]{:S(2)}) collective-permute-start(bf16[896,512]{1,0:T(8,128)(2,1)} %collective-permute-done.4), channel_id=1, source_target_pairs={{0,32},{32,64},{64,96},{96,128},{128,160},{160,192},{192,224},{224... | collective-permute-start | bytes 2752520 | tf_op jit(solution)/shard_map/ppermute | solution.py:54
  87.6 23.3 %collective-permute-start.7 = (bf16[896,512]{1,0:T(8,128)(2,1)}, bf16[896,512]{1,0:T(8,128)(2,1)}, u32[]{:S(2)}, u32[]{:S(2)}) collective-permute-start(bf16[896,512]{1,0:T(8,128)(2,1)} %collective-permute-done.6), channel_id=1, source_target_pairs={{0,224},{32,0},{64,32},{96,64},{128,96},{160,128},{192,160},{224,1... | collective-permute-start | bytes 2752520 | tf_op jit(solution)/shard_map/ppermute | solution.py:55
  90.9 7.3 %copy-start = (bf16[384,2,7168]{0,2,1:T(8,128)(2,1)S(1)}, bf16[384,2,7168]{0,2,1:T(8,128)(2,1)}, u32[]{:S(2)}) copy-start(bf16[384,2,7168]{0,2,1:T(8,128)(2,1)} %all-gather.4.cloned.1.call-done) | copy-start | bytes 33030148
  98.1 12.8 %copy-start.1 = (bf16[896,1024]{1,0:T(8,128)(2,1)S(1)}, bf16[896,1024]{1,0:T(8,128)(2,1)}, u32[]{:S(2)}) copy-start(bf16[896,1024]{1,0:T(8,128)(2,1)} %param.8) | copy-start | bytes 5505028
  113.0 22.6 %collective-permute-start.8 = (bf16[896,512]{1,0:T(8,128)(2,1)}, bf16[896,512]{1,0:T(8,128)(2,1)S(1)}, u32[]{:S(2)}, u32[]{:S(2)}) collective-permute-start(bf16[896,512]{1,0:T(8,128)(2,1)} %collective-permute-done.5), channel_id=1, source_target_pairs={{0,32},{32,64},{64,96},{96,128},{128,160},{160,192},{192,224},{224... | collective-permute-start | bytes 2752520 | tf_op jit(solution)/shard_map/ppermute | solution.py:54
  113.2 26.8 %collective-permute-start.11 = (bf16[896,512]{1,0:T(8,128)(2,1)}, bf16[896,512]{1,0:T(8,128)(2,1)S(1)}, u32[]{:S(2)}, u32[]{:S(2)}) collective-permute-start(bf16[896,512]{1,0:T(8,128)(2,1)} %collective-permute-done.7), channel_id=1, source_target_pairs={{0,224},{32,0},{64,32},{96,64},{128,96},{160,128},{192,160},{224,1... | collective-permute-start | bytes 2752520 | tf_op jit(solution)/shard_map/ppermute | solution.py:55
  135.5 21.2 %collective-permute-start.9 = (bf16[896,512]{1,0:T(8,128)(2,1)S(1)}, bf16[896,512]{1,0:T(8,128)(2,1)S(1)}, u32[]{:S(2)}, u32[]{:S(2)}) collective-permute-start(bf16[896,512]{1,0:T(8,128)(2,1)S(1)} %collective-permute-done.8), channel_id=1, source_target_pairs={{0,32},{32,64},{64,96},{96,128},{128,160},{160,192},{192,224},{224... | collective-permute-start | bytes 2752520 | tf_op jit(solution)/shard_map/ppermute | solution.py:54
  137.7 5.6 %copy-start.6 = (bf16[896,512]{1,0:T(8,128)(2,1)S(1)}, bf16[896,512]{1,0:T(8,128)(2,1)}, u32[]{:S(2)}) copy-start(bf16[896,512]{1,0:T(8,128)(2,1)} %copy-done.5) | copy-start | bytes 2752516
  140.0 20.6 %collective-permute-start.12 = (bf16[896,512]{1,0:T(8,128)(2,1)S(1)}, bf16[896,512]{1,0:T(8,128)(2,1)}, u32[]{:S(2)}, u32[]{:S(2)}) collective-permute-start(bf16[896,512]{1,0:T(8,128)(2,1)S(1)} %collective-permute-done.11), channel_id=1, source_target_pairs={{0,224},{32,0},{64,32},{96,64},{128,96},{160,128},{192,160},{224,1... | collective-permute-start | bytes 2752520 | tf_op jit(solution)/shard_map/ppermute | solution.py:55
  156.8 20.4 %collective-permute-start.10 = (bf16[896,512]{1,0:T(8,128)(2,1)S(1)}, bf16[896,512]{1,0:T(8,128)(2,1)S(1)}, u32[]{:S(2)}, u32[]{:S(2)}) collective-permute-start(bf16[896,512]{1,0:T(8,128)(2,1)S(1)} %collective-permute-done.9), channel_id=1, source_target_pairs={{0,32},{32,64},{64,96},{96,128},{128,160},{160,192},{192,224},{224... | collective-permute-start | bytes 2752520 | tf_op jit(solution)/shard_map/ppermute | solution.py:54
  160.6 20.5 %collective-permute-start.13 = (bf16[896,512]{1,0:T(8,128)(2,1)}, bf16[896,512]{1,0:T(8,128)(2,1)S(1)}, u32[]{:S(2)}, u32[]{:S(2)}) collective-permute-start(bf16[896,512]{1,0:T(8,128)(2,1)} %collective-permute-done.12), channel_id=1, source_target_pairs={{0,224},{32,0},{64,32},{96,64},{128,96},{160,128},{192,160},{224,1... | collective-permute-start | bytes 2752520 | tf_op jit(solution)/shard_map/ppermute | solution.py:55
Sparse Core Ops, SparseCore 0:
  9.9 66.8 all-gather.3

commit v9 on v4

--- a/solution.py
+++ b/solution.py
@@ -45,7 +45,7 @@
     picked = jnp.sum(
         jnp.where(targets[:, None, None] == vocab_ids[None, None, :], logits, 0.0), axis=2
     )
-    parts = lax.all_gather(jnp.stack([row_max, exp_total, picked]), "col")
+    parts = lax.all_gather(jnp.stack([row_max, exp_total, picked] * 4), "col")
     max_logit = jnp.max(parts[:, 0], axis=0)
     exp_total = jnp.sum(parts[:, 1] * jnp.exp(parts[:, 0] - max_logit[None]), axis=0)
     picked = jnp.sum(parts[:, 2], axis=0)

time: 242 us -> 269 us (1.11)
  waiting for transfers between devices: 94.5 us -> 133 us
  blocking collectives: 69.1 us -> 48.4 us
  local copies, waits for them, and re-layouts: 4.18 us -> 7.61 us
  other arithmetic: 11.7 us -> 14.4 us
    ppermute x7, waiting for transfers between devices: 93.7 us -> 1.44 us  [per_device(): left = lax.ppermute(left, 'row', forward)]
    ppermute x7, waiting for transfers between devices: 0.02 us -> 86.5 us  [per_device(): right = lax.ppermute(right, 'row', backward)]
    all_gather x0 -> x1, waiting for transfers between devices: none -> 44.4 us  [per_device(): parts = lax.all_gather(jnp.stack([row_max, exp_total, picked] * 4), 'col')]
    all_gather x1 -> x0, blocking collectives: 23.2 us -> none  [per_device(): parts = lax.all_gather(jnp.stack([row_max, exp_total, picked]), 'col')]
    ppermute x7, starting transfers between devices: 23.5 us -> 27.8 us  [per_device(): right = lax.ppermute(right, 'row', backward)]
    unnamed x45 -> x57, local copies, waits for them, and re-layouts: 1.93 us -> 5.37 us
  transfers between devices with their start and end apart: 15 -> 16, of which waited for: 5 -> 9; matrix products, arithmetic and copies ran while one was open for 14% -> 12% of each run, Pallas kernels for 0% -> 0%
where the time goes in v9:
time: 269 us; the launch traced here: 268 us
  waiting for transfers between devices  133 us (49%)
  blocking collectives  48.4 us (18%)
  starting transfers between devices  27.8 us (10%)
  matrix products  22.9 us (9%)
  other arithmetic  14.4 us (5%)
  between operations  13.8 us (5%)
  local copies, waits for them, and re-layouts  7.61 us (3%)
    ppermute x7, waiting for transfers between devices, per_device(): right = lax.ppermute(right, 'row', backward)  86.5 us
    all_gather x1, waiting for transfers between devices, per_device(): parts = lax.all_gather(jnp.stack([row_max, exp_total, picked] * 4), 'col')  44.4 us
    ppermute x7, starting transfers between devices, per_device(): right = lax.ppermute(right, 'row', backward)  27.8 us
    all_gather x1, blocking collectives, per_device(): full_gain = lax.all_gather(final_gain, 'col', axis=1, tiled=True)  24.3 us
    all_gather x1, blocking collectives, per_device(): stats = lax.all_gather(jnp.stack([ratio_sums, squares, ratio_max]), 'row')  24.1 us
    dot_general x16, matrix products, block_logits(): jnp.einsum('tmd,dv->tmv', features[shard], block, preferred_element_type=...  22.9 us
    reduce_sum x1, other arithmetic, per_device(): mean_square = jnp.sum(stream * stream, axis=2) / D  6.49 us
  transfers between devices with their start and end apart: 16, of which 9 were waited for; matrix products, arithmetic and copies ran while one was open for 12% of the time, Pallas kernels for 0%

profile of v9, /device:TPU:2, one launch (start us, length us, event | category | flops | bytes accessed | tf_op | source)
XLA Modules:
  0.0 267.9 jit_solution(5210687063062639690)
XLA Ops:
  6.5 0.7 all-gather.7.cloned.1.call-update
  7.3 1.6 fusion.87
  8.9 5.9 %collective-permute-start.7 = (bf16[896,512]{1,0:T(8,128)(2,1)S(1)}, bf16[896,512]{1,0:T(8,128)(2,1)S(1)}, u32[]{:S(2)}, u32[]{:S(2)}) collective-permute-start(bf16[896,512]{1,0:T(8,128)(2,1)S(1)} %get-tuple-element.17), channel_id=1, source_target_pairs={{0,224},{32,0},{64,32},{96,64},{128,96},{160,128},{192,160},{224,1... | collective-permute-start | bytes 2752520 | tf_op jit(solution)/shard_map/ppermute | solution.py:38
  14.8 19.6 %collective-permute-done.7 = bf16[896,512]{1,0:T(8,128)(2,1)S(1)} collective-permute-done((bf16[896,512]{1,0:T(8,128)(2,1)S(1)}, bf16[896,512]{1,0:T(8,128)(2,1)S(1)}, u32[]{:S(2)}, u32[]{:S(2)}) %collective-permute-start.7) | collective-permute-done | bytes 917536 | tf_op jit(solution)/shard_map/ppermute | solution.py:38
  34.4 3.7 %collective-permute-start.8 = (bf16[896,512]{1,0:T(8,128)(2,1)S(1)}, bf16[896,512]{1,0:T(8,128)(2,1)S(1)}, u32[]{:S(2)}, u32[]{:S(2)}) collective-permute-start(bf16[896,512]{1,0:T(8,128)(2,1)S(1)} %collective-permute-done.7), channel_id=1, source_target_pairs={{0,224},{32,0},{64,32},{96,64},{128,96},{160,128},{192,160},{224,1... | collective-permute-start | bytes 2752520 | tf_op jit(solution)/shard_map/ppermute | solution.py:38
  38.2 18.8 %collective-permute-done.8 = bf16[896,512]{1,0:T(8,128)(2,1)S(1)} collective-permute-done((bf16[896,512]{1,0:T(8,128)(2,1)S(1)}, bf16[896,512]{1,0:T(8,128)(2,1)S(1)}, u32[]{:S(2)}, u32[]{:S(2)}) %collective-permute-start.8) | collective-permute-done | bytes 917536 | tf_op jit(solution)/shard_map/ppermute | solution.py:38
  57.0 3.7 %collective-permute-start.9 = (bf16[896,512]{1,0:T(8,128)(2,1)S(1)}, bf16[896,512]{1,0:T(8,128)(2,1)S(1)}, u32[]{:S(2)}, u32[]{:S(2)}) collective-permute-start(bf16[896,512]{1,0:T(8,128)(2,1)S(1)} %collective-permute-done.8), channel_id=1, source_target_pairs={{0,224},{32,0},{64,32},{96,64},{128,96},{160,128},{192,160},{224,1... | collective-permute-start | bytes 2752520 | tf_op jit(solution)/shard_map/ppermute | solution.py:38
  60.7 0.9 copy-done.10
  61.6 17.2 %collective-permute-done.9 = bf16[896,512]{1,0:T(8,128)(2,1)S(1)} collective-permute-done((bf16[896,512]{1,0:T(8,128)(2,1)S(1)}, bf16[896,512]{1,0:T(8,128)(2,1)S(1)}, u32[]{:S(2)}, u32[]{:S(2)}) %collective-permute-start.9) | collective-permute-done | bytes 917536 | tf_op jit(solution)/shard_map/ppermute | solution.py:38
  78.8 3.7 %collective-permute-start.10 = (bf16[896,512]{1,0:T(8,128)(2,1)S(1)}, bf16[896,512]{1,0:T(8,128)(2,1)S(1)}, u32[]{:S(2)}, u32[]{:S(2)}) collective-permute-start(bf16[896,512]{1,0:T(8,128)(2,1)S(1)} %collective-permute-done.9), channel_id=1, source_target_pairs={{0,224},{32,0},{64,32},{96,64},{128,96},{160,128},{192,160},{224,1... | collective-permute-start | bytes 2752520 | tf_op jit(solution)/shard_map/ppermute | solution.py:38
  82.5 0.7 collective-permute-done.2
  83.2 0.9 copy-done.14
  84.1 15.7 %collective-permute-done.10 = bf16[896,512]{1,0:T(8,128)(2,1)S(1)} collective-permute-done((bf16[896,512]{1,0:T(8,128)(2,1)S(1)}, bf16[896,512]{1,0:T(8,128)(2,1)S(1)}, u32[]{:S(2)}, u32[]{:S(2)}) %collective-permute-start.10) | collective-permute-done | bytes 917536 | tf_op jit(solution)/shard_map/ppermute | solution.py:38
  99.7 3.7 %collective-permute-start.11 = (bf16[896,512]{1,0:T(8,128)(2,1)S(1)}, bf16[896,512]{1,0:T(8,128)(2,1)}, u32[]{:S(2)}, u32[]{:S(2)}) collective-permute-start(bf16[896,512]{1,0:T(8,128)(2,1)S(1)} %collective-permute-done.10), channel_id=1, source_target_pairs={{0,224},{32,0},{64,32},{96,64},{128,96},{160,128},{192,160},{224,1... | collective-permute-start | bytes 2752520 | tf_op jit(solution)/shard_map/ppermute | solution.py:38
  103.4 0.4 collective-permute-done.3
  103.8 0.9 copy-done.18
  104.7 15.2 %collective-permute-done.11 = bf16[896,512]{1,0:T(8,128)(2,1)} collective-permute-done((bf16[896,512]{1,0:T(8,128)(2,1)S(1)}, bf16[896,512]{1,0:T(8,128)(2,1)}, u32[]{:S(2)}, u32[]{:S(2)}) %collective-permute-start.11) | collective-permute-done | bytes 917536 | tf_op jit(solution)/shard_map/ppermute | solution.py:38
  119.9 3.8 %collective-permute-start.12 = (bf16[896,512]{1,0:T(8,128)(2,1)}, bf16[896,512]{1,0:T(8,128)(2,1)}, u32[]{:S(2)}, u32[]{:S(2)}) collective-permute-start(bf16[896,512]{1,0:T(8,128)(2,1)} %collective-permute-done.11), channel_id=1, source_target_pairs={{0,224},{32,0},{64,32},{96,64},{128,96},{160,128},{192,160},{224,1... | collective-permute-start | bytes 2752520 | tf_op jit(solution)/shard_map/ppermute | solution.py:38
  123.7 0.4 collective-permute-done.4
  124.2 24.3 %all-gather.2 = f32[32,224,2]{1,2,0:T(2,128)S(1)} all-gather(f32[1,224,2]{1,2,0:T(2,128)S(1)} %bitcast.189), channel_id=1, replica_groups=mesh['row'=8,'col'=32] {'col'}, dimensions={0}, use_global_device_ids=true | all-gather | bytes 59136 | tf_op jit(solution)/shard_map/all_gather | solution.py:20
  149.0 3.3 %collective-permute-start.13 = (bf16[896,512]{1,0:T(8,128)(2,1)}, bf16[896,512]{1,0:T(8,128)(2,1)}, u32[]{:S(2)}, u32[]{:S(2)}) collective-permute-start(bf16[896,512]{1,0:T(8,128)(2,1)} %collective-permute-done.12), channel_id=1, source_target_pairs={{0,224},{32,0},{64,32},{96,64},{128,96},{160,128},{192,160},{224,1... | collective-permute-start | bytes 2752520 | tf_op jit(solution)/shard_map/ppermute | solution.py:38
  152.3 6.5 %fusion = f32[384,2]{0,1:T(2,128)S(1)} fusion(bf16[384,2,7168]{0,2,1:T(8,128)(2,1)} %all-gather.7.cloned.1.call-done), kind=kLoop, calls=%fused_computation.2 | loop fusion | flops 16514304 | bytes 11013120 | tf_op jit(solution)/shard_map/reduce_sum | solution.py:22
  158.8 0.7 copy-done
  159.5 3.1 %fusion.2 = bf16[384,2,7168]{0,2,1:T(8,128)(2,1)S(1)} fusion(bf16[384,2,7168]{0,2,1:T(8,128)(2,1)S(1)} %copy-done, f32[2,7168]{1,0:T(2,128)S(1)} %bitcast.182, f32[384,2]{0,1:T(2,128)S(1)} %add_rsqrt_fusion), kind=kLoop, calls=%fused_computation.4 | loop fusion | flops 22020096 | bytes 22080512 | tf_op jit(solution)/shard_map/convert_element_type | solution.py:23
  162.6 1.0 fusion.29
  163.6 1.0 fusion.31
  164.7 2.2 fusion.4
  166.9 2.3 fusion.6
  169.2 1.0 fusion.8
  170.3 1.0 fusion.10
  171.5 1.0 fusion.12
  172.7 1.0 fusion.14
  173.7 2.2 fusion.17
  175.9 2.3 fusion.19
  178.2 1.0 fusion.21
  179.4 1.0 fusion.23
  180.5 1.0 fusion.25
  181.7 1.0 fusion.27
  182.7 2.5 fusion.89
  185.3 1.3 fusion.88
  186.7 1.1 select_reduce_fusion
  187.9 0.6 copy-done.2
  188.8 44.4 %all-gather.9.cloned.1.call-done = f32[384,384,2]{1,2,0:T(2,128)} async-done(((f32[12,384,2]{1,2,0:T(2,128)}), f32[384,384,2]{1,2,0:T(2,128)}) %all-gather.9.cloned.1.call-update) | async-done | bytes 1179664 | tf_op jit(solution)/shard_map/all_gather | solution.py:48
  233.2 0.9 bitcast_reduce_fusion
  234.1 0.9 slice_reduce_fusion
  235.1 1.0 fusion.66
  236.3 24.1 %all-gather.3 = f32[8,3,16]{2,1,0:T(4,128)S(1)} all-gather(f32[1,3,16]{2,1,0:T(4,128)S(1)} %maximum_bitcast_fusion), channel_id=3, replica_groups=mesh['row'=8,'col'=32] {'row'}, dimensions={0}, use_global_device_ids=true | all-gather | bytes 1728 | tf_op jit(solution)/shard_map/all_gather | solution.py:61
  260.5 0.6 copy.81
  (87 shorter events, 2.3 us)
Async XLA Ops:
  6.5 145.7 %all-gather.7.cloned.1.call-start = ((), (), s32[]{:S(2)}) async-start(), calls=%async_computation | async-start | bytes 11354112 | tf_op jit(solution)/shard_map/all_gather | solution.py:19
  7.3 116.9 %copy-start.4 = (f32[2,224]{1,0:T(2,128)S(1)}, f32[2,224]{1,0:T(2,128)}, u32[]{:S(2)}) copy-start(f32[2,224]{1,0:T(2,128)} %param.7) | copy-start | bytes 5380
  7.3 141.4 %copy-start.3 = (s32[384]{0:T(512)S(1)}, s32[384]{0:T(512)}, u32[]{:S(2)}) copy-start(s32[384]{0:T(512)} %param.10) | copy-start | bytes 4612
  7.3 225.9 %all-gather.9.cloned.1.call-start = ((), (), s32[]{:S(2)}) async-start(), calls=%async_computation.1 | async-start | bytes 1216512 | tf_op jit(solution)/shard_map/all_gather | solution.py:48
  8.9 25.5 %collective-permute-start.7 = (bf16[896,512]{1,0:T(8,128)(2,1)S(1)}, bf16[896,512]{1,0:T(8,128)(2,1)S(1)}, u32[]{:S(2)}, u32[]{:S(2)}) collective-permute-start(bf16[896,512]{1,0:T(8,128)(2,1)S(1)} %get-tuple-element.17), channel_id=1, source_target_pairs={{0,224},{32,0},{64,32},{96,64},{128,96},{160,128},{192,160},{224,1... | collective-permute-start | bytes 2752520 | tf_op jit(solution)/shard_map/ppermute | solution.py:38
  14.8 23.3 %collective-permute-start = (bf16[896,512]{1,0:T(8,128)(2,1)S(1)}, bf16[896,512]{1,0:T(8,128)(2,1)S(1)}, u32[]{:S(2)}, u32[]{:S(2)}) collective-permute-start(bf16[896,512]{1,0:T(8,128)(2,1)S(1)} %get-tuple-element.18), channel_id=1, source_target_pairs={{0,32},{32,64},{64,96},{96,128},{128,160},{160,192},{192,224},{224... | collective-permute-start | bytes 2752520 | tf_op jit(solution)/shard_map/ppermute | solution.py:37
  34.4 114.2 %copy-start.8 = (bf16[896,512]{1,0:T(8,128)(2,1)}, bf16[896,512]{1,0:T(8,128)(2,1)S(1)}, u32[]{:S(2)}) copy-start(bf16[896,512]{1,0:T(8,128)(2,1)S(1)} %collective-permute-done.7) | copy-start | bytes 2752516
  34.4 22.6 %collective-permute-start.8 = (bf16[896,512]{1,0:T(8,128)(2,1)S(1)}, bf16[896,512]{1,0:T(8,128)(2,1)S(1)}, u32[]{:S(2)}, u32[]{:S(2)}) collective-permute-start(bf16[896,512]{1,0:T(8,128)(2,1)S(1)} %collective-permute-done.7), channel_id=1, source_target_pairs={{0,224},{32,0},{64,32},{96,64},{128,96},{160,128},{192,160},{224,1... | collective-permute-start | bytes 2752520 | tf_op jit(solution)/shard_map/ppermute | solution.py:38
  38.1 86.0 %copy-start.6 = (bf16[896,512]{1,0:T(8,128)(2,1)}, bf16[896,512]{1,0:T(8,128)(2,1)S(1)}, u32[]{:S(2)}) copy-start(bf16[896,512]{1,0:T(8,128)(2,1)S(1)} %collective-permute-done) | copy-start | bytes 2752516
  38.1 22.6 %collective-permute-start.1 = (bf16[896,512]{1,0:T(8,128)(2,1)S(1)}, bf16[896,512]{1,0:T(8,128)(2,1)S(1)}, u32[]{:S(2)}, u32[]{:S(2)}) collective-permute-start(bf16[896,512]{1,0:T(8,128)(2,1)S(1)} %collective-permute-done), channel_id=1, source_target_pairs={{0,32},{32,64},{64,96},{96,128},{128,160},{160,192},{192,224},{224... | collective-permute-start | bytes 2752520 | tf_op jit(solution)/shard_map/ppermute | solution.py:37
  57.0 26.2 %copy-start.12 = (bf16[896,512]{1,0:T(8,128)(2,1)}, bf16[896,512]{1,0:T(8,128)(2,1)S(1)}, u32[]{:S(2)}) copy-start(bf16[896,512]{1,0:T(8,128)(2,1)S(1)} %collective-permute-done.8) | copy-start | bytes 2752516
  57.0 21.8 %collective-permute-start.9 = (bf16[896,512]{1,0:T(8,128)(2,1)S(1)}, bf16[896,512]{1,0:T(8,128)(2,1)S(1)}, u32[]{:S(2)}, u32[]{:S(2)}) collective-permute-start(bf16[896,512]{1,0:T(8,128)(2,1)S(1)} %collective-permute-done.8), channel_id=1, source_target_pairs={{0,224},{32,0},{64,32},{96,64},{128,96},{160,128},{192,160},{224,1... | collective-permute-start | bytes 2752520 | tf_op jit(solution)/shard_map/ppermute | solution.py:38
  60.7 0.9 copy-start.10
  61.6 21.5 %collective-permute-start.2 = (bf16[896,512]{1,0:T(8,128)(2,1)S(1)}, bf16[896,512]{1,0:T(8,128)(2,1)S(1)}, u32[]{:S(2)}, u32[]{:S(2)}) collective-permute-start(bf16[896,512]{1,0:T(8,128)(2,1)S(1)} %collective-permute-done.1), channel_id=1, source_target_pairs={{0,32},{32,64},{64,96},{96,128},{128,160},{160,192},{192,224},{224... | collective-permute-start | bytes 2752520 | tf_op jit(solution)/shard_map/ppermute | solution.py:37
  78.8 25.0 %copy-start.16 = (bf16[896,512]{1,0:T(8,128)(2,1)}, bf16[896,512]{1,0:T(8,128)(2,1)S(1)}, u32[]{:S(2)}) copy-start(bf16[896,512]{1,0:T(8,128)(2,1)S(1)} %collective-permute-done.9) | copy-start | bytes 2752516
  78.8 20.9 %collective-permute-start.10 = (bf16[896,512]{1,0:T(8,128)(2,1)S(1)}, bf16[896,512]{1,0:T(8,128)(2,1)S(1)}, u32[]{:S(2)}, u32[]{:S(2)}) collective-permute-start(bf16[896,512]{1,0:T(8,128)(2,1)S(1)} %collective-permute-done.9), channel_id=1, source_target_pairs={{0,224},{32,0},{64,32},{96,64},{128,96},{160,128},{192,160},{224,1... | collective-permute-start | bytes 2752520 | tf_op jit(solution)/shard_map/ppermute | solution.py:38
  83.2 0.9 copy-start.14
  83.2 20.7 %collective-permute-start.3 = (bf16[896,512]{1,0:T(8,128)(2,1)S(1)}, bf16[896,512]{1,0:T(8,128)(2,1)S(1)}, u32[]{:S(2)}, u32[]{:S(2)}) collective-permute-start(bf16[896,512]{1,0:T(8,128)(2,1)S(1)} %collective-permute-done.2), channel_id=1, source_target_pairs={{0,32},{32,64},{64,96},{96,128},{128,160},{160,192},{192,224},{224... | collective-permute-start | bytes 2752520 | tf_op jit(solution)/shard_map/ppermute | solution.py:37
  99.7 24.4 %copy-start.20 = (bf16[896,512]{1,0:T(8,128)(2,1)}, bf16[896,512]{1,0:T(8,128)(2,1)S(1)}, u32[]{:S(2)}) copy-start(bf16[896,512]{1,0:T(8,128)(2,1)S(1)} %collective-permute-done.10) | copy-start | bytes 2752516
  99.7 20.2 %collective-permute-start.11 = (bf16[896,512]{1,0:T(8,128)(2,1)S(1)}, bf16[896,512]{1,0:T(8,128)(2,1)}, u32[]{:S(2)}, u32[]{:S(2)}) collective-permute-start(bf16[896,512]{1,0:T(8,128)(2,1)S(1)} %collective-permute-done.10), channel_id=1, source_target_pairs={{0,224},{32,0},{64,32},{96,64},{128,96},{160,128},{192,160},{224,1... | collective-permute-start | bytes 2752520 | tf_op jit(solution)/shard_map/ppermute | solution.py:38
  103.8 0.9 copy-start.18
  103.8 20.3 %collective-permute-start.4 = (bf16[896,512]{1,0:T(8,128)(2,1)S(1)}, bf16[896,512]{1,0:T(8,128)(2,1)}, u32[]{:S(2)}, u32[]{:S(2)}) collective-permute-start(bf16[896,512]{1,0:T(8,128)(2,1)S(1)} %collective-permute-done.3), channel_id=1, source_target_pairs={{0,32},{32,64},{64,96},{96,128},{128,160},{160,192},{192,224},{224... | collective-permute-start | bytes 2752520 | tf_op jit(solution)/shard_map/ppermute | solution.py:37
  119.9 29.0 %collective-permute-start.12 = (bf16[896,512]{1,0:T(8,128)(2,1)}, bf16[896,512]{1,0:T(8,128)(2,1)}, u32[]{:S(2)}, u32[]{:S(2)}) collective-permute-start(bf16[896,512]{1,0:T(8,128)(2,1)} %collective-permute-done.11), channel_id=1, source_target_pairs={{0,224},{32,0},{64,32},{96,64},{128,96},{160,128},{192,160},{224,1... | collective-permute-start | bytes 2752520 | tf_op jit(solution)/shard_map/ppermute | solution.py:38
  124.1 28.1 %collective-permute-start.5 = (bf16[896,512]{1,0:T(8,128)(2,1)}, bf16[896,512]{1,0:T(8,128)(2,1)}, u32[]{:S(2)}, u32[]{:S(2)}) collective-permute-start(bf16[896,512]{1,0:T(8,128)(2,1)} %collective-permute-done.4), channel_id=1, source_target_pairs={{0,32},{32,64},{64,96},{96,128},{128,160},{160,192},{192,224},{224... | collective-permute-start | bytes 2752520 | tf_op jit(solution)/shard_map/ppermute | solution.py:37
  149.0 33.8 %collective-permute-start.13 = (bf16[896,512]{1,0:T(8,128)(2,1)}, bf16[896,512]{1,0:T(8,128)(2,1)}, u32[]{:S(2)}, u32[]{:S(2)}) collective-permute-start(bf16[896,512]{1,0:T(8,128)(2,1)} %collective-permute-done.12), channel_id=1, source_target_pairs={{0,224},{32,0},{64,32},{96,64},{128,96},{160,128},{192,160},{224,1... | collective-permute-start | bytes 2752520 | tf_op jit(solution)/shard_map/ppermute | solution.py:38
  152.2 33.0 %collective-permute-start.6 = (bf16[896,512]{1,0:T(8,128)(2,1)}, bf16[896,512]{1,0:T(8,128)(2,1)S(1)}, u32[]{:S(2)}, u32[]{:S(2)}) collective-permute-start(bf16[896,512]{1,0:T(8,128)(2,1)} %collective-permute-done.5), channel_id=1, source_target_pairs={{0,32},{32,64},{64,96},{96,128},{128,160},{160,192},{192,224},{224... | collective-permute-start | bytes 2752520 | tf_op jit(solution)/shard_map/ppermute | solution.py:37
  152.3 7.3 %copy-start = (bf16[384,2,7168]{0,2,1:T(8,128)(2,1)S(1)}, bf16[384,2,7168]{0,2,1:T(8,128)(2,1)}, u32[]{:S(2)}) copy-start(bf16[384,2,7168]{0,2,1:T(8,128)(2,1)} %all-gather.7.cloned.1.call-done) | copy-start | bytes 33030148
  159.5 3.1 %copy-start.1 = (bf16[896,1024]{1,0:T(8,128)(2,1)S(1)}, bf16[896,1024]{1,0:T(8,128)(2,1)}, u32[]{:S(2)}) copy-start(bf16[896,1024]{1,0:T(8,128)(2,1)} %param.8) | copy-start | bytes 5505028
  166.9 2.3 copy-start.21
  169.1 1.2 copy-start.17
  170.3 1.2 copy-start.13
  171.5 1.2 copy-start.9
  175.9 2.3 copy-start.19
  178.2 1.2 copy-start.15
  179.4 1.2 copy-start.11
  180.5 1.2 copy-start.7
  186.6 1.8 copy-start.5
  186.6 2.2 copy-start.22
  187.8 0.6 copy-start.2
Sparse Core Ops, SparseCore 0:
  9.9 66.7 all-gather.6
  188.6 44.5 all-gather.8

commit v10 on v8

--- a/solution.py
+++ b/solution.py
@@ -50,6 +50,8 @@
                 stream * lax.rsqrt(mean_square[:, :, None] + EPS) * full_gain[None, :, :]
             ).astype(jnp.bfloat16)
             left, right, features = lax.optimization_barrier((left, right, features))
+        if step == n_row - 1:
+            left, right, features = lax.optimization_barrier((left, right, features))
             features = features.reshape(tok_rows, 2, n_row, shard_rows).transpose(2, 0, 1, 3)
         left = lax.ppermute(left, "row", forward)
         right = lax.ppermute(right, "row", backward)
@@ -75,9 +77,7 @@
     ratio_sums = jnp.sum(jnp.where(member, log_ratio[:, None], 0.0), axis=0)
     squares = jnp.sum(jnp.where(member, (log_ratio * log_ratio)[:, None], 0.0), axis=0)
     ratio_max = jnp.max(jnp.where(member, log_ratio[:, None], -1e30), axis=0)
-    own_slot = (jnp.arange(n_row, dtype=jnp.int32) == row_index)[:, None, None]
-    own_stats = jnp.stack([ratio_sums, squares, ratio_max])[None]
-    stats = lax.psum(jnp.where(own_slot, own_stats, 0.0), "row")
+    stats = lax.all_gather(jnp.stack([ratio_sums, squares, ratio_max]), "row")
     seq_stats = jnp.stack(
         [jnp.sum(stats[:, 0], axis=0), jnp.sum(stats[:, 1], axis=0), jnp.max(stats[:, 2], axis=0)]
     )

time: 246 us -> 246 us (level)
  blocking collectives: 78.5 us -> 70.6 us
  matrix products: 25.1 us -> 30.3 us
  other arithmetic: 11.7 us -> 14.7 us
    ppermute x7, waiting for transfers between devices: 4.42 us -> 35.3 us  [per_device(): right = lax.ppermute(right, 'row', backward)]
    psum x1 -> x0, blocking collectives: 30.5 us -> none  [per_device(): stats = lax.psum(jnp.where(own_slot, own_stats, 0.0), 'row')]
    ppermute x7, waiting for transfers between devices: 81.5 us -> 51.2 us  [per_device(): left = lax.ppermute(left, 'row', forward)]
    all_gather x0 -> x1, blocking collectives: none -> 22.6 us  [per_device(): stats = lax.all_gather(jnp.stack([ratio_sums, squares, ratio_max]), 'row')]
    dot_general x16, matrix products: 25.1 us -> 30.3 us  [block_logits(): jnp.einsum('tmd,dv->tmv', features[shard], block, preferred_element_type=...]
    convert_element_type x1, other arithmetic: 3.08 us -> 6.14 us  [per_device(): features = (stream * lax.rsqrt(mean_square[:, :, None] + EPS) * full_gain...]
  transfers between devices with their start and end apart: 15 -> 15, of which waited for: 8 -> 6; matrix products, arithmetic and copies ran while one was open for 14% -> 14% of each run, Pallas kernels for 0% -> 0%
where the time goes in v10:
time: 246 us
  waiting for transfers between devices  87.2 us (35%)
  blocking collectives  70.6 us (29%)
  matrix products  30.3 us (12%)
  starting transfers between devices  25.8 us (10%)
  other arithmetic  14.7 us (6%)
  between operations  13.7 us (6%)
  local copies, waits for them, and re-layouts  3.31 us (1%)
    ppermute x7, waiting for transfers between devices, per_device(): left = lax.ppermute(left, 'row', forward)  51.2 us
    ppermute x7, waiting for transfers between devices, per_device(): right = lax.ppermute(right, 'row', backward)  35.3 us
    dot_general x16, matrix products, block_logits(): jnp.einsum('tmd,dv->tmv', features[shard], block, preferred_element_type=...  30.3 us
    all_gather x1, blocking collectives, per_device(): full_gain = lax.all_gather(final_gain, 'col', axis=1, tiled=True)  24.7 us
    ppermute x7, starting transfers between devices, per_device(): right = lax.ppermute(right, 'row', backward)  23.6 us
    all_gather x1, blocking collectives, per_device(): parts = lax.all_gather(jnp.stack([row_max, exp_total, picked]), 'col')  23.2 us
    all_gather x1, blocking collectives, per_device(): stats = lax.all_gather(jnp.stack([ratio_sums, squares, ratio_max]), 'row')  22.6 us
    reduce_sum x1, other arithmetic, per_device(): mean_square = jnp.sum(stream * stream, axis=2) / D  6.49 us
  transfers between devices with their start and end apart: 15, of which 6 were waited for; matrix products, arithmetic and copies ran while one was open for 14% of the time, Pallas kernels for 0%

profile of v10, /device:TPU:2, one launch (start us, length us, event | category | flops | bytes accessed | tf_op | source)
XLA Modules:
  0.0 245.6 jit_solution(18362537144855858202)
XLA Ops:
  6.5 0.7 all-gather.6.cloned.1.call-update
  7.3 1.6 fusion.87
  8.8 2.0 collective-permute-start
  10.8 4.0 %collective-permute-start.2 = (bf16[896,512]{1,0:T(8,128)(2,1)S(1)}, bf16[896,512]{1,0:T(8,128)(2,1)S(1)}, u32[]{:S(2)}, u32[]{:S(2)}) collective-permute-start(bf16[896,512]{1,0:T(8,128)(2,1)S(1)} %get-tuple-element.33), channel_id=1, source_target_pairs={{0,224},{32,0},{64,32},{96,64},{128,96},{160,128},{192,160},{224,1... | collective-permute-start | bytes 2752520 | tf_op jit(solution)/shard_map/ppermute | solution.py:57
  14.9 20.3 %collective-permute-done = bf16[896,512]{1,0:T(8,128)(2,1)S(1)} collective-permute-done((bf16[896,512]{1,0:T(8,128)(2,1)S(1)}, bf16[896,512]{1,0:T(8,128)(2,1)S(1)}, u32[]{:S(2)}, u32[]{:S(2)}) %collective-permute-start) | collective-permute-done | bytes 917536 | tf_op jit(solution)/shard_map/ppermute | solution.py:56
  35.2 3.2 %collective-permute-start.3 = (bf16[896,512]{1,0:T(8,128)(2,1)S(1)}, bf16[896,512]{1,0:T(8,128)(2,1)S(1)}, u32[]{:S(2)}, u32[]{:S(2)}) collective-permute-start(bf16[896,512]{1,0:T(8,128)(2,1)S(1)} %collective-permute-done.2), channel_id=1, source_target_pairs={{0,224},{32,0},{64,32},{96,64},{128,96},{160,128},{192,160},{224,1... | collective-permute-start | bytes 2752520 | tf_op jit(solution)/shard_map/ppermute | solution.py:57
  38.4 24.7 %all-gather.2 = f32[32,224,2]{1,2,0:T(2,128)S(1)} all-gather(f32[1,224,2]{1,2,0:T(2,128)S(1)} %bitcast.180), channel_id=1, replica_groups=mesh['row'=8,'col'=32] {'col'}, dimensions={0}, use_global_device_ids=true | all-gather | bytes 59136 | tf_op jit(solution)/shard_map/all_gather | solution.py:20
  63.1 0.1 reshape.194
  63.3 0.1 collective-permute-start.4
  63.4 3.2 %collective-permute-start.6 = (bf16[896,512]{1,0:T(8,128)(2,1)S(1)}, bf16[896,512]{1,0:T(8,128)(2,1)}, u32[]{:S(2)}, u32[]{:S(2)}) collective-permute-start(bf16[896,512]{1,0:T(8,128)(2,1)S(1)} %collective-permute-done.3), channel_id=1, source_target_pairs={{0,224},{32,0},{64,32},{96,64},{128,96},{160,128},{192,160},{224,1... | collective-permute-start | bytes 2752520 | tf_op jit(solution)/shard_map/ppermute | solution.py:57
  66.6 20.9 %collective-permute-done.4 = bf16[896,512]{1,0:T(8,128)(2,1)} collective-permute-done((bf16[896,512]{1,0:T(8,128)(2,1)}, bf16[896,512]{1,0:T(8,128)(2,1)}, u32[]{:S(2)}, u32[]{:S(2)}) %collective-permute-start.4) | collective-permute-done | bytes 917536 | tf_op jit(solution)/shard_map/ppermute | solution.py:56
  87.5 3.2 %collective-permute-start.7 = (bf16[896,512]{1,0:T(8,128)(2,1)}, bf16[896,512]{1,0:T(8,128)(2,1)}, u32[]{:S(2)}, u32[]{:S(2)}) collective-permute-start(bf16[896,512]{1,0:T(8,128)(2,1)} %collective-permute-done.6), channel_id=1, source_target_pairs={{0,224},{32,0},{64,32},{96,64},{128,96},{160,128},{192,160},{224,1... | collective-permute-start | bytes 2752520 | tf_op jit(solution)/shard_map/ppermute | solution.py:57
  90.7 6.5 %fusion = f32[384,2]{0,1:T(2,128)S(1)} fusion(bf16[384,2,7168]{0,2,1:T(8,128)(2,1)} %all-gather.6.cloned.1.call-done), kind=kLoop, calls=%fused_computation.2 | loop fusion | flops 16514304 | bytes 11013120 | tf_op jit(solution)/shard_map/reduce_sum | solution.py:48
  97.2 0.7 copy-done
  98.0 6.1 %fusion.2 = bf16[384,2,7168]{0,2,1:T(8,128)(2,1)} fusion(bf16[384,2,7168]{0,2,1:T(8,128)(2,1)S(1)} %copy-done, f32[2,7168]{1,0:T(2,128)S(1)} %bitcast.173, f32[384,2]{0,1:T(2,128)S(1)} %add_rsqrt_fusion), kind=kLoop, calls=%fused_computation.4 | loop fusion | flops 22020096 | bytes 22080512 | tf_op jit(solution)/shard_map/convert_element_type | solution.py:51
  104.2 6.6 %collective-permute-done.5 = bf16[896,512]{1,0:T(8,128)(2,1)} collective-permute-done((bf16[896,512]{1,0:T(8,128)(2,1)}, bf16[896,512]{1,0:T(8,128)(2,1)}, u32[]{:S(2)}, u32[]{:S(2)}) %collective-permute-start.5) | collective-permute-done | bytes 917536 | tf_op jit(solution)/shard_map/ppermute | solution.py:56
  110.8 3.0 %collective-permute-start.10 = (bf16[896,512]{1,0:T(8,128)(2,1)}, bf16[896,512]{1,0:T(8,128)(2,1)}, u32[]{:S(2)}, u32[]{:S(2)}) collective-permute-start(bf16[896,512]{1,0:T(8,128)(2,1)} %collective-permute-done.7), channel_id=1, source_target_pairs={{0,224},{32,0},{64,32},{96,64},{128,96},{160,128},{192,160},{224,1... | collective-permute-start | bytes 2752520 | tf_op jit(solution)/shard_map/ppermute | solution.py:57
  113.7 18.4 %collective-permute-done.10 = bf16[896,512]{1,0:T(8,128)(2,1)} collective-permute-done((bf16[896,512]{1,0:T(8,128)(2,1)}, bf16[896,512]{1,0:T(8,128)(2,1)}, u32[]{:S(2)}, u32[]{:S(2)}) %collective-permute-start.10) | collective-permute-done | bytes 917536 | tf_op jit(solution)/shard_map/ppermute | solution.py:57
  132.2 3.7 %collective-permute-start.11 = (bf16[896,512]{1,0:T(8,128)(2,1)}, bf16[896,512]{1,0:T(8,128)(2,1)S(1)}, u32[]{:S(2)}, u32[]{:S(2)}) collective-permute-start(bf16[896,512]{1,0:T(8,128)(2,1)} %collective-permute-done.10), channel_id=1, source_target_pairs={{0,224},{32,0},{64,32},{96,64},{128,96},{160,128},{192,160},{224,1... | collective-permute-start | bytes 2752520 | tf_op jit(solution)/shard_map/ppermute | solution.py:57
  136.0 0.1 reduce.7
  136.2 0.1 convert_reduce_fusion
  136.3 0.3 broadcast_compare_fusion
  136.6 16.8 %collective-permute-done.11 = bf16[896,512]{1,0:T(8,128)(2,1)S(1)} collective-permute-done((bf16[896,512]{1,0:T(8,128)(2,1)}, bf16[896,512]{1,0:T(8,128)(2,1)S(1)}, u32[]{:S(2)}, u32[]{:S(2)}) %collective-permute-start.11) | collective-permute-done | bytes 917536 | tf_op jit(solution)/shard_map/ppermute | solution.py:57
  153.5 3.4 %collective-permute-done.9 = bf16[896,512]{1,0:T(8,128)(2,1)} collective-permute-done((bf16[896,512]{1,0:T(8,128)(2,1)}, bf16[896,512]{1,0:T(8,128)(2,1)}, u32[]{:S(2)}, u32[]{:S(2)}) %collective-permute-start.9) | collective-permute-done | bytes 917536 | tf_op jit(solution)/shard_map/ppermute | solution.py:56
  156.9 2.5 %fusion.31 = f32[384,2,512]{2,0,1:T(8,128)S(1)} fusion(bf16[384,2,8,896]{0,3,2,1:T(8,128)(2,1)} %bitcast.154, s32[]{:T(128)S(6)} %select_n.130, bf16[896,1024]{1,0:T(8,128)(2,1)S(1)} %copy-done.2), kind=kOutput, calls=%fused_computation.38 | convolution fusion | flops 704643072 | bytes 3866628 | tf_op jit(solution)/shard_map/tmd,dv->tmv/dot_general | solution.py:30
  159.4 3.0 %fusion.29 = f32[384,2,512]{2,0,1:T(8,128)S(1)} fusion(bf16[384,2,8,896]{0,3,2,1:T(8,128)(2,1)} %bitcast.155, s32[]{:T(128)S(6)} %select_n.130, bf16[896,1024]{1,0:T(8,128)(2,1)S(1)} %copy-done.2), kind=kOutput, calls=%fused_computation.36 | convolution fusion | flops 704643072 | bytes 3866628 | tf_op jit(solution)/shard_map/tmd,dv->tmv/dot_general | solution.py:30
  162.5 3.2 %collective-permute-start.13 = (bf16[896,512]{1,0:T(8,128)(2,1)S(1)}, bf16[896,512]{1,0:T(8,128)(2,1)S(1)}, u32[]{:S(2)}, u32[]{:S(2)}) collective-permute-start(bf16[896,512]{1,0:T(8,128)(2,1)S(1)} %collective-permute-done.11), channel_id=1, source_target_pairs={{0,224},{32,0},{64,32},{96,64},{128,96},{160,128},{192,160},{224,1... | collective-permute-start | bytes 2752520 | tf_op jit(solution)/shard_map/ppermute | solution.py:57
  165.7 2.6 %fusion.19 = f32[384,2,512]{2,0,1:T(8,128)S(1)} fusion(bf16[384,2,8,896]{0,3,2,1:T(8,128)(2,1)} %bitcast.156, s32[]{:T(128)S(6)} %select_n.140, bf16[896,512]{1,0:T(8,128)(2,1)} %collective-permute-done.8), kind=kOutput, calls=%fused_computation.26 | convolution fusion | flops 704643072 | bytes 3866628 | tf_op jit(solution)/shard_map/tmd,dv->tmv/dot_general | solution.py:30
  168.3 2.2 fusion.21
  170.5 2.2 fusion.23
  172.7 2.3 fusion.25
  175.0 1.0 fusion.27
  176.0 2.2 fusion.10
  178.2 2.3 fusion.8
  180.5 1.0 fusion.12
  181.5 0.2 copy-done.7
  181.7 1.0 fusion.14
  182.7 2.2 fusion.6
  184.9 1.0 fusion.16
  185.9 1.0 fusion.3
  186.9 2.5 %fusion.88 = (f32[384,2]{0,1:T(2,128)S(1)}, f32[384,2,512]{2,0,1:T(8,128)S(1)}) fusion(f32[384,2,512]{2,0,1:T(8,128)S(1)} %fusion.16, bf16[896,512]{1,0:T(8,128)(2,1)} %collective-permute-done.9, bf16[384,2,8,896]{0,3,2,1:T(8,128)(2,1)S(1)} %bitcast.168, s32[]{:T(128)S(6)} %select_n.142, f32[384,2,512]{2,0,1:T(8,128)S(1)} %fusion.19, ...), kind=kOutput, calls=%fused_computation.118 | convolution fusion | flops 707788032 | bytes 14879748 | tf_op jit(solution)/shard_map/tmd,dv->tmv/dot_general | solution.py:30
  189.5 1.4 fusion.89
  190.8 1.1 exponential_reduce_fusion
  191.9 23.2 %all-gather = f32[96,384,2]{1,2,0:T(2,128)S(1)} all-gather(f32[3,384,2]{1,2,0:T(2,128)S(1)} %pad_maximum_fusion.1), channel_id=2, replica_groups=mesh['row'=8,'col'=32] {'col'}, dimensions={0}, use_global_device_ids=true | all-gather | bytes 304128 | tf_op jit(solution)/shard_map/all_gather | solution.py:67
  215.2 0.1 fusion.66
  215.4 0.2 select_reduce_fusion.3
  215.5 22.6 %all-gather.3 = f32[8,3,16]{2,1,0:T(4,128)S(1)} all-gather(f32[1,3,16]{2,1,0:T(4,128)S(1)} %maximum_bitcast_fusion), channel_id=3, replica_groups=mesh['row'=8,'col'=32] {'row'}, dimensions={0}, use_global_device_ids=true | all-gather | bytes 1728 | tf_op jit(solution)/shard_map/all_gather | solution.py:80
  238.2 0.6 copy.81
  (55 shorter events, 0.5 us)
Async XLA Ops:
  6.5 84.2 %all-gather.6.cloned.1.call-start = ((), (), s32[]{:S(2)}) async-start(), calls=%async_computation | async-start | bytes 11354112 | tf_op jit(solution)/shard_map/all_gather | solution.py:19
  7.3 31.1 %copy-start.4 = (f32[2,224]{1,0:T(2,128)S(1)}, f32[2,224]{1,0:T(2,128)}, u32[]{:S(2)}) copy-start(f32[2,224]{1,0:T(2,128)} %param.7) | copy-start | bytes 5380
  8.8 26.3 %collective-permute-start = (bf16[896,512]{1,0:T(8,128)(2,1)S(1)}, bf16[896,512]{1,0:T(8,128)(2,1)S(1)}, u32[]{:S(2)}, u32[]{:S(2)}) collective-permute-start(bf16[896,512]{1,0:T(8,128)(2,1)S(1)} %get-tuple-element.34), channel_id=1, source_target_pairs={{0,32},{32,64},{64,96},{96,128},{128,160},{160,192},{192,224},{224... | collective-permute-start | bytes 2752520 | tf_op jit(solution)/shard_map/ppermute | solution.py:56
  10.8 24.3 %collective-permute-start.2 = (bf16[896,512]{1,0:T(8,128)(2,1)S(1)}, bf16[896,512]{1,0:T(8,128)(2,1)S(1)}, u32[]{:S(2)}, u32[]{:S(2)}) collective-permute-start(bf16[896,512]{1,0:T(8,128)(2,1)S(1)} %get-tuple-element.33), channel_id=1, source_target_pairs={{0,224},{32,0},{64,32},{96,64},{128,96},{160,128},{192,160},{224,1... | collective-permute-start | bytes 2752520 | tf_op jit(solution)/shard_map/ppermute | solution.py:57
  35.1 55.6 %copy-start.8 = (bf16[896,512]{1,0:T(8,128)(2,1)}, bf16[896,512]{1,0:T(8,128)(2,1)S(1)}, u32[]{:S(2)}) copy-start(bf16[896,512]{1,0:T(8,128)(2,1)S(1)} %collective-permute-done) | copy-start | bytes 2752516
  35.1 28.1 %collective-permute-start.1 = (bf16[896,512]{1,0:T(8,128)(2,1)S(1)}, bf16[896,512]{1,0:T(8,128)(2,1)}, u32[]{:S(2)}, u32[]{:S(2)}) collective-permute-start(bf16[896,512]{1,0:T(8,128)(2,1)S(1)} %collective-permute-done), channel_id=1, source_target_pairs={{0,32},{32,64},{64,96},{96,128},{128,160},{160,192},{192,224},{224... | collective-permute-start | bytes 2752520 | tf_op jit(solution)/shard_map/ppermute | solution.py:56
  35.1 55.6 %copy-start.6 = (bf16[896,512]{1,0:T(8,128)(2,1)}, bf16[896,512]{1,0:T(8,128)(2,1)S(1)}, u32[]{:S(2)}) copy-start(bf16[896,512]{1,0:T(8,128)(2,1)S(1)} %collective-permute-done.2) | copy-start | bytes 2752516
  35.2 28.1 %collective-permute-start.3 = (bf16[896,512]{1,0:T(8,128)(2,1)S(1)}, bf16[896,512]{1,0:T(8,128)(2,1)S(1)}, u32[]{:S(2)}, u32[]{:S(2)}) collective-permute-start(bf16[896,512]{1,0:T(8,128)(2,1)S(1)} %collective-permute-done.2), channel_id=1, source_target_pairs={{0,224},{32,0},{64,32},{96,64},{128,96},{160,128},{192,160},{224,1... | collective-permute-start | bytes 2752520 | tf_op jit(solution)/shard_map/ppermute | solution.py:57
  63.3 34.0 %copy-start.10 = (bf16[896,512]{1,0:T(8,128)(2,1)}, bf16[896,512]{1,0:T(8,128)(2,1)S(1)}, u32[]{:S(2)}) copy-start(bf16[896,512]{1,0:T(8,128)(2,1)S(1)} %collective-permute-done.3) | copy-start | bytes 2752516
  63.3 24.2 %collective-permute-start.4 = (bf16[896,512]{1,0:T(8,128)(2,1)}, bf16[896,512]{1,0:T(8,128)(2,1)}, u32[]{:S(2)}, u32[]{:S(2)}) collective-permute-start(bf16[896,512]{1,0:T(8,128)(2,1)} %collective-permute-done.1), channel_id=1, source_target_pairs={{0,32},{32,64},{64,96},{96,128},{128,160},{160,192},{192,224},{224... | collective-permute-start | bytes 2752520 | tf_op jit(solution)/shard_map/ppermute | solution.py:56
  63.4 24.1 %collective-permute-start.6 = (bf16[896,512]{1,0:T(8,128)(2,1)S(1)}, bf16[896,512]{1,0:T(8,128)(2,1)}, u32[]{:S(2)}, u32[]{:S(2)}) collective-permute-start(bf16[896,512]{1,0:T(8,128)(2,1)S(1)} %collective-permute-done.3), channel_id=1, source_target_pairs={{0,224},{32,0},{64,32},{96,64},{128,96},{160,128},{192,160},{224,1... | collective-permute-start | bytes 2752520 | tf_op jit(solution)/shard_map/ppermute | solution.py:57
  87.5 23.3 %collective-permute-start.5 = (bf16[896,512]{1,0:T(8,128)(2,1)}, bf16[896,512]{1,0:T(8,128)(2,1)}, u32[]{:S(2)}, u32[]{:S(2)}) collective-permute-start(bf16[896,512]{1,0:T(8,128)(2,1)} %collective-permute-done.4), channel_id=1, source_target_pairs={{0,32},{32,64},{64,96},{96,128},{128,160},{160,192},{192,224},{224... | collective-permute-start | bytes 2752520 | tf_op jit(solution)/shard_map/ppermute | solution.py:56
  87.5 23.3 %collective-permute-start.7 = (bf16[896,512]{1,0:T(8,128)(2,1)}, bf16[896,512]{1,0:T(8,128)(2,1)}, u32[]{:S(2)}, u32[]{:S(2)}) collective-permute-start(bf16[896,512]{1,0:T(8,128)(2,1)} %collective-permute-done.6), channel_id=1, source_target_pairs={{0,224},{32,0},{64,32},{96,64},{128,96},{160,128},{192,160},{224,1... | collective-permute-start | bytes 2752520 | tf_op jit(solution)/shard_map/ppermute | solution.py:57
  90.7 7.3 %copy-start = (bf16[384,2,7168]{0,2,1:T(8,128)(2,1)S(1)}, bf16[384,2,7168]{0,2,1:T(8,128)(2,1)}, u32[]{:S(2)}) copy-start(bf16[384,2,7168]{0,2,1:T(8,128)(2,1)} %all-gather.6.cloned.1.call-done) | copy-start | bytes 33030148
  98.0 37.9 %copy-start.5 = (s32[16]{0:T(128)S(1)}, s32[16]{0:T(128)}, u32[]{:S(2)}) copy-start(s32[16]{0:T(128)} %param.9) | copy-start | bytes 196
  98.0 38.3 %copy-start.12 = (s32[16]{0:T(128)S(1)}, s32[16]{0:T(128)}, u32[]{:S(2)}) copy-start(s32[16]{0:T(128)} %param.11) | copy-start | bytes 196
  98.0 38.3 %copy-start.3 = (s32[384]{0:T(512)S(1)}, s32[384]{0:T(512)}, u32[]{:S(2)}) copy-start(s32[384]{0:T(512)} %param.10) | copy-start | bytes 4612
  98.0 58.9 %copy-start.2 = (bf16[896,1024]{1,0:T(8,128)(2,1)S(1)}, bf16[896,1024]{1,0:T(8,128)(2,1)}, u32[]{:S(2)}) copy-start(bf16[896,1024]{1,0:T(8,128)(2,1)} %param.8) | copy-start | bytes 5505028
  110.8 21.4 %collective-permute-start.10 = (bf16[896,512]{1,0:T(8,128)(2,1)}, bf16[896,512]{1,0:T(8,128)(2,1)}, u32[]{:S(2)}, u32[]{:S(2)}) collective-permute-start(bf16[896,512]{1,0:T(8,128)(2,1)} %collective-permute-done.7), channel_id=1, source_target_pairs={{0,224},{32,0},{64,32},{96,64},{128,96},{160,128},{192,160},{224,1... | collective-permute-start | bytes 2752520 | tf_op jit(solution)/shard_map/ppermute | solution.py:57
  113.7 22.1 %collective-permute-start.8 = (bf16[896,512]{1,0:T(8,128)(2,1)}, bf16[896,512]{1,0:T(8,128)(2,1)}, u32[]{:S(2)}, u32[]{:S(2)}) collective-permute-start(bf16[896,512]{1,0:T(8,128)(2,1)} %collective-permute-done.5), channel_id=1, source_target_pairs={{0,32},{32,64},{64,96},{96,128},{128,160},{160,192},{192,224},{224... | collective-permute-start | bytes 2752520 | tf_op jit(solution)/shard_map/ppermute | solution.py:56
  132.2 21.3 %collective-permute-start.11 = (bf16[896,512]{1,0:T(8,128)(2,1)}, bf16[896,512]{1,0:T(8,128)(2,1)S(1)}, u32[]{:S(2)}, u32[]{:S(2)}) collective-permute-start(bf16[896,512]{1,0:T(8,128)(2,1)} %collective-permute-done.10), channel_id=1, source_target_pairs={{0,224},{32,0},{64,32},{96,64},{128,96},{160,128},{192,160},{224,1... | collective-permute-start | bytes 2752520 | tf_op jit(solution)/shard_map/ppermute | solution.py:57
  135.9 21.0 %collective-permute-start.9 = (bf16[896,512]{1,0:T(8,128)(2,1)}, bf16[896,512]{1,0:T(8,128)(2,1)}, u32[]{:S(2)}, u32[]{:S(2)}) collective-permute-start(bf16[896,512]{1,0:T(8,128)(2,1)} %collective-permute-done.8), channel_id=1, source_target_pairs={{0,32},{32,64},{64,96},{96,128},{128,160},{160,192},{192,224},{224... | collective-permute-start | bytes 2752520 | tf_op jit(solution)/shard_map/ppermute | solution.py:56
  156.9 11.4 %copy-start.1 = (bf16[384,2,7168]{0,2,1:T(8,128)(2,1)S(1)}, bf16[384,2,7168]{0,2,1:T(8,128)(2,1)}, u32[]{:S(2)}) copy-start(bf16[384,2,7168]{0,2,1:T(8,128)(2,1)} %fusion.2) | copy-start | bytes 33030148
  162.4 22.5 %collective-permute-start.12 = (bf16[896,512]{1,0:T(8,128)(2,1)}, bf16[896,512]{1,0:T(8,128)(2,1)S(1)}, u32[]{:S(2)}, u32[]{:S(2)}) collective-permute-start(bf16[896,512]{1,0:T(8,128)(2,1)} %collective-permute-done.9), channel_id=1, source_target_pairs={{0,32},{32,64},{64,96},{96,128},{128,160},{160,192},{192,224},{224... | collective-permute-start | bytes 2752520 | tf_op jit(solution)/shard_map/ppermute | solution.py:56
  162.5 23.4 %collective-permute-start.13 = (bf16[896,512]{1,0:T(8,128)(2,1)S(1)}, bf16[896,512]{1,0:T(8,128)(2,1)S(1)}, u32[]{:S(2)}, u32[]{:S(2)}) collective-permute-start(bf16[896,512]{1,0:T(8,128)(2,1)S(1)} %collective-permute-done.11), channel_id=1, source_target_pairs={{0,224},{32,0},{64,32},{96,64},{128,96},{160,128},{192,160},{224,1... | collective-permute-start | bytes 2752520 | tf_op jit(solution)/shard_map/ppermute | solution.py:57
  172.7 2.3 copy-start.9
  178.2 2.3 copy-start.11
  180.5 1.2 copy-start.7
Sparse Core Ops, SparseCore 0:
  9.9 66.8 all-gather.5

commit v11 on v10

--- a/solution.py
+++ b/solution.py
@@ -53,6 +53,7 @@
         if step == n_row - 1:
             left, right, features = lax.optimization_barrier((left, right, features))
             features = features.reshape(tok_rows, 2, n_row, shard_rows).transpose(2, 0, 1, 3)
+        left, right = lax.optimization_barrier((left, right))
         left = lax.ppermute(left, "row", forward)
         right = lax.ppermute(right, "row", backward)
         pending.append((left, right, (row_index - step) % n_row, (row_index + step) % n_row))

time: 246 us -> 244 us (level)
    ppermute x7, waiting for transfers between devices: 35.3 us -> 0.47 us  [per_device(): right = lax.ppermute(right, 'row', backward)]
    ppermute x7, waiting for transfers between devices: 51.2 us -> 84.4 us  [per_device(): left = lax.ppermute(left, 'row', forward)]
    ppermute x7, starting transfers between devices: 23.6 us -> 16.7 us  [per_device(): right = lax.ppermute(right, 'row', backward)]
    ppermute x7, starting transfers between devices: 2.17 us -> 8.96 us  [per_device(): left = lax.ppermute(left, 'row', forward)]
  transfers between devices with their start and end apart: 15 -> 15, of which waited for: 6 -> 7; matrix products, arithmetic and copies ran while one was open for 14% -> 16% of each run, Pallas kernels for 0% -> 0%
where the time goes in v11:
time: 244 us; the launch traced here: 243 us
  waiting for transfers between devices  85.5 us (35%)
  blocking collectives  70.3 us (29%)
  matrix products  30.4 us (12%)
  starting transfers between devices  25.7 us (11%)
  other arithmetic  14.7 us (6%)
  between operations  13.7 us (6%)
  local copies, waits for them, and re-layouts  3.16 us (1%)
    ppermute x7, waiting for transfers between devices, per_device(): left = lax.ppermute(left, 'row', forward)  84.4 us
    dot_general x16, matrix products, block_logits(): jnp.einsum('tmd,dv->tmv', features[shard], block, preferred_element_type=...  30.4 us
    all_gather x1, blocking collectives, per_device(): full_gain = lax.all_gather(final_gain, 'col', axis=1, tiled=True)  24.7 us
    all_gather x1, blocking collectives, per_device(): parts = lax.all_gather(jnp.stack([row_max, exp_total, picked]), 'col')  23.2 us
    all_gather x1, blocking collectives, per_device(): stats = lax.all_gather(jnp.stack([ratio_sums, squares, ratio_max]), 'row')  22.4 us
    ppermute x7, starting transfers between devices, per_device(): right = lax.ppermute(right, 'row', backward)  16.7 us
    ppermute x7, starting transfers between devices, per_device(): left = lax.ppermute(left, 'row', forward)  8.96 us
    reduce_sum x1, other arithmetic, per_device(): mean_square = jnp.sum(stream * stream, axis=2) / D  6.49 us
  transfers between devices with their start and end apart: 15, of which 7 were waited for; matrix products, arithmetic and copies ran while one was open for 16% of the time, Pallas kernels for 0%

profile of v11, /device:TPU:2, one launch (start us, length us, event | category | flops | bytes accessed | tf_op | source)
XLA Modules:
  0.0 243.5 jit_solution(9198087560408731107)
XLA Ops:
  6.5 0.7 all-gather.6.cloned.1.call-update
  7.3 1.6 fusion.93
  8.8 2.0 collective-permute-start
  10.8 4.0 %collective-permute-start.1 = (bf16[896,512]{1,0:T(8,128)(2,1)S(1)}, bf16[896,512]{1,0:T(8,128)(2,1)S(1)}, u32[]{:S(2)}, u32[]{:S(2)}) collective-permute-start(bf16[896,512]{1,0:T(8,128)(2,1)S(1)} %get-tuple-element.29), channel_id=1, source_target_pairs={{0,224},{32,0},{64,32},{96,64},{128,96},{160,128},{192,160},{224,1... | collective-permute-start | bytes 2752520 | tf_op jit(solution)/shard_map/ppermute | solution.py:58
  14.9 20.3 %collective-permute-done = bf16[896,512]{1,0:T(8,128)(2,1)S(1)} collective-permute-done((bf16[896,512]{1,0:T(8,128)(2,1)S(1)}, bf16[896,512]{1,0:T(8,128)(2,1)S(1)}, u32[]{:S(2)}, u32[]{:S(2)}) %collective-permute-start) | collective-permute-done | bytes 917536 | tf_op jit(solution)/shard_map/ppermute | solution.py:57
  35.2 3.2 %collective-permute-start.3 = (bf16[896,512]{1,0:T(8,128)(2,1)S(1)}, bf16[896,512]{1,0:T(8,128)(2,1)S(1)}, u32[]{:S(2)}, u32[]{:S(2)}) collective-permute-start(bf16[896,512]{1,0:T(8,128)(2,1)S(1)} %collective-permute-done.1), channel_id=1, source_target_pairs={{0,224},{32,0},{64,32},{96,64},{128,96},{160,128},{192,160},{224,1... | collective-permute-start | bytes 2752520 | tf_op jit(solution)/shard_map/ppermute | solution.py:58
  38.5 24.7 %all-gather.2 = f32[32,224,2]{1,2,0:T(2,128)S(1)} all-gather(f32[1,224,2]{1,2,0:T(2,128)S(1)} %bitcast.184), channel_id=1, replica_groups=mesh['row'=8,'col'=32] {'col'}, dimensions={0}, use_global_device_ids=true | all-gather | bytes 59136 | tf_op jit(solution)/shard_map/all_gather | solution.py:20
  63.2 0.1 reshape.194
  63.4 3.2 %collective-permute-start.5 = (bf16[896,512]{1,0:T(8,128)(2,1)S(1)}, bf16[896,512]{1,0:T(8,128)(2,1)}, u32[]{:S(2)}, u32[]{:S(2)}) collective-permute-start(bf16[896,512]{1,0:T(8,128)(2,1)S(1)} %collective-permute-done.3), channel_id=1, source_target_pairs={{0,224},{32,0},{64,32},{96,64},{128,96},{160,128},{192,160},{224,1... | collective-permute-start | bytes 2752520 | tf_op jit(solution)/shard_map/ppermute | solution.py:58
  66.7 20.9 %collective-permute-done.4 = bf16[896,512]{1,0:T(8,128)(2,1)} collective-permute-done((bf16[896,512]{1,0:T(8,128)(2,1)}, bf16[896,512]{1,0:T(8,128)(2,1)}, u32[]{:S(2)}, u32[]{:S(2)}) %collective-permute-start.4) | collective-permute-done | bytes 917536 | tf_op jit(solution)/shard_map/ppermute | solution.py:57
  87.6 1.0 collective-permute-start.6
  88.5 2.3 collective-permute-start.7
  90.8 6.5 %fusion = f32[384,2]{0,1:T(2,128)S(1)} fusion(bf16[384,2,7168]{0,2,1:T(8,128)(2,1)} %all-gather.6.cloned.1.call-done), kind=kLoop, calls=%fused_computation.2 | loop fusion | flops 16514304 | bytes 11013120 | tf_op jit(solution)/shard_map/reduce_sum | solution.py:48
  97.3 0.7 copy-done
  98.1 6.1 %fusion.2 = bf16[384,2,7168]{0,2,1:T(8,128)(2,1)} fusion(bf16[384,2,7168]{0,2,1:T(8,128)(2,1)S(1)} %copy-done, f32[2,7168]{1,0:T(2,128)S(1)} %bitcast.177, f32[384,2]{0,1:T(2,128)S(1)} %add_rsqrt_fusion), kind=kLoop, calls=%fused_computation.4 | loop fusion | flops 22020096 | bytes 22080512 | tf_op jit(solution)/shard_map/convert_element_type | solution.py:51
  104.2 6.6 %collective-permute-done.6 = bf16[896,512]{1,0:T(8,128)(2,1)} collective-permute-done((bf16[896,512]{1,0:T(8,128)(2,1)}, bf16[896,512]{1,0:T(8,128)(2,1)}, u32[]{:S(2)}, u32[]{:S(2)}) %collective-permute-start.6) | collective-permute-done | bytes 917536 | tf_op jit(solution)/shard_map/ppermute | solution.py:57
  110.8 2.0 collective-permute-start.8
  112.8 1.3 collective-permute-start.9
  114.1 19.2 %collective-permute-done.8 = bf16[896,512]{1,0:T(8,128)(2,1)} collective-permute-done((bf16[896,512]{1,0:T(8,128)(2,1)}, bf16[896,512]{1,0:T(8,128)(2,1)}, u32[]{:S(2)}, u32[]{:S(2)}) %collective-permute-start.8) | collective-permute-done | bytes 917536 | tf_op jit(solution)/shard_map/ppermute | solution.py:57
  133.3 0.2 collective-permute-done.9
  133.5 2.0 collective-permute-start.10
  135.4 1.3 collective-permute-start.11
  137.1 0.3 broadcast_compare_fusion
  137.4 17.4 %collective-permute-done.10 = bf16[896,512]{1,0:T(8,128)(2,1)} collective-permute-done((bf16[896,512]{1,0:T(8,128)(2,1)}, bf16[896,512]{1,0:T(8,128)(2,1)}, u32[]{:S(2)}, u32[]{:S(2)}) %collective-permute-start.10) | collective-permute-done | bytes 917536 | tf_op jit(solution)/shard_map/ppermute | solution.py:57
  154.8 0.3 collective-permute-done.11
  155.1 2.5 %fusion.33 = f32[384,2,512]{2,0,1:T(8,128)S(1)} fusion(bf16[384,2,8,896]{0,3,2,1:T(8,128)(2,1)} %bitcast.158, s32[]{:T(128)S(6)} %select_n.130, bf16[896,1024]{1,0:T(8,128)(2,1)S(1)} %copy-done.2), kind=kOutput, calls=%fused_computation.40 | convolution fusion | flops 704643072 | bytes 3866628 | tf_op jit(solution)/shard_map/tmd,dv->tmv/dot_general | solution.py:30
  157.6 3.0 %fusion.31 = f32[384,2,512]{2,0,1:T(8,128)S(1)} fusion(bf16[384,2,8,896]{0,3,2,1:T(8,128)(2,1)} %bitcast.159, s32[]{:T(128)S(6)} %select_n.130, bf16[896,1024]{1,0:T(8,128)(2,1)S(1)} %copy-done.2), kind=kOutput, calls=%fused_computation.38 | convolution fusion | flops 704643072 | bytes 3866628 | tf_op jit(solution)/shard_map/tmd,dv->tmv/dot_general | solution.py:30
  160.6 1.9 collective-permute-start.12
  162.5 1.4 collective-permute-start.13
  163.9 2.6 %fusion.21 = f32[384,2,512]{2,0,1:T(8,128)S(1)} fusion(bf16[384,2,8,896]{0,3,2,1:T(8,128)(2,1)} %bitcast.160, s32[]{:T(128)S(6)} %select_n.140, bf16[896,512]{1,0:T(8,128)(2,1)} %collective-permute-done.8), kind=kOutput, calls=%fused_computation.28 | convolution fusion | flops 704643072 | bytes 3866628 | tf_op jit(solution)/shard_map/tmd,dv->tmv/dot_general | solution.py:30
  166.5 2.2 fusion.19
  168.7 2.2 fusion.23
  170.9 2.2 fusion.25
  173.1 2.3 fusion.27
  175.4 1.0 fusion.29
  176.4 2.3 fusion.11
  178.7 1.0 fusion.13
  179.7 2.3 fusion.9
  182.0 1.0 fusion.15
  183.0 2.2 fusion.7
  185.2 1.0 fusion.5
  186.2 1.4 fusion.94
  187.6 1.4 fusion.95
  188.9 1.1 exponential_reduce_fusion
  190.0 23.2 %all-gather = f32[96,384,2]{1,2,0:T(2,128)S(1)} all-gather(f32[3,384,2]{1,2,0:T(2,128)S(1)} %pad_maximum_fusion.1), channel_id=2, replica_groups=mesh['row'=8,'col'=32] {'col'}, dimensions={0}, use_global_device_ids=true | all-gather | bytes 304128 | tf_op jit(solution)/shard_map/all_gather | solution.py:68
  213.4 0.2 select_reduce_fusion.3
  213.6 22.4 %all-gather.3 = f32[8,3,16]{2,1,0:T(4,128)S(1)} all-gather(f32[1,3,16]{2,1,0:T(4,128)S(1)} %maximum_bitcast_fusion), channel_id=3, replica_groups=mesh['row'=8,'col'=32] {'row'}, dimensions={0}, use_global_device_ids=true | all-gather | bytes 1728 | tf_op jit(solution)/shard_map/all_gather | solution.py:81
  236.1 0.6 copy.81
  (55 shorter events, 0.9 us)
Async XLA Ops:
  6.5 84.3 %all-gather.6.cloned.1.call-start = ((), (), s32[]{:S(2)}) async-start(), calls=%async_computation | async-start | bytes 11354112 | tf_op jit(solution)/shard_map/all_gather | solution.py:19
  7.3 31.2 %copy-start.4 = (f32[2,224]{1,0:T(2,128)S(1)}, f32[2,224]{1,0:T(2,128)}, u32[]{:S(2)}) copy-start(f32[2,224]{1,0:T(2,128)} %param.7) | copy-start | bytes 5380
  8.8 26.3 %collective-permute-start = (bf16[896,512]{1,0:T(8,128)(2,1)S(1)}, bf16[896,512]{1,0:T(8,128)(2,1)S(1)}, u32[]{:S(2)}, u32[]{:S(2)}) collective-permute-start(bf16[896,512]{1,0:T(8,128)(2,1)S(1)} %get-tuple-element.28), channel_id=1, source_target_pairs={{0,32},{32,64},{64,96},{96,128},{128,160},{160,192},{192,224},{224... | collective-permute-start | bytes 2752520 | tf_op jit(solution)/shard_map/ppermute | solution.py:57
  10.8 24.3 %collective-permute-start.1 = (bf16[896,512]{1,0:T(8,128)(2,1)S(1)}, bf16[896,512]{1,0:T(8,128)(2,1)S(1)}, u32[]{:S(2)}, u32[]{:S(2)}) collective-permute-start(bf16[896,512]{1,0:T(8,128)(2,1)S(1)} %get-tuple-element.29), channel_id=1, source_target_pairs={{0,224},{32,0},{64,32},{96,64},{128,96},{160,128},{192,160},{224,1... | collective-permute-start | bytes 2752520 | tf_op jit(solution)/shard_map/ppermute | solution.py:58
  35.1 55.7 %copy-start.8 = (bf16[896,512]{1,0:T(8,128)(2,1)}, bf16[896,512]{1,0:T(8,128)(2,1)S(1)}, u32[]{:S(2)}) copy-start(bf16[896,512]{1,0:T(8,128)(2,1)S(1)} %collective-permute-done) | copy-start | bytes 2752516
  35.1 55.7 %copy-start.6 = (bf16[896,512]{1,0:T(8,128)(2,1)}, bf16[896,512]{1,0:T(8,128)(2,1)S(1)}, u32[]{:S(2)}) copy-start(bf16[896,512]{1,0:T(8,128)(2,1)S(1)} %collective-permute-done.1) | copy-start | bytes 2752516
  35.1 28.2 %collective-permute-start.2 = (bf16[896,512]{1,0:T(8,128)(2,1)S(1)}, bf16[896,512]{1,0:T(8,128)(2,1)}, u32[]{:S(2)}, u32[]{:S(2)}) collective-permute-start(bf16[896,512]{1,0:T(8,128)(2,1)S(1)} %collective-permute-done), channel_id=1, source_target_pairs={{0,32},{32,64},{64,96},{96,128},{128,160},{160,192},{192,224},{224... | collective-permute-start | bytes 2752520 | tf_op jit(solution)/shard_map/ppermute | solution.py:57
  35.2 28.1 %collective-permute-start.3 = (bf16[896,512]{1,0:T(8,128)(2,1)S(1)}, bf16[896,512]{1,0:T(8,128)(2,1)S(1)}, u32[]{:S(2)}, u32[]{:S(2)}) collective-permute-start(bf16[896,512]{1,0:T(8,128)(2,1)S(1)} %collective-permute-done.1), channel_id=1, source_target_pairs={{0,224},{32,0},{64,32},{96,64},{128,96},{160,128},{192,160},{224,1... | collective-permute-start | bytes 2752520 | tf_op jit(solution)/shard_map/ppermute | solution.py:58
  63.3 34.0 %copy-start.10 = (bf16[896,512]{1,0:T(8,128)(2,1)}, bf16[896,512]{1,0:T(8,128)(2,1)S(1)}, u32[]{:S(2)}) copy-start(bf16[896,512]{1,0:T(8,128)(2,1)S(1)} %collective-permute-done.3) | copy-start | bytes 2752516
  63.3 24.2 %collective-permute-start.4 = (bf16[896,512]{1,0:T(8,128)(2,1)}, bf16[896,512]{1,0:T(8,128)(2,1)}, u32[]{:S(2)}, u32[]{:S(2)}) collective-permute-start(bf16[896,512]{1,0:T(8,128)(2,1)} %collective-permute-done.2), channel_id=1, source_target_pairs={{0,32},{32,64},{64,96},{96,128},{128,160},{160,192},{192,224},{224... | collective-permute-start | bytes 2752520 | tf_op jit(solution)/shard_map/ppermute | solution.py:57
  63.4 24.1 %collective-permute-start.5 = (bf16[896,512]{1,0:T(8,128)(2,1)S(1)}, bf16[896,512]{1,0:T(8,128)(2,1)}, u32[]{:S(2)}, u32[]{:S(2)}) collective-permute-start(bf16[896,512]{1,0:T(8,128)(2,1)S(1)} %collective-permute-done.3), channel_id=1, source_target_pairs={{0,224},{32,0},{64,32},{96,64},{128,96},{160,128},{192,160},{224,1... | collective-permute-start | bytes 2752520 | tf_op jit(solution)/shard_map/ppermute | solution.py:58
  87.6 23.3 %collective-permute-start.6 = (bf16[896,512]{1,0:T(8,128)(2,1)}, bf16[896,512]{1,0:T(8,128)(2,1)}, u32[]{:S(2)}, u32[]{:S(2)}) collective-permute-start(bf16[896,512]{1,0:T(8,128)(2,1)} %collective-permute-done.4), channel_id=1, source_target_pairs={{0,32},{32,64},{64,96},{96,128},{128,160},{160,192},{192,224},{224... | collective-permute-start | bytes 2752520 | tf_op jit(solution)/shard_map/ppermute | solution.py:57
  88.5 22.3 %collective-permute-start.7 = (bf16[896,512]{1,0:T(8,128)(2,1)}, bf16[896,512]{1,0:T(8,128)(2,1)}, u32[]{:S(2)}, u32[]{:S(2)}) collective-permute-start(bf16[896,512]{1,0:T(8,128)(2,1)} %collective-permute-done.5), channel_id=1, source_target_pairs={{0,224},{32,0},{64,32},{96,64},{128,96},{160,128},{192,160},{224,1... | collective-permute-start | bytes 2752520 | tf_op jit(solution)/shard_map/ppermute | solution.py:58
  90.8 7.3 %copy-start = (bf16[384,2,7168]{0,2,1:T(8,128)(2,1)S(1)}, bf16[384,2,7168]{0,2,1:T(8,128)(2,1)}, u32[]{:S(2)}) copy-start(bf16[384,2,7168]{0,2,1:T(8,128)(2,1)} %all-gather.6.cloned.1.call-done) | copy-start | bytes 33030148
  98.1 38.6 %copy-start.5 = (s32[16]{0:T(128)S(1)}, s32[16]{0:T(128)}, u32[]{:S(2)}) copy-start(s32[16]{0:T(128)} %param.9) | copy-start | bytes 196
  98.1 39.1 %copy-start.12 = (s32[16]{0:T(128)S(1)}, s32[16]{0:T(128)}, u32[]{:S(2)}) copy-start(s32[16]{0:T(128)} %param.11) | copy-start | bytes 196
  98.1 39.1 %copy-start.3 = (s32[384]{0:T(512)S(1)}, s32[384]{0:T(512)}, u32[]{:S(2)}) copy-start(s32[384]{0:T(512)} %param.10) | copy-start | bytes 4612
  98.1 57.0 %copy-start.2 = (bf16[896,1024]{1,0:T(8,128)(2,1)S(1)}, bf16[896,1024]{1,0:T(8,128)(2,1)}, u32[]{:S(2)}) copy-start(bf16[896,1024]{1,0:T(8,128)(2,1)} %param.8) | copy-start | bytes 5505028
  110.8 22.4 %collective-permute-start.8 = (bf16[896,512]{1,0:T(8,128)(2,1)}, bf16[896,512]{1,0:T(8,128)(2,1)}, u32[]{:S(2)}, u32[]{:S(2)}) collective-permute-start(bf16[896,512]{1,0:T(8,128)(2,1)} %collective-permute-done.6), channel_id=1, source_target_pairs={{0,32},{32,64},{64,96},{96,128},{128,160},{160,192},{192,224},{224... | collective-permute-start | bytes 2752520 | tf_op jit(solution)/shard_map/ppermute | solution.py:57
  112.8 20.7 %collective-permute-start.9 = (bf16[896,512]{1,0:T(8,128)(2,1)}, bf16[896,512]{1,0:T(8,128)(2,1)}, u32[]{:S(2)}, u32[]{:S(2)}) collective-permute-start(bf16[896,512]{1,0:T(8,128)(2,1)} %collective-permute-done.7), channel_id=1, source_target_pairs={{0,224},{32,0},{64,32},{96,64},{128,96},{160,128},{192,160},{224,1... | collective-permute-start | bytes 2752520 | tf_op jit(solution)/shard_map/ppermute | solution.py:58
  133.5 21.4 %collective-permute-start.10 = (bf16[896,512]{1,0:T(8,128)(2,1)}, bf16[896,512]{1,0:T(8,128)(2,1)}, u32[]{:S(2)}, u32[]{:S(2)}) collective-permute-start(bf16[896,512]{1,0:T(8,128)(2,1)} %collective-permute-done.8), channel_id=1, source_target_pairs={{0,32},{32,64},{64,96},{96,128},{128,160},{160,192},{192,224},{224... | collective-permute-start | bytes 2752520 | tf_op jit(solution)/shard_map/ppermute | solution.py:57
  135.4 19.7 %collective-permute-start.11 = (bf16[896,512]{1,0:T(8,128)(2,1)}, bf16[896,512]{1,0:T(8,128)(2,1)S(1)}, u32[]{:S(2)}, u32[]{:S(2)}) collective-permute-start(bf16[896,512]{1,0:T(8,128)(2,1)} %collective-permute-done.9), channel_id=1, source_target_pairs={{0,224},{32,0},{64,32},{96,64},{128,96},{160,128},{192,160},{224,1... | collective-permute-start | bytes 2752520 | tf_op jit(solution)/shard_map/ppermute | solution.py:58
  155.1 11.4 %copy-start.1 = (bf16[384,2,7168]{0,2,1:T(8,128)(2,1)S(1)}, bf16[384,2,7168]{0,2,1:T(8,128)(2,1)}, u32[]{:S(2)}) copy-start(bf16[384,2,7168]{0,2,1:T(8,128)(2,1)} %fusion.2) | copy-start | bytes 33030148
  160.6 25.6 %collective-permute-start.12 = (bf16[896,512]{1,0:T(8,128)(2,1)}, bf16[896,512]{1,0:T(8,128)(2,1)S(1)}, u32[]{:S(2)}, u32[]{:S(2)}) collective-permute-start(bf16[896,512]{1,0:T(8,128)(2,1)} %collective-permute-done.10), channel_id=1, source_target_pairs={{0,32},{32,64},{64,96},{96,128},{128,160},{160,192},{192,224},{224... | collective-permute-start | bytes 2752520 | tf_op jit(solution)/shard_map/ppermute | solution.py:57
  162.5 25.1 %collective-permute-start.13 = (bf16[896,512]{1,0:T(8,128)(2,1)S(1)}, bf16[896,512]{1,0:T(8,128)(2,1)S(1)}, u32[]{:S(2)}, u32[]{:S(2)}) collective-permute-start(bf16[896,512]{1,0:T(8,128)(2,1)S(1)} %collective-permute-done.11), channel_id=1, source_target_pairs={{0,224},{32,0},{64,32},{96,64},{128,96},{160,128},{192,160},{224,1... | collective-permute-start | bytes 2752520 | tf_op jit(solution)/shard_map/ppermute | solution.py:58
  173.1 2.3 copy-start.9
  176.4 2.3 copy-start.11
  179.7 2.3 copy-start.7
Sparse Core Ops, SparseCore 0:
  9.9 66.8 all-gather.5

commit v12 on v7

--- a/solution.py
+++ b/solution.py
@@ -51,12 +51,15 @@
             ).astype(jnp.bfloat16)
             left, right, features = lax.optimization_barrier((left, right, features))
             features = features.reshape(tok_rows, 2, n_row, shard_rows).transpose(2, 0, 1, 3)
-        if step == 7:
+        if step >= n_row - 2:
+            newest = pending[-1]
+            pending = pending[:-1]
             logits_left, logits_right = add_pending(logits_left, logits_right)
-            pending = []
+            pending = [newest]
             left, right, logits_left, logits_right = lax.optimization_barrier(
                 (left, right, logits_left, logits_right)
             )
+        left, right = lax.optimization_barrier((left, right))
         left = lax.ppermute(left, "row", forward)
         right = lax.ppermute(right, "row", backward)
         pending.append((left, right, (row_index - step) % n_row, (row_index + step) % n_row))

time: 244 us -> 237 us (0.971)
  waiting for transfers between devices: 91.1 us -> 82.3 us
    ppermute x7, waiting for transfers between devices: 19.5 us -> 12.7 us  [per_device(): right = lax.ppermute(right, 'row', backward)]
    ppermute x7, starting transfers between devices: 24 us -> 17.3 us  [per_device(): right = lax.ppermute(right, 'row', backward)]
    ppermute x7, starting transfers between devices: 2.26 us -> 8.05 us  [per_device(): left = lax.ppermute(left, 'row', forward)]
  transfers between devices with their start and end apart: 15 -> 15, of which waited for: 7 -> 9; matrix products, arithmetic and copies ran while one was open for 13% -> 16% of each run, Pallas kernels for 0% -> 0%
where the time goes in v12:
time: 237 us; the launch traced here: 236 us
  waiting for transfers between devices  82.3 us (35%)
  blocking collectives  71.1 us (30%)
  matrix products  28.4 us (12%)
  starting transfers between devices  25.4 us (11%)
  between operations  13.7 us (6%)
  other arithmetic  12.4 us (5%)
  local copies, waits for them, and re-layouts  3.16 us (1%)
    ppermute x7, waiting for transfers between devices, per_device(): left = lax.ppermute(left, 'row', forward)  68.9 us
    dot_general x16, matrix products, block_logits(): jnp.einsum('tmd,dv->tmv', features[shard], block, preferred_element_type=...  28.4 us
    all_gather x1, blocking collectives, per_device(): full_gain = lax.all_gather(final_gain, 'col', axis=1, tiled=True)  24.7 us
    all_gather x1, blocking collectives, per_device(): parts = lax.all_gather(jnp.stack([row_max, exp_total, picked]), 'col')  23.3 us
    all_gather x1, blocking collectives, per_device(): stats = lax.all_gather(jnp.stack([ratio_sums, squares, ratio_max]), 'row')  23.1 us
    ppermute x7, starting transfers between devices, per_device(): right = lax.ppermute(right, 'row', backward)  17.3 us
    ppermute x7, waiting for transfers between devices, per_device(): right = lax.ppermute(right, 'row', backward)  12.7 us
    ppermute x7, starting transfers between devices, per_device(): left = lax.ppermute(left, 'row', forward)  8.05 us
  transfers between devices with their start and end apart: 15, of which 9 were waited for; matrix products, arithmetic and copies ran while one was open for 16% of the time, Pallas kernels for 0%

profile of v12, /device:TPU:2, one launch (start us, length us, event | category | flops | bytes accessed | tf_op | source)
XLA Modules:
  0.0 236.4 jit_solution(3512175715394060085)
XLA Ops:
  6.5 0.7 all-gather.6.cloned.1.call-update
  7.3 1.6 fusion.97
  8.8 2.0 collective-permute-start
  10.8 4.0 %collective-permute-start.1 = (bf16[896,512]{1,0:T(8,128)(2,1)S(1)}, bf16[896,512]{1,0:T(8,128)(2,1)S(1)}, u32[]{:S(2)}, u32[]{:S(2)}) collective-permute-start(bf16[896,512]{1,0:T(8,128)(2,1)S(1)} %get-tuple-element.34), channel_id=1, source_target_pairs={{0,224},{32,0},{64,32},{96,64},{128,96},{160,128},{192,160},{224,1... | collective-permute-start | bytes 2752520 | tf_op jit(solution)/shard_map/ppermute | solution.py:64
  14.9 20.3 %collective-permute-done = bf16[896,512]{1,0:T(8,128)(2,1)S(1)} collective-permute-done((bf16[896,512]{1,0:T(8,128)(2,1)S(1)}, bf16[896,512]{1,0:T(8,128)(2,1)S(1)}, u32[]{:S(2)}, u32[]{:S(2)}) %collective-permute-start) | collective-permute-done | bytes 917536 | tf_op jit(solution)/shard_map/ppermute | solution.py:63
  35.1 3.2 %collective-permute-start.3 = (bf16[896,512]{1,0:T(8,128)(2,1)S(1)}, bf16[896,512]{1,0:T(8,128)(2,1)}, u32[]{:S(2)}, u32[]{:S(2)}) collective-permute-start(bf16[896,512]{1,0:T(8,128)(2,1)S(1)} %collective-permute-done.1), channel_id=1, source_target_pairs={{0,224},{32,0},{64,32},{96,64},{128,96},{160,128},{192,160},{224,1... | collective-permute-start | bytes 2752520 | tf_op jit(solution)/shard_map/ppermute | solution.py:64
  38.4 24.7 %all-gather.2 = f32[32,224,2]{1,2,0:T(2,128)S(1)} all-gather(f32[1,224,2]{1,2,0:T(2,128)S(1)} %bitcast.188), channel_id=1, replica_groups=mesh['row'=8,'col'=32] {'col'}, dimensions={0}, use_global_device_ids=true | all-gather | bytes 59136 | tf_op jit(solution)/shard_map/all_gather | solution.py:20
  63.4 3.2 %collective-permute-start.5 = (bf16[896,512]{1,0:T(8,128)(2,1)}, bf16[896,512]{1,0:T(8,128)(2,1)}, u32[]{:S(2)}, u32[]{:S(2)}) collective-permute-start(bf16[896,512]{1,0:T(8,128)(2,1)} %collective-permute-done.3), channel_id=1, source_target_pairs={{0,224},{32,0},{64,32},{96,64},{128,96},{160,128},{192,160},{224,1... | collective-permute-start | bytes 2752520 | tf_op jit(solution)/shard_map/ppermute | solution.py:64
  66.6 20.7 %collective-permute-done.4 = bf16[896,512]{1,0:T(8,128)(2,1)} collective-permute-done((bf16[896,512]{1,0:T(8,128)(2,1)S(1)}, bf16[896,512]{1,0:T(8,128)(2,1)}, u32[]{:S(2)}, u32[]{:S(2)}) %collective-permute-start.4) | collective-permute-done | bytes 917536 | tf_op jit(solution)/shard_map/ppermute | solution.py:63
  87.3 1.5 collective-permute-start.6
  88.7 1.8 collective-permute-start.7
  90.5 6.5 %fusion = f32[384,2]{0,1:T(2,128)S(1)} fusion(bf16[384,2,7168]{0,2,1:T(8,128)(2,1)} %all-gather.6.cloned.1.call-done), kind=kLoop, calls=%fused_computation.2 | loop fusion | flops 16514304 | bytes 11013120 | tf_op jit(solution)/shard_map/reduce_sum | solution.py:48
  97.0 0.8 copy-done
  97.8 3.1 %fusion.2 = bf16[384,2,7168]{0,2,1:T(8,128)(2,1)S(1)} fusion(bf16[384,2,7168]{0,2,1:T(8,128)(2,1)S(1)} %copy-done, f32[2,7168]{1,0:T(2,128)S(1)} %bitcast.181, f32[384,2]{0,1:T(2,128)S(1)} %add_rsqrt_fusion), kind=kLoop, calls=%fused_computation.4 | loop fusion | flops 22020096 | bytes 22080512 | tf_op jit(solution)/shard_map/convert_element_type | solution.py:51
  100.9 9.7 %collective-permute-done.6 = bf16[896,512]{1,0:T(8,128)(2,1)} collective-permute-done((bf16[896,512]{1,0:T(8,128)(2,1)}, bf16[896,512]{1,0:T(8,128)(2,1)}, u32[]{:S(2)}, u32[]{:S(2)}) %collective-permute-start.6) | collective-permute-done | bytes 917536 | tf_op jit(solution)/shard_map/ppermute | solution.py:63
  110.6 1.0 fusion.35
  111.6 1.0 fusion.37
  112.6 2.6 %collective-permute-start.8 = (bf16[896,512]{1,0:T(8,128)(2,1)}, bf16[896,512]{1,0:T(8,128)(2,1)}, u32[]{:S(2)}, u32[]{:S(2)}) collective-permute-start(bf16[896,512]{1,0:T(8,128)(2,1)} %collective-permute-done.6), channel_id=1, source_target_pairs={{0,32},{32,64},{64,96},{96,128},{128,160},{160,192},{192,224},{224... | collective-permute-start | bytes 2752520 | tf_op jit(solution)/shard_map/ppermute | solution.py:63
  115.2 0.8 collective-permute-start.9
  116.1 2.2 fusion.21
  118.3 2.2 fusion.23
  120.5 1.0 fusion.25
  121.5 2.3 fusion.29
  123.8 1.0 fusion.31
  124.8 1.0 fusion.33
  125.8 2.3 add_add_fusion.2
  128.2 2.3 add_add_fusion.3
  130.6 4.7 %collective-permute-done.8 = bf16[896,512]{1,0:T(8,128)(2,1)} collective-permute-done((bf16[896,512]{1,0:T(8,128)(2,1)}, bf16[896,512]{1,0:T(8,128)(2,1)}, u32[]{:S(2)}, u32[]{:S(2)}) %collective-permute-start.8) | collective-permute-done | bytes 917536 | tf_op jit(solution)/shard_map/ppermute | solution.py:63
  135.3 0.6 collective-permute-done.9
  135.9 1.6 collective-permute-start.10
  137.4 1.7 collective-permute-start.11
  139.5 2.6 %fusion.15 = f32[384,2,512]{2,0,1:T(8,128)S(1)} fusion(bf16[384,2,8,896]{0,3,2,1:T(8,128)(2,1)} %bitcast.172, s32[]{:T(128)S(6)} %select_n.150, bf16[896,512]{1,0:T(8,128)(2,1)} %collective-permute-done.9), kind=kOutput, calls=%fused_computation.20 | convolution fusion | flops 704643072 | bytes 3866628 | tf_op jit(solution)/shard_map/tmd,dv->tmv/dot_general | solution.py:30
  142.1 0.3 add.232
  142.5 2.8 %fusion.17 = f32[384,2,512]{2,0,1:T(8,128)S(1)} fusion(bf16[384,2,8,896]{0,3,2,1:T(8,128)(2,1)} %bitcast.173, s32[]{:T(128)S(6)} %select_n.148, bf16[896,512]{1,0:T(8,128)(2,1)} %collective-permute-done.8), kind=kOutput, calls=%fused_computation.22 | convolution fusion | flops 704643072 | bytes 3866628 | tf_op jit(solution)/shard_map/tmd,dv->tmv/dot_general | solution.py:30
  145.2 0.3 add.228
  145.6 11.3 %collective-permute-done.10 = bf16[896,512]{1,0:T(8,128)(2,1)} collective-permute-done((bf16[896,512]{1,0:T(8,128)(2,1)}, bf16[896,512]{1,0:T(8,128)(2,1)}, u32[]{:S(2)}, u32[]{:S(2)}) %collective-permute-start.10) | collective-permute-done | bytes 917536 | tf_op jit(solution)/shard_map/ppermute | solution.py:63
  156.9 0.4 collective-permute-done.11
  157.3 2.5 %collective-permute-start.13 = (bf16[896,512]{1,0:T(8,128)(2,1)}, bf16[896,512]{1,0:T(8,128)(2,1)S(1)}, u32[]{:S(2)}, u32[]{:S(2)}) collective-permute-start(bf16[896,512]{1,0:T(8,128)(2,1)} %collective-permute-done.11), channel_id=1, source_target_pairs={{0,224},{32,0},{64,32},{96,64},{128,96},{160,128},{192,160},{224,1... | collective-permute-start | bytes 2752520 | tf_op jit(solution)/shard_map/ppermute | solution.py:64
  160.5 2.2 fusion.7
  162.6 2.2 fusion.13
  164.8 11.7 %collective-permute-done.13 = bf16[896,512]{1,0:T(8,128)(2,1)S(1)} collective-permute-done((bf16[896,512]{1,0:T(8,128)(2,1)}, bf16[896,512]{1,0:T(8,128)(2,1)S(1)}, u32[]{:S(2)}, u32[]{:S(2)}) %collective-permute-start.13) | collective-permute-done | bytes 917536 | tf_op jit(solution)/shard_map/ppermute | solution.py:64
  176.5 1.1 fusion.99
  177.6 2.3 collective-permute-done.12
  179.9 1.1 fusion.98
  181.0 1.1 exponential_reduce_fusion
  182.1 23.3 %all-gather = f32[96,384,2]{1,2,0:T(2,128)S(1)} all-gather(f32[3,384,2]{1,2,0:T(2,128)S(1)} %pad_maximum_fusion.1), channel_id=2, replica_groups=mesh['row'=8,'col'=32] {'col'}, dimensions={0}, use_global_device_ids=true | all-gather | bytes 304128 | tf_op jit(solution)/shard_map/all_gather | solution.py:74
  205.8 23.1 %all-gather.3 = f32[8,3,16]{2,1,0:T(4,128)S(1)} all-gather(f32[1,3,16]{2,1,0:T(4,128)S(1)} %maximum_bitcast_fusion), channel_id=3, replica_groups=mesh['row'=8,'col'=32] {'row'}, dimensions={0}, use_global_device_ids=true | all-gather | bytes 1728 | tf_op jit(solution)/shard_map/all_gather | solution.py:87
  229.0 0.6 copy.81
  (51 shorter events, 1.7 us)
Async XLA Ops:
  6.5 84.0 %all-gather.6.cloned.1.call-start = ((), (), s32[]{:S(2)}) async-start(), calls=%async_computation | async-start | bytes 11354112 | tf_op jit(solution)/shard_map/all_gather | solution.py:19
  7.3 31.1 %copy-start.5 = (f32[2,224]{1,0:T(2,128)S(1)}, f32[2,224]{1,0:T(2,128)}, u32[]{:S(2)}) copy-start(f32[2,224]{1,0:T(2,128)} %param.7) | copy-start | bytes 5380
  8.8 26.3 %collective-permute-start = (bf16[896,512]{1,0:T(8,128)(2,1)S(1)}, bf16[896,512]{1,0:T(8,128)(2,1)S(1)}, u32[]{:S(2)}, u32[]{:S(2)}) collective-permute-start(bf16[896,512]{1,0:T(8,128)(2,1)S(1)} %get-tuple-element.33), channel_id=1, source_target_pairs={{0,32},{32,64},{64,96},{96,128},{128,160},{160,192},{192,224},{224... | collective-permute-start | bytes 2752520 | tf_op jit(solution)/shard_map/ppermute | solution.py:63
  10.8 24.3 %collective-permute-start.1 = (bf16[896,512]{1,0:T(8,128)(2,1)S(1)}, bf16[896,512]{1,0:T(8,128)(2,1)S(1)}, u32[]{:S(2)}, u32[]{:S(2)}) collective-permute-start(bf16[896,512]{1,0:T(8,128)(2,1)S(1)} %get-tuple-element.34), channel_id=1, source_target_pairs={{0,224},{32,0},{64,32},{96,64},{128,96},{160,128},{192,160},{224,1... | collective-permute-start | bytes 2752520 | tf_op jit(solution)/shard_map/ppermute | solution.py:64
  35.1 28.1 %collective-permute-start.2 = (bf16[896,512]{1,0:T(8,128)(2,1)S(1)}, bf16[896,512]{1,0:T(8,128)(2,1)S(1)}, u32[]{:S(2)}, u32[]{:S(2)}) collective-permute-start(bf16[896,512]{1,0:T(8,128)(2,1)S(1)} %collective-permute-done), channel_id=1, source_target_pairs={{0,32},{32,64},{64,96},{96,128},{128,160},{160,192},{192,224},{224... | collective-permute-start | bytes 2752520 | tf_op jit(solution)/shard_map/ppermute | solution.py:63
  35.1 28.1 %collective-permute-start.3 = (bf16[896,512]{1,0:T(8,128)(2,1)S(1)}, bf16[896,512]{1,0:T(8,128)(2,1)}, u32[]{:S(2)}, u32[]{:S(2)}) collective-permute-start(bf16[896,512]{1,0:T(8,128)(2,1)S(1)} %collective-permute-done.1), channel_id=1, source_target_pairs={{0,224},{32,0},{64,32},{96,64},{128,96},{160,128},{192,160},{224,1... | collective-permute-start | bytes 2752520 | tf_op jit(solution)/shard_map/ppermute | solution.py:64
  63.2 27.3 %copy-start.7 = (bf16[896,512]{1,0:T(8,128)(2,1)}, bf16[896,512]{1,0:T(8,128)(2,1)S(1)}, u32[]{:S(2)}) copy-start(bf16[896,512]{1,0:T(8,128)(2,1)S(1)} %collective-permute-done.2) | copy-start | bytes 2752516
  63.3 24.0 %collective-permute-start.4 = (bf16[896,512]{1,0:T(8,128)(2,1)S(1)}, bf16[896,512]{1,0:T(8,128)(2,1)}, u32[]{:S(2)}, u32[]{:S(2)}) collective-permute-start(bf16[896,512]{1,0:T(8,128)(2,1)S(1)} %collective-permute-done.2), channel_id=1, source_target_pairs={{0,32},{32,64},{64,96},{96,128},{128,160},{160,192},{192,224},{224... | collective-permute-start | bytes 2752520 | tf_op jit(solution)/shard_map/ppermute | solution.py:63
  63.4 23.9 %collective-permute-start.5 = (bf16[896,512]{1,0:T(8,128)(2,1)}, bf16[896,512]{1,0:T(8,128)(2,1)}, u32[]{:S(2)}, u32[]{:S(2)}) collective-permute-start(bf16[896,512]{1,0:T(8,128)(2,1)} %collective-permute-done.3), channel_id=1, source_target_pairs={{0,224},{32,0},{64,32},{96,64},{128,96},{160,128},{192,160},{224,1... | collective-permute-start | bytes 2752520 | tf_op jit(solution)/shard_map/ppermute | solution.py:64
  87.3 23.3 %collective-permute-start.6 = (bf16[896,512]{1,0:T(8,128)(2,1)}, bf16[896,512]{1,0:T(8,128)(2,1)}, u32[]{:S(2)}, u32[]{:S(2)}) collective-permute-start(bf16[896,512]{1,0:T(8,128)(2,1)} %collective-permute-done.4), channel_id=1, source_target_pairs={{0,32},{32,64},{64,96},{96,128},{128,160},{160,192},{192,224},{224... | collective-permute-start | bytes 2752520 | tf_op jit(solution)/shard_map/ppermute | solution.py:63
  88.7 21.8 %collective-permute-start.7 = (bf16[896,512]{1,0:T(8,128)(2,1)}, bf16[896,512]{1,0:T(8,128)(2,1)}, u32[]{:S(2)}, u32[]{:S(2)}) collective-permute-start(bf16[896,512]{1,0:T(8,128)(2,1)} %collective-permute-done.5), channel_id=1, source_target_pairs={{0,224},{32,0},{64,32},{96,64},{128,96},{160,128},{192,160},{224,1... | collective-permute-start | bytes 2752520 | tf_op jit(solution)/shard_map/ppermute | solution.py:64
  90.5 7.3 %copy-start = (bf16[384,2,7168]{0,2,1:T(8,128)(2,1)S(1)}, bf16[384,2,7168]{0,2,1:T(8,128)(2,1)}, u32[]{:S(2)}) copy-start(bf16[384,2,7168]{0,2,1:T(8,128)(2,1)} %all-gather.6.cloned.1.call-done) | copy-start | bytes 33030148
  97.8 12.8 %copy-start.3 = (bf16[896,1024]{1,0:T(8,128)(2,1)S(1)}, bf16[896,1024]{1,0:T(8,128)(2,1)}, u32[]{:S(2)}) copy-start(bf16[896,1024]{1,0:T(8,128)(2,1)} %param.8) | copy-start | bytes 5505028
  100.9 27.3 %copy-start.1 = (bf16[384,2,7168]{0,2,1:T(8,128)(2,1)}, bf16[384,2,7168]{0,2,1:T(8,128)(2,1)S(1)}, u32[]{:S(2)}) copy-start(bf16[384,2,7168]{0,2,1:T(8,128)(2,1)S(1)} %fusion.2) | copy-start | bytes 33030148
  112.6 22.7 %collective-permute-start.8 = (bf16[896,512]{1,0:T(8,128)(2,1)}, bf16[896,512]{1,0:T(8,128)(2,1)}, u32[]{:S(2)}, u32[]{:S(2)}) collective-permute-start(bf16[896,512]{1,0:T(8,128)(2,1)} %collective-permute-done.6), channel_id=1, source_target_pairs={{0,32},{32,64},{64,96},{96,128},{128,160},{160,192},{192,224},{224... | collective-permute-start | bytes 2752520 | tf_op jit(solution)/shard_map/ppermute | solution.py:63
  115.2 20.6 %collective-permute-start.9 = (bf16[896,512]{1,0:T(8,128)(2,1)}, bf16[896,512]{1,0:T(8,128)(2,1)}, u32[]{:S(2)}, u32[]{:S(2)}) collective-permute-start(bf16[896,512]{1,0:T(8,128)(2,1)} %collective-permute-done.7), channel_id=1, source_target_pairs={{0,224},{32,0},{64,32},{96,64},{128,96},{160,128},{192,160},{224,1... | collective-permute-start | bytes 2752520 | tf_op jit(solution)/shard_map/ppermute | solution.py:64
  121.5 2.3 copy-start.8
  128.2 10.9 %copy-start.6 = (s32[16]{0:T(128)S(1)}, s32[16]{0:T(128)}, u32[]{:S(2)}) copy-start(s32[16]{0:T(128)} %param.9) | copy-start | bytes 196
  128.2 11.3 %copy-start.9 = (s32[16]{0:T(128)S(1)}, s32[16]{0:T(128)}, u32[]{:S(2)}) copy-start(s32[16]{0:T(128)} %param.11) | copy-start | bytes 196
  135.9 21.0 %collective-permute-start.10 = (bf16[896,512]{1,0:T(8,128)(2,1)}, bf16[896,512]{1,0:T(8,128)(2,1)}, u32[]{:S(2)}, u32[]{:S(2)}) collective-permute-start(bf16[896,512]{1,0:T(8,128)(2,1)} %collective-permute-done.8), channel_id=1, source_target_pairs={{0,32},{32,64},{64,96},{96,128},{128,160},{160,192},{192,224},{224... | collective-permute-start | bytes 2752520 | tf_op jit(solution)/shard_map/ppermute | solution.py:63
  137.4 19.9 %collective-permute-start.11 = (bf16[896,512]{1,0:T(8,128)(2,1)}, bf16[896,512]{1,0:T(8,128)(2,1)}, u32[]{:S(2)}, u32[]{:S(2)}) collective-permute-start(bf16[896,512]{1,0:T(8,128)(2,1)} %collective-permute-done.9), channel_id=1, source_target_pairs={{0,224},{32,0},{64,32},{96,64},{128,96},{160,128},{192,160},{224,1... | collective-permute-start | bytes 2752520 | tf_op jit(solution)/shard_map/ppermute | solution.py:64
  142.1 18.3 %copy-start.2 = (bf16[384,2,7168]{0,2,1:T(8,128)(2,1)S(1)}, bf16[384,2,7168]{0,2,1:T(8,128)(2,1)}, u32[]{:S(2)}) copy-start(bf16[384,2,7168]{0,2,1:T(8,128)(2,1)} %copy-done.1) | copy-start | bytes 33030148
  145.2 14.6 %copy-start.4 = (s32[384]{0:T(512)S(1)}, s32[384]{0:T(512)}, u32[]{:S(2)}) copy-start(s32[384]{0:T(512)} %param.10) | copy-start | bytes 4612
  157.3 19.2 %collective-permute-start.13 = (bf16[896,512]{1,0:T(8,128)(2,1)}, bf16[896,512]{1,0:T(8,128)(2,1)S(1)}, u32[]{:S(2)}, u32[]{:S(2)}) collective-permute-start(bf16[896,512]{1,0:T(8,128)(2,1)} %collective-permute-done.11), channel_id=1, source_target_pairs={{0,224},{32,0},{64,32},{96,64},{128,96},{160,128},{192,160},{224,1... | collective-permute-start | bytes 2752520 | tf_op jit(solution)/shard_map/ppermute | solution.py:64
  160.1 19.8 %collective-permute-start.12 = (bf16[896,512]{1,0:T(8,128)(2,1)}, bf16[896,512]{1,0:T(8,128)(2,1)S(1)}, u32[]{:S(2)}, u32[]{:S(2)}) collective-permute-start(bf16[896,512]{1,0:T(8,128)(2,1)} %collective-permute-done.10), channel_id=1, source_target_pairs={{0,32},{32,64},{64,96},{96,128},{128,160},{160,192},{192,224},{224... | collective-permute-start | bytes 2752520 | tf_op jit(solution)/shard_map/ppermute | solution.py:63
Sparse Core Ops, SparseCore 0:
  9.9 66.8 all-gather.5

commit v13 on v12

--- a/solution.py
+++ b/solution.py
@@ -84,10 +84,19 @@
     ratio_sums = jnp.sum(jnp.where(member, log_ratio[:, None], 0.0), axis=0)
     squares = jnp.sum(jnp.where(member, (log_ratio * log_ratio)[:, None], 0.0), axis=0)
     ratio_max = jnp.max(jnp.where(member, log_ratio[:, None], -1e30), axis=0)
-    stats = lax.all_gather(jnp.stack([ratio_sums, squares, ratio_max]), "row")
-    seq_stats = jnp.stack(
-        [jnp.sum(stats[:, 0], axis=0), jnp.sum(stats[:, 1], axis=0), jnp.max(stats[:, 2], axis=0)]
-    )
+    seq_stats = jnp.stack([ratio_sums, squares, ratio_max])
+    distance = 1
+    while distance < n_row:
+        partner = [(i, i ^ distance) for i in range(n_row)]
+        other = lax.ppermute(seq_stats, "row", partner)
+        seq_stats = jnp.stack(
+            [
+                seq_stats[0] + other[0],
+                seq_stats[1] + other[1],
+                jnp.maximum(seq_stats[2], other[2]),
+            ]
+        )
+        distance *= 2
     owned = owner == col_index
     return jnp.where(owned[None, :], seq_stats, 0.0)[None]
 

time: 237 us -> 230 us (0.970)
  blocking collectives: 71.1 us -> 48 us
  waiting for transfers between devices: 82.3 us -> 91.8 us
  starting transfers between devices: 25.4 us -> 31.7 us
    all_gather x1 -> x0, blocking collectives: 23.1 us -> none  [per_device(): stats = lax.all_gather(jnp.stack([ratio_sums, squares, ratio_max]), 'row')]
    ppermute x0 -> x3, waiting for transfers between devices: none -> 9.45 us  [per_device(): other = lax.ppermute(seq_stats, 'row', partner)]
    ppermute x0 -> x3, starting transfers between devices: none -> 6.35 us  [per_device(): other = lax.ppermute(seq_stats, 'row', partner)]
  transfers between devices with their start and end apart: 15 -> 18, of which waited for: 9 -> 12; matrix products, arithmetic and copies ran while one was open for 16% -> 17% of each run, Pallas kernels for 0% -> 0%
where the time goes in v13:
time: 230 us; the launch traced here: 229 us
  waiting for transfers between devices  91.8 us (40%)
  blocking collectives  48 us (21%)
  starting transfers between devices  31.7 us (14%)
  matrix products  28.4 us (12%)
  between operations  13.7 us (6%)
  other arithmetic  12.4 us (5%)
  local copies, waits for them, and re-layouts  3.17 us (1%)
    ppermute x7, waiting for transfers between devices, per_device(): left = lax.ppermute(left, 'row', forward)  68.9 us
    dot_general x16, matrix products, block_logits(): jnp.einsum('tmd,dv->tmv', features[shard], block, preferred_element_type=...  28.4 us
    all_gather x1, blocking collectives, per_device(): full_gain = lax.all_gather(final_gain, 'col', axis=1, tiled=True)  24.7 us
    all_gather x1, blocking collectives, per_device(): parts = lax.all_gather(jnp.stack([row_max, exp_total, picked]), 'col')  23.3 us
    ppermute x7, starting transfers between devices, per_device(): right = lax.ppermute(right, 'row', backward)  17.3 us
    ppermute x7, waiting for transfers between devices, per_device(): right = lax.ppermute(right, 'row', backward)  12.7 us
    ppermute x3, waiting for transfers between devices, per_device(): other = lax.ppermute(seq_stats, 'row', partner)  9.45 us
    ppermute x7, starting transfers between devices, per_device(): left = lax.ppermute(left, 'row', forward)  8.05 us
  transfers between devices with their start and end apart: 18, of which 12 were waited for; matrix products, arithmetic and copies ran while one was open for 17% of the time, Pallas kernels for 0%

profile of v13, /device:TPU:2, one launch (start us, length us, event | category | flops | bytes accessed | tf_op | source)
XLA Modules:
  0.0 229.1 jit_solution(14896100380976341794)
XLA Ops:
  6.5 0.7 all-gather.4.cloned.1.call-update
  7.3 1.6 fusion.97
  8.8 2.0 collective-permute-start
  10.8 4.0 %collective-permute-start.1 = (bf16[896,512]{1,0:T(8,128)(2,1)S(1)}, bf16[896,512]{1,0:T(8,128)(2,1)S(1)}, u32[]{:S(2)}, u32[]{:S(2)}) collective-permute-start(bf16[896,512]{1,0:T(8,128)(2,1)S(1)} %get-tuple-element.34), channel_id=1, source_target_pairs={{0,224},{32,0},{64,32},{96,64},{128,96},{160,128},{192,160},{224,1... | collective-permute-start | bytes 2752520 | tf_op jit(solution)/shard_map/ppermute | solution.py:64
  14.9 20.3 %collective-permute-done = bf16[896,512]{1,0:T(8,128)(2,1)S(1)} collective-permute-done((bf16[896,512]{1,0:T(8,128)(2,1)S(1)}, bf16[896,512]{1,0:T(8,128)(2,1)S(1)}, u32[]{:S(2)}, u32[]{:S(2)}) %collective-permute-start) | collective-permute-done | bytes 917536 | tf_op jit(solution)/shard_map/ppermute | solution.py:63
  35.1 3.2 %collective-permute-start.3 = (bf16[896,512]{1,0:T(8,128)(2,1)S(1)}, bf16[896,512]{1,0:T(8,128)(2,1)}, u32[]{:S(2)}, u32[]{:S(2)}) collective-permute-start(bf16[896,512]{1,0:T(8,128)(2,1)S(1)} %collective-permute-done.1), channel_id=1, source_target_pairs={{0,224},{32,0},{64,32},{96,64},{128,96},{160,128},{192,160},{224,1... | collective-permute-start | bytes 2752520 | tf_op jit(solution)/shard_map/ppermute | solution.py:64
  38.4 24.7 %all-gather.1 = f32[32,224,2]{1,2,0:T(2,128)S(1)} all-gather(f32[1,224,2]{1,2,0:T(2,128)S(1)} %bitcast.192), channel_id=1, replica_groups=mesh['row'=8,'col'=32] {'col'}, dimensions={0}, use_global_device_ids=true | all-gather | bytes 59136 | tf_op jit(solution)/shard_map/all_gather | solution.py:20
  63.4 3.2 %collective-permute-start.5 = (bf16[896,512]{1,0:T(8,128)(2,1)}, bf16[896,512]{1,0:T(8,128)(2,1)}, u32[]{:S(2)}, u32[]{:S(2)}) collective-permute-start(bf16[896,512]{1,0:T(8,128)(2,1)} %collective-permute-done.3), channel_id=1, source_target_pairs={{0,224},{32,0},{64,32},{96,64},{128,96},{160,128},{192,160},{224,1... | collective-permute-start | bytes 2752520 | tf_op jit(solution)/shard_map/ppermute | solution.py:64
  66.6 20.7 %collective-permute-done.4 = bf16[896,512]{1,0:T(8,128)(2,1)} collective-permute-done((bf16[896,512]{1,0:T(8,128)(2,1)S(1)}, bf16[896,512]{1,0:T(8,128)(2,1)}, u32[]{:S(2)}, u32[]{:S(2)}) %collective-permute-start.4) | collective-permute-done | bytes 917536 | tf_op jit(solution)/shard_map/ppermute | solution.py:63
  87.3 1.5 collective-permute-start.6
  88.7 1.8 collective-permute-start.7
  90.5 6.5 %fusion = f32[384,2]{0,1:T(2,128)S(1)} fusion(bf16[384,2,7168]{0,2,1:T(8,128)(2,1)} %all-gather.4.cloned.1.call-done), kind=kLoop, calls=%fused_computation.2 | loop fusion | flops 16514304 | bytes 11013120 | tf_op jit(solution)/shard_map/reduce_sum | solution.py:48
  97.0 0.8 copy-done
  97.8 3.1 %fusion.2 = bf16[384,2,7168]{0,2,1:T(8,128)(2,1)S(1)} fusion(bf16[384,2,7168]{0,2,1:T(8,128)(2,1)S(1)} %copy-done, f32[2,7168]{1,0:T(2,128)S(1)} %bitcast.185, f32[384,2]{0,1:T(2,128)S(1)} %add_rsqrt_fusion), kind=kLoop, calls=%fused_computation.4 | loop fusion | flops 22020096 | bytes 22080512 | tf_op jit(solution)/shard_map/convert_element_type | solution.py:51
  100.9 9.7 %collective-permute-done.6 = bf16[896,512]{1,0:T(8,128)(2,1)} collective-permute-done((bf16[896,512]{1,0:T(8,128)(2,1)}, bf16[896,512]{1,0:T(8,128)(2,1)}, u32[]{:S(2)}, u32[]{:S(2)}) %collective-permute-start.6) | collective-permute-done | bytes 917536 | tf_op jit(solution)/shard_map/ppermute | solution.py:63
  110.6 1.0 fusion.35
  111.6 1.0 fusion.37
  112.6 2.6 %collective-permute-start.8 = (bf16[896,512]{1,0:T(8,128)(2,1)}, bf16[896,512]{1,0:T(8,128)(2,1)}, u32[]{:S(2)}, u32[]{:S(2)}) collective-permute-start(bf16[896,512]{1,0:T(8,128)(2,1)} %collective-permute-done.6), channel_id=1, source_target_pairs={{0,32},{32,64},{64,96},{96,128},{128,160},{160,192},{192,224},{224... | collective-permute-start | bytes 2752520 | tf_op jit(solution)/shard_map/ppermute | solution.py:63
  115.2 0.8 collective-permute-start.9
  116.1 2.2 fusion.21
  118.3 2.2 fusion.23
  120.5 1.0 fusion.25
  121.5 2.3 fusion.29
  123.8 1.0 fusion.31
  124.8 1.0 fusion.33
  125.8 2.3 %add_add_fusion.2 = f32[384,2,512]{2,0,1:T(8,128)S(1)} fusion(f32[384,2,512]{2,0,1:T(8,128)S(1)} %fusion.21, f32[384,2,512]{2,0,1:T(8,128)S(1)} %fusion.23, f32[384,2,512]{2,0,1:T(8,128)S(1)} %fusion.35, f32[384,2,512]{2,0,1:T(8,128)S(1)} %fusion.25, bf16[384,2,8,896]{0,3,2,1:T(8,128)(2,1)S(1)} %bitcast.174, s32[]{:T(128)S(6)} %select_n.146, ...), kind=kOutput, calls=%fused_computation.10 | convolution fusion | flops 706215936 | bytes 10158084 | tf_op jit(solution)/shard_map/tmd,dv->tmv/dot_general | solution.py:30
  128.2 2.3 %add_add_fusion.3 = f32[384,2,512]{2,0,1:T(8,128)S(1)} fusion(f32[384,2,512]{2,0,1:T(8,128)S(1)} %fusion.29, f32[384,2,512]{2,0,1:T(8,128)S(1)} %fusion.31, f32[384,2,512]{2,0,1:T(8,128)S(1)} %fusion.37, f32[384,2,512]{2,0,1:T(8,128)S(1)} %fusion.33, bf16[384,2,8,896]{0,3,2,1:T(8,128)(2,1)S(1)} %bitcast.175, s32[]{:T(128)S(6)} %select_n.138, ...), kind=kOutput, calls=%fused_computation.11 | convolution fusion | flops 706215936 | bytes 10158084 | tf_op jit(solution)/shard_map/tmd,dv->tmv/dot_general | solution.py:30
  130.5 4.7 %collective-permute-done.8 = bf16[896,512]{1,0:T(8,128)(2,1)} collective-permute-done((bf16[896,512]{1,0:T(8,128)(2,1)}, bf16[896,512]{1,0:T(8,128)(2,1)}, u32[]{:S(2)}, u32[]{:S(2)}) %collective-permute-start.8) | collective-permute-done | bytes 917536 | tf_op jit(solution)/shard_map/ppermute | solution.py:63
  135.3 0.6 collective-permute-done.9
  135.9 1.6 collective-permute-start.10
  137.4 1.7 collective-permute-start.11
  139.5 2.6 %fusion.15 = f32[384,2,512]{2,0,1:T(8,128)S(1)} fusion(bf16[384,2,8,896]{0,3,2,1:T(8,128)(2,1)} %bitcast.176, s32[]{:T(128)S(6)} %select_n.150, bf16[896,512]{1,0:T(8,128)(2,1)} %collective-permute-done.9), kind=kOutput, calls=%fused_computation.20 | convolution fusion | flops 704643072 | bytes 3866628 | tf_op jit(solution)/shard_map/tmd,dv->tmv/dot_general | solution.py:30
  142.5 2.8 %fusion.17 = f32[384,2,512]{2,0,1:T(8,128)S(1)} fusion(bf16[384,2,8,896]{0,3,2,1:T(8,128)(2,1)} %bitcast.177, s32[]{:T(128)S(6)} %select_n.148, bf16[896,512]{1,0:T(8,128)(2,1)} %collective-permute-done.8), kind=kOutput, calls=%fused_computation.22 | convolution fusion | flops 704643072 | bytes 3866628 | tf_op jit(solution)/shard_map/tmd,dv->tmv/dot_general | solution.py:30
  145.6 11.3 %collective-permute-done.10 = bf16[896,512]{1,0:T(8,128)(2,1)} collective-permute-done((bf16[896,512]{1,0:T(8,128)(2,1)}, bf16[896,512]{1,0:T(8,128)(2,1)}, u32[]{:S(2)}, u32[]{:S(2)}) %collective-permute-start.10) | collective-permute-done | bytes 917536 | tf_op jit(solution)/shard_map/ppermute | solution.py:63
  157.3 2.5 %collective-permute-start.13 = (bf16[896,512]{1,0:T(8,128)(2,1)}, bf16[896,512]{1,0:T(8,128)(2,1)S(1)}, u32[]{:S(2)}, u32[]{:S(2)}) collective-permute-start(bf16[896,512]{1,0:T(8,128)(2,1)} %collective-permute-done.11), channel_id=1, source_target_pairs={{0,224},{32,0},{64,32},{96,64},{128,96},{160,128},{192,160},{224,1... | collective-permute-start | bytes 2752520 | tf_op jit(solution)/shard_map/ppermute | solution.py:64
  160.5 2.2 fusion.7
  162.6 2.2 fusion.13
  164.8 11.7 %collective-permute-done.13 = bf16[896,512]{1,0:T(8,128)(2,1)S(1)} collective-permute-done((bf16[896,512]{1,0:T(8,128)(2,1)}, bf16[896,512]{1,0:T(8,128)(2,1)S(1)}, u32[]{:S(2)}, u32[]{:S(2)}) %collective-permute-start.13) | collective-permute-done | bytes 917536 | tf_op jit(solution)/shard_map/ppermute | solution.py:64
  176.5 1.1 fusion.99
  177.6 2.3 %collective-permute-done.12 = bf16[896,512]{1,0:T(8,128)(2,1)S(1)} collective-permute-done((bf16[896,512]{1,0:T(8,128)(2,1)}, bf16[896,512]{1,0:T(8,128)(2,1)S(1)}, u32[]{:S(2)}, u32[]{:S(2)}) %collective-permute-start.12) | collective-permute-done | bytes 917536 | tf_op jit(solution)/shard_map/ppermute | solution.py:63
  179.9 1.1 fusion.98
  181.0 1.1 exponential_reduce_fusion
  182.2 23.3 %all-gather = f32[96,384,2]{1,2,0:T(2,128)S(1)} all-gather(f32[3,384,2]{1,2,0:T(2,128)S(1)} %pad_maximum_fusion.1), channel_id=2, replica_groups=mesh['row'=8,'col'=32] {'col'}, dimensions={0}, use_global_device_ids=true | all-gather | bytes 304128 | tf_op jit(solution)/shard_map/all_gather | solution.py:74
  206.0 3.6 %collective-permute-done.14 = f32[3,16]{1,0:T(4,128)S(1)} collective-permute-done((f32[3,16]{1,0:T(4,128)S(1)}, f32[3,16]{1,0:T(4,128)S(1)}, u32[]{:S(2)}, u32[]{:S(2)}) %collective-permute-start.14) | collective-permute-done | bytes 224 | tf_op jit(solution)/shard_map/ppermute | solution.py:91
  209.5 1.5 collective-permute-start.15
  211.0 3.1 %collective-permute-done.15 = f32[3,16]{1,0:T(4,128)S(1)} collective-permute-done((f32[3,16]{1,0:T(4,128)S(1)}, f32[3,16]{1,0:T(4,128)S(1)}, u32[]{:S(2)}, u32[]{:S(2)}) %collective-permute-start.15) | collective-permute-done | bytes 224 | tf_op jit(solution)/shard_map/ppermute | solution.py:91
  214.1 4.8 %collective-permute-start.16 = (f32[3,16]{1,0:T(4,128)S(1)}, f32[3,16]{1,0:T(4,128)S(1)}, u32[]{:S(2)}, u32[]{:S(2)}) collective-permute-start(f32[3,16]{1,0:T(4,128)S(1)} %pad_maximum_fusion.4), channel_id=1, source_target_pairs={{0,128},{32,160},{64,192},{96,224},{128,0},{160,32},{192,64},{224,... | collective-permute-start | bytes 584 | tf_op jit(solution)/shard_map/ppermute | solution.py:91
  218.9 2.8 %collective-permute-done.16 = f32[3,16]{1,0:T(4,128)S(1)} collective-permute-done((f32[3,16]{1,0:T(4,128)S(1)}, f32[3,16]{1,0:T(4,128)S(1)}, u32[]{:S(2)}, u32[]{:S(2)}) %collective-permute-start.16) | collective-permute-done | bytes 224 | tf_op jit(solution)/shard_map/ppermute | solution.py:91
  (60 shorter events, 3.5 us)
Async XLA Ops:
  6.5 84.0 %all-gather.4.cloned.1.call-start = ((), (), s32[]{:S(2)}) async-start(), calls=%async_computation | async-start | bytes 11354112 | tf_op jit(solution)/shard_map/all_gather | solution.py:19
  7.3 31.1 %copy-start.5 = (f32[2,224]{1,0:T(2,128)S(1)}, f32[2,224]{1,0:T(2,128)}, u32[]{:S(2)}) copy-start(f32[2,224]{1,0:T(2,128)} %param.7) | copy-start | bytes 5380
  8.8 26.3 %collective-permute-start = (bf16[896,512]{1,0:T(8,128)(2,1)S(1)}, bf16[896,512]{1,0:T(8,128)(2,1)S(1)}, u32[]{:S(2)}, u32[]{:S(2)}) collective-permute-start(bf16[896,512]{1,0:T(8,128)(2,1)S(1)} %get-tuple-element.33), channel_id=1, source_target_pairs={{0,32},{32,64},{64,96},{96,128},{128,160},{160,192},{192,224},{224... | collective-permute-start | bytes 2752520 | tf_op jit(solution)/shard_map/ppermute | solution.py:63
  10.8 24.3 %collective-permute-start.1 = (bf16[896,512]{1,0:T(8,128)(2,1)S(1)}, bf16[896,512]{1,0:T(8,128)(2,1)S(1)}, u32[]{:S(2)}, u32[]{:S(2)}) collective-permute-start(bf16[896,512]{1,0:T(8,128)(2,1)S(1)} %get-tuple-element.34), channel_id=1, source_target_pairs={{0,224},{32,0},{64,32},{96,64},{128,96},{160,128},{192,160},{224,1... | collective-permute-start | bytes 2752520 | tf_op jit(solution)/shard_map/ppermute | solution.py:64
  35.1 28.1 %collective-permute-start.2 = (bf16[896,512]{1,0:T(8,128)(2,1)S(1)}, bf16[896,512]{1,0:T(8,128)(2,1)S(1)}, u32[]{:S(2)}, u32[]{:S(2)}) collective-permute-start(bf16[896,512]{1,0:T(8,128)(2,1)S(1)} %collective-permute-done), channel_id=1, source_target_pairs={{0,32},{32,64},{64,96},{96,128},{128,160},{160,192},{192,224},{224... | collective-permute-start | bytes 2752520 | tf_op jit(solution)/shard_map/ppermute | solution.py:63
  35.1 28.1 %collective-permute-start.3 = (bf16[896,512]{1,0:T(8,128)(2,1)S(1)}, bf16[896,512]{1,0:T(8,128)(2,1)}, u32[]{:S(2)}, u32[]{:S(2)}) collective-permute-start(bf16[896,512]{1,0:T(8,128)(2,1)S(1)} %collective-permute-done.1), channel_id=1, source_target_pairs={{0,224},{32,0},{64,32},{96,64},{128,96},{160,128},{192,160},{224,1... | collective-permute-start | bytes 2752520 | tf_op jit(solution)/shard_map/ppermute | solution.py:64
  63.2 27.3 %copy-start.7 = (bf16[896,512]{1,0:T(8,128)(2,1)}, bf16[896,512]{1,0:T(8,128)(2,1)S(1)}, u32[]{:S(2)}) copy-start(bf16[896,512]{1,0:T(8,128)(2,1)S(1)} %collective-permute-done.2) | copy-start | bytes 2752516
  63.3 24.0 %collective-permute-start.4 = (bf16[896,512]{1,0:T(8,128)(2,1)S(1)}, bf16[896,512]{1,0:T(8,128)(2,1)}, u32[]{:S(2)}, u32[]{:S(2)}) collective-permute-start(bf16[896,512]{1,0:T(8,128)(2,1)S(1)} %collective-permute-done.2), channel_id=1, source_target_pairs={{0,32},{32,64},{64,96},{96,128},{128,160},{160,192},{192,224},{224... | collective-permute-start | bytes 2752520 | tf_op jit(solution)/shard_map/ppermute | solution.py:63
  63.4 23.9 %collective-permute-start.5 = (bf16[896,512]{1,0:T(8,128)(2,1)}, bf16[896,512]{1,0:T(8,128)(2,1)}, u32[]{:S(2)}, u32[]{:S(2)}) collective-permute-start(bf16[896,512]{1,0:T(8,128)(2,1)} %collective-permute-done.3), channel_id=1, source_target_pairs={{0,224},{32,0},{64,32},{96,64},{128,96},{160,128},{192,160},{224,1... | collective-permute-start | bytes 2752520 | tf_op jit(solution)/shard_map/ppermute | solution.py:64
  87.3 23.3 %collective-permute-start.6 = (bf16[896,512]{1,0:T(8,128)(2,1)}, bf16[896,512]{1,0:T(8,128)(2,1)}, u32[]{:S(2)}, u32[]{:S(2)}) collective-permute-start(bf16[896,512]{1,0:T(8,128)(2,1)} %collective-permute-done.4), channel_id=1, source_target_pairs={{0,32},{32,64},{64,96},{96,128},{128,160},{160,192},{192,224},{224... | collective-permute-start | bytes 2752520 | tf_op jit(solution)/shard_map/ppermute | solution.py:63
  88.7 21.8 %collective-permute-start.7 = (bf16[896,512]{1,0:T(8,128)(2,1)}, bf16[896,512]{1,0:T(8,128)(2,1)}, u32[]{:S(2)}, u32[]{:S(2)}) collective-permute-start(bf16[896,512]{1,0:T(8,128)(2,1)} %collective-permute-done.5), channel_id=1, source_target_pairs={{0,224},{32,0},{64,32},{96,64},{128,96},{160,128},{192,160},{224,1... | collective-permute-start | bytes 2752520 | tf_op jit(solution)/shard_map/ppermute | solution.py:64
  90.5 7.3 %copy-start = (bf16[384,2,7168]{0,2,1:T(8,128)(2,1)S(1)}, bf16[384,2,7168]{0,2,1:T(8,128)(2,1)}, u32[]{:S(2)}) copy-start(bf16[384,2,7168]{0,2,1:T(8,128)(2,1)} %all-gather.4.cloned.1.call-done) | copy-start | bytes 33030148
  97.8 12.8 %copy-start.3 = (bf16[896,1024]{1,0:T(8,128)(2,1)S(1)}, bf16[896,1024]{1,0:T(8,128)(2,1)}, u32[]{:S(2)}) copy-start(bf16[896,1024]{1,0:T(8,128)(2,1)} %param.8) | copy-start | bytes 5505028
  100.9 27.3 %copy-start.1 = (bf16[384,2,7168]{0,2,1:T(8,128)(2,1)}, bf16[384,2,7168]{0,2,1:T(8,128)(2,1)S(1)}, u32[]{:S(2)}) copy-start(bf16[384,2,7168]{0,2,1:T(8,128)(2,1)S(1)} %fusion.2) | copy-start | bytes 33030148
  112.6 22.7 %collective-permute-start.8 = (bf16[896,512]{1,0:T(8,128)(2,1)}, bf16[896,512]{1,0:T(8,128)(2,1)}, u32[]{:S(2)}, u32[]{:S(2)}) collective-permute-start(bf16[896,512]{1,0:T(8,128)(2,1)} %collective-permute-done.6), channel_id=1, source_target_pairs={{0,32},{32,64},{64,96},{96,128},{128,160},{160,192},{192,224},{224... | collective-permute-start | bytes 2752520 | tf_op jit(solution)/shard_map/ppermute | solution.py:63
  115.2 20.6 %collective-permute-start.9 = (bf16[896,512]{1,0:T(8,128)(2,1)}, bf16[896,512]{1,0:T(8,128)(2,1)}, u32[]{:S(2)}, u32[]{:S(2)}) collective-permute-start(bf16[896,512]{1,0:T(8,128)(2,1)} %collective-permute-done.7), channel_id=1, source_target_pairs={{0,224},{32,0},{64,32},{96,64},{128,96},{160,128},{192,160},{224,1... | collective-permute-start | bytes 2752520 | tf_op jit(solution)/shard_map/ppermute | solution.py:64
  121.5 2.3 copy-start.8
  128.2 10.9 %copy-start.6 = (s32[16]{0:T(128)S(1)}, s32[16]{0:T(128)}, u32[]{:S(2)}) copy-start(s32[16]{0:T(128)} %param.9) | copy-start | bytes 196
  135.9 21.0 %collective-permute-start.10 = (bf16[896,512]{1,0:T(8,128)(2,1)}, bf16[896,512]{1,0:T(8,128)(2,1)}, u32[]{:S(2)}, u32[]{:S(2)}) collective-permute-start(bf16[896,512]{1,0:T(8,128)(2,1)} %collective-permute-done.8), channel_id=1, source_target_pairs={{0,32},{32,64},{64,96},{96,128},{128,160},{160,192},{192,224},{224... | collective-permute-start | bytes 2752520 | tf_op jit(solution)/shard_map/ppermute | solution.py:63
  137.4 19.9 %collective-permute-start.11 = (bf16[896,512]{1,0:T(8,128)(2,1)}, bf16[896,512]{1,0:T(8,128)(2,1)}, u32[]{:S(2)}, u32[]{:S(2)}) collective-permute-start(bf16[896,512]{1,0:T(8,128)(2,1)} %collective-permute-done.9), channel_id=1, source_target_pairs={{0,224},{32,0},{64,32},{96,64},{128,96},{160,128},{192,160},{224,1... | collective-permute-start | bytes 2752520 | tf_op jit(solution)/shard_map/ppermute | solution.py:64
  142.1 18.4 %copy-start.2 = (bf16[384,2,7168]{0,2,1:T(8,128)(2,1)S(1)}, bf16[384,2,7168]{0,2,1:T(8,128)(2,1)}, u32[]{:S(2)}) copy-start(bf16[384,2,7168]{0,2,1:T(8,128)(2,1)} %copy-done.1) | copy-start | bytes 33030148
  145.2 14.6 %copy-start.4 = (s32[384]{0:T(512)S(1)}, s32[384]{0:T(512)}, u32[]{:S(2)}) copy-start(s32[384]{0:T(512)} %param.10) | copy-start | bytes 4612
  157.3 19.2 %collective-permute-start.13 = (bf16[896,512]{1,0:T(8,128)(2,1)}, bf16[896,512]{1,0:T(8,128)(2,1)S(1)}, u32[]{:S(2)}, u32[]{:S(2)}) collective-permute-start(bf16[896,512]{1,0:T(8,128)(2,1)} %collective-permute-done.11), channel_id=1, source_target_pairs={{0,224},{32,0},{64,32},{96,64},{128,96},{160,128},{192,160},{224,1... | collective-permute-start | bytes 2752520 | tf_op jit(solution)/shard_map/ppermute | solution.py:64
  160.1 19.8 %collective-permute-start.12 = (bf16[896,512]{1,0:T(8,128)(2,1)}, bf16[896,512]{1,0:T(8,128)(2,1)S(1)}, u32[]{:S(2)}, u32[]{:S(2)}) collective-permute-start(bf16[896,512]{1,0:T(8,128)(2,1)} %collective-permute-done.10), channel_id=1, source_target_pairs={{0,32},{32,64},{64,96},{96,128},{128,160},{160,192},{192,224},{224... | collective-permute-start | bytes 2752520 | tf_op jit(solution)/shard_map/ppermute | solution.py:63
  181.0 37.9 %copy-start.9 = (s32[16]{0:T(128)S(1)}, s32[16]{0:T(128)}, u32[]{:S(2)}) copy-start(s32[16]{0:T(128)} %param.11) | copy-start | bytes 196
  205.9 3.7 %collective-permute-start.14 = (f32[3,16]{1,0:T(4,128)S(1)}, f32[3,16]{1,0:T(4,128)S(1)}, u32[]{:S(2)}, u32[]{:S(2)}) collective-permute-start(f32[3,16]{1,0:T(4,128)S(1)} %pad_maximum_fusion.2), channel_id=1, source_target_pairs={{0,32},{32,0},{64,96},{96,64},{128,160},{160,128},{192,224},{224,1... | collective-permute-start | bytes 584 | tf_op jit(solution)/shard_map/ppermute | solution.py:91
  209.5 4.6 %collective-permute-start.15 = (f32[3,16]{1,0:T(4,128)S(1)}, f32[3,16]{1,0:T(4,128)S(1)}, u32[]{:S(2)}, u32[]{:S(2)}) collective-permute-start(f32[3,16]{1,0:T(4,128)S(1)} %pad_maximum_fusion.3), channel_id=1, source_target_pairs={{0,64},{32,96},{64,0},{96,32},{128,192},{160,224},{192,128},{224,1... | collective-permute-start | bytes 584 | tf_op jit(solution)/shard_map/ppermute | solution.py:91
  214.1 7.6 %collective-permute-start.16 = (f32[3,16]{1,0:T(4,128)S(1)}, f32[3,16]{1,0:T(4,128)S(1)}, u32[]{:S(2)}, u32[]{:S(2)}) collective-permute-start(f32[3,16]{1,0:T(4,128)S(1)} %pad_maximum_fusion.4), channel_id=1, source_target_pairs={{0,128},{32,160},{64,192},{96,224},{128,0},{160,32},{192,64},{224,... | collective-permute-start | bytes 584 | tf_op jit(solution)/shard_map/ppermute | solution.py:91
Sparse Core Ops, SparseCore 0:
  9.9 66.8 all-gather.3

commit v14 on v13

--- a/solution.py
+++ b/solution.py
@@ -71,10 +71,19 @@
     picked = jnp.sum(
         jnp.where(targets[:, None, None] == vocab_ids[None, None, :], logits, 0.0), axis=2
     )
-    parts = lax.all_gather(jnp.stack([row_max, exp_total, picked]), "col")
-    max_logit = jnp.max(parts[:, 0], axis=0)
-    exp_total = jnp.sum(parts[:, 1] * jnp.exp(parts[:, 0] - max_logit[None]), axis=0)
-    picked = jnp.sum(parts[:, 2], axis=0)
+    n_col = lax.axis_size("col")
+    max_logit = row_max
+    distance = 1
+    while distance < n_col:
+        partner = [(i, i ^ distance) for i in range(n_col)]
+        other = lax.ppermute(jnp.stack([max_logit, exp_total, picked]), "col", partner)
+        joint_max = jnp.maximum(max_logit, other[0])
+        exp_total = exp_total * jnp.exp(max_logit - joint_max) + other[1] * jnp.exp(
+            other[0] - joint_max
+        )
+        picked = picked + other[2]
+        max_logit = joint_max
+        distance *= 2
     logp = picked - (max_logit + jnp.log(exp_total))
     log_ratio = logp[:, 0] - logp[:, 1]
     token_index = row_index * tok_rows + jnp.arange(tok_rows, dtype=jnp.int32)

time: 230 us -> 226 us (0.983)
  blocking collectives: 48 us -> 24.7 us
  waiting for transfers between devices: 91.8 us -> 106 us
  starting transfers between devices: 31.7 us -> 36.9 us
    all_gather x1 -> x0, blocking collectives: 23.3 us -> none  [per_device(): parts = lax.all_gather(jnp.stack([row_max, exp_total, picked]), 'col')]
    ppermute x0 -> x5, waiting for transfers between devices: none -> 13.9 us  [per_device(): lax.ppermute(jnp.stack([max_logit, exp_total, picked]), 'col', partner)]
    ppermute x0 -> x5, starting transfers between devices: none -> 5.03 us  [per_device(): lax.ppermute(jnp.stack([max_logit, exp_total, picked]), 'col', partner)]
  transfers between devices with their start and end apart: 18 -> 23, of which waited for: 12 -> 17; matrix products, arithmetic and copies ran while one was open for 17% -> 17% of each run, Pallas kernels for 0% -> 0%
where the time goes in v14:
time: 226 us; the launch traced here: 225 us
  waiting for transfers between devices  106 us (47%)
  starting transfers between devices  36.9 us (16%)
  matrix products  28.3 us (13%)
  blocking collectives  24.7 us (11%)
  between operations  13.7 us (6%)
  other arithmetic  12.3 us (5%)
  local copies, waits for them, and re-layouts  3.17 us (1%)
    ppermute x7, waiting for transfers between devices, per_device(): left = lax.ppermute(left, 'row', forward)  69.3 us
    dot_general x16, matrix products, block_logits(): jnp.einsum('tmd,dv->tmv', features[shard], block, preferred_element_type=...  28.3 us
    all_gather x1, blocking collectives, per_device(): full_gain = lax.all_gather(final_gain, 'col', axis=1, tiled=True)  24.7 us
    ppermute x7, starting transfers between devices, per_device(): right = lax.ppermute(right, 'row', backward)  17.3 us
    ppermute x5, waiting for transfers between devices, per_device(): lax.ppermute(jnp.stack([max_logit, exp_total, picked]), 'col', partner)  13.9 us
    ppermute x7, waiting for transfers between devices, per_device(): right = lax.ppermute(right, 'row', backward)  12.7 us
    ppermute x3, waiting for transfers between devices, per_device(): other = lax.ppermute(seq_stats, 'row', partner)  9.32 us
    ppermute x7, starting transfers between devices, per_device(): left = lax.ppermute(left, 'row', forward)  8.05 us
  transfers between devices with their start and end apart: 23, of which 17 were waited for; matrix products, arithmetic and copies ran while one was open for 17% of the time, Pallas kernels for 0%

profile of v14, /device:TPU:2, one launch (start us, length us, event | category | flops | bytes accessed | tf_op | source)
XLA Modules:
  0.0 225.1 jit_solution(12208501743608678430)
XLA Ops:
  7.3 1.6 fusion.118
  8.8 2.0 collective-permute-start
  10.8 4.0 %collective-permute-start.1 = (bf16[896,512]{1,0:T(8,128)(2,1)S(1)}, bf16[896,512]{1,0:T(8,128)(2,1)S(1)}, u32[]{:S(2)}, u32[]{:S(2)}) collective-permute-start(bf16[896,512]{1,0:T(8,128)(2,1)S(1)} %get-tuple-element.34), channel_id=1, source_target_pairs={{0,224},{32,0},{64,32},{96,64},{128,96},{160,128},{192,160},{224,1... | collective-permute-start | bytes 2752520 | tf_op jit(solution)/shard_map/ppermute | solution.py:64
  14.9 20.3 %collective-permute-done = bf16[896,512]{1,0:T(8,128)(2,1)S(1)} collective-permute-done((bf16[896,512]{1,0:T(8,128)(2,1)S(1)}, bf16[896,512]{1,0:T(8,128)(2,1)S(1)}, u32[]{:S(2)}, u32[]{:S(2)}) %collective-permute-start) | collective-permute-done | bytes 917536 | tf_op jit(solution)/shard_map/ppermute | solution.py:63
  35.1 3.2 %collective-permute-start.3 = (bf16[896,512]{1,0:T(8,128)(2,1)S(1)}, bf16[896,512]{1,0:T(8,128)(2,1)}, u32[]{:S(2)}, u32[]{:S(2)}) collective-permute-start(bf16[896,512]{1,0:T(8,128)(2,1)S(1)} %collective-permute-done.1), channel_id=1, source_target_pairs={{0,224},{32,0},{64,32},{96,64},{128,96},{160,128},{192,160},{224,1... | collective-permute-start | bytes 2752520 | tf_op jit(solution)/shard_map/ppermute | solution.py:64
  38.4 24.7 %all-gather = f32[32,224,2]{1,2,0:T(2,128)S(1)} all-gather(f32[1,224,2]{1,2,0:T(2,128)S(1)} %bitcast.318), channel_id=1, replica_groups=mesh['row'=8,'col'=32] {'col'}, dimensions={0}, use_global_device_ids=true | all-gather | bytes 59136 | tf_op jit(solution)/shard_map/all_gather | solution.py:20
  63.4 3.2 %collective-permute-start.5 = (bf16[896,512]{1,0:T(8,128)(2,1)}, bf16[896,512]{1,0:T(8,128)(2,1)}, u32[]{:S(2)}, u32[]{:S(2)}) collective-permute-start(bf16[896,512]{1,0:T(8,128)(2,1)} %collective-permute-done.3), channel_id=1, source_target_pairs={{0,224},{32,0},{64,32},{96,64},{128,96},{160,128},{192,160},{224,1... | collective-permute-start | bytes 2752520 | tf_op jit(solution)/shard_map/ppermute | solution.py:64
  66.6 20.7 %collective-permute-done.4 = bf16[896,512]{1,0:T(8,128)(2,1)} collective-permute-done((bf16[896,512]{1,0:T(8,128)(2,1)S(1)}, bf16[896,512]{1,0:T(8,128)(2,1)}, u32[]{:S(2)}, u32[]{:S(2)}) %collective-permute-start.4) | collective-permute-done | bytes 917536 | tf_op jit(solution)/shard_map/ppermute | solution.py:63
  87.3 1.5 collective-permute-start.6
  88.7 1.8 collective-permute-start.7
  90.5 6.5 %fusion = f32[384,2]{0,1:T(2,128)S(1)} fusion(bf16[384,2,7168]{0,2,1:T(8,128)(2,1)} %all-gather.3.cloned.1.call-done), kind=kLoop, calls=%fused_computation.2 | loop fusion | flops 16514304 | bytes 11013120 | tf_op jit(solution)/shard_map/reduce_sum | solution.py:48
  97.8 3.1 %fusion.2 = bf16[384,2,7168]{0,2,1:T(8,128)(2,1)S(1)} fusion(bf16[384,2,7168]{0,2,1:T(8,128)(2,1)S(1)} %copy-done, f32[2,7168]{1,0:T(2,128)S(1)} %bitcast.311, f32[384,2]{0,1:T(2,128)S(1)} %add_rsqrt_fusion), kind=kLoop, calls=%fused_computation.4 | loop fusion | flops 22020096 | bytes 22080512 | tf_op jit(solution)/shard_map/convert_element_type | solution.py:51
  100.9 9.7 %collective-permute-done.6 = bf16[896,512]{1,0:T(8,128)(2,1)} collective-permute-done((bf16[896,512]{1,0:T(8,128)(2,1)}, bf16[896,512]{1,0:T(8,128)(2,1)}, u32[]{:S(2)}, u32[]{:S(2)}) %collective-permute-start.6) | collective-permute-done | bytes 917536 | tf_op jit(solution)/shard_map/ppermute | solution.py:63
  111.6 1.0 fusion.37
  112.6 2.6 %collective-permute-start.8 = (bf16[896,512]{1,0:T(8,128)(2,1)}, bf16[896,512]{1,0:T(8,128)(2,1)}, u32[]{:S(2)}, u32[]{:S(2)}) collective-permute-start(bf16[896,512]{1,0:T(8,128)(2,1)} %collective-permute-done.6), channel_id=1, source_target_pairs={{0,32},{32,64},{64,96},{96,128},{128,160},{160,192},{192,224},{224... | collective-permute-start | bytes 2752520 | tf_op jit(solution)/shard_map/ppermute | solution.py:63
  116.1 2.2 fusion.21
  118.3 2.2 fusion.23
  121.5 2.3 %fusion.29 = f32[384,2,512]{2,0,1:T(8,128)S(1)} fusion(bf16[384,2,8,896]{0,3,2,1:T(8,128)(2,1)S(1)} %bitcast.300, s32[]{:T(128)S(6)} %select_n.136, bf16[896,512]{1,0:T(8,128)(2,1)} %collective-permute-done.4), kind=kOutput, calls=%fused_computation.34 | convolution fusion | flops 704643072 | bytes 3866628 | tf_op jit(solution)/shard_map/tmd,dv->tmv/dot_general | solution.py:30
  123.8 1.0 fusion.31
  124.8 1.0 fusion.33
  125.8 2.3 %add_add_fusion.2 = f32[384,2,512]{2,0,1:T(8,128)S(1)} fusion(f32[384,2,512]{2,0,1:T(8,128)S(1)} %fusion.21, f32[384,2,512]{2,0,1:T(8,128)S(1)} %fusion.23, f32[384,2,512]{2,0,1:T(8,128)S(1)} %fusion.35, f32[384,2,512]{2,0,1:T(8,128)S(1)} %fusion.25, bf16[384,2,8,896]{0,3,2,1:T(8,128)(2,1)S(1)} %bitcast.303, s32[]{:T(128)S(6)} %select_n.146, ...), kind=kOutput, calls=%fused_computation.10 | convolution fusion | flops 706215936 | bytes 10158084 | tf_op jit(solution)/shard_map/tmd,dv->tmv/dot_general | solution.py:30
  128.2 2.3 %add_add_fusion.3 = f32[384,2,512]{2,0,1:T(8,128)S(1)} fusion(f32[384,2,512]{2,0,1:T(8,128)S(1)} %fusion.29, f32[384,2,512]{2,0,1:T(8,128)S(1)} %fusion.31, f32[384,2,512]{2,0,1:T(8,128)S(1)} %fusion.37, f32[384,2,512]{2,0,1:T(8,128)S(1)} %fusion.33, bf16[384,2,8,896]{0,3,2,1:T(8,128)(2,1)S(1)} %bitcast.304, s32[]{:T(128)S(6)} %select_n.138, ...), kind=kOutput, calls=%fused_computation.11 | convolution fusion | flops 706215936 | bytes 10158084 | tf_op jit(solution)/shard_map/tmd,dv->tmv/dot_general | solution.py:30
  130.5 4.7 %collective-permute-done.8 = bf16[896,512]{1,0:T(8,128)(2,1)} collective-permute-done((bf16[896,512]{1,0:T(8,128)(2,1)}, bf16[896,512]{1,0:T(8,128)(2,1)}, u32[]{:S(2)}, u32[]{:S(2)}) %collective-permute-start.8) | collective-permute-done | bytes 917536 | tf_op jit(solution)/shard_map/ppermute | solution.py:63
  135.9 1.6 collective-permute-start.10
  137.4 1.7 collective-permute-start.11
  139.1 2.6 %fusion.15 = f32[384,2,512]{2,0,1:T(8,128)S(1)} fusion(bf16[384,2,8,896]{0,3,2,1:T(8,128)(2,1)} %bitcast.305, s32[]{:T(128)S(6)} %select_n.150, bf16[896,512]{1,0:T(8,128)(2,1)} %collective-permute-done.9), kind=kOutput, calls=%fused_computation.20 | convolution fusion | flops 704643072 | bytes 3866628 | tf_op jit(solution)/shard_map/tmd,dv->tmv/dot_general | solution.py:30
  142.1 2.8 %fusion.17 = f32[384,2,512]{2,0,1:T(8,128)S(1)} fusion(bf16[384,2,8,896]{0,3,2,1:T(8,128)(2,1)} %bitcast.306, s32[]{:T(128)S(6)} %select_n.148, bf16[896,512]{1,0:T(8,128)(2,1)} %collective-permute-done.8), kind=kOutput, calls=%fused_computation.22 | convolution fusion | flops 704643072 | bytes 3866628 | tf_op jit(solution)/shard_map/tmd,dv->tmv/dot_general | solution.py:30
  145.2 11.7 %collective-permute-done.10 = bf16[896,512]{1,0:T(8,128)(2,1)} collective-permute-done((bf16[896,512]{1,0:T(8,128)(2,1)}, bf16[896,512]{1,0:T(8,128)(2,1)}, u32[]{:S(2)}, u32[]{:S(2)}) %collective-permute-start.10) | collective-permute-done | bytes 917536 | tf_op jit(solution)/shard_map/ppermute | solution.py:63
  157.3 2.5 %collective-permute-start.13 = (bf16[896,512]{1,0:T(8,128)(2,1)}, bf16[896,512]{1,0:T(8,128)(2,1)S(1)}, u32[]{:S(2)}, u32[]{:S(2)}) collective-permute-start(bf16[896,512]{1,0:T(8,128)(2,1)} %collective-permute-done.11), channel_id=1, source_target_pairs={{0,224},{32,0},{64,32},{96,64},{128,96},{160,128},{192,160},{224,1... | collective-permute-start | bytes 2752520 | tf_op jit(solution)/shard_map/ppermute | solution.py:64
  160.5 2.2 fusion.7
  162.7 2.2 fusion.13
  164.9 11.7 %collective-permute-done.13 = bf16[896,512]{1,0:T(8,128)(2,1)S(1)} collective-permute-done((bf16[896,512]{1,0:T(8,128)(2,1)}, bf16[896,512]{1,0:T(8,128)(2,1)S(1)}, u32[]{:S(2)}, u32[]{:S(2)}) %collective-permute-start.13) | collective-permute-done | bytes 917536 | tf_op jit(solution)/shard_map/ppermute | solution.py:64
  176.5 1.1 fusion.120
  177.6 2.3 %collective-permute-done.12 = bf16[896,512]{1,0:T(8,128)(2,1)S(1)} collective-permute-done((bf16[896,512]{1,0:T(8,128)(2,1)}, bf16[896,512]{1,0:T(8,128)(2,1)S(1)}, u32[]{:S(2)}, u32[]{:S(2)}) %collective-permute-start.12) | collective-permute-done | bytes 917536 | tf_op jit(solution)/shard_map/ppermute | solution.py:63
  179.9 1.1 fusion.119
  181.1 1.1 exponential_reduce_fusion
  182.3 1.2 collective-permute-done.14
  184.4 2.8 %collective-permute-done.15 = f32[3,384,2]{1,2,0:T(2,128)S(1)} collective-permute-done((f32[3,384,2]{1,2,0:T(2,128)S(1)}, f32[3,384,2]{1,2,0:T(2,128)S(1)}, u32[]{:S(2)}, u32[]{:S(2)}) %collective-permute-start.15) | collective-permute-done | bytes 9248 | tf_op jit(solution)/shard_map/ppermute | solution.py:79
  187.2 2.2 collective-permute-start.16
  189.4 3.1 %collective-permute-done.16 = f32[3,384,2]{1,2,0:T(2,128)S(1)} collective-permute-done((f32[3,384,2]{1,2,0:T(2,128)S(1)}, f32[3,384,2]{1,2,0:T(2,128)S(1)}, u32[]{:S(2)}, u32[]{:S(2)}) %collective-permute-start.16) | collective-permute-done | bytes 9248 | tf_op jit(solution)/shard_map/ppermute | solution.py:79
  193.1 3.2 %collective-permute-done.17 = f32[3,384,2]{1,2,0:T(2,128)S(1)} collective-permute-done((f32[3,384,2]{1,2,0:T(2,128)S(1)}, f32[3,384,2]{1,2,0:T(2,128)S(1)}, u32[]{:S(2)}, u32[]{:S(2)}) %collective-permute-start.17) | collective-permute-done | bytes 9248 | tf_op jit(solution)/shard_map/ppermute | solution.py:79
  196.3 1.6 collective-permute-start.18
  198.0 3.6 %collective-permute-done.18 = f32[3,384,2]{1,2,0:T(2,128)S(1)} collective-permute-done((f32[3,384,2]{1,2,0:T(2,128)S(1)}, f32[3,384,2]{1,2,0:T(2,128)S(1)}, u32[]{:S(2)}, u32[]{:S(2)}) %collective-permute-start.18) | collective-permute-done | bytes 9248 | tf_op jit(solution)/shard_map/ppermute | solution.py:79
  201.9 3.6 %collective-permute-done.19 = f32[3,16]{1,0:T(4,128)S(1)} collective-permute-done((f32[3,16]{1,0:T(4,128)S(1)}, f32[3,16]{1,0:T(4,128)S(1)}, u32[]{:S(2)}, u32[]{:S(2)}) %collective-permute-start.19) | collective-permute-done | bytes 224 | tf_op jit(solution)/shard_map/ppermute | solution.py:100
  205.5 1.5 collective-permute-start.20
  207.0 3.0 %collective-permute-done.20 = f32[3,16]{1,0:T(4,128)S(1)} collective-permute-done((f32[3,16]{1,0:T(4,128)S(1)}, f32[3,16]{1,0:T(4,128)S(1)}, u32[]{:S(2)}, u32[]{:S(2)}) %collective-permute-start.20) | collective-permute-done | bytes 224 | tf_op jit(solution)/shard_map/ppermute | solution.py:100
  210.1 4.9 %collective-permute-start.21 = (f32[3,16]{1,0:T(4,128)S(1)}, f32[3,16]{1,0:T(4,128)S(1)}, u32[]{:S(2)}, u32[]{:S(2)}) collective-permute-start(f32[3,16]{1,0:T(4,128)S(1)} %pad_maximum_fusion.8), channel_id=1, source_target_pairs={{0,128},{32,160},{64,192},{96,224},{128,0},{160,32},{192,64},{224,... | collective-permute-start | bytes 584 | tf_op jit(solution)/shard_map/ppermute | solution.py:100
  215.0 2.7 %collective-permute-done.21 = f32[3,16]{1,0:T(4,128)S(1)} collective-permute-done((f32[3,16]{1,0:T(4,128)S(1)}, f32[3,16]{1,0:T(4,128)S(1)}, u32[]{:S(2)}, u32[]{:S(2)}) %collective-permute-start.21) | collective-permute-done | bytes 224 | tf_op jit(solution)/shard_map/ppermute | solution.py:100
  (74 shorter events, 9.7 us)
Async XLA Ops:
  6.5 84.0 %all-gather.3.cloned.1.call-start = ((), (), s32[]{:S(2)}) async-start(), calls=%async_computation | async-start | bytes 11354112 | tf_op jit(solution)/shard_map/all_gather | solution.py:19
  7.3 31.1 %copy-start.5 = (f32[2,224]{1,0:T(2,128)S(1)}, f32[2,224]{1,0:T(2,128)}, u32[]{:S(2)}) copy-start(f32[2,224]{1,0:T(2,128)} %param.7) | copy-start | bytes 5380
  8.8 26.3 %collective-permute-start = (bf16[896,512]{1,0:T(8,128)(2,1)S(1)}, bf16[896,512]{1,0:T(8,128)(2,1)S(1)}, u32[]{:S(2)}, u32[]{:S(2)}) collective-permute-start(bf16[896,512]{1,0:T(8,128)(2,1)S(1)} %get-tuple-element.33), channel_id=1, source_target_pairs={{0,32},{32,64},{64,96},{96,128},{128,160},{160,192},{192,224},{224... | collective-permute-start | bytes 2752520 | tf_op jit(solution)/shard_map/ppermute | solution.py:63
  10.8 24.3 %collective-permute-start.1 = (bf16[896,512]{1,0:T(8,128)(2,1)S(1)}, bf16[896,512]{1,0:T(8,128)(2,1)S(1)}, u32[]{:S(2)}, u32[]{:S(2)}) collective-permute-start(bf16[896,512]{1,0:T(8,128)(2,1)S(1)} %get-tuple-element.34), channel_id=1, source_target_pairs={{0,224},{32,0},{64,32},{96,64},{128,96},{160,128},{192,160},{224,1... | collective-permute-start | bytes 2752520 | tf_op jit(solution)/shard_map/ppermute | solution.py:64
  35.1 28.1 %collective-permute-start.2 = (bf16[896,512]{1,0:T(8,128)(2,1)S(1)}, bf16[896,512]{1,0:T(8,128)(2,1)S(1)}, u32[]{:S(2)}, u32[]{:S(2)}) collective-permute-start(bf16[896,512]{1,0:T(8,128)(2,1)S(1)} %collective-permute-done), channel_id=1, source_target_pairs={{0,32},{32,64},{64,96},{96,128},{128,160},{160,192},{192,224},{224... | collective-permute-start | bytes 2752520 | tf_op jit(solution)/shard_map/ppermute | solution.py:63
  35.1 28.1 %collective-permute-start.3 = (bf16[896,512]{1,0:T(8,128)(2,1)S(1)}, bf16[896,512]{1,0:T(8,128)(2,1)}, u32[]{:S(2)}, u32[]{:S(2)}) collective-permute-start(bf16[896,512]{1,0:T(8,128)(2,1)S(1)} %collective-permute-done.1), channel_id=1, source_target_pairs={{0,224},{32,0},{64,32},{96,64},{128,96},{160,128},{192,160},{224,1... | collective-permute-start | bytes 2752520 | tf_op jit(solution)/shard_map/ppermute | solution.py:64
  63.2 27.3 %copy-start.7 = (bf16[896,512]{1,0:T(8,128)(2,1)}, bf16[896,512]{1,0:T(8,128)(2,1)S(1)}, u32[]{:S(2)}) copy-start(bf16[896,512]{1,0:T(8,128)(2,1)S(1)} %collective-permute-done.2) | copy-start | bytes 2752516
  63.3 24.0 %collective-permute-start.4 = (bf16[896,512]{1,0:T(8,128)(2,1)S(1)}, bf16[896,512]{1,0:T(8,128)(2,1)}, u32[]{:S(2)}, u32[]{:S(2)}) collective-permute-start(bf16[896,512]{1,0:T(8,128)(2,1)S(1)} %collective-permute-done.2), channel_id=1, source_target_pairs={{0,32},{32,64},{64,96},{96,128},{128,160},{160,192},{192,224},{224... | collective-permute-start | bytes 2752520 | tf_op jit(solution)/shard_map/ppermute | solution.py:63
  63.4 23.9 %collective-permute-start.5 = (bf16[896,512]{1,0:T(8,128)(2,1)}, bf16[896,512]{1,0:T(8,128)(2,1)}, u32[]{:S(2)}, u32[]{:S(2)}) collective-permute-start(bf16[896,512]{1,0:T(8,128)(2,1)} %collective-permute-done.3), channel_id=1, source_target_pairs={{0,224},{32,0},{64,32},{96,64},{128,96},{160,128},{192,160},{224,1... | collective-permute-start | bytes 2752520 | tf_op jit(solution)/shard_map/ppermute | solution.py:64
  87.3 23.3 %collective-permute-start.6 = (bf16[896,512]{1,0:T(8,128)(2,1)}, bf16[896,512]{1,0:T(8,128)(2,1)}, u32[]{:S(2)}, u32[]{:S(2)}) collective-permute-start(bf16[896,512]{1,0:T(8,128)(2,1)} %collective-permute-done.4), channel_id=1, source_target_pairs={{0,32},{32,64},{64,96},{96,128},{128,160},{160,192},{192,224},{224... | collective-permute-start | bytes 2752520 | tf_op jit(solution)/shard_map/ppermute | solution.py:63
  88.7 21.8 %collective-permute-start.7 = (bf16[896,512]{1,0:T(8,128)(2,1)}, bf16[896,512]{1,0:T(8,128)(2,1)}, u32[]{:S(2)}, u32[]{:S(2)}) collective-permute-start(bf16[896,512]{1,0:T(8,128)(2,1)} %collective-permute-done.5), channel_id=1, source_target_pairs={{0,224},{32,0},{64,32},{96,64},{128,96},{160,128},{192,160},{224,1... | collective-permute-start | bytes 2752520 | tf_op jit(solution)/shard_map/ppermute | solution.py:64
  90.5 7.3 %copy-start = (bf16[384,2,7168]{0,2,1:T(8,128)(2,1)S(1)}, bf16[384,2,7168]{0,2,1:T(8,128)(2,1)}, u32[]{:S(2)}) copy-start(bf16[384,2,7168]{0,2,1:T(8,128)(2,1)} %all-gather.3.cloned.1.call-done) | copy-start | bytes 33030148
  97.8 12.8 %copy-start.3 = (bf16[896,1024]{1,0:T(8,128)(2,1)S(1)}, bf16[896,1024]{1,0:T(8,128)(2,1)}, u32[]{:S(2)}) copy-start(bf16[896,1024]{1,0:T(8,128)(2,1)} %param.8) | copy-start | bytes 5505028
  100.9 27.3 %copy-start.1 = (bf16[384,2,7168]{0,2,1:T(8,128)(2,1)}, bf16[384,2,7168]{0,2,1:T(8,128)(2,1)S(1)}, u32[]{:S(2)}) copy-start(bf16[384,2,7168]{0,2,1:T(8,128)(2,1)S(1)} %fusion.2) | copy-start | bytes 33030148
  112.6 22.7 %collective-permute-start.8 = (bf16[896,512]{1,0:T(8,128)(2,1)}, bf16[896,512]{1,0:T(8,128)(2,1)}, u32[]{:S(2)}, u32[]{:S(2)}) collective-permute-start(bf16[896,512]{1,0:T(8,128)(2,1)} %collective-permute-done.6), channel_id=1, source_target_pairs={{0,32},{32,64},{64,96},{96,128},{128,160},{160,192},{192,224},{224... | collective-permute-start | bytes 2752520 | tf_op jit(solution)/shard_map/ppermute | solution.py:63
  115.2 20.6 %collective-permute-start.9 = (bf16[896,512]{1,0:T(8,128)(2,1)}, bf16[896,512]{1,0:T(8,128)(2,1)}, u32[]{:S(2)}, u32[]{:S(2)}) collective-permute-start(bf16[896,512]{1,0:T(8,128)(2,1)} %collective-permute-done.7), channel_id=1, source_target_pairs={{0,224},{32,0},{64,32},{96,64},{128,96},{160,128},{192,160},{224,1... | collective-permute-start | bytes 2752520 | tf_op jit(solution)/shard_map/ppermute | solution.py:64
  121.5 2.3 %copy-start.8 = (bf16[896,512]{1,0:T(8,128)(2,1)S(1)}, bf16[896,512]{1,0:T(8,128)(2,1)}, u32[]{:S(2)}) copy-start(bf16[896,512]{1,0:T(8,128)(2,1)} %copy-done.7) | copy-start | bytes 2752516
  135.9 21.0 %collective-permute-start.10 = (bf16[896,512]{1,0:T(8,128)(2,1)}, bf16[896,512]{1,0:T(8,128)(2,1)}, u32[]{:S(2)}, u32[]{:S(2)}) collective-permute-start(bf16[896,512]{1,0:T(8,128)(2,1)} %collective-permute-done.8), channel_id=1, source_target_pairs={{0,32},{32,64},{64,96},{96,128},{128,160},{160,192},{192,224},{224... | collective-permute-start | bytes 2752520 | tf_op jit(solution)/shard_map/ppermute | solution.py:63
  137.4 19.9 %collective-permute-start.11 = (bf16[896,512]{1,0:T(8,128)(2,1)}, bf16[896,512]{1,0:T(8,128)(2,1)}, u32[]{:S(2)}, u32[]{:S(2)}) collective-permute-start(bf16[896,512]{1,0:T(8,128)(2,1)} %collective-permute-done.9), channel_id=1, source_target_pairs={{0,224},{32,0},{64,32},{96,64},{128,96},{160,128},{192,160},{224,1... | collective-permute-start | bytes 2752520 | tf_op jit(solution)/shard_map/ppermute | solution.py:64
  141.7 18.7 %copy-start.2 = (bf16[384,2,7168]{0,2,1:T(8,128)(2,1)S(1)}, bf16[384,2,7168]{0,2,1:T(8,128)(2,1)}, u32[]{:S(2)}) copy-start(bf16[384,2,7168]{0,2,1:T(8,128)(2,1)} %copy-done.1) | copy-start | bytes 33030148
  144.8 15.0 %copy-start.4 = (s32[384]{0:T(512)S(1)}, s32[384]{0:T(512)}, u32[]{:S(2)}) copy-start(s32[384]{0:T(512)} %param.10) | copy-start | bytes 4612
  157.3 19.2 %collective-permute-start.13 = (bf16[896,512]{1,0:T(8,128)(2,1)}, bf16[896,512]{1,0:T(8,128)(2,1)S(1)}, u32[]{:S(2)}, u32[]{:S(2)}) collective-permute-start(bf16[896,512]{1,0:T(8,128)(2,1)} %collective-permute-done.11), channel_id=1, source_target_pairs={{0,224},{32,0},{64,32},{96,64},{128,96},{160,128},{192,160},{224,1... | collective-permute-start | bytes 2752520 | tf_op jit(solution)/shard_map/ppermute | solution.py:64
  160.1 19.8 %collective-permute-start.12 = (bf16[896,512]{1,0:T(8,128)(2,1)}, bf16[896,512]{1,0:T(8,128)(2,1)S(1)}, u32[]{:S(2)}, u32[]{:S(2)}) collective-permute-start(bf16[896,512]{1,0:T(8,128)(2,1)} %collective-permute-done.10), channel_id=1, source_target_pairs={{0,32},{32,64},{64,96},{96,128},{128,160},{160,192},{192,224},{224... | collective-permute-start | bytes 2752520 | tf_op jit(solution)/shard_map/ppermute | solution.py:63
  181.0 11.8 %copy-start.6 = (s32[16]{0:T(128)S(1)}, s32[16]{0:T(128)}, u32[]{:S(2)}) copy-start(s32[16]{0:T(128)} %param.9) | copy-start | bytes 196
  181.0 33.9 %copy-start.9 = (s32[16]{0:T(128)S(1)}, s32[16]{0:T(128)}, u32[]{:S(2)}) copy-start(s32[16]{0:T(128)} %param.11) | copy-start | bytes 196
  182.2 1.3 collective-permute-start.14
  183.5 3.7 %collective-permute-start.15 = (f32[3,384,2]{1,2,0:T(2,128)S(1)}, f32[3,384,2]{1,2,0:T(2,128)S(1)}, u32[]{:S(2)}, u32[]{:S(2)}) collective-permute-start(f32[3,384,2]{1,2,0:T(2,128)S(1)} %pad_maximum_fusion.2), channel_id=1, source_target_pairs={{0,2},{1,3},{2,0},{3,1},{4,6},{5,7},{6,4},{7,5},{8,10},{9,11},{10,... | collective-permute-start | bytes 27656 | tf_op jit(solution)/shard_map/ppermute | solution.py:79
  187.2 5.3 %collective-permute-start.16 = (f32[3,384,2]{1,2,0:T(2,128)S(1)}, f32[3,384,2]{1,2,0:T(2,128)S(1)}, u32[]{:S(2)}, u32[]{:S(2)}) collective-permute-start(f32[3,384,2]{1,2,0:T(2,128)S(1)} %pad_maximum_fusion.3), channel_id=1, source_target_pairs={{0,4},{1,5},{2,6},{3,7},{4,0},{5,1},{6,2},{7,3},{8,12},{9,13},{10,... | collective-permute-start | bytes 27656 | tf_op jit(solution)/shard_map/ppermute | solution.py:79
  192.5 3.7 %collective-permute-start.17 = (f32[3,384,2]{1,2,0:T(2,128)S(1)}, f32[3,384,2]{1,2,0:T(2,128)S(1)}, u32[]{:S(2)}, u32[]{:S(2)}) collective-permute-start(f32[3,384,2]{1,2,0:T(2,128)S(1)} %pad_maximum_fusion.4), channel_id=1, source_target_pairs={{0,8},{1,9},{2,10},{3,11},{4,12},{5,13},{6,14},{7,15},{8,0},{9,1},... | collective-permute-start | bytes 27656 | tf_op jit(solution)/shard_map/ppermute | solution.py:79
  196.3 5.3 %collective-permute-start.18 = (f32[3,384,2]{1,2,0:T(2,128)S(1)}, f32[3,384,2]{1,2,0:T(2,128)S(1)}, u32[]{:S(2)}, u32[]{:S(2)}) collective-permute-start(f32[3,384,2]{1,2,0:T(2,128)S(1)} %pad_maximum_fusion.5), channel_id=1, source_target_pairs={{0,16},{1,17},{2,18},{3,19},{4,20},{5,21},{6,22},{7,23},{8,24},{9,... | collective-permute-start | bytes 27656 | tf_op jit(solution)/shard_map/ppermute | solution.py:79
  201.8 3.7 %collective-permute-start.19 = (f32[3,16]{1,0:T(4,128)S(1)}, f32[3,16]{1,0:T(4,128)S(1)}, u32[]{:S(2)}, u32[]{:S(2)}) collective-permute-start(f32[3,16]{1,0:T(4,128)S(1)} %pad_maximum_fusion.6), channel_id=1, source_target_pairs={{0,32},{32,0},{64,96},{96,64},{128,160},{160,128},{192,224},{224,1... | collective-permute-start | bytes 584 | tf_op jit(solution)/shard_map/ppermute | solution.py:100
  205.5 4.6 %collective-permute-start.20 = (f32[3,16]{1,0:T(4,128)S(1)}, f32[3,16]{1,0:T(4,128)S(1)}, u32[]{:S(2)}, u32[]{:S(2)}) collective-permute-start(f32[3,16]{1,0:T(4,128)S(1)} %pad_maximum_fusion.7), channel_id=1, source_target_pairs={{0,64},{32,96},{64,0},{96,32},{128,192},{160,224},{192,128},{224,1... | collective-permute-start | bytes 584 | tf_op jit(solution)/shard_map/ppermute | solution.py:100
  210.1 7.6 %collective-permute-start.21 = (f32[3,16]{1,0:T(4,128)S(1)}, f32[3,16]{1,0:T(4,128)S(1)}, u32[]{:S(2)}, u32[]{:S(2)}) collective-permute-start(f32[3,16]{1,0:T(4,128)S(1)} %pad_maximum_fusion.8), channel_id=1, source_target_pairs={{0,128},{32,160},{64,192},{96,224},{128,0},{160,32},{192,64},{224,... | collective-permute-start | bytes 584 | tf_op jit(solution)/shard_map/ppermute | solution.py:100
Sparse Core Ops, SparseCore 0:
  9.9 66.8 all-gather.2

commit v15 on v14

--- a/solution.py
+++ b/solution.py
@@ -17,7 +17,19 @@
     col_index = lax.axis_index("col")
     row_index = lax.axis_index("row")
     full_hidden = lax.all_gather(hidden_in, "col", axis=2, tiled=True)
-    full_gain = lax.all_gather(final_gain, "col", axis=1, tiled=True)
+    n_col = lax.axis_size("col")
+    full_gain = final_gain
+    distance = 1
+    while distance < n_col:
+        partner = [(i, i ^ distance) for i in range(n_col)]
+        other = lax.ppermute(full_gain, "col", partner)
+        lower = (col_index // distance) % 2 == 0
+        full_gain = jnp.where(
+            lower,
+            jnp.concatenate([full_gain, other], axis=1),
+            jnp.concatenate([other, full_gain], axis=1),
+        )
+        distance *= 2
     forward = [(i, (i + 1) % n_row) for i in range(n_row)]
     backward = [(i, (i - 1) % n_row) for i in range(n_row)]
     left, right = unembed[:, :half], unembed[:, half:]
@@ -71,7 +83,6 @@
     picked = jnp.sum(
         jnp.where(targets[:, None, None] == vocab_ids[None, None, :], logits, 0.0), axis=2
     )
-    n_col = lax.axis_size("col")
     max_logit = row_max
     distance = 1
     while distance < n_col:

time: 226 us -> 212 us (0.938)
  blocking collectives: 24.7 us -> 0 us
  starting transfers between devices: 36.9 us -> 43.7 us
  waiting for transfers between devices: 106 us -> 109 us
    all_gather x1 -> x0, blocking collectives: 24.7 us -> none  [per_device(): full_gain = lax.all_gather(final_gain, 'col', axis=1, tiled=True)]
    ppermute x7, waiting for transfers between devices: 69.3 us -> 56 us  [per_device(): left = lax.ppermute(left, 'row', forward)]
    ppermute x0 -> x5, waiting for transfers between devices: none -> 9.43 us  [per_device(): other = lax.ppermute(full_gain, 'col', partner)]
    ppermute x0 -> x5, starting transfers between devices: none -> 7.66 us  [per_device(): other = lax.ppermute(full_gain, 'col', partner)]
    ppermute x7, waiting for transfers between devices: 12.7 us -> 18.3 us  [per_device(): right = lax.ppermute(right, 'row', backward)]
    ppermute x7, starting transfers between devices: 17.3 us -> 21.9 us  [per_device(): right = lax.ppermute(right, 'row', backward)]
    ppermute x7, starting transfers between devices: 8.05 us -> 3.73 us  [per_device(): left = lax.ppermute(left, 'row', forward)]
    ppermute x3, starting transfers between devices: 6.5 us -> 3.72 us  [per_device(): other = lax.ppermute(seq_stats, 'row', partner)]
  transfers between devices with their start and end apart: 23 -> 28, of which waited for: 17 -> 20; matrix products, arithmetic and copies ran while one was open for 17% -> 19% of each run, Pallas kernels for 0% -> 0%
where the time goes in v15:
time: 212 us; the launch traced here: 211 us
  waiting for transfers between devices  109 us (51%)
  starting transfers between devices  43.7 us (21%)
  matrix products  29.5 us (14%)
  between operations  13.7 us (6%)
  other arithmetic  12.5 us (6%)
  local copies, waits for them, and re-layouts  3.03 us (1%)
    ppermute x7, waiting for transfers between devices, per_device(): left = lax.ppermute(left, 'row', forward)  56 us
    dot_general x16, matrix products, block_logits(): jnp.einsum('tmd,dv->tmv', features[shard], block, preferred_element_type=...  29.5 us
    ppermute x7, starting transfers between devices, per_device(): right = lax.ppermute(right, 'row', backward)  21.9 us
    ppermute x7, waiting for transfers between devices, per_device(): right = lax.ppermute(right, 'row', backward)  18.3 us
    ppermute x5, waiting for transfers between devices, per_device(): lax.ppermute(jnp.stack([max_logit, exp_total, picked]), 'col', partner)  12.2 us
    ppermute x3, waiting for transfers between devices, per_device(): other = lax.ppermute(seq_stats, 'row', partner)  12.1 us
    ppermute x5, waiting for transfers between devices, per_device(): other = lax.ppermute(full_gain, 'col', partner)  9.43 us
    ppermute x5, starting transfers between devices, per_device(): other = lax.ppermute(full_gain, 'col', partner)  7.66 us
  transfers between devices with their start and end apart: 28, of which 20 were waited for; matrix products, arithmetic and copies ran while one was open for 19% of the time, Pallas kernels for 0%

profile of v15, /device:TPU:2, one launch (start us, length us, event | category | flops | bytes accessed | tf_op | source)
XLA Modules:
  0.0 211.3 jit_solution(5664511896212416527)
XLA Ops:
  7.3 1.6 fusion.118
  8.8 2.0 collective-permute-start
  10.8 4.0 %collective-permute-start.1 = (bf16[896,512]{1,0:T(8,128)(2,1)S(1)}, bf16[896,512]{1,0:T(8,128)(2,1)}, u32[]{:S(2)}, u32[]{:S(2)}) collective-permute-start(bf16[896,512]{1,0:T(8,128)(2,1)S(1)} %get-tuple-element.34), channel_id=1, source_target_pairs={{0,224},{32,0},{64,32},{96,64},{128,96},{160,128},{192,160},{224,1... | collective-permute-start | bytes 2752520 | tf_op jit(solution)/shard_map/ppermute | solution.py:76
  14.9 1.2 collective-permute-done.4
  16.7 3.1 %collective-permute-done.5 = f32[2,448]{1,0:T(2,128)S(1)} collective-permute-done((f32[2,448]{1,0:T(2,128)S(1)}, f32[2,448]{1,0:T(2,128)S(1)}, u32[]{:S(2)}, u32[]{:S(2)}) %collective-permute-start.5) | collective-permute-done | bytes 3616 | tf_op jit(solution)/shard_map/ppermute | solution.py:25
  19.8 2.2 %collective-permute-start.6 = (f32[2,896]{1,0:T(2,128)S(1)}, f32[2,896]{1,0:T(2,128)S(1)}, u32[]{:S(2)}, u32[]{:S(2)}) collective-permute-start(f32[2,896]{1,0:T(2,128)S(1)} %maximum_select_fusion.3), channel_id=1, source_target_pairs={{0,4},{1,5},{2,6},{3,7},{4,0},{5,1},{6,2},{7,3},{8,12},{9,13},{10,... | collective-permute-start | bytes 21512 | tf_op jit(solution)/shard_map/ppermute | solution.py:25
  22.0 3.0 %collective-permute-done.6 = f32[2,896]{1,0:T(2,128)S(1)} collective-permute-done((f32[2,896]{1,0:T(2,128)S(1)}, f32[2,896]{1,0:T(2,128)S(1)}, u32[]{:S(2)}, u32[]{:S(2)}) %collective-permute-start.6) | collective-permute-done | bytes 7200 | tf_op jit(solution)/shard_map/ppermute | solution.py:25
  25.0 1.7 collective-permute-start.7
  26.7 8.5 %collective-permute-done = bf16[896,512]{1,0:T(8,128)(2,1)S(1)} collective-permute-done((bf16[896,512]{1,0:T(8,128)(2,1)S(1)}, bf16[896,512]{1,0:T(8,128)(2,1)S(1)}, u32[]{:S(2)}, u32[]{:S(2)}) %collective-permute-start) | collective-permute-done | bytes 917536 | tf_op jit(solution)/shard_map/ppermute | solution.py:75
  35.1 3.2 %collective-permute-start.3 = (bf16[896,512]{1,0:T(8,128)(2,1)}, bf16[896,512]{1,0:T(8,128)(2,1)}, u32[]{:S(2)}, u32[]{:S(2)}) collective-permute-start(bf16[896,512]{1,0:T(8,128)(2,1)} %collective-permute-done.1), channel_id=1, source_target_pairs={{0,224},{32,0},{64,32},{96,64},{128,96},{160,128},{192,160},{224,1... | collective-permute-start | bytes 2752520 | tf_op jit(solution)/shard_map/ppermute | solution.py:76
  38.4 3.3 %collective-permute-start.8 = (f32[2,3584]{1,0:T(2,128)S(1)}, f32[2,3584]{1,0:T(2,128)S(1)}, u32[]{:S(2)}, u32[]{:S(2)}) collective-permute-start(f32[2,3584]{1,0:T(2,128)S(1)} %maximum_select_fusion.1), channel_id=1, source_target_pairs={{0,16},{1,17},{2,18},{3,19},{4,20},{5,21},{6,22},{7,23},{8,24},{9,... | collective-permute-start | bytes 86024 | tf_op jit(solution)/shard_map/ppermute | solution.py:25
  41.7 2.2 %collective-permute-done.8 = f32[2,3584]{1,0:T(2,128)S(1)} collective-permute-done((f32[2,3584]{1,0:T(2,128)S(1)}, f32[2,3584]{1,0:T(2,128)S(1)}, u32[]{:S(2)}, u32[]{:S(2)}) %collective-permute-start.8) | collective-permute-done | bytes 28704 | tf_op jit(solution)/shard_map/ppermute | solution.py:25
  43.9 14.1 %collective-permute-done.2 = bf16[896,512]{1,0:T(8,128)(2,1)S(1)} collective-permute-done((bf16[896,512]{1,0:T(8,128)(2,1)S(1)}, bf16[896,512]{1,0:T(8,128)(2,1)S(1)}, u32[]{:S(2)}, u32[]{:S(2)}) %collective-permute-start.2) | collective-permute-done | bytes 917536 | tf_op jit(solution)/shard_map/ppermute | solution.py:75
  58.0 3.3 %collective-permute-start.10 = (bf16[896,512]{1,0:T(8,128)(2,1)}, bf16[896,512]{1,0:T(8,128)(2,1)}, u32[]{:S(2)}, u32[]{:S(2)}) collective-permute-start(bf16[896,512]{1,0:T(8,128)(2,1)} %collective-permute-done.3), channel_id=1, source_target_pairs={{0,224},{32,0},{64,32},{96,64},{128,96},{160,128},{192,160},{224,1... | collective-permute-start | bytes 2752520 | tf_op jit(solution)/shard_map/ppermute | solution.py:76
  61.2 18.3 %collective-permute-done.10 = bf16[896,512]{1,0:T(8,128)(2,1)} collective-permute-done((bf16[896,512]{1,0:T(8,128)(2,1)}, bf16[896,512]{1,0:T(8,128)(2,1)}, u32[]{:S(2)}, u32[]{:S(2)}) %collective-permute-start.10) | collective-permute-done | bytes 917536 | tf_op jit(solution)/shard_map/ppermute | solution.py:76
  79.6 3.2 %collective-permute-done.9 = bf16[896,512]{1,0:T(8,128)(2,1)} collective-permute-done((bf16[896,512]{1,0:T(8,128)(2,1)S(1)}, bf16[896,512]{1,0:T(8,128)(2,1)}, u32[]{:S(2)}, u32[]{:S(2)}) %collective-permute-start.9) | collective-permute-done | bytes 917536 | tf_op jit(solution)/shard_map/ppermute | solution.py:75
  82.8 3.2 %collective-permute-start.12 = (bf16[896,512]{1,0:T(8,128)(2,1)}, bf16[896,512]{1,0:T(8,128)(2,1)}, u32[]{:S(2)}, u32[]{:S(2)}) collective-permute-start(bf16[896,512]{1,0:T(8,128)(2,1)} %collective-permute-done.10), channel_id=1, source_target_pairs={{0,224},{32,0},{64,32},{96,64},{128,96},{160,128},{192,160},{224,1... | collective-permute-start | bytes 2752520 | tf_op jit(solution)/shard_map/ppermute | solution.py:76
  86.0 6.5 %fusion = f32[384,2]{0,1:T(2,128)S(1)} fusion(bf16[384,2,7168]{0,2,1:T(8,128)(2,1)} %all-gather.2.cloned.1.call-done), kind=kLoop, calls=%fused_computation.2 | loop fusion | flops 16514304 | bytes 11013120 | tf_op jit(solution)/shard_map/reduce_sum | solution.py:60
  93.3 3.1 %fusion.2 = bf16[384,2,7168]{0,2,1:T(8,128)(2,1)S(1)} fusion(bf16[384,2,7168]{0,2,1:T(8,128)(2,1)S(1)} %copy-done, f32[2,7168]{1,0:T(2,128)S(1)} %maximum_select_fusion, f32[384,2]{0,1:T(2,128)S(1)} %add_rsqrt_fusion), kind=kLoop, calls=%fused_computation.4 | loop fusion | flops 22020096 | bytes 22080512 | tf_op jit(solution)/shard_map/convert_element_type | solution.py:63
  96.4 7.3 %collective-permute-done.11 = bf16[896,512]{1,0:T(8,128)(2,1)} collective-permute-done((bf16[896,512]{1,0:T(8,128)(2,1)}, bf16[896,512]{1,0:T(8,128)(2,1)}, u32[]{:S(2)}, u32[]{:S(2)}) %collective-permute-start.11) | collective-permute-done | bytes 917536 | tf_op jit(solution)/shard_map/ppermute | solution.py:75
  105.8 3.2 %collective-permute-start.14 = (bf16[896,512]{1,0:T(8,128)(2,1)}, bf16[896,512]{1,0:T(8,128)(2,1)}, u32[]{:S(2)}, u32[]{:S(2)}) collective-permute-start(bf16[896,512]{1,0:T(8,128)(2,1)} %collective-permute-done.12), channel_id=1, source_target_pairs={{0,224},{32,0},{64,32},{96,64},{128,96},{160,128},{192,160},{224,1... | collective-permute-start | bytes 2752520 | tf_op jit(solution)/shard_map/ppermute | solution.py:76
  109.0 2.2 %fusion.21 = f32[384,2,512]{2,0,1:T(8,128)S(1)} fusion(bf16[384,2,8,896]{0,3,2,1:T(8,128)(2,1)S(1)} %bitcast.291, s32[]{:T(128)S(6)} %select_n.237, bf16[896,512]{1,0:T(8,128)(2,1)} %collective-permute-done.10), kind=kOutput, calls=%fused_computation.26 | convolution fusion | flops 704643072 | bytes 3866628 | tf_op jit(solution)/shard_map/tmd,dv->tmv/dot_general | solution.py:42
  111.2 2.2 %fusion.23 = f32[384,2,512]{2,0,1:T(8,128)S(1)} fusion(bf16[384,2,8,896]{0,3,2,1:T(8,128)(2,1)S(1)} %bitcast.292, s32[]{:T(128)S(6)} %select_n.235, bf16[896,512]{1,0:T(8,128)(2,1)} %collective-permute-done.3), kind=kOutput, calls=%fused_computation.28 | convolution fusion | flops 704643072 | bytes 3866628 | tf_op jit(solution)/shard_map/tmd,dv->tmv/dot_general | solution.py:42
  113.4 2.3 %fusion.25 = f32[384,2,512]{2,0,1:T(8,128)S(1)} fusion(bf16[384,2,8,896]{0,3,2,1:T(8,128)(2,1)S(1)} %bitcast.293, s32[]{:T(128)S(6)} %select_n.233, bf16[896,512]{1,0:T(8,128)(2,1)} %collective-permute-done.1), kind=kOutput, calls=%fused_computation.30 | convolution fusion | flops 704643072 | bytes 3866628 | tf_op jit(solution)/shard_map/tmd,dv->tmv/dot_general | solution.py:42
  117.7 2.2 %fusion.29 = f32[384,2,512]{2,0,1:T(8,128)S(1)} fusion(bf16[384,2,8,896]{0,3,2,1:T(8,128)(2,1)S(1)} %bitcast.296, s32[]{:T(128)S(6)} %select_n.229, bf16[896,512]{1,0:T(8,128)(2,1)} %collective-permute-done.9), kind=kOutput, calls=%fused_computation.34 | convolution fusion | flops 704643072 | bytes 3866628 | tf_op jit(solution)/shard_map/tmd,dv->tmv/dot_general | solution.py:42
  119.9 2.3 %add_add_fusion.2 = f32[384,2,512]{2,0,1:T(8,128)S(1)} fusion(f32[384,2,512]{2,0,1:T(8,128)S(1)} %fusion.21, f32[384,2,512]{2,0,1:T(8,128)S(1)} %fusion.23, f32[384,2,512]{2,0,1:T(8,128)S(1)} %fusion.35, f32[384,2,512]{2,0,1:T(8,128)S(1)} %fusion.25, bf16[384,2,8,896]{0,3,2,1:T(8,128)(2,1)S(1)} %bitcast.297, s32[]{:T(128)S(6)} %select_n.239, ...), kind=kOutput, calls=%fused_computation.10 | convolution fusion | flops 706215936 | bytes 10158084 | tf_op jit(solution)/shard_map/tmd,dv->tmv/dot_general | solution.py:42
  122.3 2.3 %add_add_fusion.3 = f32[384,2,512]{2,0,1:T(8,128)S(1)} fusion(f32[384,2,512]{2,0,1:T(8,128)S(1)} %fusion.29, f32[384,2,512]{2,0,1:T(8,128)S(1)} %fusion.31, f32[384,2,512]{2,0,1:T(8,128)S(1)} %fusion.37, f32[384,2,512]{2,0,1:T(8,128)S(1)} %fusion.33, bf16[384,2,8,896]{0,3,2,1:T(8,128)(2,1)S(1)} %bitcast.298, s32[]{:T(128)S(6)} %select_n.231, ...), kind=kOutput, calls=%fused_computation.11 | convolution fusion | flops 706215936 | bytes 10158084 | tf_op jit(solution)/shard_map/tmd,dv->tmv/dot_general | solution.py:42
  124.6 1.6 collective-permute-done.13
  127.3 2.2 %collective-permute-start.16 = (bf16[896,512]{1,0:T(8,128)(2,1)}, bf16[896,512]{1,0:T(8,128)(2,1)}, u32[]{:S(2)}, u32[]{:S(2)}) collective-permute-start(bf16[896,512]{1,0:T(8,128)(2,1)} %collective-permute-done.14), channel_id=1, source_target_pairs={{0,224},{32,0},{64,32},{96,64},{128,96},{160,128},{192,160},{224,1... | collective-permute-start | bytes 2752520 | tf_op jit(solution)/shard_map/ppermute | solution.py:76
  129.5 2.6 %fusion.15 = f32[384,2,512]{2,0,1:T(8,128)S(1)} fusion(bf16[384,2,8,896]{0,3,2,1:T(8,128)(2,1)} %bitcast.299, s32[]{:T(128)S(6)} %select_n.243, bf16[896,512]{1,0:T(8,128)(2,1)} %collective-permute-done.14), kind=kOutput, calls=%fused_computation.20 | convolution fusion | flops 704643072 | bytes 3866628 | tf_op jit(solution)/shard_map/tmd,dv->tmv/dot_general | solution.py:42
  132.5 2.8 %fusion.17 = f32[384,2,512]{2,0,1:T(8,128)S(1)} fusion(bf16[384,2,8,896]{0,3,2,1:T(8,128)(2,1)} %bitcast.300, s32[]{:T(128)S(6)} %select_n.241, bf16[896,512]{1,0:T(8,128)(2,1)} %collective-permute-done.13), kind=kOutput, calls=%fused_computation.22 | convolution fusion | flops 704643072 | bytes 3866628 | tf_op jit(solution)/shard_map/tmd,dv->tmv/dot_general | solution.py:42
  135.6 11.2 %collective-permute-done.15 = bf16[896,512]{1,0:T(8,128)(2,1)} collective-permute-done((bf16[896,512]{1,0:T(8,128)(2,1)}, bf16[896,512]{1,0:T(8,128)(2,1)}, u32[]{:S(2)}, u32[]{:S(2)}) %collective-permute-start.15) | collective-permute-done | bytes 917536 | tf_op jit(solution)/shard_map/ppermute | solution.py:75
  147.7 2.7 %collective-permute-start.18 = (bf16[896,512]{1,0:T(8,128)(2,1)}, bf16[896,512]{1,0:T(8,128)(2,1)S(1)}, u32[]{:S(2)}, u32[]{:S(2)}) collective-permute-start(bf16[896,512]{1,0:T(8,128)(2,1)} %collective-permute-done.16), channel_id=1, source_target_pairs={{0,224},{32,0},{64,32},{96,64},{128,96},{160,128},{192,160},{224,1... | collective-permute-start | bytes 2752520 | tf_op jit(solution)/shard_map/ppermute | solution.py:76
  150.4 2.2 %fusion.13 = f32[384,2,512]{2,0,1:T(8,128)S(1)} fusion(bf16[384,2,8,896]{0,3,2,1:T(8,128)(2,1)S(1)} %bitcast.301, s32[]{:T(128)S(6)} %select_n.245, bf16[896,512]{1,0:T(8,128)(2,1)} %collective-permute-done.15), kind=kOutput, calls=%fused_computation.18 | convolution fusion | flops 704643072 | bytes 3866628 | tf_op jit(solution)/shard_map/tmd,dv->tmv/dot_general | solution.py:42
  152.6 2.2 %fusion.7 = f32[384,2,512]{2,0,1:T(8,128)S(1)} fusion(bf16[384,2,8,896]{0,3,2,1:T(8,128)(2,1)S(1)} %bitcast.302, s32[]{:T(128)S(6)} %select_n.249, bf16[896,512]{1,0:T(8,128)(2,1)} %collective-permute-done.16), kind=kOutput, calls=%fused_computation.14 | convolution fusion | flops 704643072 | bytes 3866628 | tf_op jit(solution)/shard_map/tmd,dv->tmv/dot_general | solution.py:42
  154.8 10.2 %collective-permute-done.17 = bf16[896,512]{1,0:T(8,128)(2,1)S(1)} collective-permute-done((bf16[896,512]{1,0:T(8,128)(2,1)}, bf16[896,512]{1,0:T(8,128)(2,1)S(1)}, u32[]{:S(2)}, u32[]{:S(2)}) %collective-permute-start.17) | collective-permute-done | bytes 917536 | tf_op jit(solution)/shard_map/ppermute | solution.py:75
  168.5 1.2 collective-permute-done.19
  169.9 3.5 %collective-permute-done.20 = f32[3,384,2]{1,2,0:T(2,128)S(1)} collective-permute-done((f32[3,384,2]{1,2,0:T(2,128)S(1)}, f32[3,384,2]{1,2,0:T(2,128)S(1)}, u32[]{:S(2)}, u32[]{:S(2)}) %collective-permute-start.20) | collective-permute-done | bytes 9248 | tf_op jit(solution)/shard_map/ppermute | solution.py:90
  173.4 2.2 %collective-permute-start.21 = (f32[3,384,2]{1,2,0:T(2,128)S(1)}, f32[3,384,2]{1,2,0:T(2,128)S(1)}, u32[]{:S(2)}, u32[]{:S(2)}) collective-permute-start(f32[3,384,2]{1,2,0:T(2,128)S(1)} %pad_maximum_fusion.3), channel_id=1, source_target_pairs={{0,4},{1,5},{2,6},{3,7},{4,0},{5,1},{6,2},{7,3},{8,12},{9,13},{10,... | collective-permute-start | bytes 27656 | tf_op jit(solution)/shard_map/ppermute | solution.py:90
  175.7 3.0 %collective-permute-done.21 = f32[3,384,2]{1,2,0:T(2,128)S(1)} collective-permute-done((f32[3,384,2]{1,2,0:T(2,128)S(1)}, f32[3,384,2]{1,2,0:T(2,128)S(1)}, u32[]{:S(2)}, u32[]{:S(2)}) %collective-permute-start.21) | collective-permute-done | bytes 9248 | tf_op jit(solution)/shard_map/ppermute | solution.py:90
  178.7 1.2 collective-permute-start.22
  180.2 2.3 %collective-permute-done.22 = f32[3,384,2]{1,2,0:T(2,128)S(1)} collective-permute-done((f32[3,384,2]{1,2,0:T(2,128)S(1)}, f32[3,384,2]{1,2,0:T(2,128)S(1)}, u32[]{:S(2)}, u32[]{:S(2)}) %collective-permute-start.22) | collective-permute-done | bytes 9248 | tf_op jit(solution)/shard_map/ppermute | solution.py:90
  182.5 2.9 %collective-permute-start.23 = (f32[3,384,2]{1,2,0:T(2,128)S(1)}, f32[3,384,2]{1,2,0:T(2,128)S(1)}, u32[]{:S(2)}, u32[]{:S(2)}) collective-permute-start(f32[3,384,2]{1,2,0:T(2,128)S(1)} %pad_maximum_fusion.5), channel_id=1, source_target_pairs={{0,16},{1,17},{2,18},{3,19},{4,20},{5,21},{6,22},{7,23},{8,24},{9,... | collective-permute-start | bytes 27656 | tf_op jit(solution)/shard_map/ppermute | solution.py:90
  185.5 2.2 %collective-permute-done.23 = f32[3,384,2]{1,2,0:T(2,128)S(1)} collective-permute-done((f32[3,384,2]{1,2,0:T(2,128)S(1)}, f32[3,384,2]{1,2,0:T(2,128)S(1)}, u32[]{:S(2)}, u32[]{:S(2)}) %collective-permute-start.23) | collective-permute-done | bytes 9248 | tf_op jit(solution)/shard_map/ppermute | solution.py:90
  188.1 3.6 %collective-permute-done.24 = f32[3,16]{1,0:T(4,128)S(1)} collective-permute-done((f32[3,16]{1,0:T(4,128)S(1)}, f32[3,16]{1,0:T(4,128)S(1)}, u32[]{:S(2)}, u32[]{:S(2)}) %collective-permute-start.24) | collective-permute-done | bytes 224 | tf_op jit(solution)/shard_map/ppermute | solution.py:111
  192.5 3.8 %collective-permute-done.25 = f32[3,16]{1,0:T(4,128)S(1)} collective-permute-done((f32[3,16]{1,0:T(4,128)S(1)}, f32[3,16]{1,0:T(4,128)S(1)}, u32[]{:S(2)}, u32[]{:S(2)}) %collective-permute-start.25) | collective-permute-done | bytes 224 | tf_op jit(solution)/shard_map/ppermute | solution.py:111
  196.3 2.8 %collective-permute-start.26 = (f32[3,16]{1,0:T(4,128)S(1)}, f32[3,16]{1,0:T(4,128)S(1)}, u32[]{:S(2)}, u32[]{:S(2)}) collective-permute-start(f32[3,16]{1,0:T(4,128)S(1)} %pad_maximum_fusion.8), channel_id=1, source_target_pairs={{0,128},{32,160},{64,192},{96,224},{128,0},{160,32},{192,64},{224,... | collective-permute-start | bytes 584 | tf_op jit(solution)/shard_map/ppermute | solution.py:111
  199.1 4.7 %collective-permute-done.26 = f32[3,16]{1,0:T(4,128)S(1)} collective-permute-done((f32[3,16]{1,0:T(4,128)S(1)}, f32[3,16]{1,0:T(4,128)S(1)}, u32[]{:S(2)}, u32[]{:S(2)}) %collective-permute-start.26) | collective-permute-done | bytes 224 | tf_op jit(solution)/shard_map/ppermute | solution.py:111
  (86 shorter events, 14.9 us)
Async XLA Ops:
  6.5 79.5 %all-gather.2.cloned.1.call-start = ((), (), s32[]{:S(2)}) async-start(), calls=%async_computation | async-start | bytes 11354112 | tf_op jit(solution)/shard_map/all_gather | solution.py:19
  7.3 7.6 %copy-start.5 = (f32[2,224]{1,0:T(2,128)S(1)}, f32[2,224]{1,0:T(2,128)}, u32[]{:S(2)}) copy-start(f32[2,224]{1,0:T(2,128)} %param.7) | copy-start | bytes 5380
  8.8 26.3 %collective-permute-start = (bf16[896,512]{1,0:T(8,128)(2,1)S(1)}, bf16[896,512]{1,0:T(8,128)(2,1)S(1)}, u32[]{:S(2)}, u32[]{:S(2)}) collective-permute-start(bf16[896,512]{1,0:T(8,128)(2,1)S(1)} %get-tuple-element.33), channel_id=1, source_target_pairs={{0,32},{32,64},{64,96},{96,128},{128,160},{160,192},{192,224},{224... | collective-permute-start | bytes 2752520 | tf_op jit(solution)/shard_map/ppermute | solution.py:75
  10.8 24.3 %collective-permute-start.1 = (bf16[896,512]{1,0:T(8,128)(2,1)S(1)}, bf16[896,512]{1,0:T(8,128)(2,1)}, u32[]{:S(2)}, u32[]{:S(2)}) collective-permute-start(bf16[896,512]{1,0:T(8,128)(2,1)S(1)} %get-tuple-element.34), channel_id=1, source_target_pairs={{0,224},{32,0},{64,32},{96,64},{128,96},{160,128},{192,160},{224,1... | collective-permute-start | bytes 2752520 | tf_op jit(solution)/shard_map/ppermute | solution.py:76
  14.9 1.2 collective-permute-start.4
  16.1 3.6 %collective-permute-start.5 = (f32[2,448]{1,0:T(2,128)S(1)}, f32[2,448]{1,0:T(2,128)S(1)}, u32[]{:S(2)}, u32[]{:S(2)}) collective-permute-start(f32[2,448]{1,0:T(2,128)S(1)} %maximum_select_fusion.4), channel_id=1, source_target_pairs={{0,2},{1,3},{2,0},{3,1},{4,6},{5,7},{6,4},{7,5},{8,10},{9,11},{10,... | collective-permute-start | bytes 10760 | tf_op jit(solution)/shard_map/ppermute | solution.py:25
  19.8 5.2 %collective-permute-start.6 = (f32[2,896]{1,0:T(2,128)S(1)}, f32[2,896]{1,0:T(2,128)S(1)}, u32[]{:S(2)}, u32[]{:S(2)}) collective-permute-start(f32[2,896]{1,0:T(2,128)S(1)} %maximum_select_fusion.3), channel_id=1, source_target_pairs={{0,4},{1,5},{2,6},{3,7},{4,0},{5,1},{6,2},{7,3},{8,12},{9,13},{10,... | collective-permute-start | bytes 21512 | tf_op jit(solution)/shard_map/ppermute | solution.py:25
  25.0 13.4 %collective-permute-start.7 = (f32[2,1792]{1,0:T(2,128)S(1)}, f32[2,1792]{1,0:T(2,128)S(1)}, u32[]{:S(2)}, u32[]{:S(2)}) collective-permute-start(f32[2,1792]{1,0:T(2,128)S(1)} %maximum_select_fusion.2), channel_id=1, source_target_pairs={{0,8},{1,9},{2,10},{3,11},{4,12},{5,13},{6,14},{7,15},{8,0},{9,1},... | collective-permute-start | bytes 43016 | tf_op jit(solution)/shard_map/ppermute | solution.py:25
  35.1 22.8 %collective-permute-start.2 = (bf16[896,512]{1,0:T(8,128)(2,1)S(1)}, bf16[896,512]{1,0:T(8,128)(2,1)S(1)}, u32[]{:S(2)}, u32[]{:S(2)}) collective-permute-start(bf16[896,512]{1,0:T(8,128)(2,1)S(1)} %collective-permute-done), channel_id=1, source_target_pairs={{0,32},{32,64},{64,96},{96,128},{128,160},{160,192},{192,224},{224... | collective-permute-start | bytes 2752520 | tf_op jit(solution)/shard_map/ppermute | solution.py:75
  35.1 22.8 %collective-permute-start.3 = (bf16[896,512]{1,0:T(8,128)(2,1)}, bf16[896,512]{1,0:T(8,128)(2,1)}, u32[]{:S(2)}, u32[]{:S(2)}) collective-permute-start(bf16[896,512]{1,0:T(8,128)(2,1)} %collective-permute-done.1), channel_id=1, source_target_pairs={{0,224},{32,0},{64,32},{96,64},{128,96},{160,128},{192,160},{224,1... | collective-permute-start | bytes 2752520 | tf_op jit(solution)/shard_map/ppermute | solution.py:76
  38.4 5.5 %collective-permute-start.8 = (f32[2,3584]{1,0:T(2,128)S(1)}, f32[2,3584]{1,0:T(2,128)S(1)}, u32[]{:S(2)}, u32[]{:S(2)}) collective-permute-start(f32[2,3584]{1,0:T(2,128)S(1)} %maximum_select_fusion.1), channel_id=1, source_target_pairs={{0,16},{1,17},{2,18},{3,19},{4,20},{5,21},{6,22},{7,23},{8,24},{9,... | collective-permute-start | bytes 86024 | tf_op jit(solution)/shard_map/ppermute | solution.py:25
  58.0 28.0 %copy-start.7 = (bf16[896,512]{1,0:T(8,128)(2,1)}, bf16[896,512]{1,0:T(8,128)(2,1)S(1)}, u32[]{:S(2)}) copy-start(bf16[896,512]{1,0:T(8,128)(2,1)S(1)} %collective-permute-done.2) | copy-start | bytes 2752516
  58.0 21.6 %collective-permute-start.10 = (bf16[896,512]{1,0:T(8,128)(2,1)}, bf16[896,512]{1,0:T(8,128)(2,1)}, u32[]{:S(2)}, u32[]{:S(2)}) collective-permute-start(bf16[896,512]{1,0:T(8,128)(2,1)} %collective-permute-done.3), channel_id=1, source_target_pairs={{0,224},{32,0},{64,32},{96,64},{128,96},{160,128},{192,160},{224,1... | collective-permute-start | bytes 2752520 | tf_op jit(solution)/shard_map/ppermute | solution.py:76
  61.2 21.5 %collective-permute-start.9 = (bf16[896,512]{1,0:T(8,128)(2,1)S(1)}, bf16[896,512]{1,0:T(8,128)(2,1)}, u32[]{:S(2)}, u32[]{:S(2)}) collective-permute-start(bf16[896,512]{1,0:T(8,128)(2,1)S(1)} %collective-permute-done.2), channel_id=1, source_target_pairs={{0,32},{32,64},{64,96},{96,128},{128,160},{160,192},{192,224},{224... | collective-permute-start | bytes 2752520 | tf_op jit(solution)/shard_map/ppermute | solution.py:75
  82.8 20.9 %collective-permute-start.11 = (bf16[896,512]{1,0:T(8,128)(2,1)}, bf16[896,512]{1,0:T(8,128)(2,1)}, u32[]{:S(2)}, u32[]{:S(2)}) collective-permute-start(bf16[896,512]{1,0:T(8,128)(2,1)} %collective-permute-done.9), channel_id=1, source_target_pairs={{0,32},{32,64},{64,96},{96,128},{128,160},{160,192},{192,224},{224... | collective-permute-start | bytes 2752520 | tf_op jit(solution)/shard_map/ppermute | solution.py:75
  82.8 20.9 %collective-permute-start.12 = (bf16[896,512]{1,0:T(8,128)(2,1)}, bf16[896,512]{1,0:T(8,128)(2,1)}, u32[]{:S(2)}, u32[]{:S(2)}) collective-permute-start(bf16[896,512]{1,0:T(8,128)(2,1)} %collective-permute-done.10), channel_id=1, source_target_pairs={{0,224},{32,0},{64,32},{96,64},{128,96},{160,128},{192,160},{224,1... | collective-permute-start | bytes 2752520 | tf_op jit(solution)/shard_map/ppermute | solution.py:76
  86.0 7.3 %copy-start = (bf16[384,2,7168]{0,2,1:T(8,128)(2,1)S(1)}, bf16[384,2,7168]{0,2,1:T(8,128)(2,1)}, u32[]{:S(2)}) copy-start(bf16[384,2,7168]{0,2,1:T(8,128)(2,1)} %all-gather.2.cloned.1.call-done) | copy-start | bytes 33030148
  93.3 10.4 %copy-start.3 = (bf16[896,1024]{1,0:T(8,128)(2,1)S(1)}, bf16[896,1024]{1,0:T(8,128)(2,1)}, u32[]{:S(2)}) copy-start(bf16[896,1024]{1,0:T(8,128)(2,1)} %param.8) | copy-start | bytes 5505028
  96.4 25.9 %copy-start.1 = (bf16[384,2,7168]{0,2,1:T(8,128)(2,1)}, bf16[384,2,7168]{0,2,1:T(8,128)(2,1)S(1)}, u32[]{:S(2)}) copy-start(bf16[384,2,7168]{0,2,1:T(8,128)(2,1)S(1)} %fusion.2) | copy-start | bytes 33030148
  105.7 20.6 %collective-permute-start.13 = (bf16[896,512]{1,0:T(8,128)(2,1)}, bf16[896,512]{1,0:T(8,128)(2,1)}, u32[]{:S(2)}, u32[]{:S(2)}) collective-permute-start(bf16[896,512]{1,0:T(8,128)(2,1)} %collective-permute-done.11), channel_id=1, source_target_pairs={{0,32},{32,64},{64,96},{96,128},{128,160},{160,192},{192,224},{224... | collective-permute-start | bytes 2752520 | tf_op jit(solution)/shard_map/ppermute | solution.py:75
  105.8 20.5 %collective-permute-start.14 = (bf16[896,512]{1,0:T(8,128)(2,1)}, bf16[896,512]{1,0:T(8,128)(2,1)}, u32[]{:S(2)}, u32[]{:S(2)}) collective-permute-start(bf16[896,512]{1,0:T(8,128)(2,1)} %collective-permute-done.12), channel_id=1, source_target_pairs={{0,224},{32,0},{64,32},{96,64},{128,96},{160,128},{192,160},{224,1... | collective-permute-start | bytes 2752520 | tf_op jit(solution)/shard_map/ppermute | solution.py:76
  113.4 2.3 %copy-start.8 = (bf16[896,512]{1,0:T(8,128)(2,1)S(1)}, bf16[896,512]{1,0:T(8,128)(2,1)}, u32[]{:S(2)}) copy-start(bf16[896,512]{1,0:T(8,128)(2,1)} %copy-done.7) | copy-start | bytes 2752516
  126.3 20.5 %collective-permute-start.15 = (bf16[896,512]{1,0:T(8,128)(2,1)}, bf16[896,512]{1,0:T(8,128)(2,1)}, u32[]{:S(2)}, u32[]{:S(2)}) collective-permute-start(bf16[896,512]{1,0:T(8,128)(2,1)} %collective-permute-done.13), channel_id=1, source_target_pairs={{0,32},{32,64},{64,96},{96,128},{128,160},{160,192},{192,224},{224... | collective-permute-start | bytes 2752520 | tf_op jit(solution)/shard_map/ppermute | solution.py:75
  127.3 19.5 %collective-permute-start.16 = (bf16[896,512]{1,0:T(8,128)(2,1)}, bf16[896,512]{1,0:T(8,128)(2,1)}, u32[]{:S(2)}, u32[]{:S(2)}) collective-permute-start(bf16[896,512]{1,0:T(8,128)(2,1)} %collective-permute-done.14), channel_id=1, source_target_pairs={{0,224},{32,0},{64,32},{96,64},{128,96},{160,128},{192,160},{224,1... | collective-permute-start | bytes 2752520 | tf_op jit(solution)/shard_map/ppermute | solution.py:76
  132.1 18.3 %copy-start.2 = (bf16[384,2,7168]{0,2,1:T(8,128)(2,1)S(1)}, bf16[384,2,7168]{0,2,1:T(8,128)(2,1)}, u32[]{:S(2)}) copy-start(bf16[384,2,7168]{0,2,1:T(8,128)(2,1)} %copy-done.1) | copy-start | bytes 33030148
  135.2 12.2 %copy-start.4 = (s32[384]{0:T(512)S(1)}, s32[384]{0:T(512)}, u32[]{:S(2)}) copy-start(s32[384]{0:T(512)} %param.10) | copy-start | bytes 4612
  146.8 18.2 %collective-permute-start.17 = (bf16[896,512]{1,0:T(8,128)(2,1)}, bf16[896,512]{1,0:T(8,128)(2,1)S(1)}, u32[]{:S(2)}, u32[]{:S(2)}) collective-permute-start(bf16[896,512]{1,0:T(8,128)(2,1)} %collective-permute-done.15), channel_id=1, source_target_pairs={{0,32},{32,64},{64,96},{96,128},{128,160},{160,192},{192,224},{224... | collective-permute-start | bytes 2752520 | tf_op jit(solution)/shard_map/ppermute | solution.py:75
  147.7 18.4 %collective-permute-start.18 = (bf16[896,512]{1,0:T(8,128)(2,1)}, bf16[896,512]{1,0:T(8,128)(2,1)S(1)}, u32[]{:S(2)}, u32[]{:S(2)}) collective-permute-start(bf16[896,512]{1,0:T(8,128)(2,1)} %collective-permute-done.16), channel_id=1, source_target_pairs={{0,224},{32,0},{64,32},{96,64},{128,96},{160,128},{192,160},{224,1... | collective-permute-start | bytes 2752520 | tf_op jit(solution)/shard_map/ppermute | solution.py:76
  167.2 12.8 %copy-start.6 = (s32[16]{0:T(128)S(1)}, s32[16]{0:T(128)}, u32[]{:S(2)}) copy-start(s32[16]{0:T(128)} %param.9) | copy-start | bytes 196
  167.2 31.9 %copy-start.9 = (s32[16]{0:T(128)S(1)}, s32[16]{0:T(128)}, u32[]{:S(2)}) copy-start(s32[16]{0:T(128)} %param.11) | copy-start | bytes 196
  168.4 1.3 collective-permute-start.19
  169.7 3.7 %collective-permute-start.20 = (f32[3,384,2]{1,2,0:T(2,128)S(1)}, f32[3,384,2]{1,2,0:T(2,128)S(1)}, u32[]{:S(2)}, u32[]{:S(2)}) collective-permute-start(f32[3,384,2]{1,2,0:T(2,128)S(1)} %pad_maximum_fusion.2), channel_id=1, source_target_pairs={{0,2},{1,3},{2,0},{3,1},{4,6},{5,7},{6,4},{7,5},{8,10},{9,11},{10,... | collective-permute-start | bytes 27656 | tf_op jit(solution)/shard_map/ppermute | solution.py:90
  173.4 5.3 %collective-permute-start.21 = (f32[3,384,2]{1,2,0:T(2,128)S(1)}, f32[3,384,2]{1,2,0:T(2,128)S(1)}, u32[]{:S(2)}, u32[]{:S(2)}) collective-permute-start(f32[3,384,2]{1,2,0:T(2,128)S(1)} %pad_maximum_fusion.3), channel_id=1, source_target_pairs={{0,4},{1,5},{2,6},{3,7},{4,0},{5,1},{6,2},{7,3},{8,12},{9,13},{10,... | collective-permute-start | bytes 27656 | tf_op jit(solution)/shard_map/ppermute | solution.py:90
  178.7 3.7 %collective-permute-start.22 = (f32[3,384,2]{1,2,0:T(2,128)S(1)}, f32[3,384,2]{1,2,0:T(2,128)S(1)}, u32[]{:S(2)}, u32[]{:S(2)}) collective-permute-start(f32[3,384,2]{1,2,0:T(2,128)S(1)} %pad_maximum_fusion.4), channel_id=1, source_target_pairs={{0,8},{1,9},{2,10},{3,11},{4,12},{5,13},{6,14},{7,15},{8,0},{9,1},... | collective-permute-start | bytes 27656 | tf_op jit(solution)/shard_map/ppermute | solution.py:90
  182.5 5.3 %collective-permute-start.23 = (f32[3,384,2]{1,2,0:T(2,128)S(1)}, f32[3,384,2]{1,2,0:T(2,128)S(1)}, u32[]{:S(2)}, u32[]{:S(2)}) collective-permute-start(f32[3,384,2]{1,2,0:T(2,128)S(1)} %pad_maximum_fusion.5), channel_id=1, source_target_pairs={{0,16},{1,17},{2,18},{3,19},{4,20},{5,21},{6,22},{7,23},{8,24},{9,... | collective-permute-start | bytes 27656 | tf_op jit(solution)/shard_map/ppermute | solution.py:90
  188.0 3.7 %collective-permute-start.24 = (f32[3,16]{1,0:T(4,128)S(1)}, f32[3,16]{1,0:T(4,128)S(1)}, u32[]{:S(2)}, u32[]{:S(2)}) collective-permute-start(f32[3,16]{1,0:T(4,128)S(1)} %pad_maximum_fusion.6), channel_id=1, source_target_pairs={{0,32},{32,0},{64,96},{96,64},{128,160},{160,128},{192,224},{224,1... | collective-permute-start | bytes 584 | tf_op jit(solution)/shard_map/ppermute | solution.py:111
  191.7 4.6 %collective-permute-start.25 = (f32[3,16]{1,0:T(4,128)S(1)}, f32[3,16]{1,0:T(4,128)S(1)}, u32[]{:S(2)}, u32[]{:S(2)}) collective-permute-start(f32[3,16]{1,0:T(4,128)S(1)} %pad_maximum_fusion.7), channel_id=1, source_target_pairs={{0,64},{32,96},{64,0},{96,32},{128,192},{160,224},{192,128},{224,1... | collective-permute-start | bytes 584 | tf_op jit(solution)/shard_map/ppermute | solution.py:111
  196.3 7.6 %collective-permute-start.26 = (f32[3,16]{1,0:T(4,128)S(1)}, f32[3,16]{1,0:T(4,128)S(1)}, u32[]{:S(2)}, u32[]{:S(2)}) collective-permute-start(f32[3,16]{1,0:T(4,128)S(1)} %pad_maximum_fusion.8), channel_id=1, source_target_pairs={{0,128},{32,160},{64,192},{96,224},{128,0},{160,32},{192,64},{224,... | collective-permute-start | bytes 584 | tf_op jit(solution)/shard_map/ppermute | solution.py:111
Sparse Core Ops, SparseCore 0:
  9.9 66.7 all-gather.1
